TPU v7x, 256 devices: a whole 4x4x8 slice. The times are simulated.
256 devices in a mesh: ctx: 32 (over y, x, core), tp: 8 (over z).
Axes of the slice: x: 4, y: 4, z: 8, core: 2. Of those that a mesh axis runs over, the one named last changes fastest.
Arguments:
- queries: bfloat16 [24576, 8192], P('ctx', 'tp'), may hold values from -6 to 6
- keys: bfloat16 [24576, 8192], P('ctx', 'tp'), may hold values from -6 to 6
- values: bfloat16 [24576, 8192], P('ctx', 'tp'), may hold values from -40 to 40
- out_grad: bfloat16 [24576, 8192], P('ctx', 'tp'), may hold values from -6 to 6
- gain: float32 [8192], P('tp'), may hold values from 0.1 to 1.9
- doc_ids: int32 [24576], P('ctx'), may hold values from 0 to 7, never falling along the last dimension, each value on 1 to 12288 neighbouring positions
Outputs:
- normed: bfloat16 [24576, 8192], P('ctx', 'tp')
- grad_query: bfloat16 [24576, 8192], P('ctx', 'tp')
- grad_key: bfloat16 [24576, 8192], P('ctx', 'tp')
- grad_value: bfloat16 [24576, 8192], P('ctx', 'tp')
Inputs may be any that keep to these rules, and one draw needn't show every extreme that they name: doc_ids never fall along the sequence; every one of the 8 documents has 1 to 12288 tokens and one has exactly 12288.
All inputs are finite; a program needn't handle non-finite values.
Results may differ from a plain program's by a relative error of at most 0.0062.
Values may be sent and summed in bfloat16 or wider, within the bound.
No kernel may reach another device: no remote copies, remote signals or barrier semaphores. Data moves between devices by JAX's collectives and lax.ppermute only.
A program may use at most 128 MiB of HBM per device.

v0:
```python
import jax
import jax.numpy as jnp
from jax import lax
from jax.sharding import PartitionSpec as P

HEADS = 64
HD = 128


NORM_EPS = 1e-06
BIG_TAG = 1000000000.0


def carried_in(shard, axis, join, neutral, backward):
    count = lax.axis_size(axis)
    place = lax.axis_index(axis)
    ahead = count - 1 - place if backward else place
    gathered = jax.tree.map(
        lambda a, kind: lax.all_gather(a.astype(kind), axis), shard, (jnp.bfloat16, jnp.bfloat16)
    )
    state = jax.tree.map(lambda a, e: jnp.zeros_like(a) + jnp.asarray(e, a.dtype), shard, neutral)

    def one(step, state):
        source = count - 1 - step if backward else step
        return join(
            state,
            jax.tree.map(
                lambda a, own: lax.dynamic_index_in_dim(a, source, 0, False).astype(own.dtype),
                gathered,
                shard,
            ),
        )

    return lax.fori_loop(0, ahead, one, state)


def keep_largest(earlier, later_part):
    top_tag = jnp.maximum(earlier[1], later_part[1])
    summed = jnp.where(earlier[1] == top_tag, earlier[0], 0.0) + jnp.where(
        later_part[1] == top_tag, later_part[0], 0.0
    )
    return (summed, top_tag)


def keep_smallest(earlier, later_part):
    low_tag = jnp.minimum(earlier[1], later_part[1])
    summed = jnp.where(earlier[1] == low_tag, earlier[0], 0.0) + jnp.where(
        later_part[1] == low_tag, later_part[0], 0.0
    )
    return (summed, low_tag)


def shards(queries, keys, values, out_grad, gain, doc_ids):
    tokens_here = queries.shape[0]
    heads_here = queries.shape[1] // HD
    width_all = HEADS * HD
    flat_width = heads_here * HD
    query_heads = queries.reshape(tokens_here, heads_here, HD).transpose(1, 0, 2)
    key_heads = keys.reshape(tokens_here, heads_here, HD).transpose(1, 0, 2)
    value_heads = values.reshape(tokens_here, heads_here, HD).transpose(1, 0, 2)
    position = jnp.arange(tokens_here)
    doc_mask = (
        (doc_ids[:, None] == doc_ids[None, :]) & (position[:, None] >= position[None, :])
    ).astype(jnp.bfloat16)
    first_doc = doc_ids[0]
    last_doc = doc_ids[tokens_here - 1]
    first_rows = (doc_ids == first_doc).astype(jnp.bfloat16)[None, :, None]
    last_rows = (doc_ids == last_doc).astype(jnp.bfloat16)[None, :, None]
    zero_state = jnp.zeros((heads_here, HD, HD), jnp.float32)
    query_first = query_heads * first_rows
    key_last = key_heads * last_rows
    value_last = value_heads * last_rows
    own_state = jnp.einsum(
        "hta,htb->hab", key_last, value_heads, preferred_element_type=jnp.float32
    ).astype(jnp.bfloat16)
    before, before_tag = carried_in(
        (own_state.astype(jnp.float32), last_doc.astype(jnp.float32)),
        "ctx",
        keep_largest,
        (zero_state, jnp.float32(-1.0)),
        False,
    )
    incoming = jnp.where(before_tag == first_doc.astype(jnp.float32), before, 0.0).astype(
        jnp.bfloat16
    )
    scores = (
        jnp.einsum("hta,hsa->hts", query_heads, key_heads, preferred_element_type=jnp.float32)
        * doc_mask[None]
    ).astype(jnp.bfloat16)
    attended_heads = jnp.einsum(
        "htk,hkb->htb",
        jnp.concatenate([scores, query_first], axis=2),
        jnp.concatenate([value_heads, incoming], axis=1),
        preferred_element_type=jnp.float32,
    )
    flat = attended_heads.transpose(1, 0, 2).reshape(tokens_here, flat_width)
    scaled_grad = gain[None, :] * out_grad.astype(jnp.float32)
    square_sum, cross_sum = lax.psum(
        (jnp.sum(flat * flat, axis=1), jnp.sum(scaled_grad * flat, axis=1)), "tp"
    )
    inverse = lax.rsqrt(square_sum / width_all + NORM_EPS)
    normed = (flat * inverse[:, None] * gain[None, :]).astype(jnp.bfloat16)
    delta = (
        inverse[:, None] * scaled_grad - flat * (inverse**3 * cross_sum / width_all)[:, None]
    ).astype(jnp.bfloat16)
    delta_heads = delta.reshape(tokens_here, heads_here, HD).transpose(1, 0, 2)
    own_reverse = jnp.einsum(
        "hta,htb->hab", query_first, delta_heads, preferred_element_type=jnp.float32
    ).astype(jnp.bfloat16)
    after, after_tag = carried_in(
        (own_reverse.astype(jnp.float32), first_doc.astype(jnp.float32)),
        "ctx",
        keep_smallest,
        (zero_state, jnp.float32(BIG_TAG)),
        True,
    )
    outgoing = jnp.where(after_tag == last_doc.astype(jnp.float32), after, 0.0).astype(jnp.bfloat16)
    dscores = (
        jnp.einsum("htb,hsb->hts", delta_heads, value_heads, preferred_element_type=jnp.float32)
        * doc_mask[None]
    ).astype(jnp.bfloat16)
    grad_query = jnp.einsum(
        "htk,hka->hta",
        jnp.concatenate([dscores, delta_heads * first_rows], axis=2),
        jnp.concatenate([key_heads, incoming.transpose(0, 2, 1)], axis=1),
        preferred_element_type=jnp.float32,
    )
    grad_key = jnp.einsum(
        "hks,hka->hsa",
        jnp.concatenate([dscores, value_last.transpose(0, 2, 1)], axis=1),
        jnp.concatenate([query_heads, outgoing.transpose(0, 2, 1)], axis=1),
        preferred_element_type=jnp.float32,
    )
    grad_value = jnp.einsum(
        "hks,hkb->hsb",
        jnp.concatenate([scores, key_last.transpose(0, 2, 1)], axis=1),
        jnp.concatenate([delta_heads, outgoing], axis=1),
        preferred_element_type=jnp.float32,
    )
    return (
        normed,
        grad_query.astype(jnp.bfloat16).transpose(1, 0, 2).reshape(tokens_here, flat_width),
        grad_key.astype(jnp.bfloat16).transpose(1, 0, 2).reshape(tokens_here, flat_width),
        grad_value.astype(jnp.bfloat16).transpose(1, 0, 2).reshape(tokens_here, flat_width),
    )


def solution(mesh):
    in_specs = (P("ctx", "tp"), P("ctx", "tp"), P("ctx", "tp"), P("ctx", "tp"), P("tp"), P("ctx"))
    out_specs = (P("ctx", "tp"), P("ctx", "tp"), P("ctx", "tp"), P("ctx", "tp"))
    return jax.shard_map(shards, mesh=mesh, in_specs=in_specs, out_specs=out_specs, check_vma=False)
```

profile of v0, /device:TPU:32, one launch (start us, length us, event | category | flops | bytes accessed | tf_op | source)
XLA Modules:
  0.0 399.0 jit_solution(2660360565029537263)
XLA Ops:
  7.2 1.3 fusion.67
  8.6 1.7 copy.56
  10.3 2.3 copy.54
  12.6 1.3 compare_convert_fusion
  13.9 1.3 fusion.53
  18.7 68.2 %all-reduce.3 = (bf16[32]{0:T(256)(128)(2,1)S(1)}, bf16[32]{0:T(256)(128)(2,1)S(1)}) all-reduce(bf16[32]{0:T(256)(128)(2,1)S(1)} %dynamic-update-slice, bf16[32]{0:T(256)(128)(2,1)S(1)} %dynamic-update-slice.1), channel_id=1, replica_groups=mesh['ctx'=32,'tp'=8] {'ctx'}, use_global_device_ids=true, to_apply=%add | all-reduce | flops 64 | bytes 256
  86.9 2.6 copy.52
  89.4 1.9 copy.53
  91.4 3.2 copy.60
  94.8 1.4 broadcast_multiply_fusion.1
  96.7 5.1 %multiply_convert_fusion.1 = bf16[8,768,768]{2,1,0:T(8,128)(2,1)} fusion(f32[768,768]{1,0:T(8,128)S(1)} %fusion.56, bf16[8,768,128]{1,2,0:T(8,128)(2,1)S(1)} %bitcast.84, bf16[768,8,128]{2,0,1:T(8,128)(2,1)S(1)} %copy.53), kind=kOutput, calls=%fused_computation.3 | convolution fusion | flops 1217396736 | bytes 14942208 | tf_op jit(solution)/shard_map/hta,hsa->hts/dot_general | solution.py:87
  102.1 6.7 %fusion.21 = (f32[768]{0:T(1024)S(1)}, f32[8,768,128]{1,2,0:T(8,128)S(1)}) fusion(bf16[8,128,128]{1,2,0:T(8,128)(2,1)S(1)} %select_convert_fusion.1, bf16[8,768,128]{1,2,0:T(8,128)(2,1)} %bitcast.88, bf16[8,768,128]{2,1,0:T(8,128)(2,1)} %broadcast_multiply_fusion.1, bf16[8,768,768]{2,1,0:T(8,128)(2,1)} %multiply_convert_fusion.1), kind=kOutput, calls=%fused_computation.29 | convolution fusion | flops 1436548352 | bytes 15993856 | tf_op jit(solution)/shard_map/htk,hkb->htb/dot_general | solution.py:90
  109.3 1.1 copy-done.6
  110.5 18.2 %all-reduce.2 = (f32[768]{0:T(1024)S(1)}, f32[768]{0:T(1024)S(1)}) all-reduce(f32[768]{0:T(1024)S(1)} %get-tuple-element.209, f32[768]{0:T(1024)S(1)} %fusion.18), channel_id=1, replica_groups=mesh['ctx'=32,'tp'=8] {'tp'}, use_global_device_ids=true, to_apply=%region_3.4 | all-reduce | flops 1536 | bytes 12288 | tf_op jit(solution)/shard_map/psum | solution.py:98
  128.8 4.4 %fusion.20 = (bf16[768,1024]{0,1:T(8,128)(2,1)}, bf16[768,1024]{0,1:T(8,128)(2,1)}) fusion(f32[8,768,128]{1,2,0:T(8,128)} %copy-done.6, bf16[768,1024]{0,1:T(8,128)(2,1)S(1)} %copy-done.5, f32[768]{0:T(1024)S(1)} %get-tuple-element.201, f32[1024]{0:T(1024)S(1)} %copy-done.10, f32[768]{0:T(1024)S(1)} %get-tuple-element.202), kind=kLoop, calls=%fused_computation.27 | loop fusion | flops 7077888 | bytes 7874560 | tf_op jit(solution)/shard_map/convert_element_type | solution.py:105
  133.2 1.9 copy.61
  135.1 2.7 convolution_convert_fusion
  137.9 3.3 multiply_bitcast_fusion
  143.2 1.5 copy-done.1
  144.7 4.3 %multiply_convert_fusion = bf16[8,768,768]{2,1,0:T(8,128)(2,1)S(1)} fusion(f32[768,768]{1,0:T(8,128)S(1)} %copy-done.1, bf16[8,768,128]{1,2,0:T(8,128)(2,1)} %bitcast.90, bf16[768,8,128]{2,0,1:T(8,128)(2,1)S(1)} %copy.61), kind=kOutput, calls=%fused_computation.2 | convolution fusion | flops 1217396736 | bytes 14942208 | tf_op jit(solution)/shard_map/htb,hsb->hts/dot_general | solution.py:119
  149.0 4.6 %fusion.46 = bf16[8,768,128]{1,2,0:T(8,128)(2,1)} fusion(bf16[8,128,128]{1,2,0:T(8,128)(2,1)S(1)} %copy.63, bf16[8,768,128]{1,2,0:T(8,128)(2,1)S(1)} %bitcast.86, bf16[8,768,128]{2,1,0:T(8,128)(2,1)S(1)} %broadcast_multiply_fusion, bf16[8,768,768]{2,1,0:T(8,128)(2,1)S(1)} %multiply_convert_fusion), kind=kOutput, calls=%fused_computation.48 | convolution fusion | flops 1435762688 | bytes 14417920 | tf_op jit(solution)/shard_map/htk,hka->hta/dot_general | solution.py:122
  153.7 2.7 copy.71
  156.4 1.6 copy.70
  158.0 122.8 %all-gather.7.cloned.1.call-done = bf16[256,128,128]{2,1,0:T(8,128)(2,1)} async-done(((bf16[8,128,128]{2,1,0:T(8,128)(2,1)}), bf16[256,128,128]{2,1,0:T(8,128)(2,1)}) %all-gather.7.cloned.1.call-update) | async-done | bytes 8388624 | tf_op jit(solution)/shard_map/all_gather | solution.py:19
  280.8 95.0 %while.27 = (s32[]{:T(128)}, f32[8,128,128]{2,1,0:T(8,128)S(1)}, f32[]{:T(128)}, s32[]{:T(128)}, bf16[32]{0:T(256)(128)(2,1)S(1)}, /*index=5*/bf16[32,8,128,128]...) while((s32[]{:T(128)}, f32[8,128,128]{2,1,0:T(8,128)S(1)}, f32[]{:T(128)}, s32[]{:T(128)}, ...), condition=%wide.region_7.8_spmd, body=%wide.region_6.7_spmd.sunk | while | flops 524297 | bytes 1310915 | solution.py:34
  295.0 1.1 bitcast_add_fusion.5
  298.1 1.1 bitcast_add_fusion.5
  313.4 1.1 bitcast_add_fusion.5
  376.3 6.2 %fusion.36 = bf16[8,768,128]{1,2,0:T(8,128)(2,1)} fusion(bf16[8,128,128]{2,1,0:T(8,128)(2,1)S(1)} %copy.68, bf16[8,768,128]{2,1,0:T(8,128)(2,1)S(1)} %bitcast.81, bf16[8,128,768]{2,1,0:T(8,128)(2,1)} %get-tuple-element.207, bf16[8,768,768]{2,1,0:T(8,128)(2,1)} %multiply_convert_fusion.1), kind=kOutput, calls=%fused_computation.46 | convolution fusion | flops 1435762688 | bytes 14417920 | tf_op jit(solution)/shard_map/hks,hkb->hsb/dot_general | solution.py:134
  382.5 2.7 copy.73
  385.2 5.3 %fusion.41 = bf16[8,768,128]{1,2,0:T(8,128)(2,1)S(1)} fusion(bf16[8,128,128]{2,1,0:T(8,128)(2,1)S(1)} %fusion.72, bf16[8,768,128]{2,1,0:T(8,128)(2,1)S(1)} %bitcast.82, bf16[8,128,768]{2,1,0:T(8,128)(2,1)} %get-tuple-element.208, bf16[8,768,768]{2,1,0:T(8,128)(2,1)} %copy-done.7), kind=kOutput, calls=%fused_computation.47 | convolution fusion | flops 1435762688 | bytes 14417920 | tf_op jit(solution)/shard_map/hks,hka->hsa/dot_general | solution.py:128
  390.5 1.6 copy.72
  (106 shorter events, 56.4 us)
Async XLA Ops:
  7.2 94.6 %all-gather.5.cloned.1.call-start = ((), (), s32[]{:S(2)}) async-start(), calls=%async_computation | async-start | bytes 8650752 | tf_op jit(solution)/shard_map/all_gather | solution.py:19
  10.3 4.9 %copy-start.4 = (bf16[768,1024]{0,1:T(8,128)(2,1)}, bf16[768,1024]{0,1:T(8,128)(2,1)S(1)}, u32[]{:S(2)}) copy-start(bf16[768,1024]{0,1:T(8,128)(2,1)S(1)} %copy.56) | copy-start | bytes 4718596
  10.3 2.3 copy-start.9
  13.9 2.7 copy-start.11
  15.2 265.6 %all-gather.7.cloned.1.call-start = ((), (), s32[]{:S(2)}) async-start(), calls=%async_computation.1 | async-start | bytes 8650752 | tf_op jit(solution)/shard_map/all_gather | solution.py:19
  91.4 4.9 %copy-start.2 = (bf16[768,8,128]{2,0,1:T(8,128)(2,1)}, bf16[768,8,128]{2,0,1:T(8,128)(2,1)S(1)}, u32[]{:S(2)}) copy-start(bf16[768,8,128]{2,0,1:T(8,128)(2,1)S(1)} %copy.53) | copy-start | bytes 4718596
  94.8 1.9 copy-start
  102.0 6.8 %copy-start.5 = (bf16[768,1024]{0,1:T(8,128)(2,1)S(1)}, bf16[768,1024]{0,1:T(8,128)(2,1)}, u32[]{:S(2)}) copy-start(bf16[768,1024]{0,1:T(8,128)(2,1)} %copy.60) | copy-start | bytes 4718596
  102.1 6.8 %copy-start.10 = (f32[1024]{0:T(1024)S(1)}, f32[1024]{0:T(1024)}, u32[]{:S(2)}) copy-start(f32[1024]{0:T(1024)} %param.14) | copy-start | bytes 12292
  108.8 1.7 copy-start.6
  143.0 1.7 copy-start.1
  149.0 4.7 %copy-start.7 = (bf16[8,768,768]{2,1,0:T(8,128)(2,1)}, bf16[8,768,768]{2,1,0:T(8,128)(2,1)S(1)}, u32[]{:S(2)}) copy-start(bf16[8,768,768]{2,1,0:T(8,128)(2,1)S(1)} %multiply_convert_fusion) | copy-start | bytes 28311556
  153.7 2.7 copy-start.8
  382.5 2.7 copy-start.3
Sparse Core Ops, SparseCore 0:
  15.3 60.6 all-gather.4
  138.0 142.7 all-gather.6
where the time goes:
time: 401 us; the launch traced here: 399 us
  waiting for transfers between devices  123 us (31%)
  blocking collectives  86.4 us (22%)
  local copies, waits for them, and re-layouts  48.7 us (12%)
  other arithmetic  47.7 us (12%)
  loops' own time  41.5 us (10%)
  matrix products  36.3 us (9%)
  between operations  15.7 us (4%)
    all_gather x2, waiting for transfers between devices, carried_in(): lax.all_gather(a.astype(kind), axis)  123 us
    unnamed x1, blocking collectives  68.2 us
    another operation x2, loops' own time, carried_in(): return lax.fori_loop(0, ahead, one, state)  41.5 us
    add x31, other arithmetic, keep_smallest(): jnp.where(earlier[1] == low_tag, earlier[0], 0.0)  35.4 us
    unnamed x37, local copies, waits for them, and re-layouts  23.6 us
    psum x1, blocking collectives, shards(): lax.psum((jnp.sum(flat * flat, axis=1), jnp.sum(scaled_grad * flat, axis=...  18.2 us
    dynamic_slice x31, local copies, waits for them, and re-layouts, one(): lax.dynamic_index_in_dim(a, source, 0, False).astype(own.dtype)  18.2 us
  transfers between devices with their start and end apart: 2, of which 1 were waited for; matrix products, arithmetic and copies ran while one was open for 9% of the time, Pallas kernels for 0%

commit v1 on v0

--- a/solution.py
+++ b/solution.py
@@ -8,46 +8,41 @@
 
 
 NORM_EPS = 1e-06
-BIG_TAG = 1000000000.0
 
 
-def carried_in(shard, axis, join, neutral, backward):
-    count = lax.axis_size(axis)
-    place = lax.axis_index(axis)
-    ahead = count - 1 - place if backward else place
-    gathered = jax.tree.map(
-        lambda a, kind: lax.all_gather(a.astype(kind), axis), shard, (jnp.bfloat16, jnp.bfloat16)
-    )
-    state = jax.tree.map(lambda a, e: jnp.zeros_like(a) + jnp.asarray(e, a.dtype), shard, neutral)
-
-    def one(step, state):
-        source = count - 1 - step if backward else step
-        return join(
-            state,
-            jax.tree.map(
-                lambda a, own: lax.dynamic_index_in_dim(a, source, 0, False).astype(own.dtype),
-                gathered,
-                shard,
-            ),
-        )
-
-    return lax.fori_loop(0, ahead, one, state)
+DOC_MOST = 12288
 
 
-def keep_largest(earlier, later_part):
-    top_tag = jnp.maximum(earlier[1], later_part[1])
-    summed = jnp.where(earlier[1] == top_tag, earlier[0], 0.0) + jnp.where(
-        later_part[1] == top_tag, later_part[0], 0.0
-    )
-    return (summed, top_tag)
+def moved(x, axis, count, by, backward):
+    if backward:
+        pairs = [(i, i - by) for i in range(by, count)]
+    else:
+        pairs = [(i, i + by) for i in range(count - by)]
+    return lax.ppermute(x, axis, pairs)
 
 
-def keep_smallest(earlier, later_part):
-    low_tag = jnp.minimum(earlier[1], later_part[1])
-    summed = jnp.where(earlier[1] == low_tag, earlier[0], 0.0) + jnp.where(
-        later_part[1] == low_tag, later_part[0], 0.0
-    )
-    return (summed, low_tag)
+def carried(state, first_tag, last_tag, tokens_here, axis, backward):
+    count = lax.axis_size(axis)
+    window = min((DOC_MOST - 1) // tokens_here + 1, count)
+    link_tag = first_tag if backward else last_tag
+    meet_tag = last_tag if backward else first_tag
+    near_tag = moved(link_tag, axis, count, 1, backward)
+    own_link = (near_tag == link_tag).astype(jnp.float32)
+    own_meet = (near_tag == meet_tag).astype(jnp.float32)
+    total = moved(state, axis, count, 1, backward).astype(jnp.float32)
+    link = moved(own_link, axis, count, 1, backward)
+    span = 1
+    if window > 1:
+        total = total + link * moved(state, axis, count, 2, backward).astype(jnp.float32)
+        link = link * moved(own_link, axis, count, 2, backward)
+        span = 2
+    while span < window:
+        far_total = moved(total, axis, count, span, backward)
+        far_link = moved(link, axis, count, span, backward)
+        total = total + link * far_total
+        link = link * far_link
+        span = span * 2
+    return (own_meet * total).astype(jnp.bfloat16)
 
 
 def shards(queries, keys, values, out_grad, gain, doc_ids):
@@ -73,16 +68,9 @@
     own_state = jnp.einsum(
         "hta,htb->hab", key_last, value_heads, preferred_element_type=jnp.float32
     ).astype(jnp.bfloat16)
-    before, before_tag = carried_in(
-        (own_state.astype(jnp.float32), last_doc.astype(jnp.float32)),
-        "ctx",
-        keep_largest,
-        (zero_state, jnp.float32(-1.0)),
-        False,
-    )
-    incoming = jnp.where(before_tag == first_doc.astype(jnp.float32), before, 0.0).astype(
-        jnp.bfloat16
-    )
+    first_tag = first_doc.astype(jnp.float32) + 1.0
+    last_tag = last_doc.astype(jnp.float32) + 1.0
+    incoming = carried(own_state, first_tag, last_tag, tokens_here, "ctx", False)
     scores = (
         jnp.einsum("hta,hsa->hts", query_heads, key_heads, preferred_element_type=jnp.float32)
         * doc_mask[None]
@@ -107,14 +95,7 @@
     own_reverse = jnp.einsum(
         "hta,htb->hab", query_first, delta_heads, preferred_element_type=jnp.float32
     ).astype(jnp.bfloat16)
-    after, after_tag = carried_in(
-        (own_reverse.astype(jnp.float32), first_doc.astype(jnp.float32)),
-        "ctx",
-        keep_smallest,
-        (zero_state, jnp.float32(BIG_TAG)),
-        True,
-    )
-    outgoing = jnp.where(after_tag == last_doc.astype(jnp.float32), after, 0.0).astype(jnp.bfloat16)
+    outgoing = carried(own_reverse, first_tag, last_tag, tokens_here, "ctx", True)
     dscores = (
         jnp.einsum("htb,hsb->hts", delta_heads, value_heads, preferred_element_type=jnp.float32)
         * doc_mask[None]

time: 401 us -> 236 us (0.59)
  the two profiles are of different devices: /device:TPU:32 before, /device:TPU:6 now
where the time goes in v1:
time: 236 us; the launch traced here: 235 us
  starting transfers between devices  75.2 us (32%)
  waiting for transfers between devices  46.5 us (20%)
  matrix products  38.2 us (16%)
  local copies, waits for them, and re-layouts  22.6 us (10%)
  other arithmetic  22.4 us (9%)
  blocking collectives  20.2 us (9%)
  between operations  9.81 us (4%)
    ppermute x20, starting transfers between devices, moved(): return lax.ppermute(x, axis, pairs)  75.2 us
    ppermute x20, waiting for transfers between devices, moved(): return lax.ppermute(x, axis, pairs)  46.5 us
    psum x1, blocking collectives, shards(): lax.psum((jnp.sum(flat * flat, axis=1), jnp.sum(scaled_grad * flat, axis=...  20.2 us
    unnamed x40, local copies, waits for them, and re-layouts  17.1 us
    dot_general x1, matrix products, shards(): jnp.einsum('hta,hsa->hts', query_heads, key_heads, preferred_element_type...  7.68 us
    dot_general x1, matrix products, shards(): jnp.einsum('htk,hkb->htb', jnp.concatenate([scores, query_first], axis=2)...  6.75 us
    dot_general x1, matrix products, shards(): jnp.einsum('htk,hka->hta', jnp.concatenate([dscores, delta_heads * first_...  5.78 us
    dot_general x1, matrix products, shards(): jnp.einsum('hks,hka->hsa', jnp.concatenate([dscores, value_last.transpose...  5.66 us
  transfers between devices with their start and end apart: 20, of which 12 were waited for; matrix products, arithmetic and copies ran while one was open for 14% of the time, Pallas kernels for 0%

profile of v1, /device:TPU:6, one launch (start us, length us, event | category | flops | bytes accessed | tf_op | source)
XLA Modules:
  0.0 235.0 jit_solution(7597388396715725915)
XLA Ops:
  10.5 3.4 %collective-permute-start.3 = (bf16[8,128,128]{1,2,0:T(8,128)(2,1)}, bf16[8,128,128]{1,2,0:T(8,128)(2,1)S(1)}, u32[]{:S(2)}, u32[]{:S(2)}) collective-permute-start(bf16[8,128,128]{1,2,0:T(8,128)(2,1)} %fusion.53), channel_id=1, source_target_pairs={{0,16},{8,24},{16,32},{24,40},{32,48},{40,56},{48,64},{56,72},{64,... | collective-permute-start | bytes 786440 | tf_op jit(solution)/shard_map/ppermute | solution.py:21
  14.6 4.0 %collective-permute-start = (f32[]{:T(128)}, f32[]{:T(128)}, u32[]{:S(2)}, u32[]{:S(2)}) collective-permute-start(f32[]{:T(128)} %add.40), channel_id=1, source_target_pairs={{0,8},{8,16},{16,24},{24,32},{32,40},{40,48},{48,56},{56,64},{64,7... | collective-permute-start | bytes 20 | tf_op jit(solution)/shard_map/ppermute | solution.py:21
  18.6 3.5 %collective-permute-done = f32[]{:T(128)} collective-permute-done((f32[]{:T(128)}, f32[]{:T(128)}, u32[]{:S(2)}, u32[]{:S(2)}) %collective-permute-start) | collective-permute-done | bytes 36 | tf_op jit(solution)/shard_map/ppermute | solution.py:21
  22.7 2.9 %collective-permute-start.2 = (f32[]{:T(128)}, f32[]{:T(128)}, u32[]{:S(2)}, u32[]{:S(2)}) collective-permute-start(f32[]{:T(128)} %convert_element_type.110), channel_id=1, source_target_pairs={{0,8},{8,16},{16,24},{24,32},{32,40},{40,48},{48,56},{56,64},{64,7... | collective-permute-start | bytes 20 | tf_op jit(solution)/shard_map/ppermute | solution.py:21
  28.4 7.6 %collective-permute-start.5 = (f32[8,128,128]{1,2,0:T(8,128)S(1)}, f32[8,128,128]{1,2,0:T(8,128)S(1)}, u32[]{:S(2)}, u32[]{:S(2)}) collective-permute-start(f32[8,128,128]{1,2,0:T(8,128)S(1)} %multiply_add_fusion.5), channel_id=1, source_target_pairs={{0,16},{8,24},{16,32},{24,40},{32,48},{40,56},{48,64},{56,72},{64,... | collective-permute-start | bytes 1572872 | tf_op jit(solution)/shard_map/ppermute | solution.py:21
  39.9 2.6 %copy.34 = bf16[768,1024]{0,1:T(8,128)(2,1)} copy(bf16[768,1024]{1,0:T(8,128)(2,1)} %param.9) | data formatting | bytes 3145728 | tf_op args[3]
  42.5 3.2 %collective-permute-start.4 = (f32[]{:T(128)}, f32[]{:T(128)}, u32[]{:S(2)}, u32[]{:S(2)}) collective-permute-start(f32[]{:T(128)} %convert_element_type.110), channel_id=1, source_target_pairs={{0,16},{8,24},{16,32},{24,40},{32,48},{40,56},{48,64},{56,72},{64,... | collective-permute-start | bytes 20 | tf_op jit(solution)/shard_map/ppermute | solution.py:21
  53.2 6.5 %collective-permute-start.6 = (f32[]{:T(128)}, f32[]{:T(128)}, u32[]{:S(2)}, u32[]{:S(2)}) collective-permute-start(f32[]{:T(128)} %mul.187), channel_id=1, source_target_pairs={{0,16},{8,24},{16,32},{24,40},{32,48},{40,56},{48,64},{56,72},{64,... | collective-permute-start | bytes 20 | tf_op jit(solution)/shard_map/ppermute | solution.py:21
  64.8 4.3 %collective-permute-start.9 = (f32[8,128,128]{1,2,0:T(8,128)S(1)}, f32[8,128,128]{1,2,0:T(8,128)}, u32[]{:S(2)}, u32[]{:S(2)}) collective-permute-start(f32[8,128,128]{1,2,0:T(8,128)S(1)} %multiply_add_fusion.3), channel_id=1, source_target_pairs={{0,64},{8,72},{16,80},{24,88},{32,96},{40,104},{48,112},{56,120},{... | collective-permute-start | bytes 1572872 | tf_op jit(solution)/shard_map/ppermute | solution.py:21
  69.1 7.7 %multiply_convert_fusion.1 = bf16[8,768,768]{2,1,0:T(8,128)(2,1)} fusion(f32[768,768]{1,0:T(8,128)S(1)} %fusion.56, bf16[8,768,128]{1,2,0:T(8,128)(2,1)S(1)} %bitcast.60, bf16[768,8,128]{2,0,1:T(8,128)(2,1)} %copy.28), kind=kOutput, calls=%fused_computation.1 | convolution fusion | flops 1217396736 | bytes 14942208 | tf_op jit(solution)/shard_map/hta,hsa->hts/dot_general | solution.py:75
  77.4 4.8 %collective-permute-start.8 = (f32[]{:T(128)}, f32[]{:T(128)}, u32[]{:S(2)}, u32[]{:S(2)}) collective-permute-start(f32[]{:T(128)} %mul.190), channel_id=1, source_target_pairs={{0,32},{8,40},{16,48},{24,56},{32,64},{40,72},{48,80},{56,88},{64,... | collective-permute-start | bytes 20 | tf_op jit(solution)/shard_map/ppermute | solution.py:21
  86.1 6.7 %fusion.21 = (f32[768]{0:T(1024)S(1)}, f32[8,768,128]{1,2,0:T(8,128)S(1)}) fusion(bf16[8,128,128]{1,2,0:T(8,128)(2,1)S(1)} %multiply_convert_fusion.3, bf16[8,768,128]{1,2,0:T(8,128)(2,1)} %bitcast.64, bf16[8,768,128]{2,1,0:T(8,128)(2,1)} %broadcast_multiply_fusion.1, bf16[8,768,768]{2,1,0:T(8,128)(2,1)} %multiply_convert_fusion.1), kind=kOutput, calls=%fused_computation.27 | convolution fusion | flops 1436548352 | bytes 15993856 | tf_op jit(solution)/shard_map/htk,hkb->htb/dot_general | solution.py:78
  94.5 20.2 %all-reduce = (f32[768]{0:T(1024)S(1)}, f32[768]{0:T(1024)S(1)}) all-reduce(f32[768]{0:T(1024)S(1)} %get-tuple-element.24, f32[768]{0:T(1024)S(1)} %fusion.18), channel_id=1, replica_groups=mesh['ctx'=32,'tp'=8] {'tp'}, use_global_device_ids=true, to_apply=%region_1.0 | all-reduce | flops 1536 | bytes 12288 | tf_op jit(solution)/shard_map/psum | solution.py:86
  114.8 3.9 %fusion.20 = (bf16[768,1024]{0,1:T(8,128)(2,1)S(1)}, bf16[768,1024]{0,1:T(8,128)(2,1)}) fusion(f32[8,768,128]{1,2,0:T(8,128)} %copy-done.10, bf16[768,1024]{0,1:T(8,128)(2,1)S(1)} %copy-done.9, f32[768]{0:T(1024)S(1)} %get-tuple-element.16, f32[1024]{0:T(1024)S(1)} %copy-done.15, f32[768]{0:T(1024)S(1)} %get-tuple-element.17), kind=kLoop, calls=%fused_computation.25 | loop fusion | flops 7077888 | bytes 7874560 | tf_op jit(solution)/shard_map/convert_element_type | solution.py:93
  119.6 2.9 %convolution_convert_fusion = bf16[8,128,128]{2,1,0:T(8,128)(2,1)} fusion(bf16[8,768,128]{2,1,0:T(8,128)(2,1)} %broadcast_multiply_fusion.1, bf16[768,8,128]{2,0,1:T(8,128)(2,1)S(1)} %copy.35), kind=kOutput, calls=%fused_computation.52 | convolution fusion | flops 201457664 | bytes 3407872 | tf_op jit(solution)/shard_map/hta,htb->hab/dot_general | solution.py:95
  126.3 7.9 %collective-permute-start.10 = (f32[]{:T(128)}, f32[]{:T(128)}, u32[]{:S(2)}, u32[]{:S(2)}) collective-permute-start(f32[]{:T(128)} %add.41), channel_id=1, source_target_pairs={{8,0},{16,8},{24,16},{32,24},{40,32},{48,40},{56,48},{64,56},{72,6... | collective-permute-start | bytes 20 | tf_op jit(solution)/shard_map/ppermute | solution.py:21
  134.9 5.4 %collective-permute-start.12 = (f32[]{:T(128)}, f32[]{:T(128)}, u32[]{:S(2)}, u32[]{:S(2)}) collective-permute-start(f32[]{:T(128)} %convert_element_type.122), channel_id=1, source_target_pairs={{8,0},{16,8},{24,16},{32,24},{40,32},{48,40},{56,48},{64,56},{72,6... | collective-permute-start | bytes 20 | tf_op jit(solution)/shard_map/ppermute | solution.py:21
  140.9 2.5 %multiply_add_fusion.2 = f32[8,128,128]{2,1,0:T(8,128)} fusion(bf16[8,128,128]{2,1,0:T(8,128)(2,1)} %collective-permute-done.13, bf16[8,128,128]{2,1,0:T(8,128)(2,1)} %collective-permute-done.11, f32[]{:T(128)} %collective-permute-done.12), kind=kLoop, calls=%fused_computation.60 | loop fusion | flops 524288 | bytes 1048580 | tf_op jit(solution)/shard_map/add | solution.py:36
  145.3 3.3 %multiply_bitcast_fusion = (bf16[8,128,768]{2,1,0:T(8,128)(2,1)}, bf16[8,128,768]{2,1,0:T(8,128)(2,1)}) fusion(bf16[768,8,128]{0,2,1:T(8,128)(2,1)S(1)} %bitcast.61, bf16[768]{0:T(1024)(128)(2,1)S(1)} %get-tuple-element.18, bf16[768,8,128]{0,2,1:T(8,128)(2,1)} %bitcast.65), kind=kLoop, calls=%fused_computation.47 | loop fusion | flops 1572864 | bytes 6292992 | tf_op jit(solution)/shard_map/mul | solution.py:66
  148.6 5.7 %collective-permute-start.14 = (f32[]{:T(128)}, f32[]{:T(128)}, u32[]{:S(2)}, u32[]{:S(2)}) collective-permute-start(f32[]{:T(128)} %convert_element_type.122), channel_id=1, source_target_pairs={{16,0},{24,8},{32,16},{40,24},{48,32},{56,40},{64,48},{72,56},{80,... | collective-permute-start | bytes 20 | tf_op jit(solution)/shard_map/ppermute | solution.py:21
  155.0 4.5 %collective-permute-done.14 = f32[]{:T(128)} collective-permute-done((f32[]{:T(128)}, f32[]{:T(128)}, u32[]{:S(2)}, u32[]{:S(2)}) %collective-permute-start.14) | collective-permute-done | bytes 36 | tf_op jit(solution)/shard_map/ppermute | solution.py:21
  160.8 3.2 %collective-permute-start.16 = (f32[]{:T(128)}, f32[]{:T(128)}, u32[]{:S(2)}, u32[]{:S(2)}) collective-permute-start(f32[]{:T(128)} %mul.216), channel_id=1, source_target_pairs={{16,0},{24,8},{32,16},{40,24},{48,32},{56,40},{64,48},{72,56},{80,... | collective-permute-start | bytes 20 | tf_op jit(solution)/shard_map/ppermute | solution.py:21
  164.0 4.3 %collective-permute-done.16 = f32[]{:T(128)} collective-permute-done((f32[]{:T(128)}, f32[]{:T(128)}, u32[]{:S(2)}, u32[]{:S(2)}) %collective-permute-start.16) | collective-permute-done | bytes 36 | tf_op jit(solution)/shard_map/ppermute | solution.py:21
  169.0 3.2 %collective-permute-start.18 = (f32[]{:T(128)}, f32[]{:T(128)}, u32[]{:S(2)}, u32[]{:S(2)}) collective-permute-start(f32[]{:T(128)} %mul.219), channel_id=1, source_target_pairs={{32,0},{40,8},{48,16},{56,24},{64,32},{72,40},{80,48},{88,56},{96,... | collective-permute-start | bytes 20 | tf_op jit(solution)/shard_map/ppermute | solution.py:21
  172.2 4.6 %collective-permute-done.18 = f32[]{:T(128)} collective-permute-done((f32[]{:T(128)}, f32[]{:T(128)}, u32[]{:S(2)}, u32[]{:S(2)}) %collective-permute-start.18) | collective-permute-done | bytes 36 | tf_op jit(solution)/shard_map/ppermute | solution.py:21
  183.6 2.8 %multiply_convert_fusion = bf16[8,768,768]{2,1,0:T(8,128)(2,1)S(1)} fusion(f32[768,768]{1,0:T(8,128)S(1)} %copy-done.1, bf16[8,768,128]{1,2,0:T(8,128)(2,1)S(1)} %bitcast.66, bf16[768,8,128]{2,0,1:T(8,128)(2,1)S(1)} %copy.35), kind=kOutput, calls=%fused_computation | convolution fusion | flops 1217396736 | bytes 14942208 | tf_op jit(solution)/shard_map/htb,hsb->hts/dot_general | solution.py:100
  186.4 14.1 %collective-permute-done.17 = f32[8,128,128]{2,1,0:T(8,128)} collective-permute-done((f32[8,128,128]{2,1,0:T(8,128)S(1)}, f32[8,128,128]{2,1,0:T(8,128)}, u32[]{:S(2)}, u32[]{:S(2)}) %collective-permute-start.17) | collective-permute-done | bytes 524320 | tf_op jit(solution)/shard_map/ppermute | solution.py:21
  203.8 5.8 %fusion.46 = bf16[8,768,128]{1,2,0:T(8,128)(2,1)} fusion(bf16[8,128,128]{1,2,0:T(8,128)(2,1)S(1)} %copy-done.13, bf16[8,768,128]{1,2,0:T(8,128)(2,1)S(1)} %bitcast.62, bf16[8,768,128]{2,1,0:T(8,128)(2,1)} %broadcast_multiply_fusion, bf16[8,768,768]{2,1,0:T(8,128)(2,1)S(1)} %multiply_convert_fusion), kind=kOutput, calls=%fused_computation.46 | convolution fusion | flops 1435762688 | bytes 14417920 | tf_op jit(solution)/shard_map/htk,hka->hta/dot_general | solution.py:103
  209.6 2.7 %copy.43 = bf16[768,1024]{1,0:T(8,128)(2,1)} copy(bf16[768,1024]{0,1:T(8,128)(2,1)} %bitcast.71) | data formatting | bytes 3145728
  213.9 4.7 %collective-permute-done.19 = f32[8,128,128]{2,1,0:T(8,128)} collective-permute-done((f32[8,128,128]{2,1,0:T(8,128)}, f32[8,128,128]{2,1,0:T(8,128)}, u32[]{:S(2)}, u32[]{:S(2)}) %collective-permute-start.19) | collective-permute-done | bytes 524320 | tf_op jit(solution)/shard_map/ppermute | solution.py:21
  219.9 5.3 %fusion.36 = bf16[8,768,128]{1,2,0:T(8,128)(2,1)S(1)} fusion(bf16[8,128,128]{2,1,0:T(8,128)(2,1)S(1)} %multiply_convert_fusion.2, bf16[8,768,128]{2,1,0:T(8,128)(2,1)S(1)} %bitcast.58, bf16[8,128,768]{2,1,0:T(8,128)(2,1)} %get-tuple-element.22, bf16[8,768,768]{2,1,0:T(8,128)(2,1)} %multiply_convert_fusion.1), kind=kOutput, calls=%fused_computation.44 | convolution fusion | flops 1435762688 | bytes 14417920 | tf_op jit(solution)/shard_map/hks,hkb->hsb/dot_general | solution.py:115
  227.7 5.7 %fusion.41 = bf16[8,768,128]{1,2,0:T(8,128)(2,1)S(1)} fusion(bf16[8,128,128]{2,1,0:T(8,128)(2,1)} %copy.39, bf16[8,768,128]{2,1,0:T(8,128)(2,1)S(1)} %bitcast.67, bf16[8,128,768]{2,1,0:T(8,128)(2,1)} %get-tuple-element.23, bf16[8,768,768]{2,1,0:T(8,128)(2,1)} %copy-done.11), kind=kOutput, calls=%fused_computation.45 | convolution fusion | flops 1435762688 | bytes 14417920 | tf_op jit(solution)/shard_map/hks,hka->hsa/dot_general | solution.py:109
  (78 shorter events, 55.3 us)
Async XLA Ops:
  3.7 4.9 %copy-start.2 = (bf16[768,1024]{0,1:T(8,128)(2,1)}, bf16[768,1024]{0,1:T(8,128)(2,1)S(1)}, u32[]{:S(2)}) copy-start(bf16[768,1024]{0,1:T(8,128)(2,1)S(1)} %copy.29) | copy-start | bytes 4718596
  6.0 2.6 %copy-start.5 = (bf16[768,1024]{0,1:T(8,128)(2,1)}, bf16[768,1024]{0,1:T(8,128)(2,1)S(1)}, u32[]{:S(2)}) copy-start(bf16[768,1024]{0,1:T(8,128)(2,1)S(1)} %copy.31) | copy-start | bytes 4718596
  8.6 19.1 %collective-permute-start.1 = (bf16[8,128,128]{1,2,0:T(8,128)(2,1)}, bf16[8,128,128]{1,2,0:T(8,128)(2,1)S(1)}, u32[]{:S(2)}, u32[]{:S(2)}) collective-permute-start(bf16[8,128,128]{1,2,0:T(8,128)(2,1)} %fusion.53), channel_id=1, source_target_pairs={{0,8},{8,16},{16,24},{24,32},{32,40},{40,48},{48,56},{56,64},{64,7... | collective-permute-start | bytes 786440 | tf_op jit(solution)/shard_map/ppermute | solution.py:21
  10.5 17.2 %collective-permute-start.3 = (bf16[8,128,128]{1,2,0:T(8,128)(2,1)}, bf16[8,128,128]{1,2,0:T(8,128)(2,1)S(1)}, u32[]{:S(2)}, u32[]{:S(2)}) collective-permute-start(bf16[8,128,128]{1,2,0:T(8,128)(2,1)} %fusion.53), channel_id=1, source_target_pairs={{0,16},{8,24},{16,32},{24,40},{32,48},{40,56},{48,64},{56,72},{64,... | collective-permute-start | bytes 786440 | tf_op jit(solution)/shard_map/ppermute | solution.py:21
  14.6 7.5 %collective-permute-start = (f32[]{:T(128)}, f32[]{:T(128)}, u32[]{:S(2)}, u32[]{:S(2)}) collective-permute-start(f32[]{:T(128)} %add.40), channel_id=1, source_target_pairs={{0,8},{8,16},{16,24},{24,32},{32,40},{40,48},{48,56},{56,64},{64,7... | collective-permute-start | bytes 20 | tf_op jit(solution)/shard_map/ppermute | solution.py:21
  22.7 5.0 %collective-permute-start.2 = (f32[]{:T(128)}, f32[]{:T(128)}, u32[]{:S(2)}, u32[]{:S(2)}) collective-permute-start(f32[]{:T(128)} %convert_element_type.110), channel_id=1, source_target_pairs={{0,8},{8,16},{16,24},{24,32},{32,40},{40,48},{48,56},{56,64},{64,7... | collective-permute-start | bytes 20 | tf_op jit(solution)/shard_map/ppermute | solution.py:21
  28.4 20.9 %collective-permute-start.5 = (f32[8,128,128]{1,2,0:T(8,128)S(1)}, f32[8,128,128]{1,2,0:T(8,128)S(1)}, u32[]{:S(2)}, u32[]{:S(2)}) collective-permute-start(f32[8,128,128]{1,2,0:T(8,128)S(1)} %multiply_add_fusion.5), channel_id=1, source_target_pairs={{0,16},{8,24},{16,32},{24,40},{32,48},{40,56},{48,64},{56,72},{64,... | collective-permute-start | bytes 1572872 | tf_op jit(solution)/shard_map/ppermute | solution.py:21
  42.5 5.6 %collective-permute-start.4 = (f32[]{:T(128)}, f32[]{:T(128)}, u32[]{:S(2)}, u32[]{:S(2)}) collective-permute-start(f32[]{:T(128)} %convert_element_type.110), channel_id=1, source_target_pairs={{0,16},{8,24},{16,32},{24,40},{32,48},{40,56},{48,64},{56,72},{64,... | collective-permute-start | bytes 20 | tf_op jit(solution)/shard_map/ppermute | solution.py:21
  49.4 14.4 %collective-permute-start.7 = (f32[8,128,128]{1,2,0:T(8,128)S(1)}, f32[8,128,128]{1,2,0:T(8,128)}, u32[]{:S(2)}, u32[]{:S(2)}) collective-permute-start(f32[8,128,128]{1,2,0:T(8,128)S(1)} %multiply_add_fusion.4), channel_id=1, source_target_pairs={{0,32},{8,40},{16,48},{24,56},{32,64},{40,72},{48,80},{56,88},{64,... | collective-permute-start | bytes 1572872 | tf_op jit(solution)/shard_map/ppermute | solution.py:21
  51.7 17.4 %copy-start = (f32[768,768]{1,0:T(8,128)}, f32[768,768]{1,0:T(8,128)S(1)}, u32[]{:S(2)}) copy-start(f32[768,768]{1,0:T(8,128)S(1)} %fusion.56) | copy-start | bytes 7077892
  53.2 8.4 %collective-permute-start.6 = (f32[]{:T(128)}, f32[]{:T(128)}, u32[]{:S(2)}, u32[]{:S(2)}) collective-permute-start(f32[]{:T(128)} %mul.187), channel_id=1, source_target_pairs={{0,16},{8,24},{16,32},{24,40},{32,48},{40,56},{48,64},{56,72},{64,... | collective-permute-start | bytes 20 | tf_op jit(solution)/shard_map/ppermute | solution.py:21
  62.3 6.8 %copy-start.3 = (bf16[768,1024]{0,1:T(8,128)(2,1)S(1)}, bf16[768,1024]{0,1:T(8,128)(2,1)}, u32[]{:S(2)}) copy-start(bf16[768,1024]{0,1:T(8,128)(2,1)} %copy-done.2) | copy-start | bytes 4718596
  64.8 20.1 %collective-permute-start.9 = (f32[8,128,128]{1,2,0:T(8,128)S(1)}, f32[8,128,128]{1,2,0:T(8,128)}, u32[]{:S(2)}, u32[]{:S(2)}) collective-permute-start(f32[8,128,128]{1,2,0:T(8,128)S(1)} %multiply_add_fusion.3), channel_id=1, source_target_pairs={{0,64},{8,72},{16,80},{24,88},{32,96},{40,104},{48,112},{56,120},{... | collective-permute-start | bytes 1572872 | tf_op jit(solution)/shard_map/ppermute | solution.py:21
  77.4 6.9 %collective-permute-start.8 = (f32[]{:T(128)}, f32[]{:T(128)}, u32[]{:S(2)}, u32[]{:S(2)}) collective-permute-start(f32[]{:T(128)} %mul.190), channel_id=1, source_target_pairs={{0,32},{8,40},{16,48},{24,56},{32,64},{40,72},{48,80},{56,88},{64,... | collective-permute-start | bytes 20 | tf_op jit(solution)/shard_map/ppermute | solution.py:21
  86.1 6.8 %copy-start.9 = (bf16[768,1024]{0,1:T(8,128)(2,1)S(1)}, bf16[768,1024]{0,1:T(8,128)(2,1)}, u32[]{:S(2)}) copy-start(bf16[768,1024]{0,1:T(8,128)(2,1)} %copy.34) | copy-start | bytes 4718596
  86.1 6.8 %copy-start.15 = (f32[1024]{0:T(1024)S(1)}, f32[1024]{0:T(1024)}, u32[]{:S(2)}) copy-start(f32[1024]{0:T(1024)} %param.10) | copy-start | bytes 12292
  119.6 25.7 %copy-start.4 = (bf16[768,1024]{0,1:T(8,128)(2,1)S(1)}, bf16[768,1024]{0,1:T(8,128)(2,1)}, u32[]{:S(2)}) copy-start(bf16[768,1024]{0,1:T(8,128)(2,1)} %copy-done.2) | copy-start | bytes 4718596
  122.5 18.4 %collective-permute-start.11 = (bf16[8,128,128]{2,1,0:T(8,128)(2,1)}, bf16[8,128,128]{2,1,0:T(8,128)(2,1)}, u32[]{:S(2)}, u32[]{:S(2)}) collective-permute-start(bf16[8,128,128]{2,1,0:T(8,128)(2,1)} %convolution_convert_fusion), channel_id=1, source_target_pairs={{8,0},{16,8},{24,16},{32,24},{40,32},{48,40},{56,48},{64,56},{72,6... | collective-permute-start | bytes 786440 | tf_op jit(solution)/shard_map/ppermute | solution.py:21
  124.4 16.5 %collective-permute-start.13 = (bf16[8,128,128]{2,1,0:T(8,128)(2,1)}, bf16[8,128,128]{2,1,0:T(8,128)(2,1)}, u32[]{:S(2)}, u32[]{:S(2)}) collective-permute-start(bf16[8,128,128]{2,1,0:T(8,128)(2,1)} %convolution_convert_fusion), channel_id=1, source_target_pairs={{16,0},{24,8},{32,16},{40,24},{48,32},{56,40},{64,48},{72,56},{80,... | collective-permute-start | bytes 786440 | tf_op jit(solution)/shard_map/ppermute | solution.py:21
  126.3 7.9 %collective-permute-start.10 = (f32[]{:T(128)}, f32[]{:T(128)}, u32[]{:S(2)}, u32[]{:S(2)}) collective-permute-start(f32[]{:T(128)} %add.41), channel_id=1, source_target_pairs={{8,0},{16,8},{24,16},{32,24},{40,32},{48,40},{56,48},{64,56},{72,6... | collective-permute-start | bytes 20 | tf_op jit(solution)/shard_map/ppermute | solution.py:21
  134.9 6.0 %collective-permute-start.12 = (f32[]{:T(128)}, f32[]{:T(128)}, u32[]{:S(2)}, u32[]{:S(2)}) collective-permute-start(f32[]{:T(128)} %convert_element_type.122), channel_id=1, source_target_pairs={{8,0},{16,8},{24,16},{32,24},{40,32},{48,40},{56,48},{64,56},{72,6... | collective-permute-start | bytes 20 | tf_op jit(solution)/shard_map/ppermute | solution.py:21
  143.4 36.2 %collective-permute-start.15 = (f32[8,128,128]{2,1,0:T(8,128)}, f32[8,128,128]{2,1,0:T(8,128)}, u32[]{:S(2)}, u32[]{:S(2)}) collective-permute-start(f32[8,128,128]{2,1,0:T(8,128)} %multiply_add_fusion.2), channel_id=1, source_target_pairs={{16,0},{24,8},{32,16},{40,24},{48,32},{56,40},{64,48},{72,56},{80,... | collective-permute-start | bytes 1572872 | tf_op jit(solution)/shard_map/ppermute | solution.py:21
  148.6 10.9 %collective-permute-start.14 = (f32[]{:T(128)}, f32[]{:T(128)}, u32[]{:S(2)}, u32[]{:S(2)}) collective-permute-start(f32[]{:T(128)} %convert_element_type.122), channel_id=1, source_target_pairs={{16,0},{24,8},{32,16},{40,24},{48,32},{56,40},{64,48},{72,56},{80,... | collective-permute-start | bytes 20 | tf_op jit(solution)/shard_map/ppermute | solution.py:21
  160.8 7.5 %collective-permute-start.16 = (f32[]{:T(128)}, f32[]{:T(128)}, u32[]{:S(2)}, u32[]{:S(2)}) collective-permute-start(f32[]{:T(128)} %mul.216), channel_id=1, source_target_pairs={{16,0},{24,8},{32,16},{40,24},{48,32},{56,40},{64,48},{72,56},{80,... | collective-permute-start | bytes 20 | tf_op jit(solution)/shard_map/ppermute | solution.py:21
  169.0 7.8 %collective-permute-start.18 = (f32[]{:T(128)}, f32[]{:T(128)}, u32[]{:S(2)}, u32[]{:S(2)}) collective-permute-start(f32[]{:T(128)} %mul.219), channel_id=1, source_target_pairs={{32,0},{40,8},{48,16},{56,24},{64,32},{72,40},{80,48},{88,56},{96,... | collective-permute-start | bytes 20 | tf_op jit(solution)/shard_map/ppermute | solution.py:21
  178.3 5.3 %copy-start.1 = (f32[768,768]{1,0:T(8,128)S(1)}, f32[768,768]{1,0:T(8,128)}, u32[]{:S(2)}) copy-start(f32[768,768]{1,0:T(8,128)} %copy-done) | copy-start | bytes 7077892
  178.3 5.3 %copy-start.6 = (bf16[768,1024]{0,1:T(8,128)(2,1)S(1)}, bf16[768,1024]{0,1:T(8,128)(2,1)}, u32[]{:S(2)}) copy-start(bf16[768,1024]{0,1:T(8,128)(2,1)} %copy-done.5) | copy-start | bytes 4718596
  181.3 22.5 %copy-start.13 = (bf16[8,128,128]{1,2,0:T(8,128)(2,1)S(1)}, bf16[8,128,128]{1,2,0:T(8,128)(2,1)}, u32[]{:S(2)}) copy-start(bf16[8,128,128]{1,2,0:T(8,128)(2,1)} %copy.37) | copy-start | bytes 786436
  181.3 19.3 %collective-permute-start.17 = (f32[8,128,128]{2,1,0:T(8,128)S(1)}, f32[8,128,128]{2,1,0:T(8,128)}, u32[]{:S(2)}, u32[]{:S(2)}) collective-permute-start(f32[8,128,128]{2,1,0:T(8,128)S(1)} %multiply_add_fusion.1), channel_id=1, source_target_pairs={{32,0},{40,8},{48,16},{56,24},{64,32},{72,40},{80,48},{88,56},{96,... | collective-permute-start | bytes 1572872 | tf_op jit(solution)/shard_map/ppermute | solution.py:21
  186.4 23.2 %copy-start.11 = (bf16[8,768,768]{2,1,0:T(8,128)(2,1)}, bf16[8,768,768]{2,1,0:T(8,128)(2,1)S(1)}, u32[]{:S(2)}) copy-start(bf16[8,768,768]{2,1,0:T(8,128)(2,1)S(1)} %multiply_convert_fusion) | copy-start | bytes 28311556
  202.5 16.1 %collective-permute-start.19 = (f32[8,128,128]{2,1,0:T(8,128)}, f32[8,128,128]{2,1,0:T(8,128)}, u32[]{:S(2)}, u32[]{:S(2)}) collective-permute-start(f32[8,128,128]{2,1,0:T(8,128)} %multiply_add_fusion), channel_id=1, source_target_pairs={{64,0},{72,8},{80,16},{88,24},{96,32},{104,40},{112,48},{120,56},{... | collective-permute-start | bytes 1572872 | tf_op jit(solution)/shard_map/ppermute | solution.py:21
  209.6 2.7 %copy-start.12 = (bf16[768,1024]{0,1:T(8,128)(2,1)S(1)}, bf16[768,1024]{0,1:T(8,128)(2,1)}, u32[]{:S(2)}) copy-start(bf16[768,1024]{0,1:T(8,128)(2,1)} %get-tuple-element.15) | copy-start | bytes 4718596
  (4 other events, 8.9 us)

commit v2 on v1

v2 whole, which is shorter than its diff:
```python
import jax
import jax.numpy as jnp
from jax import lax
from jax.sharding import PartitionSpec as P

HEADS = 64
HD = 128
DOC_MOST = 12288

NORM_EPS = 1e-06


def moved(x, axis, count, by, backward):
    if backward:
        pairs = [(i, i - by) for i in range(by, count)]
    else:
        pairs = [(i, i + by) for i in range(count - by)]
    return lax.ppermute(x, axis, pairs)


def swapped(x, axis, count):
    return lax.ppermute(x, axis, [(i, i ^ 1) for i in range(count)])


def carried(state, firsts, lasts, tokens_here, axis, backward, partial_type):
    count = lax.axis_size(axis)
    index = lax.axis_index(axis)
    if backward:
        link_tags, meet_tags, place = firsts[::-1], lasts[::-1], count - 1 - index
    else:
        link_tags, meet_tags, place = lasts, firsts, index
    earlier = jnp.concatenate([jnp.full((1,), -1.0, jnp.float32), link_tags[:-1]])
    links = (earlier == link_tags).astype(jnp.float32)
    meets = (earlier == meet_tags).astype(jnp.float32)
    chips = count // 2
    terms = min((DOC_MOST - 1) // tokens_here + 1, count)
    window = min((terms + 1) // 2, chips)
    chip_links = links[0::2] * links[1::2]
    padded_links = jnp.concatenate([jnp.zeros((window,), jnp.float32), chip_links])
    chip = place // 2
    core = place % 2
    half = state.shape[0] // 2
    own_half = lax.dynamic_slice_in_dim(state, core * half, half, 0)
    other_half = lax.dynamic_slice_in_dim(state, (1 - core) * half, half, 0)
    partner_half = swapped(other_half, axis, count)
    low = jnp.where(core == 0, own_half, partner_half).astype(jnp.float32)
    high = jnp.where(core == 0, partner_half, own_half).astype(jnp.float32)
    chip_total = high + links[2 * chip + 1] * low
    total = moved(chip_total, axis, count, 2, backward)
    span = 1
    while span < window:
        reach = jnp.prod(lax.dynamic_slice_in_dim(padded_links, chip + window - span, span, 0))
        far = moved(total.astype(partial_type), axis, count, 2 * span, backward)
        total = total + reach * far.astype(jnp.float32)
        span = span * 2
    out_low = meets[2 * chip] * total
    out_high = meets[2 * chip + 1] * (low + links[2 * chip] * total)
    mine = jnp.where(core == 0, out_low, out_high).astype(jnp.bfloat16)
    theirs = jnp.where(core == 0, out_high, out_low).astype(jnp.bfloat16)
    got = swapped(theirs, axis, count)
    return jnp.where(
        core == 0, jnp.concatenate([mine, got], axis=0), jnp.concatenate([got, mine], axis=0)
    )


def group_sum(x, axis):
    count = lax.axis_size(axis)
    step = 1
    while step < count:
        x = x + lax.ppermute(x, axis, [(i, i ^ step) for i in range(count)])
        step = step * 2
    return x


def shards(queries, keys, values, out_grad, gain, doc_ids):
    tokens_here = queries.shape[0]
    heads_here = queries.shape[1] // HD
    width_all = HEADS * HD
    flat_width = heads_here * HD
    query_heads = queries.reshape(tokens_here, heads_here, HD).transpose(1, 0, 2)
    key_heads = keys.reshape(tokens_here, heads_here, HD).transpose(1, 0, 2)
    value_heads = values.reshape(tokens_here, heads_here, HD).transpose(1, 0, 2)
    position = jnp.arange(tokens_here)
    doc_mask = (
        (doc_ids[:, None] == doc_ids[None, :]) & (position[:, None] >= position[None, :])
    ).astype(jnp.bfloat16)
    first_doc = doc_ids[0]
    last_doc = doc_ids[tokens_here - 1]
    ends = lax.all_gather(
        jnp.stack([first_doc, last_doc]).astype(jnp.float32) + 1.0, "ctx"
    )
    firsts, lasts = ends[:, 0], ends[:, 1]
    first_rows = (doc_ids == first_doc).astype(jnp.bfloat16)[None, :, None]
    last_rows = (doc_ids == last_doc).astype(jnp.bfloat16)[None, :, None]
    query_first = query_heads * first_rows
    key_last = key_heads * last_rows
    value_last = value_heads * last_rows
    own_state = jnp.einsum(
        "hta,htb->hab", key_last, value_heads, preferred_element_type=jnp.float32
    ).astype(jnp.bfloat16)
    incoming = carried(own_state, firsts, lasts, tokens_here, "ctx", False, jnp.bfloat16)
    scores = (
        jnp.einsum("hta,hsa->hts", query_heads, key_heads, preferred_element_type=jnp.float32)
        * doc_mask[None]
    ).astype(jnp.bfloat16)
    attended_heads = jnp.einsum(
        "hts,hsb->htb", scores, value_heads, preferred_element_type=jnp.float32
    ) + jnp.einsum("hta,hab->htb", query_first, incoming, preferred_element_type=jnp.float32)
    flat = attended_heads.transpose(1, 0, 2).reshape(tokens_here, flat_width)
    scaled_grad = gain[None, :] * out_grad.astype(jnp.float32)
    sums = group_sum(
        jnp.stack([jnp.sum(flat * flat, axis=1), jnp.sum(scaled_grad * flat, axis=1)]), "tp"
    )
    square_sum, cross_sum = sums[0], sums[1]
    inverse = lax.rsqrt(square_sum / width_all + NORM_EPS)
    normed = (flat * inverse[:, None] * gain[None, :]).astype(jnp.bfloat16)
    delta = (
        inverse[:, None] * scaled_grad - flat * (inverse**3 * cross_sum / width_all)[:, None]
    ).astype(jnp.bfloat16)
    delta_heads = delta.reshape(tokens_here, heads_here, HD).transpose(1, 0, 2)
    own_reverse = jnp.einsum(
        "hta,htb->hab", query_first, delta_heads, preferred_element_type=jnp.float32
    ).astype(jnp.bfloat16)
    outgoing = carried(own_reverse, firsts, lasts, tokens_here, "ctx", True, jnp.bfloat16)
    dscores = (
        jnp.einsum("htb,hsb->hts", delta_heads, value_heads, preferred_element_type=jnp.float32)
        * doc_mask[None]
    ).astype(jnp.bfloat16)
    grad_query = jnp.einsum(
        "hts,hsa->hta", dscores, key_heads, preferred_element_type=jnp.float32
    ) + jnp.einsum(
        "htb,hab->hta", delta_heads * first_rows, incoming, preferred_element_type=jnp.float32
    )
    grad_key = jnp.einsum(
        "hts,hta->hsa", dscores, query_heads, preferred_element_type=jnp.float32
    ) + jnp.einsum("hsb,hab->hsa", value_last, outgoing, preferred_element_type=jnp.float32)
    grad_value = jnp.einsum(
        "hts,htb->hsb", scores, delta_heads, preferred_element_type=jnp.float32
    ) + jnp.einsum("hsa,hab->hsb", key_last, outgoing, preferred_element_type=jnp.float32)
    return (
        normed,
        grad_query.astype(jnp.bfloat16).transpose(1, 0, 2).reshape(tokens_here, flat_width),
        grad_key.astype(jnp.bfloat16).transpose(1, 0, 2).reshape(tokens_here, flat_width),
        grad_value.astype(jnp.bfloat16).transpose(1, 0, 2).reshape(tokens_here, flat_width),
    )


def solution(mesh):
    in_specs = (P("ctx", "tp"), P("ctx", "tp"), P("ctx", "tp"), P("ctx", "tp"), P("tp"), P("ctx"))
    out_specs = (P("ctx", "tp"), P("ctx", "tp"), P("ctx", "tp"), P("ctx", "tp"))
    return jax.shard_map(shards, mesh=mesh, in_specs=in_specs, out_specs=out_specs, check_vma=False)
```

time: 236 us -> 199 us (0.84)
  the two profiles are of different devices: /device:TPU:6 before, /device:TPU:17 now
where the time goes in v2:
time: 199 us; the launch traced here: 197 us
  matrix products  55.8 us (28%)
  starting transfers between devices  42.3 us (21%)
  other arithmetic  30 us (15%)
  local copies, waits for them, and re-layouts  27.9 us (14%)
  blocking collectives  20.9 us (11%)
  waiting for transfers between devices  19.4 us (10%)
    ppermute x8, starting transfers between devices, moved(): return lax.ppermute(x, axis, pairs)  21.6 us
    all_gather x1, blocking collectives, shards(): lax.all_gather(jnp.stack([first_doc, last_doc]).astype(jnp.float32) + 1.0...  20.9 us
    ppermute x8, waiting for transfers between devices, moved(): return lax.ppermute(x, axis, pairs)  16.3 us
    unnamed x41, local copies, waits for them, and re-layouts  14.1 us
    ppermute x3, starting transfers between devices, group_sum(): x = x + lax.ppermute(x, axis, [(i, i ^ step) for i in range(count)])  11.2 us
    ppermute x4, starting transfers between devices, swapped(): return lax.ppermute(x, axis, [(i, i ^ 1) for i in range(count)])  9.46 us
    dot_general x1, matrix products, shards(): jnp.einsum('hts,hsa->hta', dscores, key_heads, preferred_element_type=jnp...  9.11 us
    dot_general x1, matrix products, shards(): jnp.einsum('htb,hsb->hts', delta_heads, value_heads, preferred_element_ty...  9.05 us
  transfers between devices with their start and end apart: 15, of which 7 were waited for; matrix products, arithmetic and copies ran while one was open for 32% of the time, Pallas kernels for 0%

profile of v2, /device:TPU:17, one launch (start us, length us, event | category | flops | bytes accessed | tf_op | source)
XLA Modules:
  0.0 197.2 jit_solution(7664759436001812096)
XLA Ops:
  4.0 2.8 %fusion.20 = bf16[8,128,128]{2,1,0:T(8,128)(2,1)S(1)} fusion(bf16[768]{0:T(1024)(128)(2,1)S(1)} %get-tuple-element.24, bf16[768,1024]{1,0:T(8,128)(2,1)} %param.8, bf16[768,1024]{1,0:T(8,128)(2,1)} %param.7), kind=kOutput, calls=%fused_computation.29 | convolution fusion | flops 204603392 | bytes 3409408 | tf_op jit(solution)/shard_map/hta,htb->hab/dot_general | solution.py:98
  9.0 20.9 %all-gather = f32[32,1,2]{2,1,0:T(1,128)S(1)} all-gather(f32[1,1,2]{2,1,0:T(1,128)S(1)} %fusion.48), channel_id=1, replica_groups=mesh['ctx'=32,'tp'=8] {'ctx'}, dimensions={0}, use_global_device_ids=true | all-gather | bytes 264 | tf_op jit(solution)/shard_map/all_gather | solution.py:89
  31.7 2.8 %collective-permute-start.1 = (f32[4,128,128]{2,1,0:T(8,128)S(1)}, f32[4,128,128]{2,1,0:T(8,128)S(1)}, u32[]{:S(2)}, u32[]{:S(2)}) collective-permute-start(f32[4,128,128]{2,1,0:T(8,128)S(1)} %fusion.36), channel_id=1, source_target_pairs={{0,16},{8,24},{16,32},{24,40},{32,48},{40,56},{48,64},{56,72},{64,... | collective-permute-start | bytes 786440 | tf_op jit(solution)/shard_map/ppermute | solution.py:18
  34.5 8.9 %collective-permute-done.1 = f32[4,128,128]{2,1,0:T(8,128)S(1)} collective-permute-done((f32[4,128,128]{2,1,0:T(8,128)S(1)}, f32[4,128,128]{2,1,0:T(8,128)S(1)}, u32[]{:S(2)}, u32[]{:S(2)}) %collective-permute-start.1) | collective-permute-done | bytes 262176 | tf_op jit(solution)/shard_map/ppermute | solution.py:18
  46.2 5.1 %collective-permute-done.2 = bf16[4,128,128]{2,1,0:T(8,128)(2,1)S(1)} collective-permute-done((bf16[4,128,128]{2,1,0:T(8,128)(2,1)S(1)}, bf16[4,128,128]{2,1,0:T(8,128)(2,1)S(1)}, u32[]{:S(2)}, u32[]{:S(2)}) %collective-permute-start.2) | collective-permute-done | bytes 131104 | tf_op jit(solution)/shard_map/ppermute | solution.py:18
  61.4 2.5 %collective-permute-start.4 = (bf16[4,128,128]{2,1,0:T(8,128)(2,1)S(1)}, bf16[4,128,128]{2,1,0:T(8,128)(2,1)S(1)}, u32[]{:S(2)}, u32[]{:S(2)}) collective-permute-start(bf16[4,128,128]{2,1,0:T(8,128)(2,1)S(1)} %get-tuple-element.16), channel_id=1, source_target_pairs={{0,64},{8,72},{16,80},{24,88},{32,96},{40,104},{48,112},{56,120},{... | collective-permute-start | bytes 393224 | tf_op jit(solution)/shard_map/ppermute | solution.py:18
  63.9 6.9 %multiply_convert_fusion.1 = bf16[8,768,768]{2,1,0:T(8,128)(2,1)} fusion(f32[768,768]{1,0:T(8,128)} %fusion.29, bf16[8,768,128]{1,2,0:T(8,128)(2,1)S(1)} %bitcast.127, bf16[768,1024]{1,0:T(8,128)(2,1)} %param.7), kind=kOutput, calls=%fused_computation.1 | convolution fusion | flops 1217396736 | bytes 14942208 | tf_op jit(solution)/shard_map/hta,hsa->hts/dot_general | solution.py:103
  70.8 3.0 %copy.70 = bf16[96,8,8,128]{3,2,1,0:T(8,128)(2,1)} copy(bf16[96,8,8,128]{3,1,2,0:T(8,128)(2,1)} %bitcast.136) | data formatting | bytes 3145728
  75.1 2.6 %select_convert_fusion.3 = (bf16[4,128,128]{2,1,0:T(8,128)(2,1)S(1)}, bf16[4,128,128]{2,1,0:T(8,128)(2,1)S(1)}) fusion(f32[4,128,128]{2,1,0:T(8,128)S(1)} %get-tuple-element.17, bf16[4,128,128]{2,1,0:T(8,128)(2,1)S(1)} %collective-permute-done.4, f32[]{:T(128)} %bitcast.19, f32[]{:T(128)} %bitcast.18, f32[]{:T(128)} %dynamic-slice_reduce_fusion.2, ...), kind=kLoop, calls=%fused_computation.59 | loop fusion | flops 851968 | bytes 917525 | tf_op jit(solution)/shard_map/convert_element_type | solution.py:58
  77.7 3.7 %collective-permute-start.5 = (bf16[4,128,128]{2,1,0:T(8,128)(2,1)S(1)}, bf16[4,128,128]{2,1,0:T(8,128)(2,1)S(1)}, u32[]{:S(2)}, u32[]{:S(2)}) collective-permute-start(bf16[4,128,128]{2,1,0:T(8,128)(2,1)S(1)} %get-tuple-element.23), channel_id=1, source_target_pairs={{0,8},{8,0},{16,24},{24,16},{32,40},{40,32},{48,56},{56,48},{64,72... | collective-permute-start | bytes 393224 | tf_op jit(solution)/shard_map/ppermute | solution.py:22
  81.4 7.3 %fusion.9 = f32[8,768,128]{1,2,0:T(8,128)S(1)} fusion(bf16[8,768,768]{2,1,0:T(8,128)(2,1)} %multiply_convert_fusion.1, bf16[8,768,128]{2,0,1:T(8,128)(2,1)} %bitcast.139), kind=kOutput, calls=%fused_computation.22 | convolution fusion | flops 1207959552 | bytes 14155776 | tf_op jit(solution)/shard_map/hts,hsb->htb/dot_general | solution.py:106
  91.1 3.6 %copy.41 = f32[768,1024]{1,0:T(8,128)} copy(f32[768,1024]{0,1:T(8,128)} %bitcast.137) | data formatting | bytes 6291456 | tf_op jit(solution)/shard_map/reshape | solution.py:109
  94.7 2.8 %multiply_reduce_fusion = f32[768]{0:T(1024)S(1)} fusion(f32[768,1024]{1,0:T(8,128)} %copy.41, bf16[768,1024]{1,0:T(8,128)(2,1)} %param.9, f32[1024]{0:T(1024)S(1)} %copy-done.11), kind=kLoop, calls=%fused_computation.9 | loop fusion | flops 3144960 | bytes 4725760 | tf_op jit(solution)/shard_map/reduce_sum | solution.py:112
  100.3 3.1 %collective-permute-start.7 = (f32[2,768]{1,0:T(2,128)S(1)}, f32[2,768]{1,0:T(2,128)S(1)}, u32[]{:S(2)}, u32[]{:S(2)}) collective-permute-start(f32[2,768]{1,0:T(2,128)S(1)} %fusion.53), channel_id=1, source_target_pairs={{0,2},{1,3},{2,0},{3,1},{4,6},{5,7},{6,4},{7,5},{8,10},{9,11},{10,... | collective-permute-start | bytes 18440 | tf_op jit(solution)/shard_map/ppermute | solution.py:70
  104.4 6.4 %collective-permute-start.8 = (f32[2,768]{1,0:T(2,128)S(1)}, f32[2,768]{1,0:T(2,128)S(1)}, u32[]{:S(2)}, u32[]{:S(2)}) collective-permute-start(f32[2,768]{1,0:T(2,128)S(1)} %fusion.72), channel_id=1, source_target_pairs={{0,4},{1,5},{2,6},{3,7},{4,0},{5,1},{6,2},{7,3},{8,12},{9,13},{10,... | collective-permute-start | bytes 18440 | tf_op jit(solution)/shard_map/ppermute | solution.py:70
  111.9 4.9 %subtract_convert_fusion = (bf16[768,1024]{1,0:T(8,128)(2,1)}, bf16[768,1024]{1,0:T(8,128)(2,1)}) fusion(f32[768,1024]{1,0:T(8,128)} %copy.41, bf16[768,1024]{1,0:T(8,128)(2,1)} %param.9, f32[768]{0:T(1024)S(1)} %fusion.43, f32[768]{0:T(1024)S(1)} %get-tuple-element.13, f32[1024]{0:T(1024)S(1)} %copy-done.11), kind=kLoop, calls=%fused_computation.7 | loop fusion | flops 7077888 | bytes 7874560 | tf_op jit(solution)/shard_map/convert_element_type | solution.py:119
  116.8 2.6 %copy.65 = bf16[768,1024]{0,1:T(8,128)(2,1)} copy(bf16[768,1024]{1,0:T(8,128)(2,1)} %get-tuple-element.18) | data formatting | bytes 3145728 | tf_op jit(solution)/shard_map/reshape | solution.py:120
  121.4 3.3 %collective-permute-start.9 = (bf16[4,128,128]{2,1,0:T(8,128)(2,1)S(1)}, bf16[4,128,128]{2,1,0:T(8,128)(2,1)S(1)}, u32[]{:S(2)}, u32[]{:S(2)}) collective-permute-start(bf16[4,128,128]{2,1,0:T(8,128)(2,1)S(1)} %constant_dynamic-slice_fusion), channel_id=1, source_target_pairs={{0,8},{8,0},{16,24},{24,16},{32,40},{40,32},{48,56},{56,48},{64,72... | collective-permute-start | bytes 393224 | tf_op jit(solution)/shard_map/ppermute | solution.py:22
  124.9 3.0 %copy.71 = bf16[96,8,8,128]{3,2,1,0:T(8,128)(2,1)} copy(bf16[96,8,8,128]{3,1,2,0:T(8,128)(2,1)} %bitcast.135) | data formatting | bytes 3145728
  133.9 9.0 %multiply_convert_fusion = bf16[8,768,768]{2,1,0:T(8,128)(2,1)} fusion(f32[768,768]{1,0:T(8,128)} %fusion.29, bf16[8,768,128]{1,2,0:T(8,128)(2,1)} %bitcast.132, bf16[768,1024]{1,0:T(8,128)(2,1)} %param.8), kind=kOutput, calls=%fused_computation | convolution fusion | flops 1217396736 | bytes 14942208 | tf_op jit(solution)/shard_map/htb,hsb->hts/dot_general | solution.py:126
  143.6 3.2 %collective-permute-start.11 = (bf16[4,128,128]{2,1,0:T(8,128)(2,1)}, bf16[4,128,128]{2,1,0:T(8,128)(2,1)}, u32[]{:S(2)}, u32[]{:S(2)}) collective-permute-start(bf16[4,128,128]{2,1,0:T(8,128)(2,1)} %convert_element_type.176), channel_id=1, source_target_pairs={{16,0},{24,8},{32,16},{40,24},{48,32},{56,40},{64,48},{72,56},{80,... | collective-permute-start | bytes 393224 | tf_op jit(solution)/shard_map/ppermute | solution.py:18
  146.8 9.1 %fusion.7 = f32[8,768,128]{1,2,0:T(8,128)} fusion(bf16[8,768,768]{2,1,0:T(8,128)(2,1)} %multiply_convert_fusion, bf16[8,768,128]{2,0,1:T(8,128)(2,1)} %bitcast.138), kind=kOutput, calls=%fused_computation.20 | convolution fusion | flops 1207959552 | bytes 14155776 | tf_op jit(solution)/shard_map/hts,hsa->hta/dot_general | solution.py:129
  157.9 4.7 %collective-permute-start.12 = (bf16[4,128,128]{2,1,0:T(8,128)(2,1)S(1)}, bf16[4,128,128]{2,1,0:T(8,128)(2,1)S(1)}, u32[]{:S(2)}, u32[]{:S(2)}) collective-permute-start(bf16[4,128,128]{2,1,0:T(8,128)(2,1)S(1)} %fusion.41), channel_id=1, source_target_pairs={{32,0},{40,8},{48,16},{56,24},{64,32},{72,40},{80,48},{88,56},{96,... | collective-permute-start | bytes 393224 | tf_op jit(solution)/shard_map/ppermute | solution.py:18
  162.7 4.5 %fusion.62 = f32[8,768,128]{1,2,0:T(8,128)} fusion(bf16[8,768,128]{1,2,0:T(8,128)(2,1)} %bitcast.133, bf16[8,768,768]{2,1,0:T(8,128)(2,1)S(1)} %bitcast.124), kind=kOutput, calls=%fused_computation.112 | convolution fusion | flops 1207959552 | bytes 14155776 | tf_op jit(solution)/shard_map/hts,htb->hsb/dot_general | solution.py:137
  169.4 2.7 %collective-permute-start.13 = (bf16[4,128,128]{2,1,0:T(8,128)(2,1)S(1)}, bf16[4,128,128]{2,1,0:T(8,128)(2,1)S(1)}, u32[]{:S(2)}, u32[]{:S(2)}) collective-permute-start(bf16[4,128,128]{2,1,0:T(8,128)(2,1)S(1)} %get-tuple-element.14), channel_id=1, source_target_pairs={{64,0},{72,8},{80,16},{88,24},{96,32},{104,40},{112,48},{120,56},{... | collective-permute-start | bytes 393224 | tf_op jit(solution)/shard_map/ppermute | solution.py:18
  172.2 3.1 %fusion.61 = f32[8,768,128]{1,2,0:T(8,128)} fusion(bf16[8,768,128]{1,2,0:T(8,128)(2,1)S(1)} %bitcast.130, bf16[8,768,768]{2,1,0:T(8,128)(2,1)S(1)} %bitcast.126), kind=kOutput, calls=%fused_computation.111 | convolution fusion | flops 1207959552 | bytes 14155776 | tf_op jit(solution)/shard_map/hts,hta->hsa/dot_general | solution.py:134
  175.6 3.3 %select_convert_fusion.1 = (bf16[4,128,128]{2,1,0:T(8,128)(2,1)S(1)}, bf16[4,128,128]{2,1,0:T(8,128)(2,1)}) fusion(f32[4,128,128]{2,1,0:T(8,128)S(1)} %get-tuple-element.15, bf16[4,128,128]{2,1,0:T(8,128)(2,1)S(1)} %collective-permute-done.13, f32[]{:T(128)} %bitcast.34, f32[]{:T(128)} %bitcast.33, f32[]{:T(128)} %dynamic-slice_reduce_fusion, f32[]{:T(128)} %bitcast.30, ...), kind=kLoop, calls=%fused_computation.54 | loop fusion | flops 851968 | bytes 917525 | tf_op jit(solution)/shard_map/convert_element_type | solution.py:58
  182.4 2.7 %copy.49 = bf16[768,1024]{1,0:T(8,128)(2,1)} copy(bf16[768,1024]{0,1:T(8,128)(2,1)} %bitcast.140) | data formatting | bytes 3145728
  185.2 3.4 %add_convert_fusion = bf16[8,768,128]{1,2,0:T(8,128)(2,1)} fusion(f32[8,768,128]{1,2,0:T(8,128)S(1)} %copy-done.1, bf16[768]{0:T(1024)(128)(2,1)S(1)} %get-tuple-element.24, bf16[4,128,128]{2,1,0:T(8,128)(2,1)} %collective-permute-done.14, bf16[4,128,128]{2,1,0:T(8,128)(2,1)S(1)} %get-tuple-element.20, pred[]{:T(512)S(6)} %eq.68, bf16[768,1024]{1,0:T(8,128)(2,1)} %param.7), kind=kOutput, calls=%fused_computation.4 | convolution fusion | flops 206438400 | bytes 6555137 | tf_op jit(solution)/shard_map/hsa,hab->hsb/dot_general | solution.py:139
  188.5 2.7 %copy.51 = bf16[768,1024]{1,0:T(8,128)(2,1)} copy(bf16[768,1024]{0,1:T(8,128)(2,1)} %bitcast.142) | data formatting | bytes 3145728
  191.3 3.4 %add_convert_fusion.1 = bf16[8,768,128]{1,2,0:T(8,128)(2,1)} fusion(f32[8,768,128]{1,2,0:T(8,128)S(1)} %copy-done.2, bf16[768]{0:T(1024)(128)(2,1)S(1)} %get-tuple-element.24, bf16[4,128,128]{2,1,0:T(8,128)(2,1)} %collective-permute-done.14, bf16[4,128,128]{2,1,0:T(8,128)(2,1)S(1)} %get-tuple-element.20, pred[]{:T(512)S(6)} %eq.68, bf16[768,1024]{1,0:T(8,128)(2,1)} %param.8), kind=kOutput, calls=%fused_computation.5 | convolution fusion | flops 206438400 | bytes 6555137 | tf_op jit(solution)/shard_map/hsb,hab->hsa/dot_general | solution.py:136
  194.7 2.6 %copy.50 = bf16[768,1024]{1,0:T(8,128)(2,1)} copy(bf16[768,1024]{0,1:T(8,128)(2,1)} %bitcast.141) | data formatting | bytes 3145728
  (106 shorter events, 45.6 us)
Async XLA Ops:
  6.8 47.0 %copy-start.10 = (s32[768]{0:T(1024)S(1)}, s32[768]{0:T(1024)}, u32[]{:S(2)}) copy-start(s32[768]{0:T(1024)} %param.11) | copy-start | bytes 9220
  6.9 24.1 %collective-permute-start = (bf16[4,128,128]{2,1,0:T(8,128)(2,1)S(1)}, bf16[4,128,128]{2,1,0:T(8,128)(2,1)S(1)}, u32[]{:S(2)}, u32[]{:S(2)}) collective-permute-start(bf16[4,128,128]{2,1,0:T(8,128)(2,1)S(1)} %constant_dynamic-slice_fusion.1), channel_id=1, source_target_pairs={{0,8},{8,0},{16,24},{24,16},{32,40},{40,32},{48,56},{56,48},{64,72... | collective-permute-start | bytes 393224 | tf_op jit(solution)/shard_map/ppermute | solution.py:22
  31.7 11.7 %collective-permute-start.1 = (f32[4,128,128]{2,1,0:T(8,128)S(1)}, f32[4,128,128]{2,1,0:T(8,128)S(1)}, u32[]{:S(2)}, u32[]{:S(2)}) collective-permute-start(f32[4,128,128]{2,1,0:T(8,128)S(1)} %fusion.36), channel_id=1, source_target_pairs={{0,16},{8,24},{16,32},{24,40},{32,48},{40,56},{48,64},{56,72},{64,... | collective-permute-start | bytes 786440 | tf_op jit(solution)/shard_map/ppermute | solution.py:18
  43.4 7.8 %collective-permute-start.2 = (bf16[4,128,128]{2,1,0:T(8,128)(2,1)S(1)}, bf16[4,128,128]{2,1,0:T(8,128)(2,1)S(1)}, u32[]{:S(2)}, u32[]{:S(2)}) collective-permute-start(bf16[4,128,128]{2,1,0:T(8,128)(2,1)S(1)} %convert_element_type.157), channel_id=1, source_target_pairs={{0,16},{8,24},{16,32},{24,40},{32,48},{40,56},{48,64},{56,72},{64,... | collective-permute-start | bytes 393224 | tf_op jit(solution)/shard_map/ppermute | solution.py:18
  51.9 8.1 %collective-permute-start.3 = (bf16[4,128,128]{2,1,0:T(8,128)(2,1)S(1)}, bf16[4,128,128]{2,1,0:T(8,128)(2,1)S(1)}, u32[]{:S(2)}, u32[]{:S(2)}) collective-permute-start(bf16[4,128,128]{2,1,0:T(8,128)(2,1)S(1)} %fusion.40), channel_id=1, source_target_pairs={{0,32},{8,40},{16,48},{24,56},{32,64},{40,72},{48,80},{56,88},{64,... | collective-permute-start | bytes 393224 | tf_op jit(solution)/shard_map/ppermute | solution.py:18
  61.4 13.7 %collective-permute-start.4 = (bf16[4,128,128]{2,1,0:T(8,128)(2,1)S(1)}, bf16[4,128,128]{2,1,0:T(8,128)(2,1)S(1)}, u32[]{:S(2)}, u32[]{:S(2)}) collective-permute-start(bf16[4,128,128]{2,1,0:T(8,128)(2,1)S(1)} %get-tuple-element.16), channel_id=1, source_target_pairs={{0,64},{8,72},{16,80},{24,88},{32,96},{40,104},{48,112},{56,120},{... | collective-permute-start | bytes 393224 | tf_op jit(solution)/shard_map/ppermute | solution.py:18
  77.7 11.0 %collective-permute-start.5 = (bf16[4,128,128]{2,1,0:T(8,128)(2,1)S(1)}, bf16[4,128,128]{2,1,0:T(8,128)(2,1)S(1)}, u32[]{:S(2)}, u32[]{:S(2)}) collective-permute-start(bf16[4,128,128]{2,1,0:T(8,128)(2,1)S(1)} %get-tuple-element.23), channel_id=1, source_target_pairs={{0,8},{8,0},{16,24},{24,16},{32,40},{40,32},{48,56},{56,48},{64,72... | collective-permute-start | bytes 393224 | tf_op jit(solution)/shard_map/ppermute | solution.py:22
  88.7 2.4 %copy-start.6 = (bf16[4,128,128]{2,1,0:T(8,128)(2,1)}, bf16[4,128,128]{2,1,0:T(8,128)(2,1)S(1)}, u32[]{:S(2)}) copy-start(bf16[4,128,128]{2,1,0:T(8,128)(2,1)S(1)} %collective-permute-done.5) | copy-start | bytes 393220
  91.1 3.6 %copy-start.11 = (f32[1024]{0:T(1024)S(1)}, f32[1024]{0:T(1024)}, u32[]{:S(2)}) copy-start(f32[1024]{0:T(1024)} %param.10) | copy-start | bytes 12292
  97.6 2.7 %collective-permute-start.6 = (f32[2,768]{1,0:T(2,128)S(1)}, f32[2,768]{1,0:T(2,128)S(1)}, u32[]{:S(2)}, u32[]{:S(2)}) collective-permute-start(f32[2,768]{1,0:T(2,128)S(1)} %pad_maximum_fusion), channel_id=1, source_target_pairs={{0,1},{1,0},{2,3},{3,2},{4,5},{5,4},{6,7},{7,6},{8,9},{9,8},{10,11... | collective-permute-start | bytes 18440 | tf_op jit(solution)/shard_map/ppermute | solution.py:70
  100.3 4.1 %collective-permute-start.7 = (f32[2,768]{1,0:T(2,128)S(1)}, f32[2,768]{1,0:T(2,128)S(1)}, u32[]{:S(2)}, u32[]{:S(2)}) collective-permute-start(f32[2,768]{1,0:T(2,128)S(1)} %fusion.53), channel_id=1, source_target_pairs={{0,2},{1,3},{2,0},{3,1},{4,6},{5,7},{6,4},{7,5},{8,10},{9,11},{10,... | collective-permute-start | bytes 18440 | tf_op jit(solution)/shard_map/ppermute | solution.py:70
  104.4 7.4 %collective-permute-start.8 = (f32[2,768]{1,0:T(2,128)S(1)}, f32[2,768]{1,0:T(2,128)S(1)}, u32[]{:S(2)}, u32[]{:S(2)}) collective-permute-start(f32[2,768]{1,0:T(2,128)S(1)} %fusion.72), channel_id=1, source_target_pairs={{0,4},{1,5},{2,6},{3,7},{4,0},{5,1},{6,2},{7,3},{8,12},{9,13},{10,... | collective-permute-start | bytes 18440 | tf_op jit(solution)/shard_map/ppermute | solution.py:70
  121.3 9.9 %copy-start.4 = (bf16[8,128,128]{2,1,0:T(8,128)(2,1)}, bf16[8,128,128]{2,1,0:T(8,128)(2,1)S(1)}, u32[]{:S(2)}) copy-start(bf16[8,128,128]{2,1,0:T(8,128)(2,1)S(1)} %fusion.17) | copy-start | bytes 786436
  121.4 9.9 %collective-permute-start.9 = (bf16[4,128,128]{2,1,0:T(8,128)(2,1)S(1)}, bf16[4,128,128]{2,1,0:T(8,128)(2,1)S(1)}, u32[]{:S(2)}, u32[]{:S(2)}) collective-permute-start(bf16[4,128,128]{2,1,0:T(8,128)(2,1)S(1)} %constant_dynamic-slice_fusion), channel_id=1, source_target_pairs={{0,8},{8,0},{16,24},{24,16},{32,40},{40,32},{48,56},{56,48},{64,72... | collective-permute-start | bytes 393224 | tf_op jit(solution)/shard_map/ppermute | solution.py:22
  132.0 11.0 %collective-permute-start.10 = (f32[4,128,128]{2,1,0:T(8,128)S(1)}, f32[4,128,128]{2,1,0:T(8,128)S(1)}, u32[]{:S(2)}, u32[]{:S(2)}) collective-permute-start(f32[4,128,128]{2,1,0:T(8,128)S(1)} %fusion.38), channel_id=1, source_target_pairs={{16,0},{24,8},{32,16},{40,24},{48,32},{56,40},{64,48},{72,56},{80,... | collective-permute-start | bytes 786440 | tf_op jit(solution)/shard_map/ppermute | solution.py:18
  133.9 28.8 %slice-start = ((s8[9437184]{0:T(1024)(128)(4,1)}), s8[4194304]{0:T(1024)(128)(4,1)S(1)}, s32[]{:S(2)}) async-start(s8[9437184]{0:T(1024)(128)(4,1)} %bitcast.123), calls=%async_computation | async-start | bytes 8388608
  133.9 28.8 %slice-start.1 = ((s8[9437184]{0:T(1024)(128)(4,1)}), s8[4194304]{0:T(1024)(128)(4,1)S(1)}, s32[]{:S(2)}) async-start(s8[9437184]{0:T(1024)(128)(4,1)} %bitcast.123), calls=%async_computation.1 | async-start | bytes 8388608
  143.6 12.3 %collective-permute-start.11 = (bf16[4,128,128]{2,1,0:T(8,128)(2,1)}, bf16[4,128,128]{2,1,0:T(8,128)(2,1)}, u32[]{:S(2)}, u32[]{:S(2)}) collective-permute-start(bf16[4,128,128]{2,1,0:T(8,128)(2,1)} %convert_element_type.176), channel_id=1, source_target_pairs={{16,0},{24,8},{32,16},{40,24},{48,32},{56,40},{64,48},{72,56},{80,... | collective-permute-start | bytes 393224 | tf_op jit(solution)/shard_map/ppermute | solution.py:18
  146.8 15.9 %slice-start.2 = ((s8[9437184]{0:T(1024)(128)(4,1)}), s8[1048576]{0:T(1024)(128)(4,1)S(1)}, s32[]{:S(2)}) async-start(s8[9437184]{0:T(1024)(128)(4,1)} %bitcast.123), calls=%async_computation.2 | async-start | bytes 2097152
  155.9 16.2 %slice-start.3 = ((s8[9437184]{0:T(1024)(128)(4,1)}), s8[4194304]{0:T(1024)(128)(4,1)S(1)}, s32[]{:S(2)}) async-start(s8[9437184]{0:T(1024)(128)(4,1)} %bitcast.125), calls=%async_computation.3 | async-start | bytes 8388608
  157.9 14.2 %slice-start.4 = ((s8[9437184]{0:T(1024)(128)(4,1)}), s8[4194304]{0:T(1024)(128)(4,1)S(1)}, s32[]{:S(2)}) async-start(s8[9437184]{0:T(1024)(128)(4,1)} %bitcast.125), calls=%async_computation.4 | async-start | bytes 8388608
  157.9 14.2 %slice-start.5 = ((s8[9437184]{0:T(1024)(128)(4,1)}), s8[1048576]{0:T(1024)(128)(4,1)S(1)}, s32[]{:S(2)}) async-start(s8[9437184]{0:T(1024)(128)(4,1)} %bitcast.125), calls=%async_computation.5 | async-start | bytes 2097152
  157.9 9.3 %collective-permute-start.12 = (bf16[4,128,128]{2,1,0:T(8,128)(2,1)S(1)}, bf16[4,128,128]{2,1,0:T(8,128)(2,1)S(1)}, u32[]{:S(2)}, u32[]{:S(2)}) collective-permute-start(bf16[4,128,128]{2,1,0:T(8,128)(2,1)S(1)} %fusion.41), channel_id=1, source_target_pairs={{32,0},{40,8},{48,16},{56,24},{64,32},{72,40},{80,48},{88,56},{96,... | collective-permute-start | bytes 393224 | tf_op jit(solution)/shard_map/ppermute | solution.py:18
  169.4 6.2 %copy-start.5 = (bf16[8,128,128]{2,1,0:T(8,128)(2,1)S(1)}, bf16[8,128,128]{2,1,0:T(8,128)(2,1)}, u32[]{:S(2)}) copy-start(bf16[8,128,128]{2,1,0:T(8,128)(2,1)} %copy-done.4) | copy-start | bytes 786436
  169.4 6.2 %copy-start.9 = (bf16[4,128,128]{2,1,0:T(8,128)(2,1)S(1)}, bf16[4,128,128]{2,1,0:T(8,128)(2,1)}, u32[]{:S(2)}) copy-start(bf16[4,128,128]{2,1,0:T(8,128)(2,1)} %copy-done.8) | copy-start | bytes 393220
  169.4 11.2 %copy-start.7 = (bf16[4,128,128]{2,1,0:T(8,128)(2,1)S(1)}, bf16[4,128,128]{2,1,0:T(8,128)(2,1)}, u32[]{:S(2)}) copy-start(bf16[4,128,128]{2,1,0:T(8,128)(2,1)} %copy-done.6) | copy-start | bytes 393220
  169.4 6.2 %collective-permute-start.13 = (bf16[4,128,128]{2,1,0:T(8,128)(2,1)S(1)}, bf16[4,128,128]{2,1,0:T(8,128)(2,1)S(1)}, u32[]{:S(2)}, u32[]{:S(2)}) collective-permute-start(bf16[4,128,128]{2,1,0:T(8,128)(2,1)S(1)} %get-tuple-element.14), channel_id=1, source_target_pairs={{64,0},{72,8},{80,16},{88,24},{96,32},{104,40},{112,48},{120,56},{... | collective-permute-start | bytes 393224 | tf_op jit(solution)/shard_map/ppermute | solution.py:18
  172.1 8.5 %copy-start = (bf16[768,1024]{0,1:T(8,128)(2,1)S(1)}, bf16[768,1024]{0,1:T(8,128)(2,1)}, u32[]{:S(2)}) copy-start(bf16[768,1024]{0,1:T(8,128)(2,1)} %copy.65) | copy-start | bytes 4718596
  172.1 8.5 %copy-start.3 = (f32[8,768,128]{1,2,0:T(8,128)S(1)}, f32[8,768,128]{1,2,0:T(8,128)}, u32[]{:S(2)}) copy-start(f32[8,768,128]{1,2,0:T(8,128)} %fusion.7) | copy-start | bytes 9437188
  178.9 6.2 %collective-permute-start.14 = (bf16[4,128,128]{2,1,0:T(8,128)(2,1)}, bf16[4,128,128]{2,1,0:T(8,128)(2,1)}, u32[]{:S(2)}, u32[]{:S(2)}) collective-permute-start(bf16[4,128,128]{2,1,0:T(8,128)(2,1)} %get-tuple-element.21), channel_id=1, source_target_pairs={{0,8},{8,0},{16,24},{24,16},{32,40},{40,32},{48,56},{56,48},{64,72... | collective-permute-start | bytes 393224 | tf_op jit(solution)/shard_map/ppermute | solution.py:22
  182.4 2.7 %copy-start.1 = (f32[8,768,128]{1,2,0:T(8,128)S(1)}, f32[8,768,128]{1,2,0:T(8,128)}, u32[]{:S(2)}) copy-start(f32[8,768,128]{1,2,0:T(8,128)} %fusion.62) | copy-start | bytes 9437188
  188.5 2.7 %copy-start.2 = (f32[8,768,128]{1,2,0:T(8,128)S(1)}, f32[8,768,128]{1,2,0:T(8,128)}, u32[]{:S(2)}) copy-start(f32[8,768,128]{1,2,0:T(8,128)} %fusion.61) | copy-start | bytes 9437188
  (1 other events, 0.7 us)

commit v3 on v2

--- a/solution.py
+++ b/solution.py
@@ -22,44 +22,66 @@
     return lax.ppermute(x, axis, [(i, i ^ 1) for i in range(count)])
 
 
-def carried(state, firsts, lasts, tokens_here, axis, backward, partial_type):
+def packed(data, tags):
+    rows = data.reshape(-1, data.shape[-1])
+    tail = jnp.zeros((16, rows.shape[1]), data.dtype)
+    tail = tail.at[0, : len(tags)].set(jnp.stack(tags).astype(data.dtype))
+    return jnp.concatenate([rows, tail], axis=0)
+
+
+def unpacked(message, shape):
+    data = message[: message.shape[0] - 16].reshape(shape)
+    return data, message[message.shape[0] - 16, :4].astype(jnp.float32)
+
+
+def carried(state, first_tag, last_tag, tokens_here, axis, backward, partial_type):
     count = lax.axis_size(axis)
     index = lax.axis_index(axis)
     if backward:
-        link_tags, meet_tags, place = firsts[::-1], lasts[::-1], count - 1 - index
+        link_tag, meet_tag, place = first_tag, last_tag, count - 1 - index
     else:
-        link_tags, meet_tags, place = lasts, firsts, index
-    earlier = jnp.concatenate([jnp.full((1,), -1.0, jnp.float32), link_tags[:-1]])
-    links = (earlier == link_tags).astype(jnp.float32)
-    meets = (earlier == meet_tags).astype(jnp.float32)
+        link_tag, meet_tag, place = last_tag, first_tag, index
     chips = count // 2
     terms = min((DOC_MOST - 1) // tokens_here + 1, count)
     window = min((terms + 1) // 2, chips)
-    chip_links = links[0::2] * links[1::2]
-    padded_links = jnp.concatenate([jnp.zeros((window,), jnp.float32), chip_links])
-    chip = place // 2
     core = place % 2
     half = state.shape[0] // 2
+    half_shape = (half,) + state.shape[1:]
     own_half = lax.dynamic_slice_in_dim(state, core * half, half, 0)
     other_half = lax.dynamic_slice_in_dim(state, (1 - core) * half, half, 0)
-    partner_half = swapped(other_half, axis, count)
-    low = jnp.where(core == 0, own_half, partner_half).astype(jnp.float32)
-    high = jnp.where(core == 0, partner_half, own_half).astype(jnp.float32)
-    chip_total = high + links[2 * chip + 1] * low
-    total = moved(chip_total, axis, count, 2, backward)
+    partner_half, partner_tags = unpacked(
+        swapped(packed(other_half, [link_tag, meet_tag]), axis, count), half_shape
+    )
+    first_core = core == 0
+    low = jnp.where(first_core, own_half, partner_half).astype(jnp.float32)
+    high = jnp.where(first_core, partner_half, own_half).astype(jnp.float32)
+    low_link = jnp.where(first_core, link_tag, partner_tags[0])
+    high_link = jnp.where(first_core, partner_tags[0], link_tag)
+    low_meet = jnp.where(first_core, meet_tag, partner_tags[1])
+    high_meet = jnp.where(first_core, partner_tags[1], meet_tag)
+    chip_total = high + (low_link == high_link).astype(jnp.float32) * low
+    total, near_tags = unpacked(
+        moved(packed(chip_total, [high_link]), axis, count, 2, backward), half_shape
+    )
+    before = near_tags[0]
     span = 1
     while span < window:
-        reach = jnp.prod(lax.dynamic_slice_in_dim(padded_links, chip + window - span, span, 0))
-        far = moved(total.astype(partial_type), axis, count, 2 * span, backward)
+        far, far_tags = unpacked(
+            moved(packed(total.astype(partial_type), [before]), axis, count, 2 * span, backward),
+            half_shape,
+        )
+        reach = (far_tags[0] == before).astype(jnp.float32)
         total = total + reach * far.astype(jnp.float32)
         span = span * 2
-    out_low = meets[2 * chip] * total
-    out_high = meets[2 * chip + 1] * (low + links[2 * chip] * total)
-    mine = jnp.where(core == 0, out_low, out_high).astype(jnp.bfloat16)
-    theirs = jnp.where(core == 0, out_high, out_low).astype(jnp.bfloat16)
+    out_low = (before == low_meet).astype(jnp.float32) * total
+    out_high = (low_link == high_meet).astype(jnp.float32) * (
+        low + (before == low_link).astype(jnp.float32) * total
+    )
+    mine = jnp.where(first_core, out_low, out_high).astype(jnp.bfloat16)
+    theirs = jnp.where(first_core, out_high, out_low).astype(jnp.bfloat16)
     got = swapped(theirs, axis, count)
     return jnp.where(
-        core == 0, jnp.concatenate([mine, got], axis=0), jnp.concatenate([got, mine], axis=0)
+        first_core, jnp.concatenate([mine, got], axis=0), jnp.concatenate([got, mine], axis=0)
     )
 
 
@@ -86,10 +108,8 @@
     ).astype(jnp.bfloat16)
     first_doc = doc_ids[0]
     last_doc = doc_ids[tokens_here - 1]
-    ends = lax.all_gather(
-        jnp.stack([first_doc, last_doc]).astype(jnp.float32) + 1.0, "ctx"
-    )
-    firsts, lasts = ends[:, 0], ends[:, 1]
+    first_tag = first_doc.astype(jnp.float32) + 1.0
+    last_tag = last_doc.astype(jnp.float32) + 1.0
     first_rows = (doc_ids == first_doc).astype(jnp.bfloat16)[None, :, None]
     last_rows = (doc_ids == last_doc).astype(jnp.bfloat16)[None, :, None]
     query_first = query_heads * first_rows
@@ -98,7 +118,7 @@
     own_state = jnp.einsum(
         "hta,htb->hab", key_last, value_heads, preferred_element_type=jnp.float32
     ).astype(jnp.bfloat16)
-    incoming = carried(own_state, firsts, lasts, tokens_here, "ctx", False, jnp.bfloat16)
+    incoming = carried(own_state, first_tag, last_tag, tokens_here, "ctx", False, jnp.bfloat16)
     scores = (
         jnp.einsum("hta,hsa->hts", query_heads, key_heads, preferred_element_type=jnp.float32)
         * doc_mask[None]
@@ -121,7 +141,7 @@
     own_reverse = jnp.einsum(
         "hta,htb->hab", query_first, delta_heads, preferred_element_type=jnp.float32
     ).astype(jnp.bfloat16)
-    outgoing = carried(own_reverse, firsts, lasts, tokens_here, "ctx", True, jnp.bfloat16)
+    outgoing = carried(own_reverse, first_tag, last_tag, tokens_here, "ctx", True, jnp.bfloat16)
     dscores = (
         jnp.einsum("htb,hsb->hts", delta_heads, value_heads, preferred_element_type=jnp.float32)
         * doc_mask[None]

time: 199 us -> 189 us (0.950)
  blocking collectives: 20.9 us -> 0 us
  between operations: 1.11 us -> 18.4 us
  other arithmetic: 30 us -> 16.9 us
  waiting for transfers between devices: 19.4 us -> 23.9 us
    all_gather x1 -> x0, blocking collectives: 20.9 us -> none  [shards(): lax.all_gather(jnp.stack([first_doc, last_doc]).astype(jnp.float32) + 1.0...]
    convert_element_type x9 -> x8, other arithmetic: 12.9 us -> 1.34 us  [the longest x2 1.11 us: carried(): mine = jnp.where(first_core, out_low, out_high).astype(jnp.bfloat16)]
    slice x6 -> x14, local copies, waits for them, and re-layouts: 0.59 us -> 6.28 us  [the longest x6 3.77 us: carried(): reach = (far_tags[0] == before).astype(jnp.float32)]
    dot_general x1, matrix products: 9.05 us -> 5.28 us  [shards(): jnp.einsum('htb,hsb->hts', delta_heads, value_heads, preferred_element_ty...]
    dynamic_slice x6 -> x0, local copies, waits for them, and re-layouts: 3.7 us -> none  [the longest x2 1.25 us: carried(): lax.dynamic_slice_in_dim(padded_links, chip + window - span, span, 0)]
    ppermute x8, waiting for transfers between devices: 16.3 us -> 20 us  [moved(): return lax.ppermute(x, axis, pairs)]
    dot_general x1, matrix products: 3.15 us -> 6.75 us  [shards(): jnp.einsum('hts,hta->hsa', dscores, query_heads, preferred_element_type=j...]
    reduce_prod x4 -> x0, other arithmetic: 2.81 us -> none  [carried(): jnp.prod(lax.dynamic_slice_in_dim(padded_links, chip + window - span, spa...]
  transfers between devices with their start and end apart: 15 -> 15, of which waited for: 7 -> 8; matrix products, arithmetic and copies ran while one was open for 32% -> 29% of each run, Pallas kernels for 0% -> 0%
where the time goes in v3:
time: 189 us; the launch traced here: 187 us
  matrix products  57.2 us (30%)
  starting transfers between devices  41.7 us (22%)
  local copies, waits for them, and re-layouts  28.8 us (15%)
  waiting for transfers between devices  23.9 us (13%)
  between operations  18.4 us (10%)
  other arithmetic  16.9 us (9%)
    ppermute x8, starting transfers between devices, moved(): return lax.ppermute(x, axis, pairs)  20.1 us
    ppermute x8, waiting for transfers between devices, moved(): return lax.ppermute(x, axis, pairs)  20 us
    unnamed x35, local copies, waits for them, and re-layouts  13.2 us
    ppermute x3, starting transfers between devices, group_sum(): x = x + lax.ppermute(x, axis, [(i, i ^ step) for i in range(count)])  11.2 us
    ppermute x4, starting transfers between devices, swapped(): return lax.ppermute(x, axis, [(i, i ^ 1) for i in range(count)])  10.5 us
    dot_general x1, matrix products, shards(): jnp.einsum('hts,htb->hsb', scores, delta_heads, preferred_element_type=jn...  7.28 us
    dot_general x1, matrix products, shards(): jnp.einsum('hta,hsa->hts', query_heads, key_heads, preferred_element_type...  7.05 us
    dot_general x1, matrix products, shards(): jnp.einsum('hts,hsb->htb', scores, value_heads, preferred_element_type=jn...  6.91 us
  transfers between devices with their start and end apart: 15, of which 8 were waited for; matrix products, arithmetic and copies ran while one was open for 29% of the time, Pallas kernels for 0%

profile of v3, /device:TPU:17, one launch (start us, length us, event | category | flops | bytes accessed | tf_op | source)
XLA Modules:
  0.0 187.0 jit_solution(18208878949615092481)
XLA Ops:
  5.3 2.8 %fusion.20 = bf16[8,128,128]{2,1,0:T(8,128)(2,1)S(1)} fusion(bf16[768]{0:T(1024)(128)(2,1)S(1)} %get-tuple-element.120, bf16[768,1024]{1,0:T(8,128)(2,1)} %param.28, bf16[768,1024]{1,0:T(8,128)(2,1)} %param.27), kind=kOutput, calls=%fused_computation.29 | convolution fusion | flops 204603392 | bytes 3409408 | tf_op jit(solution)/shard_map/hta,htb->hab/dot_general | solution.py:118
  12.1 3.1 %collective-permute-start.1 = (f32[528,128]{1,0:T(8,128)S(1)}, f32[528,128]{1,0:T(8,128)S(1)}, u32[]{:S(2)}, u32[]{:S(2)}) collective-permute-start(f32[528,128]{1,0:T(8,128)S(1)} %select_maximum_fusion.1), channel_id=1, source_target_pairs={{0,16},{8,24},{16,32},{24,40},{32,48},{40,56},{48,64},{56,72},{64,... | collective-permute-start | bytes 811016 | tf_op jit(solution)/shard_map/ppermute | solution.py:18
  15.2 8.6 %collective-permute-done.1 = f32[528,128]{1,0:T(8,128)S(1)} collective-permute-done((f32[528,128]{1,0:T(8,128)S(1)}, f32[528,128]{1,0:T(8,128)S(1)}, u32[]{:S(2)}, u32[]{:S(2)}) %collective-permute-start.1) | collective-permute-done | bytes 270368 | tf_op jit(solution)/shard_map/ppermute | solution.py:18
  26.8 5.9 %collective-permute-done.2 = bf16[528,128]{1,0:T(8,128)(2,1)S(1)} collective-permute-done((bf16[528,128]{1,0:T(8,128)(2,1)S(1)}, bf16[528,128]{1,0:T(8,128)(2,1)S(1)}, u32[]{:S(2)}, u32[]{:S(2)}) %collective-permute-start.2) | collective-permute-done | bytes 135200 | tf_op jit(solution)/shard_map/ppermute | solution.py:18
  39.9 2.8 %collective-permute-done.3 = bf16[528,128]{1,0:T(8,128)(2,1)S(1)} collective-permute-done((bf16[528,128]{1,0:T(8,128)(2,1)S(1)}, bf16[528,128]{1,0:T(8,128)(2,1)S(1)}, u32[]{:S(2)}, u32[]{:S(2)}) %collective-permute-start.3) | collective-permute-done | bytes 135200 | tf_op jit(solution)/shard_map/ppermute | solution.py:18
  44.5 2.9 %collective-permute-start.4 = (bf16[528,128]{1,0:T(8,128)(2,1)S(1)}, bf16[528,128]{1,0:T(8,128)(2,1)S(1)}, u32[]{:S(2)}, u32[]{:S(2)}) collective-permute-start(bf16[528,128]{1,0:T(8,128)(2,1)S(1)} %fusion.49), channel_id=1, source_target_pairs={{0,64},{8,72},{16,80},{24,88},{32,96},{40,104},{48,112},{56,120},{... | collective-permute-start | bytes 405512 | tf_op jit(solution)/shard_map/ppermute | solution.py:18
  47.5 7.1 %multiply_convert_fusion.1 = bf16[8,768,768]{2,1,0:T(8,128)(2,1)} fusion(f32[768,768]{1,0:T(8,128)} %fusion.29, bf16[8,768,128]{1,2,0:T(8,128)(2,1)S(1)} %bitcast.128, bf16[768,1024]{1,0:T(8,128)(2,1)} %param.27), kind=kOutput, calls=%fused_computation.1 | convolution fusion | flops 1217396736 | bytes 14942208 | tf_op jit(solution)/shard_map/hta,hsa->hts/dot_general | solution.py:123
  60.7 3.9 %collective-permute-start.5 = (bf16[4,128,128]{2,1,0:T(8,128)(2,1)S(1)}, bf16[4,128,128]{2,1,0:T(8,128)(2,1)S(1)}, u32[]{:S(2)}, u32[]{:S(2)}) collective-permute-start(bf16[4,128,128]{2,1,0:T(8,128)(2,1)S(1)} %get-tuple-element.119), channel_id=1, source_target_pairs={{0,8},{8,0},{16,24},{24,16},{32,40},{40,32},{48,56},{56,48},{64,72... | collective-permute-start | bytes 393224 | tf_op jit(solution)/shard_map/ppermute | solution.py:22
  64.6 6.9 %fusion.9 = f32[8,768,128]{1,2,0:T(8,128)S(1)} fusion(bf16[8,768,768]{2,1,0:T(8,128)(2,1)} %multiply_convert_fusion.1, bf16[8,768,128]{2,0,1:T(8,128)(2,1)S(1)} %bitcast.139), kind=kOutput, calls=%fused_computation.22 | convolution fusion | flops 1207959552 | bytes 14155776 | tf_op jit(solution)/shard_map/hts,hsb->htb/dot_general | solution.py:126
  71.5 2.4 %fusion = (f32[768]{0:T(1024)S(1)}, f32[8,768,128]{1,2,0:T(8,128)}) fusion(f32[8,768,128]{1,2,0:T(8,128)S(1)} %fusion.9, bf16[4,128,128]{2,1,0:T(8,128)(2,1)S(1)} %collective-permute-done.5, bf16[4,128,128]{2,1,0:T(8,128)(2,1)S(1)} %get-tuple-element.118, pred[]{:T(512)S(6)} %eq.85, bf16[8,768,128]{1,2,0:T(8,128)(2,1)S(1)} %bitcast.129, ...), kind=kOutput, calls=%fused_computation.3 | convolution fusion | flops 204864768 | bytes 8131073 | tf_op jit(solution)/shard_map/hta,hab->htb/dot_general | solution.py:128
  73.9 3.6 %copy.19 = f32[768,1024]{1,0:T(8,128)} copy(f32[768,1024]{0,1:T(8,128)} %bitcast.138) | data formatting | bytes 6291456 | tf_op jit(solution)/shard_map/reshape | solution.py:129
  77.4 2.8 %multiply_reduce_fusion = f32[768]{0:T(1024)S(1)} fusion(f32[768,1024]{1,0:T(8,128)} %copy.19, bf16[768,1024]{1,0:T(8,128)(2,1)} %param.29, f32[1024]{0:T(1024)S(1)} %copy-done.14), kind=kLoop, calls=%fused_computation.9 | loop fusion | flops 3144960 | bytes 4725760 | tf_op jit(solution)/shard_map/reduce_sum | solution.py:132
  83.1 3.1 %collective-permute-start.7 = (f32[2,768]{1,0:T(2,128)S(1)}, f32[2,768]{1,0:T(2,128)S(1)}, u32[]{:S(2)}, u32[]{:S(2)}) collective-permute-start(f32[2,768]{1,0:T(2,128)S(1)} %fusion.70), channel_id=1, source_target_pairs={{0,2},{1,3},{2,0},{3,1},{4,6},{5,7},{6,4},{7,5},{8,10},{9,11},{10,... | collective-permute-start | bytes 18440 | tf_op jit(solution)/shard_map/ppermute | solution.py:92
  87.2 6.4 %collective-permute-start.8 = (f32[2,768]{1,0:T(2,128)S(1)}, f32[2,768]{1,0:T(2,128)S(1)}, u32[]{:S(2)}, u32[]{:S(2)}) collective-permute-start(f32[2,768]{1,0:T(2,128)S(1)} %fusion.87), channel_id=1, source_target_pairs={{0,4},{1,5},{2,6},{3,7},{4,0},{5,1},{6,2},{7,3},{8,12},{9,13},{10,... | collective-permute-start | bytes 18440 | tf_op jit(solution)/shard_map/ppermute | solution.py:92
  94.6 4.9 %subtract_convert_fusion = (bf16[768,1024]{1,0:T(8,128)(2,1)}, bf16[768,1024]{1,0:T(8,128)(2,1)}) fusion(f32[768,1024]{1,0:T(8,128)} %copy.19, bf16[768,1024]{1,0:T(8,128)(2,1)} %param.29, f32[768]{0:T(1024)S(1)} %fusion.56, f32[768]{0:T(1024)S(1)} %get-tuple-element.113, f32[1024]{0:T(1024)S(1)} %copy-done.14), kind=kLoop, calls=%fused_computation.7 | loop fusion | flops 7077888 | bytes 7874560 | tf_op jit(solution)/shard_map/convert_element_type | solution.py:139
  99.5 2.6 %copy.43 = bf16[768,1024]{0,1:T(8,128)(2,1)} copy(bf16[768,1024]{1,0:T(8,128)(2,1)} %get-tuple-element.114) | data formatting | bytes 3145728 | tf_op jit(solution)/shard_map/reshape | solution.py:140
  102.1 2.0 %fusion.17 = bf16[8,128,128]{2,1,0:T(8,128)(2,1)S(1)} fusion(bf16[8,768,128]{1,2,0:T(8,128)(2,1)} %bitcast.132, bf16[8,768,128]{1,2,0:T(8,128)(2,1)S(1)} %bitcast.130, bf16[768]{0:T(1024)(128)(2,1)S(1)} %get-tuple-element.121), kind=kOutput, calls=%fused_computation.28 | convolution fusion | flops 202244096 | bytes 3409408 | tf_op jit(solution)/shard_map/hta,htb->hab/dot_general | solution.py:141
  104.2 4.3 %collective-permute-start.9 = (bf16[528,128]{1,0:T(8,128)(2,1)S(1)}, bf16[528,128]{1,0:T(8,128)(2,1)S(1)}, u32[]{:S(2)}, u32[]{:S(2)}) collective-permute-start(bf16[528,128]{1,0:T(8,128)(2,1)S(1)} %pad_maximum_fusion.1), channel_id=1, source_target_pairs={{0,8},{8,0},{16,24},{24,16},{32,40},{40,32},{48,56},{56,48},{64,72... | collective-permute-start | bytes 405512 | tf_op jit(solution)/shard_map/ppermute | solution.py:22
  108.4 3.0 %copy.49 = bf16[96,8,8,128]{3,2,1,0:T(8,128)(2,1)} copy(bf16[96,8,8,128]{3,1,2,0:T(8,128)(2,1)} %bitcast.136) | data formatting | bytes 3145728
  115.9 5.3 %multiply_convert_fusion = bf16[8,768,768]{2,1,0:T(8,128)(2,1)S(1)} fusion(f32[768,768]{1,0:T(8,128)} %fusion.29, bf16[8,768,128]{1,2,0:T(8,128)(2,1)} %bitcast.133, bf16[768,1024]{1,0:T(8,128)(2,1)} %param.28), kind=kOutput, calls=%fused_computation | convolution fusion | flops 1217396736 | bytes 14942208 | tf_op jit(solution)/shard_map/htb,hsb->hts/dot_general | solution.py:146
  121.2 2.7 %collective-permute-done.10 = f32[528,128]{1,0:T(8,128)S(1)} collective-permute-done((f32[528,128]{1,0:T(8,128)S(1)}, f32[528,128]{1,0:T(8,128)S(1)}, u32[]{:S(2)}, u32[]{:S(2)}) %collective-permute-start.10) | collective-permute-done | bytes 270368 | tf_op jit(solution)/shard_map/ppermute | solution.py:18
  125.9 4.0 %collective-permute-start.11 = (bf16[528,128]{1,0:T(8,128)(2,1)}, bf16[528,128]{1,0:T(8,128)(2,1)S(1)}, u32[]{:S(2)}, u32[]{:S(2)}) collective-permute-start(bf16[528,128]{1,0:T(8,128)(2,1)} %fusion.45), channel_id=1, source_target_pairs={{16,0},{24,8},{32,16},{40,24},{48,32},{56,40},{64,48},{72,56},{80,... | collective-permute-start | bytes 405512 | tf_op jit(solution)/shard_map/ppermute | solution.py:18
  129.9 6.4 %fusion.7 = f32[8,768,128]{1,2,0:T(8,128)} fusion(bf16[8,768,768]{2,1,0:T(8,128)(2,1)S(1)} %multiply_convert_fusion, bf16[8,768,128]{2,0,1:T(8,128)(2,1)} %bitcast.140), kind=kOutput, calls=%fused_computation.20 | convolution fusion | flops 1207959552 | bytes 14155776 | tf_op jit(solution)/shard_map/hts,hsa->hta/dot_general | solution.py:149
  140.0 7.3 %fusion.77 = f32[8,768,128]{1,2,0:T(8,128)} fusion(bf16[8,768,128]{1,2,0:T(8,128)(2,1)} %bitcast.134, bf16[8,768,768]{2,1,0:T(8,128)(2,1)} %multiply_convert_fusion.1), kind=kOutput, calls=%fused_computation.125 | convolution fusion | flops 1207959552 | bytes 14155776 | tf_op jit(solution)/shard_map/hts,htb->hsb/dot_general | solution.py:157
  149.8 2.4 %collective-permute-start.13 = (bf16[528,128]{1,0:T(8,128)(2,1)}, bf16[528,128]{1,0:T(8,128)(2,1)}, u32[]{:S(2)}, u32[]{:S(2)}) collective-permute-start(bf16[528,128]{1,0:T(8,128)(2,1)} %fusion.46), channel_id=1, source_target_pairs={{64,0},{72,8},{80,16},{88,24},{96,32},{104,40},{112,48},{120,56},{... | collective-permute-start | bytes 405512 | tf_op jit(solution)/shard_map/ppermute | solution.py:18
  152.2 6.8 %fusion.76 = f32[8,768,128]{1,2,0:T(8,128)} fusion(bf16[8,768,128]{1,2,0:T(8,128)(2,1)S(1)} %bitcast.131, bf16[8,768,768]{2,1,0:T(8,128)(2,1)} %copy-done), kind=kOutput, calls=%fused_computation.124 | convolution fusion | flops 1207959552 | bytes 14155776 | tf_op jit(solution)/shard_map/hts,hta->hsa/dot_general | solution.py:154
  168.6 3.6 %add_convert_fusion.2 = bf16[8,768,128]{1,2,0:T(8,128)(2,1)} fusion(f32[8,768,128]{1,2,0:T(8,128)} %fusion.7, bf16[8,768,128]{1,2,0:T(8,128)(2,1)S(1)} %bitcast.135, bf16[768]{0:T(1024)(128)(2,1)S(1)} %get-tuple-element.121, bf16[4,128,128]{2,1,0:T(8,128)(2,1)S(1)} %copy-done.12, bf16[4,128,128]{2,1,0:T(8,128)(2,1)S(1)} %copy-done.7, pred[]{:T(512)S(6)} %eq.85), kind=kOutput, calls=%fused_computation.6 | convolution fusion | flops 207224832 | bytes 6555137 | tf_op jit(solution)/shard_map/htb,hab->hta/dot_general | solution.py:151
  172.2 2.7 %copy.27 = bf16[768,1024]{1,0:T(8,128)(2,1)} copy(bf16[768,1024]{0,1:T(8,128)(2,1)} %bitcast.141) | data formatting | bytes 3145728
  175.0 3.4 %add_convert_fusion = bf16[8,768,128]{1,2,0:T(8,128)(2,1)} fusion(f32[8,768,128]{1,2,0:T(8,128)S(1)} %copy-done.2, bf16[768]{0:T(1024)(128)(2,1)S(1)} %get-tuple-element.120, bf16[4,128,128]{2,1,0:T(8,128)(2,1)S(1)} %collective-permute-done.14, bf16[4,128,128]{2,1,0:T(8,128)(2,1)S(1)} %get-tuple-element.116, pred[]{:T(512)S(6)} %eq.95, ...), kind=kOutput, calls=%fused_computation.4 | convolution fusion | flops 206438400 | bytes 6555137 | tf_op jit(solution)/shard_map/hsa,hab->hsb/dot_general | solution.py:159
  178.3 2.7 %copy.29 = bf16[768,1024]{1,0:T(8,128)(2,1)} copy(bf16[768,1024]{0,1:T(8,128)(2,1)} %bitcast.143) | data formatting | bytes 3145728
  181.0 3.4 %add_convert_fusion.1 = bf16[8,768,128]{1,2,0:T(8,128)(2,1)} fusion(f32[8,768,128]{1,2,0:T(8,128)S(1)} %copy-done.3, bf16[768]{0:T(1024)(128)(2,1)S(1)} %get-tuple-element.120, bf16[4,128,128]{2,1,0:T(8,128)(2,1)S(1)} %collective-permute-done.14, bf16[4,128,128]{2,1,0:T(8,128)(2,1)S(1)} %get-tuple-element.116, pred[]{:T(512)S(6)} %eq.95, ...), kind=kOutput, calls=%fused_computation.5 | convolution fusion | flops 206438400 | bytes 6555137 | tf_op jit(solution)/shard_map/hsb,hab->hsa/dot_general | solution.py:156
  184.4 2.6 %copy.28 = bf16[768,1024]{1,0:T(8,128)(2,1)} copy(bf16[768,1024]{0,1:T(8,128)(2,1)} %bitcast.142) | data formatting | bytes 3145728
  (103 shorter events, 36.4 us)
Async XLA Ops:
  8.2 28.3 %copy-start.13 = (s32[768]{0:T(1024)S(1)}, s32[768]{0:T(1024)}, u32[]{:S(2)}) copy-start(s32[768]{0:T(1024)} %param.31) | copy-start | bytes 9220
  8.3 1.8 collective-permute-start
  12.1 11.7 %collective-permute-start.1 = (f32[528,128]{1,0:T(8,128)S(1)}, f32[528,128]{1,0:T(8,128)S(1)}, u32[]{:S(2)}, u32[]{:S(2)}) collective-permute-start(f32[528,128]{1,0:T(8,128)S(1)} %select_maximum_fusion.1), channel_id=1, source_target_pairs={{0,16},{8,24},{16,32},{24,40},{32,48},{40,56},{48,64},{56,72},{64,... | collective-permute-start | bytes 811016 | tf_op jit(solution)/shard_map/ppermute | solution.py:18
  24.9 7.9 %collective-permute-start.2 = (bf16[528,128]{1,0:T(8,128)(2,1)S(1)}, bf16[528,128]{1,0:T(8,128)(2,1)S(1)}, u32[]{:S(2)}, u32[]{:S(2)}) collective-permute-start(bf16[528,128]{1,0:T(8,128)(2,1)S(1)} %fusion.48), channel_id=1, source_target_pairs={{0,16},{8,24},{16,32},{24,40},{32,48},{40,56},{48,64},{56,72},{64,... | collective-permute-start | bytes 405512 | tf_op jit(solution)/shard_map/ppermute | solution.py:18
  34.5 8.2 %collective-permute-start.3 = (bf16[528,128]{1,0:T(8,128)(2,1)S(1)}, bf16[528,128]{1,0:T(8,128)(2,1)S(1)}, u32[]{:S(2)}, u32[]{:S(2)}) collective-permute-start(bf16[528,128]{1,0:T(8,128)(2,1)S(1)} %fusion.47), channel_id=1, source_target_pairs={{0,32},{8,40},{16,48},{24,56},{32,64},{40,72},{48,80},{56,88},{64,... | collective-permute-start | bytes 405512 | tf_op jit(solution)/shard_map/ppermute | solution.py:18
  44.5 14.0 %collective-permute-start.4 = (bf16[528,128]{1,0:T(8,128)(2,1)S(1)}, bf16[528,128]{1,0:T(8,128)(2,1)S(1)}, u32[]{:S(2)}, u32[]{:S(2)}) collective-permute-start(bf16[528,128]{1,0:T(8,128)(2,1)S(1)} %fusion.49), channel_id=1, source_target_pairs={{0,64},{8,72},{16,80},{24,88},{32,96},{40,104},{48,112},{56,120},{... | collective-permute-start | bytes 405512 | tf_op jit(solution)/shard_map/ppermute | solution.py:18
  47.5 7.1 %copy-start.4 = (bf16[768,1024]{1,0:T(8,128)(2,1)S(1)}, bf16[768,1024]{1,0:T(8,128)(2,1)}, u32[]{:S(2)}) copy-start(bf16[768,1024]{1,0:T(8,128)(2,1)} %param.28) | copy-start | bytes 4718596
  60.3 4.2 %copy-start.5 = (bf16[96,8,8,128]{3,2,1,0:T(8,128)(2,1)S(1)}, bf16[96,8,8,128]{3,2,1,0:T(8,128)(2,1)}, u32[]{:S(2)}) copy-start(bf16[96,8,8,128]{3,2,1,0:T(8,128)(2,1)} %copy.48) | copy-start | bytes 4718596
  60.7 10.8 %copy-start.6 = (bf16[4,128,128]{2,1,0:T(8,128)(2,1)}, bf16[4,128,128]{2,1,0:T(8,128)(2,1)S(1)}, u32[]{:S(2)}) copy-start(bf16[4,128,128]{2,1,0:T(8,128)(2,1)S(1)} %get-tuple-element.118) | copy-start | bytes 393220
  60.7 10.8 %collective-permute-start.5 = (bf16[4,128,128]{2,1,0:T(8,128)(2,1)S(1)}, bf16[4,128,128]{2,1,0:T(8,128)(2,1)S(1)}, u32[]{:S(2)}, u32[]{:S(2)}) collective-permute-start(bf16[4,128,128]{2,1,0:T(8,128)(2,1)S(1)} %get-tuple-element.119), channel_id=1, source_target_pairs={{0,8},{8,0},{16,24},{24,16},{32,40},{40,32},{48,56},{56,48},{64,72... | collective-permute-start | bytes 393224 | tf_op jit(solution)/shard_map/ppermute | solution.py:22
  71.5 2.4 %copy-start.11 = (bf16[4,128,128]{2,1,0:T(8,128)(2,1)}, bf16[4,128,128]{2,1,0:T(8,128)(2,1)S(1)}, u32[]{:S(2)}) copy-start(bf16[4,128,128]{2,1,0:T(8,128)(2,1)S(1)} %collective-permute-done.5) | copy-start | bytes 393220
  73.9 3.6 %copy-start.14 = (f32[1024]{0:T(1024)S(1)}, f32[1024]{0:T(1024)}, u32[]{:S(2)}) copy-start(f32[1024]{0:T(1024)} %param.30) | copy-start | bytes 12292
  80.3 2.7 %collective-permute-start.6 = (f32[2,768]{1,0:T(2,128)S(1)}, f32[2,768]{1,0:T(2,128)S(1)}, u32[]{:S(2)}, u32[]{:S(2)}) collective-permute-start(f32[2,768]{1,0:T(2,128)S(1)} %pad_maximum_fusion.2), channel_id=1, source_target_pairs={{0,1},{1,0},{2,3},{3,2},{4,5},{5,4},{6,7},{7,6},{8,9},{9,8},{10,11... | collective-permute-start | bytes 18440 | tf_op jit(solution)/shard_map/ppermute | solution.py:92
  83.1 4.1 %collective-permute-start.7 = (f32[2,768]{1,0:T(2,128)S(1)}, f32[2,768]{1,0:T(2,128)S(1)}, u32[]{:S(2)}, u32[]{:S(2)}) collective-permute-start(f32[2,768]{1,0:T(2,128)S(1)} %fusion.70), channel_id=1, source_target_pairs={{0,2},{1,3},{2,0},{3,1},{4,6},{5,7},{6,4},{7,5},{8,10},{9,11},{10,... | collective-permute-start | bytes 18440 | tf_op jit(solution)/shard_map/ppermute | solution.py:92
  87.2 7.4 %collective-permute-start.8 = (f32[2,768]{1,0:T(2,128)S(1)}, f32[2,768]{1,0:T(2,128)S(1)}, u32[]{:S(2)}, u32[]{:S(2)}) collective-permute-start(f32[2,768]{1,0:T(2,128)S(1)} %fusion.87), channel_id=1, source_target_pairs={{0,4},{1,5},{2,6},{3,7},{4,0},{5,1},{6,2},{7,3},{8,12},{9,13},{10,... | collective-permute-start | bytes 18440 | tf_op jit(solution)/shard_map/ppermute | solution.py:92
  104.1 9.2 %copy-start.10 = (bf16[8,128,128]{2,1,0:T(8,128)(2,1)}, bf16[8,128,128]{2,1,0:T(8,128)(2,1)S(1)}, u32[]{:S(2)}) copy-start(bf16[8,128,128]{2,1,0:T(8,128)(2,1)S(1)} %fusion.17) | copy-start | bytes 786436
  104.2 7.3 %collective-permute-start.9 = (bf16[528,128]{1,0:T(8,128)(2,1)S(1)}, bf16[528,128]{1,0:T(8,128)(2,1)S(1)}, u32[]{:S(2)}, u32[]{:S(2)}) collective-permute-start(bf16[528,128]{1,0:T(8,128)(2,1)S(1)} %pad_maximum_fusion.1), channel_id=1, source_target_pairs={{0,8},{8,0},{16,24},{24,16},{32,40},{40,32},{48,56},{56,48},{64,72... | collective-permute-start | bytes 405512 | tf_op jit(solution)/shard_map/ppermute | solution.py:22
  113.3 0.7 copy-start.8
  113.9 9.9 %collective-permute-start.10 = (f32[528,128]{1,0:T(8,128)S(1)}, f32[528,128]{1,0:T(8,128)S(1)}, u32[]{:S(2)}, u32[]{:S(2)}) collective-permute-start(f32[528,128]{1,0:T(8,128)S(1)} %select_maximum_fusion), channel_id=1, source_target_pairs={{16,0},{24,8},{32,16},{40,24},{48,32},{56,40},{64,48},{72,56},{80,... | collective-permute-start | bytes 811016 | tf_op jit(solution)/shard_map/ppermute | solution.py:18
  121.1 15.1 %copy-start = (bf16[8,768,768]{2,1,0:T(8,128)(2,1)}, bf16[8,768,768]{2,1,0:T(8,128)(2,1)S(1)}, u32[]{:S(2)}) copy-start(bf16[8,768,768]{2,1,0:T(8,128)(2,1)S(1)} %multiply_convert_fusion) | copy-start | bytes 28311556
  125.9 10.4 %collective-permute-start.11 = (bf16[528,128]{1,0:T(8,128)(2,1)}, bf16[528,128]{1,0:T(8,128)(2,1)S(1)}, u32[]{:S(2)}, u32[]{:S(2)}) collective-permute-start(bf16[528,128]{1,0:T(8,128)(2,1)} %fusion.45), channel_id=1, source_target_pairs={{16,0},{24,8},{32,16},{40,24},{48,32},{56,40},{64,48},{72,56},{80,... | collective-permute-start | bytes 405512 | tf_op jit(solution)/shard_map/ppermute | solution.py:18
  138.1 9.2 %collective-permute-start.12 = (bf16[528,128]{1,0:T(8,128)(2,1)S(1)}, bf16[528,128]{1,0:T(8,128)(2,1)S(1)}, u32[]{:S(2)}, u32[]{:S(2)}) collective-permute-start(bf16[528,128]{1,0:T(8,128)(2,1)S(1)} %fusion.44), channel_id=1, source_target_pairs={{32,0},{40,8},{48,16},{56,24},{64,32},{72,40},{80,48},{88,56},{96,... | collective-permute-start | bytes 405512 | tf_op jit(solution)/shard_map/ppermute | solution.py:18
  147.3 4.9 %copy-start.9 = (bf16[528,128]{1,0:T(8,128)(2,1)}, bf16[528,128]{1,0:T(8,128)(2,1)S(1)}, u32[]{:S(2)}) copy-start(bf16[528,128]{1,0:T(8,128)(2,1)S(1)} %collective-permute-done.12) | copy-start | bytes 405508
  149.8 11.7 %collective-permute-start.13 = (bf16[528,128]{1,0:T(8,128)(2,1)}, bf16[528,128]{1,0:T(8,128)(2,1)}, u32[]{:S(2)}, u32[]{:S(2)}) collective-permute-start(bf16[528,128]{1,0:T(8,128)(2,1)} %fusion.46), channel_id=1, source_target_pairs={{64,0},{72,8},{80,16},{88,24},{96,32},{104,40},{112,48},{120,56},{... | collective-permute-start | bytes 405512 | tf_op jit(solution)/shard_map/ppermute | solution.py:18
  158.9 9.6 %copy-start.1 = (bf16[768,1024]{0,1:T(8,128)(2,1)S(1)}, bf16[768,1024]{0,1:T(8,128)(2,1)}, u32[]{:S(2)}) copy-start(bf16[768,1024]{0,1:T(8,128)(2,1)} %copy.43) | copy-start | bytes 4718596
  158.9 9.6 %copy-start.7 = (bf16[4,128,128]{2,1,0:T(8,128)(2,1)S(1)}, bf16[4,128,128]{2,1,0:T(8,128)(2,1)}, u32[]{:S(2)}) copy-start(bf16[4,128,128]{2,1,0:T(8,128)(2,1)} %copy-done.6) | copy-start | bytes 393220
  158.9 9.6 %copy-start.12 = (bf16[4,128,128]{2,1,0:T(8,128)(2,1)S(1)}, bf16[4,128,128]{2,1,0:T(8,128)(2,1)}, u32[]{:S(2)}) copy-start(bf16[4,128,128]{2,1,0:T(8,128)(2,1)} %copy-done.11) | copy-start | bytes 393220
  167.1 7.9 %collective-permute-start.14 = (bf16[4,128,128]{2,1,0:T(8,128)(2,1)S(1)}, bf16[4,128,128]{2,1,0:T(8,128)(2,1)S(1)}, u32[]{:S(2)}, u32[]{:S(2)}) collective-permute-start(bf16[4,128,128]{2,1,0:T(8,128)(2,1)S(1)} %get-tuple-element.117), channel_id=1, source_target_pairs={{0,8},{8,0},{16,24},{24,16},{32,40},{40,32},{48,56},{56,48},{64,72... | collective-permute-start | bytes 393224 | tf_op jit(solution)/shard_map/ppermute | solution.py:22
  172.2 2.7 %copy-start.2 = (f32[8,768,128]{1,2,0:T(8,128)S(1)}, f32[8,768,128]{1,2,0:T(8,128)}, u32[]{:S(2)}) copy-start(f32[8,768,128]{1,2,0:T(8,128)} %fusion.77) | copy-start | bytes 9437188
  178.3 2.7 %copy-start.3 = (f32[8,768,128]{1,2,0:T(8,128)S(1)}, f32[8,768,128]{1,2,0:T(8,128)}, u32[]{:S(2)}) copy-start(f32[8,768,128]{1,2,0:T(8,128)} %fusion.76) | copy-start | bytes 9437188

commit v4 on v3

--- a/solution.py
+++ b/solution.py
@@ -1,6 +1,7 @@
 import jax
 import jax.numpy as jnp
 from jax import lax
+from jax.experimental import pallas as pl
 from jax.sharding import PartitionSpec as P
 
 HEADS = 64
@@ -87,11 +88,46 @@
 
 def group_sum(x, axis):
     count = lax.axis_size(axis)
-    step = 1
-    while step < count:
-        x = x + lax.ppermute(x, axis, [(i, i ^ step) for i in range(count)])
-        step = step * 2
-    return x
+    index = lax.axis_index(axis)
+    parts = [x]
+    for step in range(1, count):
+        parts.append(lax.ppermute(x, axis, [(i, (i + step) % count) for i in range(count)]))
+    ordered = jnp.stack(parts)
+    slot = (index - jnp.arange(count)) % count
+    ordered = ordered[slot]
+    total = ordered[0]
+    for source in range(1, count):
+        total = total + ordered[source]
+    return total
+
+
+def finish_body(local_ref, rows_ref, mask_ref, state_ref, out_ref, *, flip):
+    rows = rows_ref[...] * mask_ref[...]
+    state = state_ref[0]
+    if flip:
+        extra = lax.dot_general(
+            rows, state, (((1,), (1,)), ((), ())), preferred_element_type=jnp.float32
+        )
+    else:
+        extra = jnp.dot(rows, state, preferred_element_type=jnp.float32)
+    out_ref[...] = (local_ref[0] + extra).astype(out_ref.dtype)
+
+
+def finished(local, rows, mask, state, flip, kind, interpret=False):
+    heads, tokens, width = local.shape
+    return pl.pallas_call(
+        lambda *refs: finish_body(*refs, flip=flip),
+        grid=(heads,),
+        in_specs=[
+            pl.BlockSpec((1, tokens, width), lambda h: (h, 0, 0)),
+            pl.BlockSpec((tokens, width), lambda h: (0, h)),
+            pl.BlockSpec((tokens, 1), lambda h: (0, 0)),
+            pl.BlockSpec((1, width, width), lambda h: (h, 0, 0)),
+        ],
+        out_specs=pl.BlockSpec((tokens, width), lambda h: (0, h)),
+        out_shape=jax.ShapeDtypeStruct((tokens, heads * width), kind),
+        interpret=interpret,
+    )(local, rows, mask, state)
 
 
 def shards(queries, keys, values, out_grad, gain, doc_ids):
@@ -110,11 +146,12 @@
     last_doc = doc_ids[tokens_here - 1]
     first_tag = first_doc.astype(jnp.float32) + 1.0
     last_tag = last_doc.astype(jnp.float32) + 1.0
-    first_rows = (doc_ids == first_doc).astype(jnp.bfloat16)[None, :, None]
-    last_rows = (doc_ids == last_doc).astype(jnp.bfloat16)[None, :, None]
+    first_mask = (doc_ids == first_doc).astype(jnp.bfloat16)[:, None]
+    last_mask = (doc_ids == last_doc).astype(jnp.bfloat16)[:, None]
+    first_rows = first_mask[None]
+    last_rows = last_mask[None]
     query_first = query_heads * first_rows
     key_last = key_heads * last_rows
-    value_last = value_heads * last_rows
     own_state = jnp.einsum(
         "hta,htb->hab", key_last, value_heads, preferred_element_type=jnp.float32
     ).astype(jnp.bfloat16)
@@ -123,10 +160,10 @@
         jnp.einsum("hta,hsa->hts", query_heads, key_heads, preferred_element_type=jnp.float32)
         * doc_mask[None]
     ).astype(jnp.bfloat16)
-    attended_heads = jnp.einsum(
+    attended_local = jnp.einsum(
         "hts,hsb->htb", scores, value_heads, preferred_element_type=jnp.float32
-    ) + jnp.einsum("hta,hab->htb", query_first, incoming, preferred_element_type=jnp.float32)
-    flat = attended_heads.transpose(1, 0, 2).reshape(tokens_here, flat_width)
+    )
+    flat = finished(attended_local, queries, first_mask, incoming, False, jnp.float32)
     scaled_grad = gain[None, :] * out_grad.astype(jnp.float32)
     sums = group_sum(
         jnp.stack([jnp.sum(flat * flat, axis=1), jnp.sum(scaled_grad * flat, axis=1)]), "tp"
@@ -148,20 +185,14 @@
     ).astype(jnp.bfloat16)
     grad_query = jnp.einsum(
         "hts,hsa->hta", dscores, key_heads, preferred_element_type=jnp.float32
-    ) + jnp.einsum(
-        "htb,hab->hta", delta_heads * first_rows, incoming, preferred_element_type=jnp.float32
-    )
-    grad_key = jnp.einsum(
-        "hts,hta->hsa", dscores, query_heads, preferred_element_type=jnp.float32
-    ) + jnp.einsum("hsb,hab->hsa", value_last, outgoing, preferred_element_type=jnp.float32)
-    grad_value = jnp.einsum(
-        "hts,htb->hsb", scores, delta_heads, preferred_element_type=jnp.float32
-    ) + jnp.einsum("hsa,hab->hsb", key_last, outgoing, preferred_element_type=jnp.float32)
+    )
+    grad_key = jnp.einsum("hts,hta->hsa", dscores, query_heads, preferred_element_type=jnp.float32)
+    grad_value = jnp.einsum("hts,htb->hsb", scores, delta_heads, preferred_element_type=jnp.float32)
     return (
         normed,
-        grad_query.astype(jnp.bfloat16).transpose(1, 0, 2).reshape(tokens_here, flat_width),
-        grad_key.astype(jnp.bfloat16).transpose(1, 0, 2).reshape(tokens_here, flat_width),
-        grad_value.astype(jnp.bfloat16).transpose(1, 0, 2).reshape(tokens_here, flat_width),
+        finished(grad_query, delta, first_mask, incoming, True, jnp.bfloat16),
+        finished(grad_key, values, last_mask, outgoing, True, jnp.bfloat16),
+        finished(grad_value, keys, last_mask, outgoing, False, jnp.bfloat16),
     )
 
 

time: 189 us -> 198 us (1.048)
  Pallas kernels: 0 us -> 29.6 us
  local copies, waits for them, and re-layouts: 28.8 us -> 13.8 us
  starting transfers between devices: 41.7 us -> 49.3 us
  matrix products: 57.2 us -> 51.5 us
  other arithmetic: 16.9 us -> 12.7 us
  waiting for transfers between devices: 23.9 us -> 20.2 us
    pallas_call x0 -> x4, Pallas kernels: none -> 29.6 us  [finished(): pl.pallas_call(lambda *refs: finish_body(*refs, flip=flip), grid=(heads,)...]
    dot_general x4 -> x0, matrix products: 12.7 us -> none  [the longest x1 3.63 us: shards(): jnp.einsum('htb,hab->hta', delta_heads * first_rows, incoming, preferred_...]
    unnamed x35 -> x36, local copies, waits for them, and re-layouts: 13.2 us -> 1.28 us
    reshape x2 -> x0, local copies, waits for them, and re-layouts: 6.13 us -> none  [the longest x1 3.56 us: shards(): flat = attended_heads.transpose(1, 0, 2).reshape(tokens_here, flat_width)]
    ppermute x3 -> x7, starting transfers between devices: 11.2 us -> 16.6 us  [group_sum(): lax.ppermute(x, axis, [(i, (i + step) % count) for i in range(count)])]
    ppermute x8, starting transfers between devices: 20.1 us -> 24.1 us  [moved(): return lax.ppermute(x, axis, pairs)]
    ppermute x8, waiting for transfers between devices: 20 us -> 16.4 us  [moved(): return lax.ppermute(x, axis, pairs)]
  transfers between devices with their start and end apart: 15 -> 19, of which waited for: 8 -> 8; matrix products, arithmetic and copies ran while one was open for 29% -> 27% of each run, Pallas kernels for 0% -> 4%
where the time goes in v4:
time: 198 us; the launch traced here: 196 us
  matrix products  51.5 us (26%)
  starting transfers between devices  49.3 us (25%)
  Pallas kernels  29.6 us (15%)
  waiting for transfers between devices  20.2 us (10%)
  between operations  19.1 us (10%)
  local copies, waits for them, and re-layouts  13.8 us (7%)
  other arithmetic  12.7 us (6%)
    pallas_call x4, Pallas kernels, finished(): pl.pallas_call(lambda *refs: finish_body(*refs, flip=flip), grid=(heads,)...  29.6 us
    ppermute x8, starting transfers between devices, moved(): return lax.ppermute(x, axis, pairs)  24.1 us
    ppermute x7, starting transfers between devices, group_sum(): lax.ppermute(x, axis, [(i, (i + step) % count) for i in range(count)])  16.6 us
    ppermute x8, waiting for transfers between devices, moved(): return lax.ppermute(x, axis, pairs)  16.4 us
    ppermute x4, starting transfers between devices, swapped(): return lax.ppermute(x, axis, [(i, i ^ 1) for i in range(count)])  8.64 us
    dot_general x1, matrix products, shards(): jnp.einsum('hts,htb->hsb', scores, delta_heads, preferred_element_type=jn...  8.38 us
    dot_general x1, matrix products, shards(): jnp.einsum('hts,hsb->htb', scores, value_heads, preferred_element_type=jn...  8.37 us
    dot_general x1, matrix products, shards(): jnp.einsum('hts,hta->hsa', dscores, query_heads, preferred_element_type=j...  8.28 us
  transfers between devices with their start and end apart: 19, of which 8 were waited for; matrix products, arithmetic and copies ran while one was open for 27% of the time, Pallas kernels for 4%

profile of v4, /device:TPU:17, one launch (start us, length us, event | category | flops | bytes accessed | tf_op | source)
XLA Modules:
  0.0 196.3 jit_solution(14986131765761260327)
XLA Ops:
  2.6 2.0 %compare_convert_fusion = (bf16[768]{0:T(1024)(128)(2,1)S(1)}, bf16[768]{0:T(1024)(128)(2,1)S(1)}) fusion(s32[768]{0:T(1024)} %param.31, s32[]{:T(128)} %bitcast.5, s32[]{:T(128)} %bitcast.4), kind=kLoop, calls=%fused_computation.111 | loop fusion | flops 3072 | bytes 6152 | tf_op jit(solution)/shard_map/convert_element_type | solution.py:150
  5.3 2.8 %fusion.10 = bf16[8,128,128]{2,1,0:T(8,128)(2,1)S(1)} fusion(bf16[768]{0:T(1024)(128)(2,1)S(1)} %get-tuple-element.118, bf16[768,1024]{1,0:T(8,128)(2,1)} %refs_1_.4, bf16[768,1024]{1,0:T(8,128)(2,1)} %refs_1_.5), kind=kOutput, calls=%fused_computation.21 | convolution fusion | flops 204603392 | bytes 3409408 | tf_op jit(solution)/shard_map/hta,htb->hab/dot_general | solution.py:155
  12.1 3.1 %collective-permute-start.1 = (f32[528,128]{1,0:T(8,128)S(1)}, f32[528,128]{1,0:T(8,128)S(1)}, u32[]{:S(2)}, u32[]{:S(2)}) collective-permute-start(f32[528,128]{1,0:T(8,128)S(1)} %select_maximum_fusion.1), channel_id=1, source_target_pairs={{0,16},{8,24},{16,32},{24,40},{32,48},{40,56},{48,64},{56,72},{64,... | collective-permute-start | bytes 811016 | tf_op jit(solution)/shard_map/ppermute | solution.py:19
  15.2 8.6 %collective-permute-done.1 = f32[528,128]{1,0:T(8,128)S(1)} collective-permute-done((f32[528,128]{1,0:T(8,128)S(1)}, f32[528,128]{1,0:T(8,128)S(1)}, u32[]{:S(2)}, u32[]{:S(2)}) %collective-permute-start.1) | collective-permute-done | bytes 270368 | tf_op jit(solution)/shard_map/ppermute | solution.py:19
  24.9 1.9 collective-permute-start.2
  27.1 3.4 %copy.37 = bf16[768,1024]{0,1:T(8,128)(2,1)} copy(bf16[768,1024]{1,0:T(8,128)(2,1)} %refs_1_.3) | data formatting | bytes 3145728 | tf_op jit(solution)/shard_map/reshape | solution.py:138
  30.5 2.3 %collective-permute-done.2 = bf16[528,128]{1,0:T(8,128)(2,1)S(1)} collective-permute-done((bf16[528,128]{1,0:T(8,128)(2,1)S(1)}, bf16[528,128]{1,0:T(8,128)(2,1)S(1)}, u32[]{:S(2)}, u32[]{:S(2)}) %collective-permute-start.2) | collective-permute-done | bytes 135200 | tf_op jit(solution)/shard_map/ppermute | solution.py:19
  34.6 1.9 collective-permute-start.3
  36.5 8.2 %multiply_convert_fusion.1 = bf16[8,768,768]{2,1,0:T(8,128)(2,1)} fusion(f32[768,768]{1,0:T(8,128)S(1)} %fusion.25, bf16[8,768,128]{1,2,0:T(8,128)(2,1)} %bitcast.137, bf16[768,1024]{1,0:T(8,128)(2,1)} %refs_1_.5), kind=kOutput, calls=%fused_computation.2 | convolution fusion | flops 1217396736 | bytes 14942208 | tf_op jit(solution)/shard_map/hta,hsa->hts/dot_general | solution.py:160
  46.5 2.9 %collective-permute-start.4 = (bf16[528,128]{1,0:T(8,128)(2,1)S(1)}, bf16[528,128]{1,0:T(8,128)(2,1)S(1)}, u32[]{:S(2)}, u32[]{:S(2)}) collective-permute-start(bf16[528,128]{1,0:T(8,128)(2,1)S(1)} %fusion.41), channel_id=1, source_target_pairs={{0,64},{8,72},{16,80},{24,88},{32,96},{40,104},{48,112},{56,120},{... | collective-permute-start | bytes 405512 | tf_op jit(solution)/shard_map/ppermute | solution.py:19
  49.4 8.4 %fusion.5.refs_0_ = f32[8,768,128]{2,1,0:T(8,128)} fusion(bf16[8,768,768]{2,1,0:T(8,128)(2,1)} %multiply_convert_fusion.1, bf16[768,1024]{1,0:T(8,128)(2,1)} %refs_1_.4), kind=kOutput, calls=%fused_computation.16 | convolution fusion | flops 1207959552 | bytes 14155776 | tf_op jit(solution)/shard_map/hts,hsb->htb/dot_general | solution.py:163
  62.5 2.7 %collective-permute-start.5 = (bf16[4,128,128]{2,1,0:T(8,128)(2,1)S(1)}, bf16[4,128,128]{2,1,0:T(8,128)(2,1)S(1)}, u32[]{:S(2)}, u32[]{:S(2)}) collective-permute-start(bf16[4,128,128]{2,1,0:T(8,128)(2,1)S(1)} %get-tuple-element.117), channel_id=1, source_target_pairs={{0,8},{8,0},{16,24},{24,16},{32,40},{40,32},{48,56},{56,48},{64,72... | collective-permute-start | bytes 393224 | tf_op jit(solution)/shard_map/ppermute | solution.py:23
  66.9 7.8 %shard_map.93 = f32[768,1024]{1,0:T(8,128)} custom-call(f32[8,768,128]{2,1,0:T(8,128)} %fusion.5.refs_0_, bf16[768,1024]{1,0:T(8,128)(2,1)} %refs_1_.3, bf16[768,1]{1,0:T(8,128)(2,1)} %broadcast_in_dim.6.refs_2_, bf16[8,128,128]{2,1,0:T(8,128)(2,1)} %maximum_select_fusion.refs_3_), custom_call_target="tpu_custom_call" | custom-call | tf_op jit(solution)/shard_map/pallas_call | solution.py:118
  74.7 3.2 %multiply_reduce_fusion.1 = (f32[768]{0:T(1024)S(1)}, f32[768]{0:T(1024)S(1)}) fusion(f32[768,1024]{1,0:T(8,128)} %shard_map.93, bf16[768,1024]{1,0:T(8,128)(2,1)} %param.29, f32[1024]{0:T(1024)S(1)} %copy-done.14), kind=kLoop, calls=%fused_computation.7 | loop fusion | flops 4717056 | bytes 4728832 | tf_op jit(solution)/shard_map/reduce_sum | solution.py:169
  79.7 3.1 %collective-permute-start.7 = (f32[2,768]{1,0:T(2,128)S(1)}, f32[2,768]{1,0:T(2,128)S(1)}, u32[]{:S(2)}, u32[]{:S(2)}) collective-permute-start(f32[2,768]{1,0:T(2,128)S(1)} %pad_maximum_fusion.2), channel_id=1, source_target_pairs={{0,2},{1,3},{2,4},{3,5},{4,6},{5,7},{6,0},{7,1},{8,10},{9,11},{10,... | collective-permute-start | bytes 18440 | tf_op jit(solution)/shard_map/ppermute | solution.py:94
  82.8 3.8 %collective-permute-start.8 = (f32[2,768]{1,0:T(2,128)S(1)}, f32[2,768]{1,0:T(2,128)S(1)}, u32[]{:S(2)}, u32[]{:S(2)}) collective-permute-start(f32[2,768]{1,0:T(2,128)S(1)} %pad_maximum_fusion.2), channel_id=1, source_target_pairs={{0,3},{1,4},{2,5},{3,6},{4,7},{5,0},{6,1},{7,2},{8,11},{9,12},{10,... | collective-permute-start | bytes 18440 | tf_op jit(solution)/shard_map/ppermute | solution.py:94
  87.0 4.5 %collective-permute-start.10 = (f32[2,768]{1,0:T(2,128)S(1)}, f32[2,768]{1,0:T(2,128)S(1)}, u32[]{:S(2)}, u32[]{:S(2)}) collective-permute-start(f32[2,768]{1,0:T(2,128)S(1)} %pad_maximum_fusion.2), channel_id=1, source_target_pairs={{0,5},{1,6},{2,7},{3,0},{4,1},{5,2},{6,3},{7,4},{8,13},{9,14},{10,... | collective-permute-start | bytes 18440 | tf_op jit(solution)/shard_map/ppermute | solution.py:94
  91.4 2.4 %collective-permute-start.11 = (f32[2,768]{1,0:T(2,128)S(1)}, f32[2,768]{1,0:T(2,128)S(1)}, u32[]{:S(2)}, u32[]{:S(2)}) collective-permute-start(f32[2,768]{1,0:T(2,128)S(1)} %pad_maximum_fusion.2), channel_id=1, source_target_pairs={{0,6},{1,7},{2,0},{3,1},{4,2},{5,3},{6,4},{7,5},{8,14},{9,15},{10,... | collective-permute-start | bytes 18440 | tf_op jit(solution)/shard_map/ppermute | solution.py:94
  97.0 3.5 %subtract_convert_fusion = (bf16[768,1024]{1,0:T(8,128)(2,1)S(1)}, bf16[768,1024]{1,0:T(8,128)(2,1)}) fusion(f32[768,1024]{1,0:T(8,128)S(1)} %copy-done, bf16[768,1024]{1,0:T(8,128)(2,1)} %param.29, f32[768]{0:T(1024)S(1)} %fusion.48, f32[768]{0:T(1024)S(1)} %get-tuple-element.111, f32[1024]{0:T(1024)S(1)} %copy-done.14), kind=kLoop, calls=%fused_computation.3 | loop fusion | flops 7077888 | bytes 7874560 | tf_op jit(solution)/shard_map/convert_element_type | solution.py:176
  101.8 3.3 %collective-permute-start.13 = (bf16[528,128]{1,0:T(8,128)(2,1)S(1)}, bf16[528,128]{1,0:T(8,128)(2,1)S(1)}, u32[]{:S(2)}, u32[]{:S(2)}) collective-permute-start(bf16[528,128]{1,0:T(8,128)(2,1)S(1)} %pad_maximum_fusion.1), channel_id=1, source_target_pairs={{0,8},{8,0},{16,24},{24,16},{32,40},{40,32},{48,56},{56,48},{64,72... | collective-permute-start | bytes 405512 | tf_op jit(solution)/shard_map/ppermute | solution.py:23
  108.1 3.1 %collective-permute-start.14 = (f32[528,128]{1,0:T(8,128)S(1)}, f32[528,128]{1,0:T(8,128)S(1)}, u32[]{:S(2)}, u32[]{:S(2)}) collective-permute-start(f32[528,128]{1,0:T(8,128)S(1)} %select_maximum_fusion), channel_id=1, source_target_pairs={{16,0},{24,8},{32,16},{40,24},{48,32},{56,40},{64,48},{72,56},{80,... | collective-permute-start | bytes 811016 | tf_op jit(solution)/shard_map/ppermute | solution.py:19
  112.1 5.6 %collective-permute-done.14 = f32[528,128]{1,0:T(8,128)S(1)} collective-permute-done((f32[528,128]{1,0:T(8,128)S(1)}, f32[528,128]{1,0:T(8,128)S(1)}, u32[]{:S(2)}, u32[]{:S(2)}) %collective-permute-start.14) | collective-permute-done | bytes 270368 | tf_op jit(solution)/shard_map/ppermute | solution.py:19
  119.0 5.4 %collective-permute-start.15 = (bf16[528,128]{1,0:T(8,128)(2,1)S(1)}, bf16[528,128]{1,0:T(8,128)(2,1)S(1)}, u32[]{:S(2)}, u32[]{:S(2)}) collective-permute-start(bf16[528,128]{1,0:T(8,128)(2,1)S(1)} %fusion.37), channel_id=1, source_target_pairs={{16,0},{24,8},{32,16},{40,24},{48,32},{56,40},{64,48},{72,56},{80,... | collective-permute-start | bytes 405512 | tf_op jit(solution)/shard_map/ppermute | solution.py:19
  124.4 6.8 %multiply_convert_fusion = bf16[8,768,768]{2,1,0:T(8,128)(2,1)} fusion(f32[768,768]{1,0:T(8,128)} %copy-done.3, bf16[768,1024]{1,0:T(8,128)(2,1)S(1)} %copy-done.2, bf16[768,1024]{1,0:T(8,128)(2,1)} %refs_1_.4), kind=kOutput, calls=%fused_computation.1 | convolution fusion | flops 1217396736 | bytes 14942208 | tf_op jit(solution)/shard_map/htb,hsb->hts/dot_general | solution.py:183
  133.3 3.0 %collective-permute-start.16 = (bf16[528,128]{1,0:T(8,128)(2,1)S(1)}, bf16[528,128]{1,0:T(8,128)(2,1)S(1)}, u32[]{:S(2)}, u32[]{:S(2)}) collective-permute-start(bf16[528,128]{1,0:T(8,128)(2,1)S(1)} %fusion.36), channel_id=1, source_target_pairs={{32,0},{40,8},{48,16},{56,24},{64,32},{72,40},{80,48},{88,56},{96,... | collective-permute-start | bytes 405512 | tf_op jit(solution)/shard_map/ppermute | solution.py:19
  136.3 8.0 %fusion.6.refs_0_ = f32[8,768,128]{2,1,0:T(8,128)} fusion(bf16[8,768,768]{2,1,0:T(8,128)(2,1)} %multiply_convert_fusion, bf16[768,1024]{1,0:T(8,128)(2,1)S(1)} %copy-done.6), kind=kOutput, calls=%fused_computation.18 | convolution fusion | flops 1207959552 | bytes 14155776 | tf_op jit(solution)/shard_map/hts,hsa->hta/dot_general | solution.py:186
  147.7 2.7 %collective-permute-start.17 = (bf16[528,128]{1,0:T(8,128)(2,1)S(1)}, bf16[528,128]{1,0:T(8,128)(2,1)S(1)}, u32[]{:S(2)}, u32[]{:S(2)}) collective-permute-start(bf16[528,128]{1,0:T(8,128)(2,1)S(1)} %fusion.38), channel_id=1, source_target_pairs={{64,0},{72,8},{80,16},{88,24},{96,32},{104,40},{112,48},{120,56},{... | collective-permute-start | bytes 405512 | tf_op jit(solution)/shard_map/ppermute | solution.py:19
  150.4 8.4 %fusion.2.refs_0_ = f32[8,768,128]{2,1,0:T(8,128)} fusion(bf16[8,768,768]{2,1,0:T(8,128)(2,1)} %multiply_convert_fusion.1, bf16[768,1024]{1,0:T(8,128)(2,1)S(1)} %copy-done.2), kind=kOutput, calls=%fused_computation.12 | convolution fusion | flops 1207959552 | bytes 14155776 | tf_op jit(solution)/shard_map/hts,htb->hsb/dot_general | solution.py:190
  165.5 8.3 %fusion.65.refs_0_ = f32[8,768,128]{2,1,0:T(8,128)} fusion(bf16[8,768,768]{2,1,0:T(8,128)(2,1)} %multiply_convert_fusion, bf16[8,768,128]{1,2,0:T(8,128)(2,1)S(1)} %bitcast.139), kind=kOutput, calls=%fused_computation.133 | convolution fusion | flops 1207959552 | bytes 14155776 | tf_op jit(solution)/shard_map/hts,hta->hsa/dot_general | solution.py:189
  173.7 7.3 %shard_map.94 = bf16[768,1024]{1,0:T(8,128)(2,1)} custom-call(f32[8,768,128]{2,1,0:T(8,128)} %fusion.6.refs_0_, bf16[768,1024]{1,0:T(8,128)(2,1)} %copy-done.1, bf16[768,1]{1,0:T(8,128)(2,1)} %broadcast_in_dim.6.refs_2_, bf16[8,128,128]{2,1,0:T(8,128)(2,1)} %maximum_select_fusion.refs_3_), custom_call_target="tpu_custom_call" | custom-call | tf_op jit(solution)/shard_map/pallas_call | solution.py:118
  181.7 7.3 %shard_map.96 = bf16[768,1024]{1,0:T(8,128)(2,1)} custom-call(f32[8,768,128]{2,1,0:T(8,128)} %fusion.2.refs_0_, bf16[768,1024]{1,0:T(8,128)(2,1)} %refs_1_.5, bf16[768,1]{1,0:T(8,128)(2,1)} %broadcast_in_dim.7.refs_2_, bf16[8,128,128]{2,1,0:T(8,128)(2,1)} %maximum_select_fusion.1.refs_3_), custom_call_target="tpu_custom_call" | custom-call | tf_op jit(solution)/shard_map/pallas_call | solution.py:118
  189.0 7.3 %shard_map.95 = bf16[768,1024]{1,0:T(8,128)(2,1)} custom-call(f32[8,768,128]{2,1,0:T(8,128)} %fusion.65.refs_0_, bf16[768,1024]{1,0:T(8,128)(2,1)} %refs_1_.4, bf16[768,1]{1,0:T(8,128)(2,1)} %broadcast_in_dim.7.refs_2_, bf16[8,128,128]{2,1,0:T(8,128)(2,1)} %maximum_select_fusion.1.refs_3_), custom_call_target="tpu_custom_call" | custom-call | tf_op jit(solution)/shard_map/pallas_call | solution.py:118
  (117 shorter events, 24.3 us)
Async XLA Ops:
  8.2 18.7 %copy-start.13 = (s32[768]{0:T(1024)S(1)}, s32[768]{0:T(1024)}, u32[]{:S(2)}) copy-start(s32[768]{0:T(1024)} %param.31) | copy-start | bytes 9220
  8.3 1.8 collective-permute-start
  12.1 11.7 %collective-permute-start.1 = (f32[528,128]{1,0:T(8,128)S(1)}, f32[528,128]{1,0:T(8,128)S(1)}, u32[]{:S(2)}, u32[]{:S(2)}) collective-permute-start(f32[528,128]{1,0:T(8,128)S(1)} %select_maximum_fusion.1), channel_id=1, source_target_pairs={{0,16},{8,24},{16,32},{24,40},{32,48},{40,56},{48,64},{56,72},{64,... | collective-permute-start | bytes 811016 | tf_op jit(solution)/shard_map/ppermute | solution.py:19
  24.9 7.9 %collective-permute-start.2 = (bf16[528,128]{1,0:T(8,128)(2,1)S(1)}, bf16[528,128]{1,0:T(8,128)(2,1)S(1)}, u32[]{:S(2)}, u32[]{:S(2)}) collective-permute-start(bf16[528,128]{1,0:T(8,128)(2,1)S(1)} %fusion.40), channel_id=1, source_target_pairs={{0,16},{8,24},{16,32},{24,40},{32,48},{40,56},{48,64},{56,72},{64,... | collective-permute-start | bytes 405512 | tf_op jit(solution)/shard_map/ppermute | solution.py:19
  27.1 9.4 %copy-start.3 = (f32[768,768]{1,0:T(8,128)}, f32[768,768]{1,0:T(8,128)S(1)}, u32[]{:S(2)}) copy-start(f32[768,768]{1,0:T(8,128)S(1)} %fusion.25) | copy-start | bytes 7077892
  34.6 10.1 %collective-permute-start.3 = (bf16[528,128]{1,0:T(8,128)(2,1)S(1)}, bf16[528,128]{1,0:T(8,128)(2,1)S(1)}, u32[]{:S(2)}, u32[]{:S(2)}) collective-permute-start(bf16[528,128]{1,0:T(8,128)(2,1)S(1)} %fusion.39), channel_id=1, source_target_pairs={{0,32},{8,40},{16,48},{24,56},{32,64},{40,72},{48,80},{56,88},{64,... | collective-permute-start | bytes 405512 | tf_op jit(solution)/shard_map/ppermute | solution.py:19
  46.5 13.9 %collective-permute-start.4 = (bf16[528,128]{1,0:T(8,128)(2,1)S(1)}, bf16[528,128]{1,0:T(8,128)(2,1)S(1)}, u32[]{:S(2)}, u32[]{:S(2)}) collective-permute-start(bf16[528,128]{1,0:T(8,128)(2,1)S(1)} %fusion.41), channel_id=1, source_target_pairs={{0,64},{8,72},{16,80},{24,88},{32,96},{40,104},{48,112},{56,120},{... | collective-permute-start | bytes 405512 | tf_op jit(solution)/shard_map/ppermute | solution.py:19
  62.5 3.7 %collective-permute-start.5 = (bf16[4,128,128]{2,1,0:T(8,128)(2,1)S(1)}, bf16[4,128,128]{2,1,0:T(8,128)(2,1)S(1)}, u32[]{:S(2)}, u32[]{:S(2)}) collective-permute-start(bf16[4,128,128]{2,1,0:T(8,128)(2,1)S(1)} %get-tuple-element.117), channel_id=1, source_target_pairs={{0,8},{8,0},{16,24},{24,16},{32,40},{40,32},{48,56},{56,48},{64,72... | collective-permute-start | bytes 393224 | tf_op jit(solution)/shard_map/ppermute | solution.py:23
  66.9 7.8 %copy-start.14 = (f32[1024]{0:T(1024)S(1)}, f32[1024]{0:T(1024)}, u32[]{:S(2)}) copy-start(f32[1024]{0:T(1024)} %param.30) | copy-start | bytes 12292
  74.7 22.3 %copy-start = (f32[768,1024]{1,0:T(8,128)S(1)}, f32[768,1024]{1,0:T(8,128)}, u32[]{:S(2)}) copy-start(f32[768,1024]{1,0:T(8,128)} %shard_map.93) | copy-start | bytes 9437188
  78.0 13.5 %collective-permute-start.6 = (f32[2,768]{1,0:T(2,128)S(1)}, f32[2,768]{1,0:T(2,128)S(1)}, u32[]{:S(2)}, u32[]{:S(2)}) collective-permute-start(f32[2,768]{1,0:T(2,128)S(1)} %pad_maximum_fusion.2), channel_id=1, source_target_pairs={{0,1},{1,2},{2,3},{3,4},{4,5},{5,6},{6,7},{7,0},{8,9},{9,10},{10,1... | collective-permute-start | bytes 18440 | tf_op jit(solution)/shard_map/ppermute | solution.py:94
  79.7 14.2 %collective-permute-start.7 = (f32[2,768]{1,0:T(2,128)S(1)}, f32[2,768]{1,0:T(2,128)S(1)}, u32[]{:S(2)}, u32[]{:S(2)}) collective-permute-start(f32[2,768]{1,0:T(2,128)S(1)} %pad_maximum_fusion.2), channel_id=1, source_target_pairs={{0,2},{1,3},{2,4},{3,5},{4,6},{5,7},{6,0},{7,1},{8,10},{9,11},{10,... | collective-permute-start | bytes 18440 | tf_op jit(solution)/shard_map/ppermute | solution.py:94
  82.8 11.8 %collective-permute-start.8 = (f32[2,768]{1,0:T(2,128)S(1)}, f32[2,768]{1,0:T(2,128)S(1)}, u32[]{:S(2)}, u32[]{:S(2)}) collective-permute-start(f32[2,768]{1,0:T(2,128)S(1)} %pad_maximum_fusion.2), channel_id=1, source_target_pairs={{0,3},{1,4},{2,5},{3,6},{4,7},{5,0},{6,1},{7,2},{8,11},{9,12},{10,... | collective-permute-start | bytes 18440 | tf_op jit(solution)/shard_map/ppermute | solution.py:94
  86.5 8.1 %collective-permute-start.9 = (f32[2,768]{1,0:T(2,128)S(1)}, f32[2,768]{1,0:T(2,128)S(1)}, u32[]{:S(2)}, u32[]{:S(2)}) collective-permute-start(f32[2,768]{1,0:T(2,128)S(1)} %pad_maximum_fusion.2), channel_id=1, source_target_pairs={{0,4},{1,5},{2,6},{3,7},{4,0},{5,1},{6,2},{7,3},{8,12},{9,13},{10,... | collective-permute-start | bytes 18440 | tf_op jit(solution)/shard_map/ppermute | solution.py:94
  87.0 7.6 %collective-permute-start.10 = (f32[2,768]{1,0:T(2,128)S(1)}, f32[2,768]{1,0:T(2,128)S(1)}, u32[]{:S(2)}, u32[]{:S(2)}) collective-permute-start(f32[2,768]{1,0:T(2,128)S(1)} %pad_maximum_fusion.2), channel_id=1, source_target_pairs={{0,5},{1,6},{2,7},{3,0},{4,1},{5,2},{6,3},{7,4},{8,13},{9,14},{10,... | collective-permute-start | bytes 18440 | tf_op jit(solution)/shard_map/ppermute | solution.py:94
  91.4 3.4 %collective-permute-start.11 = (f32[2,768]{1,0:T(2,128)S(1)}, f32[2,768]{1,0:T(2,128)S(1)}, u32[]{:S(2)}, u32[]{:S(2)}) collective-permute-start(f32[2,768]{1,0:T(2,128)S(1)} %pad_maximum_fusion.2), channel_id=1, source_target_pairs={{0,6},{1,7},{2,0},{3,1},{4,2},{5,3},{6,4},{7,5},{8,14},{9,15},{10,... | collective-permute-start | bytes 18440 | tf_op jit(solution)/shard_map/ppermute | solution.py:94
  93.8 2.5 %collective-permute-start.12 = (f32[2,768]{1,0:T(2,128)S(1)}, f32[2,768]{1,0:T(2,128)S(1)}, u32[]{:S(2)}, u32[]{:S(2)}) collective-permute-start(f32[2,768]{1,0:T(2,128)S(1)} %pad_maximum_fusion.2), channel_id=1, source_target_pairs={{0,7},{1,0},{2,1},{3,2},{4,3},{5,4},{6,5},{7,6},{8,15},{9,8},{10,9... | collective-permute-start | bytes 18440 | tf_op jit(solution)/shard_map/ppermute | solution.py:94
  97.0 3.6 %copy-start.4 = (bf16[768,1024]{0,1:T(8,128)(2,1)S(1)}, bf16[768,1024]{0,1:T(8,128)(2,1)}, u32[]{:S(2)}) copy-start(bf16[768,1024]{0,1:T(8,128)(2,1)} %copy.37) | copy-start | bytes 4718596
  101.7 17.3 %copy-start.11 = (bf16[8,128,128]{2,1,0:T(8,128)(2,1)}, bf16[8,128,128]{2,1,0:T(8,128)(2,1)S(1)}, u32[]{:S(2)}) copy-start(bf16[8,128,128]{2,1,0:T(8,128)(2,1)S(1)} %fusion.13) | copy-start | bytes 786436
  101.7 22.7 %copy-start.2 = (bf16[768,1024]{1,0:T(8,128)(2,1)S(1)}, bf16[768,1024]{1,0:T(8,128)(2,1)}, u32[]{:S(2)}) copy-start(bf16[768,1024]{1,0:T(8,128)(2,1)} %copy-done.1) | copy-start | bytes 4718596
  101.8 4.3 %collective-permute-start.13 = (bf16[528,128]{1,0:T(8,128)(2,1)S(1)}, bf16[528,128]{1,0:T(8,128)(2,1)S(1)}, u32[]{:S(2)}, u32[]{:S(2)}) collective-permute-start(bf16[528,128]{1,0:T(8,128)(2,1)S(1)} %pad_maximum_fusion.1), channel_id=1, source_target_pairs={{0,8},{8,0},{16,24},{24,16},{32,40},{40,32},{48,56},{56,48},{64,72... | collective-permute-start | bytes 405512 | tf_op jit(solution)/shard_map/ppermute | solution.py:23
  108.0 11.0 %copy-start.7 = (bf16[512,128]{1,0:T(8,128)(2,1)}, bf16[512,128]{1,0:T(8,128)(2,1)S(1)}, u32[]{:S(2)}) copy-start(bf16[512,128]{1,0:T(8,128)(2,1)S(1)} %slice.342) | copy-start | bytes 393220
  108.1 9.6 %collective-permute-start.14 = (f32[528,128]{1,0:T(8,128)S(1)}, f32[528,128]{1,0:T(8,128)S(1)}, u32[]{:S(2)}, u32[]{:S(2)}) collective-permute-start(f32[528,128]{1,0:T(8,128)S(1)} %select_maximum_fusion), channel_id=1, source_target_pairs={{16,0},{24,8},{32,16},{40,24},{48,32},{56,40},{64,48},{72,56},{80,... | collective-permute-start | bytes 811016 | tf_op jit(solution)/shard_map/ppermute | solution.py:19
  119.0 17.2 %copy-start.6 = (bf16[768,1024]{1,0:T(8,128)(2,1)S(1)}, bf16[768,1024]{1,0:T(8,128)(2,1)}, u32[]{:S(2)}) copy-start(bf16[768,1024]{1,0:T(8,128)(2,1)} %refs_1_.5) | copy-start | bytes 4718596
  119.0 12.3 %collective-permute-start.15 = (bf16[528,128]{1,0:T(8,128)(2,1)S(1)}, bf16[528,128]{1,0:T(8,128)(2,1)S(1)}, u32[]{:S(2)}, u32[]{:S(2)}) collective-permute-start(bf16[528,128]{1,0:T(8,128)(2,1)S(1)} %fusion.37), channel_id=1, source_target_pairs={{16,0},{24,8},{32,16},{40,24},{48,32},{56,40},{64,48},{72,56},{80,... | collective-permute-start | bytes 405512 | tf_op jit(solution)/shard_map/ppermute | solution.py:19
  133.3 11.0 %collective-permute-start.16 = (bf16[528,128]{1,0:T(8,128)(2,1)S(1)}, bf16[528,128]{1,0:T(8,128)(2,1)S(1)}, u32[]{:S(2)}, u32[]{:S(2)}) collective-permute-start(bf16[528,128]{1,0:T(8,128)(2,1)S(1)} %fusion.36), channel_id=1, source_target_pairs={{32,0},{40,8},{48,16},{56,24},{64,32},{72,40},{80,48},{88,56},{96,... | collective-permute-start | bytes 405512 | tf_op jit(solution)/shard_map/ppermute | solution.py:19
  147.7 15.6 %copy-start.10 = (bf16[528,128]{1,0:T(8,128)(2,1)S(1)}, bf16[528,128]{1,0:T(8,128)(2,1)}, u32[]{:S(2)}) copy-start(bf16[528,128]{1,0:T(8,128)(2,1)} %copy-done.9) | copy-start | bytes 405508
  147.7 13.8 %collective-permute-start.17 = (bf16[528,128]{1,0:T(8,128)(2,1)S(1)}, bf16[528,128]{1,0:T(8,128)(2,1)S(1)}, u32[]{:S(2)}, u32[]{:S(2)}) collective-permute-start(bf16[528,128]{1,0:T(8,128)(2,1)S(1)} %fusion.38), channel_id=1, source_target_pairs={{64,0},{72,8},{80,16},{88,24},{96,32},{104,40},{112,48},{120,56},{... | collective-permute-start | bytes 405512 | tf_op jit(solution)/shard_map/ppermute | solution.py:19
  150.4 13.1 %copy-start.12 = (bf16[8,128,128]{2,1,0:T(8,128)(2,1)S(1)}, bf16[8,128,128]{2,1,0:T(8,128)(2,1)}, u32[]{:S(2)}) copy-start(bf16[8,128,128]{2,1,0:T(8,128)(2,1)} %copy-done.11) | copy-start | bytes 786436
  158.8 4.7 %copy-start.8 = (bf16[512,128]{1,0:T(8,128)(2,1)S(1)}, bf16[512,128]{1,0:T(8,128)(2,1)}, u32[]{:S(2)}) copy-start(bf16[512,128]{1,0:T(8,128)(2,1)} %copy-done.7) | copy-start | bytes 393220
  158.8 6.7 %copy-start.5 = (bf16[768,1024]{0,1:T(8,128)(2,1)S(1)}, bf16[768,1024]{0,1:T(8,128)(2,1)}, u32[]{:S(2)}) copy-start(bf16[768,1024]{0,1:T(8,128)(2,1)} %copy.37) | copy-start | bytes 4718596
  163.6 17.4 %collective-permute-start.18 = (bf16[4,128,128]{2,1,0:T(8,128)(2,1)S(1)}, bf16[4,128,128]{2,1,0:T(8,128)(2,1)S(1)}, u32[]{:S(2)}, u32[]{:S(2)}) collective-permute-start(bf16[4,128,128]{2,1,0:T(8,128)(2,1)S(1)} %get-tuple-element.115), channel_id=1, source_target_pairs={{0,8},{8,0},{16,24},{24,16},{32,40},{40,32},{48,56},{56,48},{64,72... | collective-permute-start | bytes 393224 | tf_op jit(solution)/shard_map/ppermute | solution.py:23
  (2 other events, 1.8 us)

commit v5 on v4

--- a/solution.py
+++ b/solution.py
@@ -88,43 +88,42 @@
 
 def group_sum(x, axis):
     count = lax.axis_size(axis)
-    index = lax.axis_index(axis)
-    parts = [x]
-    for step in range(1, count):
-        parts.append(lax.ppermute(x, axis, [(i, (i + step) % count) for i in range(count)]))
-    ordered = jnp.stack(parts)
-    slot = (index - jnp.arange(count)) % count
-    ordered = ordered[slot]
-    total = ordered[0]
-    for source in range(1, count):
-        total = total + ordered[source]
-    return total
+    step = 1
+    while step < count:
+        x = x + lax.ppermute(x, axis, [(i, i ^ step) for i in range(count)])
+        step = step * 2
+    return x
 
 
 def finish_body(local_ref, rows_ref, mask_ref, state_ref, out_ref, *, flip):
-    rows = rows_ref[...] * mask_ref[...]
-    state = state_ref[0]
-    if flip:
-        extra = lax.dot_general(
-            rows, state, (((1,), (1,)), ((), ())), preferred_element_type=jnp.float32
-        )
-    else:
-        extra = jnp.dot(rows, state, preferred_element_type=jnp.float32)
-    out_ref[...] = (local_ref[0] + extra).astype(out_ref.dtype)
+    width = local_ref.shape[2]
+    mask = mask_ref[...]
+    for head in range(local_ref.shape[0]):
+        cols = slice(head * width, (head + 1) * width)
+        rows = rows_ref[:, cols] * mask
+        state = state_ref[head]
+        if flip:
+            extra = lax.dot_general(
+                rows, state, (((1,), (1,)), ((), ())), preferred_element_type=jnp.float32
+            )
+        else:
+            extra = jnp.dot(rows, state, preferred_element_type=jnp.float32)
+        out_ref[:, cols] = (local_ref[head] + extra).astype(out_ref.dtype)
 
 
 def finished(local, rows, mask, state, flip, kind, interpret=False):
     heads, tokens, width = local.shape
+    block = 256 if tokens % 256 == 0 else tokens
     return pl.pallas_call(
         lambda *refs: finish_body(*refs, flip=flip),
-        grid=(heads,),
+        grid=(tokens // block,),
         in_specs=[
-            pl.BlockSpec((1, tokens, width), lambda h: (h, 0, 0)),
-            pl.BlockSpec((tokens, width), lambda h: (0, h)),
-            pl.BlockSpec((tokens, 1), lambda h: (0, 0)),
-            pl.BlockSpec((1, width, width), lambda h: (h, 0, 0)),
+            pl.BlockSpec((heads, block, width), lambda t: (0, t, 0)),
+            pl.BlockSpec((block, heads * width), lambda t: (t, 0)),
+            pl.BlockSpec((block, 1), lambda t: (t, 0)),
+            pl.BlockSpec((heads, width, width), lambda t: (0, 0, 0)),
         ],
-        out_specs=pl.BlockSpec((tokens, width), lambda h: (0, h)),
+        out_specs=pl.BlockSpec((block, heads * width), lambda t: (t, 0)),
         out_shape=jax.ShapeDtypeStruct((tokens, heads * width), kind),
         interpret=interpret,
     )(local, rows, mask, state)

time: 198 us -> 188 us (0.949)
  Pallas kernels: 29.6 us -> 19.5 us
  waiting for transfers between devices: 20.2 us -> 28.8 us
  starting transfers between devices: 49.3 us -> 41.5 us
    pallas_call x4, Pallas kernels: 29.6 us -> 19.5 us  [finished(): pl.pallas_call(lambda *refs: finish_body(*refs, flip=flip), grid=(tokens...]
    ppermute x8, waiting for transfers between devices: 16.4 us -> 23.9 us  [moved(): return lax.ppermute(x, axis, pairs)]
    ppermute x7 -> x3, starting transfers between devices: 16.6 us -> 11.2 us  [group_sum(): x = x + lax.ppermute(x, axis, [(i, i ^ step) for i in range(count)])]
    ppermute x8, starting transfers between devices: 24.1 us -> 20.6 us  [moved(): return lax.ppermute(x, axis, pairs)]
  transfers between devices with their start and end apart: 19 -> 15, of which waited for: 8 -> 9; matrix products, arithmetic and copies ran while one was open for 27% -> 28% of each run, Pallas kernels for 4% -> 3%
where the time goes in v5:
time: 188 us; the launch traced here: 187 us
  matrix products  51.1 us (27%)
  starting transfers between devices  41.5 us (22%)
  waiting for transfers between devices  28.8 us (15%)
  Pallas kernels  19.5 us (10%)
  between operations  18.9 us (10%)
  other arithmetic  13.4 us (7%)
  local copies, waits for them, and re-layouts  13.3 us (7%)
    ppermute x8, waiting for transfers between devices, moved(): return lax.ppermute(x, axis, pairs)  23.9 us
    ppermute x8, starting transfers between devices, moved(): return lax.ppermute(x, axis, pairs)  20.6 us
    pallas_call x4, Pallas kernels, finished(): pl.pallas_call(lambda *refs: finish_body(*refs, flip=flip), grid=(tokens...  19.5 us
    ppermute x3, starting transfers between devices, group_sum(): x = x + lax.ppermute(x, axis, [(i, i ^ step) for i in range(count)])  11.2 us
    ppermute x4, starting transfers between devices, swapped(): return lax.ppermute(x, axis, [(i, i ^ 1) for i in range(count)])  9.73 us
    dot_general x1, matrix products, shards(): jnp.einsum('hts,htb->hsb', scores, delta_heads, preferred_element_type=jn...  8.4 us
    dot_general x1, matrix products, shards(): jnp.einsum('hts,hta->hsa', dscores, query_heads, preferred_element_type=j...  8.27 us
    dot_general x1, matrix products, shards(): jnp.einsum('hta,hsa->hts', query_heads, key_heads, preferred_element_type...  8.21 us
  transfers between devices with their start and end apart: 15, of which 9 were waited for; matrix products, arithmetic and copies ran while one was open for 28% of the time, Pallas kernels for 3%

profile of v5, /device:TPU:17, one launch (start us, length us, event | category | flops | bytes accessed | tf_op | source)
XLA Modules:
  0.0 186.6 jit_solution(9465997645021816540)
XLA Ops:
  2.6 2.0 %compare_convert_fusion = (bf16[768]{0:T(1024)(128)(2,1)S(1)}, bf16[768]{0:T(1024)(128)(2,1)S(1)}) fusion(s32[768]{0:T(1024)} %param.31, s32[]{:T(128)} %bitcast.5, s32[]{:T(128)} %bitcast.4), kind=kLoop, calls=%fused_computation.94 | loop fusion | flops 3072 | bytes 6152 | tf_op jit(solution)/shard_map/convert_element_type | solution.py:149
  5.3 2.8 %fusion.10 = bf16[8,128,128]{2,1,0:T(8,128)(2,1)S(1)} fusion(bf16[768]{0:T(1024)(128)(2,1)S(1)} %get-tuple-element.118, bf16[768,1024]{1,0:T(8,128)(2,1)} %refs_1_.4, bf16[768,1024]{1,0:T(8,128)(2,1)} %refs_1_.5), kind=kOutput, calls=%fused_computation.20 | convolution fusion | flops 204603392 | bytes 3409408 | tf_op jit(solution)/shard_map/hta,htb->hab/dot_general | solution.py:154
  12.1 3.1 %collective-permute-start.1 = (f32[528,128]{1,0:T(8,128)S(1)}, f32[528,128]{1,0:T(8,128)S(1)}, u32[]{:S(2)}, u32[]{:S(2)}) collective-permute-start(f32[528,128]{1,0:T(8,128)S(1)} %select_maximum_fusion.1), channel_id=1, source_target_pairs={{0,16},{8,24},{16,32},{24,40},{32,48},{40,56},{48,64},{56,72},{64,... | collective-permute-start | bytes 811016 | tf_op jit(solution)/shard_map/ppermute | solution.py:19
  15.3 8.6 %collective-permute-done.1 = f32[528,128]{1,0:T(8,128)S(1)} collective-permute-done((f32[528,128]{1,0:T(8,128)S(1)}, f32[528,128]{1,0:T(8,128)S(1)}, u32[]{:S(2)}, u32[]{:S(2)}) %collective-permute-start.1) | collective-permute-done | bytes 270368 | tf_op jit(solution)/shard_map/ppermute | solution.py:19
  25.1 1.9 %collective-permute-start.2 = (bf16[528,128]{1,0:T(8,128)(2,1)S(1)}, bf16[528,128]{1,0:T(8,128)(2,1)S(1)}, u32[]{:S(2)}, u32[]{:S(2)}) collective-permute-start(bf16[528,128]{1,0:T(8,128)(2,1)S(1)} %fusion.40), channel_id=1, source_target_pairs={{0,16},{8,24},{16,32},{24,40},{32,48},{40,56},{48,64},{56,72},{64,... | collective-permute-start | bytes 405512 | tf_op jit(solution)/shard_map/ppermute | solution.py:19
  27.0 5.9 %collective-permute-done.2 = bf16[528,128]{1,0:T(8,128)(2,1)S(1)} collective-permute-done((bf16[528,128]{1,0:T(8,128)(2,1)S(1)}, bf16[528,128]{1,0:T(8,128)(2,1)S(1)}, u32[]{:S(2)}, u32[]{:S(2)}) %collective-permute-start.2) | collective-permute-done | bytes 135200 | tf_op jit(solution)/shard_map/ppermute | solution.py:19
  34.8 1.9 %collective-permute-start.3 = (bf16[528,128]{1,0:T(8,128)(2,1)S(1)}, bf16[528,128]{1,0:T(8,128)(2,1)S(1)}, u32[]{:S(2)}, u32[]{:S(2)}) collective-permute-start(bf16[528,128]{1,0:T(8,128)(2,1)S(1)} %fusion.39), channel_id=1, source_target_pairs={{0,32},{8,40},{16,48},{24,56},{32,64},{40,72},{48,80},{56,88},{64,... | collective-permute-start | bytes 405512 | tf_op jit(solution)/shard_map/ppermute | solution.py:19
  37.0 3.4 %copy.37 = bf16[768,1024]{0,1:T(8,128)(2,1)} copy(bf16[768,1024]{1,0:T(8,128)(2,1)} %refs_1_.3) | data formatting | bytes 3145728 | tf_op jit(solution)/shard_map/reshape | solution.py:137
  40.4 2.6 %collective-permute-done.3 = bf16[528,128]{1,0:T(8,128)(2,1)S(1)} collective-permute-done((bf16[528,128]{1,0:T(8,128)(2,1)S(1)}, bf16[528,128]{1,0:T(8,128)(2,1)S(1)}, u32[]{:S(2)}, u32[]{:S(2)}) %collective-permute-start.3) | collective-permute-done | bytes 135200 | tf_op jit(solution)/shard_map/ppermute | solution.py:19
  45.5 2.9 %collective-permute-start.4 = (bf16[528,128]{1,0:T(8,128)(2,1)}, bf16[528,128]{1,0:T(8,128)(2,1)S(1)}, u32[]{:S(2)}, u32[]{:S(2)}) collective-permute-start(bf16[528,128]{1,0:T(8,128)(2,1)} %fusion.41), channel_id=1, source_target_pairs={{0,64},{8,72},{16,80},{24,88},{32,96},{40,104},{48,112},{56,120},{... | collective-permute-start | bytes 405512 | tf_op jit(solution)/shard_map/ppermute | solution.py:19
  48.4 8.2 %multiply_convert_fusion.1 = bf16[8,768,768]{2,1,0:T(8,128)(2,1)} fusion(f32[768,768]{1,0:T(8,128)S(1)} %fusion.25, bf16[8,768,128]{1,2,0:T(8,128)(2,1)} %bitcast.119, bf16[768,1024]{1,0:T(8,128)(2,1)} %refs_1_.5), kind=kOutput, calls=%fused_computation.1 | convolution fusion | flops 1217396736 | bytes 14942208 | tf_op jit(solution)/shard_map/hta,hsa->hts/dot_general | solution.py:159
  61.5 3.9 %collective-permute-start.5 = (bf16[4,128,128]{2,1,0:T(8,128)(2,1)S(1)}, bf16[4,128,128]{2,1,0:T(8,128)(2,1)S(1)}, u32[]{:S(2)}, u32[]{:S(2)}) collective-permute-start(bf16[4,128,128]{2,1,0:T(8,128)(2,1)S(1)} %get-tuple-element.117), channel_id=1, source_target_pairs={{0,8},{8,0},{16,24},{24,16},{32,40},{40,32},{48,56},{56,48},{64,72... | collective-permute-start | bytes 393224 | tf_op jit(solution)/shard_map/ppermute | solution.py:23
  65.4 8.0 %fusion.5.refs_0_ = f32[8,768,128]{2,1,0:T(8,128)} fusion(bf16[8,768,768]{2,1,0:T(8,128)(2,1)} %multiply_convert_fusion.1, bf16[768,1024]{1,0:T(8,128)(2,1)S(1)} %copy-done.7), kind=kOutput, calls=%fused_computation.15 | convolution fusion | flops 1207959552 | bytes 14155776 | tf_op jit(solution)/shard_map/hts,hsb->htb/dot_general | solution.py:162
  75.0 5.3 %shard_map.93 = f32[768,1024]{1,0:T(8,128)} custom-call(f32[8,768,128]{2,1,0:T(8,128)} %fusion.5.refs_0_, bf16[768,1024]{1,0:T(8,128)(2,1)} %refs_1_.3, bf16[768,1]{1,0:T(8,128)(2,1)} %broadcast_in_dim.6.refs_2_, bf16[8,128,128]{2,1,0:T(8,128)(2,1)} %maximum_select_fusion.refs_3_), custom_call_target="tpu_custom_call" | custom-call | tf_op jit(solution)/shard_map/pallas_call | solution.py:117
  80.3 3.2 %multiply_reduce_fusion.1 = (f32[768]{0:T(1024)S(1)}, f32[768]{0:T(1024)S(1)}) fusion(f32[768,1024]{1,0:T(8,128)} %shard_map.93, bf16[768,1024]{1,0:T(8,128)(2,1)} %param.29, f32[1024]{0:T(1024)S(1)} %copy-done.15), kind=kLoop, calls=%fused_computation.6 | loop fusion | flops 4717056 | bytes 4728832 | tf_op jit(solution)/shard_map/reduce_sum | solution.py:168
  86.3 3.1 %collective-permute-start.7 = (f32[2,768]{1,0:T(2,128)S(1)}, f32[2,768]{1,0:T(2,128)S(1)}, u32[]{:S(2)}, u32[]{:S(2)}) collective-permute-start(f32[2,768]{1,0:T(2,128)S(1)} %fusion.58), channel_id=1, source_target_pairs={{0,2},{1,3},{2,0},{3,1},{4,6},{5,7},{6,4},{7,5},{8,10},{9,11},{10,... | collective-permute-start | bytes 18440 | tf_op jit(solution)/shard_map/ppermute | solution.py:93
  90.4 6.4 %collective-permute-start.8 = (f32[2,768]{1,0:T(2,128)S(1)}, f32[2,768]{1,0:T(2,128)S(1)}, u32[]{:S(2)}, u32[]{:S(2)}) collective-permute-start(f32[2,768]{1,0:T(2,128)S(1)} %fusion.71), channel_id=1, source_target_pairs={{0,4},{1,5},{2,6},{3,7},{4,0},{5,1},{6,2},{7,3},{8,12},{9,13},{10,... | collective-permute-start | bytes 18440 | tf_op jit(solution)/shard_map/ppermute | solution.py:93
  97.9 3.5 %subtract_convert_fusion = (bf16[768,1024]{1,0:T(8,128)(2,1)S(1)}, bf16[768,1024]{1,0:T(8,128)(2,1)}) fusion(f32[768,1024]{1,0:T(8,128)S(1)} %copy-done, bf16[768,1024]{1,0:T(8,128)(2,1)} %param.29, f32[768]{0:T(1024)S(1)} %fusion.48, f32[768]{0:T(1024)S(1)} %get-tuple-element.111, f32[1024]{0:T(1024)S(1)} %copy-done.15), kind=kLoop, calls=%fused_computation.2 | loop fusion | flops 7077888 | bytes 7874560 | tf_op jit(solution)/shard_map/convert_element_type | solution.py:175
  102.6 3.3 %collective-permute-start.9 = (bf16[528,128]{1,0:T(8,128)(2,1)S(1)}, bf16[528,128]{1,0:T(8,128)(2,1)S(1)}, u32[]{:S(2)}, u32[]{:S(2)}) collective-permute-start(bf16[528,128]{1,0:T(8,128)(2,1)S(1)} %pad_maximum_fusion.1), channel_id=1, source_target_pairs={{0,8},{8,0},{16,24},{24,16},{32,40},{40,32},{48,56},{56,48},{64,72... | collective-permute-start | bytes 405512 | tf_op jit(solution)/shard_map/ppermute | solution.py:23
  108.7 1.9 %collective-permute-start.10 = (f32[528,128]{1,0:T(8,128)S(1)}, f32[528,128]{1,0:T(8,128)S(1)}, u32[]{:S(2)}, u32[]{:S(2)}) collective-permute-start(f32[528,128]{1,0:T(8,128)S(1)} %select_maximum_fusion), channel_id=1, source_target_pairs={{16,0},{24,8},{32,16},{40,24},{48,32},{56,40},{64,48},{72,56},{80,... | collective-permute-start | bytes 811016 | tf_op jit(solution)/shard_map/ppermute | solution.py:19
  111.5 6.8 %collective-permute-done.10 = f32[528,128]{1,0:T(8,128)S(1)} collective-permute-done((f32[528,128]{1,0:T(8,128)S(1)}, f32[528,128]{1,0:T(8,128)S(1)}, u32[]{:S(2)}, u32[]{:S(2)}) %collective-permute-start.10) | collective-permute-done | bytes 270368 | tf_op jit(solution)/shard_map/ppermute | solution.py:19
  119.5 4.4 %collective-permute-start.11 = (bf16[528,128]{1,0:T(8,128)(2,1)S(1)}, bf16[528,128]{1,0:T(8,128)(2,1)S(1)}, u32[]{:S(2)}, u32[]{:S(2)}) collective-permute-start(bf16[528,128]{1,0:T(8,128)(2,1)S(1)} %fusion.37), channel_id=1, source_target_pairs={{16,0},{24,8},{32,16},{40,24},{48,32},{56,40},{64,48},{72,56},{80,... | collective-permute-start | bytes 405512 | tf_op jit(solution)/shard_map/ppermute | solution.py:19
  124.0 6.8 %multiply_convert_fusion = bf16[8,768,768]{2,1,0:T(8,128)(2,1)} fusion(f32[768,768]{1,0:T(8,128)} %copy-done.3, bf16[768,1024]{1,0:T(8,128)(2,1)S(1)} %copy-done.2, bf16[768,1024]{1,0:T(8,128)(2,1)} %refs_1_.4), kind=kOutput, calls=%fused_computation | convolution fusion | flops 1217396736 | bytes 14942208 | tf_op jit(solution)/shard_map/htb,hsb->hts/dot_general | solution.py:182
  132.6 1.9 %collective-permute-start.12 = (bf16[528,128]{1,0:T(8,128)(2,1)S(1)}, bf16[528,128]{1,0:T(8,128)(2,1)S(1)}, u32[]{:S(2)}, u32[]{:S(2)}) collective-permute-start(bf16[528,128]{1,0:T(8,128)(2,1)S(1)} %fusion.36), channel_id=1, source_target_pairs={{32,0},{40,8},{48,16},{56,24},{64,32},{72,40},{80,48},{88,56},{96,... | collective-permute-start | bytes 405512 | tf_op jit(solution)/shard_map/ppermute | solution.py:19
  134.6 8.0 %fusion.6.refs_0_ = f32[8,768,128]{2,1,0:T(8,128)} fusion(bf16[8,768,768]{2,1,0:T(8,128)(2,1)} %multiply_convert_fusion, bf16[768,1024]{1,0:T(8,128)(2,1)S(1)} %copy-done.6), kind=kOutput, calls=%fused_computation.17 | convolution fusion | flops 1207959552 | bytes 14155776 | tf_op jit(solution)/shard_map/hts,hsa->hta/dot_general | solution.py:185
  145.9 2.5 %collective-permute-start.13 = (bf16[528,128]{1,0:T(8,128)(2,1)S(1)}, bf16[528,128]{1,0:T(8,128)(2,1)S(1)}, u32[]{:S(2)}, u32[]{:S(2)}) collective-permute-start(bf16[528,128]{1,0:T(8,128)(2,1)S(1)} %fusion.38), channel_id=1, source_target_pairs={{64,0},{72,8},{80,16},{88,24},{96,32},{104,40},{112,48},{120,56},{... | collective-permute-start | bytes 405512 | tf_op jit(solution)/shard_map/ppermute | solution.py:19
  148.4 8.4 %fusion.2.refs_0_ = f32[8,768,128]{2,1,0:T(8,128)} fusion(bf16[8,768,768]{2,1,0:T(8,128)(2,1)} %multiply_convert_fusion.1, bf16[768,1024]{1,0:T(8,128)(2,1)S(1)} %copy-done.2), kind=kOutput, calls=%fused_computation.11 | convolution fusion | flops 1207959552 | bytes 14155776 | tf_op jit(solution)/shard_map/hts,htb->hsb/dot_general | solution.py:189
  161.5 1.8 collective-permute-start.14
  163.3 8.3 %fusion.64.refs_0_ = f32[8,768,128]{2,1,0:T(8,128)} fusion(bf16[8,768,768]{2,1,0:T(8,128)(2,1)} %multiply_convert_fusion, bf16[8,768,128]{1,2,0:T(8,128)(2,1)S(1)} %bitcast.121), kind=kOutput, calls=%fused_computation.111 | convolution fusion | flops 1207959552 | bytes 14155776 | tf_op jit(solution)/shard_map/hts,hta->hsa/dot_general | solution.py:188
  171.6 4.7 %shard_map.94 = bf16[768,1024]{1,0:T(8,128)(2,1)} custom-call(f32[8,768,128]{2,1,0:T(8,128)} %fusion.6.refs_0_, bf16[768,1024]{1,0:T(8,128)(2,1)} %copy-done.1, bf16[768,1]{1,0:T(8,128)(2,1)} %broadcast_in_dim.6.refs_2_, bf16[8,128,128]{2,1,0:T(8,128)(2,1)} %maximum_select_fusion.refs_3_), custom_call_target="tpu_custom_call" | custom-call | tf_op jit(solution)/shard_map/pallas_call | solution.py:117
  177.1 4.7 %shard_map.96 = bf16[768,1024]{1,0:T(8,128)(2,1)} custom-call(f32[8,768,128]{2,1,0:T(8,128)} %fusion.2.refs_0_, bf16[768,1024]{1,0:T(8,128)(2,1)} %refs_1_.5, bf16[768,1]{1,0:T(8,128)(2,1)} %broadcast_in_dim.7.refs_2_, bf16[8,128,128]{2,1,0:T(8,128)(2,1)} %maximum_select_fusion.1.refs_3_), custom_call_target="tpu_custom_call" | custom-call | tf_op jit(solution)/shard_map/pallas_call | solution.py:117
  181.8 4.7 %shard_map.95 = bf16[768,1024]{1,0:T(8,128)(2,1)} custom-call(f32[8,768,128]{2,1,0:T(8,128)} %fusion.64.refs_0_, bf16[768,1024]{1,0:T(8,128)(2,1)} %refs_1_.4, bf16[768,1]{1,0:T(8,128)(2,1)} %broadcast_in_dim.7.refs_2_, bf16[8,128,128]{2,1,0:T(8,128)(2,1)} %maximum_select_fusion.1.refs_3_), custom_call_target="tpu_custom_call" | custom-call | tf_op jit(solution)/shard_map/pallas_call | solution.py:117
  (102 shorter events, 22.6 us)
Async XLA Ops:
  8.2 28.6 %copy-start.14 = (s32[768]{0:T(1024)S(1)}, s32[768]{0:T(1024)}, u32[]{:S(2)}) copy-start(s32[768]{0:T(1024)} %param.31) | copy-start | bytes 9220
  8.3 1.8 collective-permute-start
  12.1 11.7 %collective-permute-start.1 = (f32[528,128]{1,0:T(8,128)S(1)}, f32[528,128]{1,0:T(8,128)S(1)}, u32[]{:S(2)}, u32[]{:S(2)}) collective-permute-start(f32[528,128]{1,0:T(8,128)S(1)} %select_maximum_fusion.1), channel_id=1, source_target_pairs={{0,16},{8,24},{16,32},{24,40},{32,48},{40,56},{48,64},{56,72},{64,... | collective-permute-start | bytes 811016 | tf_op jit(solution)/shard_map/ppermute | solution.py:19
  25.1 7.9 %collective-permute-start.2 = (bf16[528,128]{1,0:T(8,128)(2,1)S(1)}, bf16[528,128]{1,0:T(8,128)(2,1)S(1)}, u32[]{:S(2)}, u32[]{:S(2)}) collective-permute-start(bf16[528,128]{1,0:T(8,128)(2,1)S(1)} %fusion.40), channel_id=1, source_target_pairs={{0,16},{8,24},{16,32},{24,40},{32,48},{40,56},{48,64},{56,72},{64,... | collective-permute-start | bytes 405512 | tf_op jit(solution)/shard_map/ppermute | solution.py:19
  34.8 8.2 %collective-permute-start.3 = (bf16[528,128]{1,0:T(8,128)(2,1)S(1)}, bf16[528,128]{1,0:T(8,128)(2,1)S(1)}, u32[]{:S(2)}, u32[]{:S(2)}) collective-permute-start(bf16[528,128]{1,0:T(8,128)(2,1)S(1)} %fusion.39), channel_id=1, source_target_pairs={{0,32},{8,40},{16,48},{24,56},{32,64},{40,72},{48,80},{56,88},{64,... | collective-permute-start | bytes 405512 | tf_op jit(solution)/shard_map/ppermute | solution.py:19
  37.0 11.4 %copy-start.3 = (f32[768,768]{1,0:T(8,128)}, f32[768,768]{1,0:T(8,128)S(1)}, u32[]{:S(2)}) copy-start(f32[768,768]{1,0:T(8,128)S(1)} %fusion.25) | copy-start | bytes 7077892
  45.5 13.9 %collective-permute-start.4 = (bf16[528,128]{1,0:T(8,128)(2,1)}, bf16[528,128]{1,0:T(8,128)(2,1)S(1)}, u32[]{:S(2)}, u32[]{:S(2)}) collective-permute-start(bf16[528,128]{1,0:T(8,128)(2,1)} %fusion.41), channel_id=1, source_target_pairs={{0,64},{8,72},{16,80},{24,88},{32,96},{40,104},{48,112},{56,120},{... | collective-permute-start | bytes 405512 | tf_op jit(solution)/shard_map/ppermute | solution.py:19
  56.6 8.8 %copy-start.7 = (bf16[768,1024]{1,0:T(8,128)(2,1)S(1)}, bf16[768,1024]{1,0:T(8,128)(2,1)}, u32[]{:S(2)}) copy-start(bf16[768,1024]{1,0:T(8,128)(2,1)} %refs_1_.4) | copy-start | bytes 4718596
  61.5 12.7 %collective-permute-start.5 = (bf16[4,128,128]{2,1,0:T(8,128)(2,1)S(1)}, bf16[4,128,128]{2,1,0:T(8,128)(2,1)S(1)}, u32[]{:S(2)}, u32[]{:S(2)}) collective-permute-start(bf16[4,128,128]{2,1,0:T(8,128)(2,1)S(1)} %get-tuple-element.117), channel_id=1, source_target_pairs={{0,8},{8,0},{16,24},{24,16},{32,40},{40,32},{48,56},{56,48},{64,72... | collective-permute-start | bytes 393224 | tf_op jit(solution)/shard_map/ppermute | solution.py:23
  75.0 5.3 %copy-start.15 = (f32[1024]{0:T(1024)S(1)}, f32[1024]{0:T(1024)}, u32[]{:S(2)}) copy-start(f32[1024]{0:T(1024)} %param.30) | copy-start | bytes 12292
  80.3 17.6 %copy-start = (f32[768,1024]{1,0:T(8,128)S(1)}, f32[768,1024]{1,0:T(8,128)}, u32[]{:S(2)}) copy-start(f32[768,1024]{1,0:T(8,128)} %shard_map.93) | copy-start | bytes 9437188
  83.6 2.7 %collective-permute-start.6 = (f32[2,768]{1,0:T(2,128)S(1)}, f32[2,768]{1,0:T(2,128)S(1)}, u32[]{:S(2)}, u32[]{:S(2)}) collective-permute-start(f32[2,768]{1,0:T(2,128)S(1)} %pad_maximum_fusion.2), channel_id=1, source_target_pairs={{0,1},{1,0},{2,3},{3,2},{4,5},{5,4},{6,7},{7,6},{8,9},{9,8},{10,11... | collective-permute-start | bytes 18440 | tf_op jit(solution)/shard_map/ppermute | solution.py:93
  86.3 4.1 %collective-permute-start.7 = (f32[2,768]{1,0:T(2,128)S(1)}, f32[2,768]{1,0:T(2,128)S(1)}, u32[]{:S(2)}, u32[]{:S(2)}) collective-permute-start(f32[2,768]{1,0:T(2,128)S(1)} %fusion.58), channel_id=1, source_target_pairs={{0,2},{1,3},{2,0},{3,1},{4,6},{5,7},{6,4},{7,5},{8,10},{9,11},{10,... | collective-permute-start | bytes 18440 | tf_op jit(solution)/shard_map/ppermute | solution.py:93
  90.4 7.4 %collective-permute-start.8 = (f32[2,768]{1,0:T(2,128)S(1)}, f32[2,768]{1,0:T(2,128)S(1)}, u32[]{:S(2)}, u32[]{:S(2)}) collective-permute-start(f32[2,768]{1,0:T(2,128)S(1)} %fusion.71), channel_id=1, source_target_pairs={{0,4},{1,5},{2,6},{3,7},{4,0},{5,1},{6,2},{7,3},{8,12},{9,13},{10,... | collective-permute-start | bytes 18440 | tf_op jit(solution)/shard_map/ppermute | solution.py:93
  97.9 3.6 %copy-start.4 = (bf16[768,1024]{0,1:T(8,128)(2,1)S(1)}, bf16[768,1024]{0,1:T(8,128)(2,1)}, u32[]{:S(2)}) copy-start(bf16[768,1024]{0,1:T(8,128)(2,1)} %copy.37) | copy-start | bytes 4718596
  101.4 1.1 copy-start.1
  102.6 16.9 %copy-start.12 = (bf16[8,128,128]{2,1,0:T(8,128)(2,1)}, bf16[8,128,128]{2,1,0:T(8,128)(2,1)S(1)}, u32[]{:S(2)}) copy-start(bf16[8,128,128]{2,1,0:T(8,128)(2,1)S(1)} %fusion.13) | copy-start | bytes 786436
  102.6 21.4 %copy-start.2 = (bf16[768,1024]{1,0:T(8,128)(2,1)S(1)}, bf16[768,1024]{1,0:T(8,128)(2,1)}, u32[]{:S(2)}) copy-start(bf16[768,1024]{1,0:T(8,128)(2,1)} %copy-done.1) | copy-start | bytes 4718596
  102.6 4.3 %collective-permute-start.9 = (bf16[528,128]{1,0:T(8,128)(2,1)S(1)}, bf16[528,128]{1,0:T(8,128)(2,1)S(1)}, u32[]{:S(2)}, u32[]{:S(2)}) collective-permute-start(bf16[528,128]{1,0:T(8,128)(2,1)S(1)} %pad_maximum_fusion.1), channel_id=1, source_target_pairs={{0,8},{8,0},{16,24},{24,16},{32,40},{40,32},{48,56},{56,48},{64,72... | collective-permute-start | bytes 405512 | tf_op jit(solution)/shard_map/ppermute | solution.py:23
  108.6 10.9 %copy-start.8 = (bf16[512,128]{1,0:T(8,128)(2,1)}, bf16[512,128]{1,0:T(8,128)(2,1)S(1)}, u32[]{:S(2)}) copy-start(bf16[512,128]{1,0:T(8,128)(2,1)S(1)} %slice.298) | copy-start | bytes 393220
  108.7 9.6 %collective-permute-start.10 = (f32[528,128]{1,0:T(8,128)S(1)}, f32[528,128]{1,0:T(8,128)S(1)}, u32[]{:S(2)}, u32[]{:S(2)}) collective-permute-start(f32[528,128]{1,0:T(8,128)S(1)} %select_maximum_fusion), channel_id=1, source_target_pairs={{16,0},{24,8},{32,16},{40,24},{48,32},{56,40},{64,48},{72,56},{80,... | collective-permute-start | bytes 811016 | tf_op jit(solution)/shard_map/ppermute | solution.py:19
  119.5 15.1 %copy-start.6 = (bf16[768,1024]{1,0:T(8,128)(2,1)S(1)}, bf16[768,1024]{1,0:T(8,128)(2,1)}, u32[]{:S(2)}) copy-start(bf16[768,1024]{1,0:T(8,128)(2,1)} %refs_1_.5) | copy-start | bytes 4718596
  119.5 11.3 %collective-permute-start.11 = (bf16[528,128]{1,0:T(8,128)(2,1)S(1)}, bf16[528,128]{1,0:T(8,128)(2,1)S(1)}, u32[]{:S(2)}, u32[]{:S(2)}) collective-permute-start(bf16[528,128]{1,0:T(8,128)(2,1)S(1)} %fusion.37), channel_id=1, source_target_pairs={{16,0},{24,8},{32,16},{40,24},{48,32},{56,40},{64,48},{72,56},{80,... | collective-permute-start | bytes 405512 | tf_op jit(solution)/shard_map/ppermute | solution.py:19
  132.6 9.9 %collective-permute-start.12 = (bf16[528,128]{1,0:T(8,128)(2,1)S(1)}, bf16[528,128]{1,0:T(8,128)(2,1)S(1)}, u32[]{:S(2)}, u32[]{:S(2)}) collective-permute-start(bf16[528,128]{1,0:T(8,128)(2,1)S(1)} %fusion.36), channel_id=1, source_target_pairs={{32,0},{40,8},{48,16},{56,24},{64,32},{72,40},{80,48},{88,56},{96,... | collective-permute-start | bytes 405512 | tf_op jit(solution)/shard_map/ppermute | solution.py:19
  142.6 0.7 copy-start.10
  145.9 15.3 %copy-start.11 = (bf16[528,128]{1,0:T(8,128)(2,1)S(1)}, bf16[528,128]{1,0:T(8,128)(2,1)}, u32[]{:S(2)}) copy-start(bf16[528,128]{1,0:T(8,128)(2,1)} %copy-done.10) | copy-start | bytes 405508
  145.9 13.5 %collective-permute-start.13 = (bf16[528,128]{1,0:T(8,128)(2,1)S(1)}, bf16[528,128]{1,0:T(8,128)(2,1)S(1)}, u32[]{:S(2)}, u32[]{:S(2)}) collective-permute-start(bf16[528,128]{1,0:T(8,128)(2,1)S(1)} %fusion.38), channel_id=1, source_target_pairs={{64,0},{72,8},{80,16},{88,24},{96,32},{104,40},{112,48},{120,56},{... | collective-permute-start | bytes 405512 | tf_op jit(solution)/shard_map/ppermute | solution.py:19
  148.4 13.0 %copy-start.13 = (bf16[8,128,128]{2,1,0:T(8,128)(2,1)S(1)}, bf16[8,128,128]{2,1,0:T(8,128)(2,1)}, u32[]{:S(2)}) copy-start(bf16[8,128,128]{2,1,0:T(8,128)(2,1)} %copy-done.12) | copy-start | bytes 786436
  156.8 4.6 %copy-start.9 = (bf16[512,128]{1,0:T(8,128)(2,1)S(1)}, bf16[512,128]{1,0:T(8,128)(2,1)}, u32[]{:S(2)}) copy-start(bf16[512,128]{1,0:T(8,128)(2,1)} %copy-done.8) | copy-start | bytes 393220
  156.8 6.5 %copy-start.5 = (bf16[768,1024]{0,1:T(8,128)(2,1)S(1)}, bf16[768,1024]{0,1:T(8,128)(2,1)}, u32[]{:S(2)}) copy-start(bf16[768,1024]{0,1:T(8,128)(2,1)} %copy.37) | copy-start | bytes 4718596
  161.5 14.8 %collective-permute-start.14 = (bf16[4,128,128]{2,1,0:T(8,128)(2,1)S(1)}, bf16[4,128,128]{2,1,0:T(8,128)(2,1)S(1)}, u32[]{:S(2)}, u32[]{:S(2)}) collective-permute-start(bf16[4,128,128]{2,1,0:T(8,128)(2,1)S(1)} %get-tuple-element.115), channel_id=1, source_target_pairs={{0,8},{8,0},{16,24},{24,16},{32,40},{40,32},{48,56},{56,48},{64,72... | collective-permute-start | bytes 393224 | tf_op jit(solution)/shard_map/ppermute | solution.py:23

commit v6 on v5

--- a/solution.py
+++ b/solution.py
@@ -37,53 +37,24 @@
 
 def carried(state, first_tag, last_tag, tokens_here, axis, backward, partial_type):
     count = lax.axis_size(axis)
-    index = lax.axis_index(axis)
     if backward:
-        link_tag, meet_tag, place = first_tag, last_tag, count - 1 - index
+        link_tag, meet_tag = first_tag, last_tag
     else:
-        link_tag, meet_tag, place = last_tag, first_tag, index
-    chips = count // 2
-    terms = min((DOC_MOST - 1) // tokens_here + 1, count)
-    window = min((terms + 1) // 2, chips)
-    core = place % 2
-    half = state.shape[0] // 2
-    half_shape = (half,) + state.shape[1:]
-    own_half = lax.dynamic_slice_in_dim(state, core * half, half, 0)
-    other_half = lax.dynamic_slice_in_dim(state, (1 - core) * half, half, 0)
-    partner_half, partner_tags = unpacked(
-        swapped(packed(other_half, [link_tag, meet_tag]), axis, count), half_shape
-    )
-    first_core = core == 0
-    low = jnp.where(first_core, own_half, partner_half).astype(jnp.float32)
-    high = jnp.where(first_core, partner_half, own_half).astype(jnp.float32)
-    low_link = jnp.where(first_core, link_tag, partner_tags[0])
-    high_link = jnp.where(first_core, partner_tags[0], link_tag)
-    low_meet = jnp.where(first_core, meet_tag, partner_tags[1])
-    high_meet = jnp.where(first_core, partner_tags[1], meet_tag)
-    chip_total = high + (low_link == high_link).astype(jnp.float32) * low
-    total, near_tags = unpacked(
-        moved(packed(chip_total, [high_link]), axis, count, 2, backward), half_shape
-    )
+        link_tag, meet_tag = last_tag, first_tag
+    window = min((DOC_MOST - 1) // tokens_here + 1, count)
+    shape = state.shape
+    total, near_tags = unpacked(moved(packed(state, [link_tag]), axis, count, 1, backward), shape)
+    total = total.astype(jnp.float32)
     before = near_tags[0]
     span = 1
     while span < window:
         far, far_tags = unpacked(
-            moved(packed(total.astype(partial_type), [before]), axis, count, 2 * span, backward),
-            half_shape,
+            moved(packed(total.astype(partial_type), [before]), axis, count, span, backward), shape
         )
         reach = (far_tags[0] == before).astype(jnp.float32)
         total = total + reach * far.astype(jnp.float32)
         span = span * 2
-    out_low = (before == low_meet).astype(jnp.float32) * total
-    out_high = (low_link == high_meet).astype(jnp.float32) * (
-        low + (before == low_link).astype(jnp.float32) * total
-    )
-    mine = jnp.where(first_core, out_low, out_high).astype(jnp.bfloat16)
-    theirs = jnp.where(first_core, out_high, out_low).astype(jnp.bfloat16)
-    got = swapped(theirs, axis, count)
-    return jnp.where(
-        first_core, jnp.concatenate([mine, got], axis=0), jnp.concatenate([got, mine], axis=0)
-    )
+    return ((before == meet_tag).astype(jnp.float32) * total).astype(jnp.bfloat16)
 
 
 def group_sum(x, axis):

time: 188 us -> 185 us (0.984)
  starting transfers between devices: 41.5 us -> 57.3 us
  waiting for transfers between devices: 28.8 us -> 15.9 us
  between operations: 18.9 us -> 13.9 us
  other arithmetic: 13.4 us -> 18.1 us
  matrix products: 51.1 us -> 48 us
  local copies, waits for them, and re-layouts: 13.3 us -> 10.6 us
    ppermute x8 -> x10, starting transfers between devices: 20.6 us -> 46.3 us  [moved(): return lax.ppermute(x, axis, pairs)]
    ppermute x8 -> x10, waiting for transfers between devices: 23.9 us -> 12.8 us  [moved(): return lax.ppermute(x, axis, pairs)]
    ppermute x4 -> x0, starting transfers between devices: 9.73 us -> none  [swapped(): return lax.ppermute(x, axis, [(i, i ^ 1) for i in range(count)])]
    concatenate x10, other arithmetic: 0.79 us -> 5.29 us  [packed(): return jnp.concatenate([rows, tail], axis=0)]
    convert_element_type x4 -> x2, other arithmetic: 0.2 us -> 2.9 us  [carried(): ((before == meet_tag).astype(jnp.float32) * total).astype(jnp.bfloat16)]
    ppermute x4 -> x0, waiting for transfers between devices: 1.99 us -> none  [swapped(): return lax.ppermute(x, axis, [(i, i ^ 1) for i in range(count)])]
    slice x6 -> x8, local copies, waits for them, and re-layouts: 3.1 us -> 4.78 us  [carried(): reach = (far_tags[0] == before).astype(jnp.float32)]
  transfers between devices with their start and end apart: 15 -> 13, of which waited for: 9 -> 7; matrix products, arithmetic and copies ran while one was open for 28% -> 26% of each run, Pallas kernels for 3% -> 3%
where the time goes in v6:
time: 185 us; the launch traced here: 183 us
  starting transfers between devices  57.3 us (31%)
  matrix products  48 us (26%)
  Pallas kernels  19.5 us (11%)
  other arithmetic  18.1 us (10%)
  waiting for transfers between devices  15.9 us (9%)
  between operations  13.9 us (8%)
  local copies, waits for them, and re-layouts  10.6 us (6%)
    ppermute x10, starting transfers between devices, moved(): return lax.ppermute(x, axis, pairs)  46.3 us
    pallas_call x4, Pallas kernels, finished(): pl.pallas_call(lambda *refs: finish_body(*refs, flip=flip), grid=(tokens...  19.5 us
    ppermute x10, waiting for transfers between devices, moved(): return lax.ppermute(x, axis, pairs)  12.8 us
    ppermute x3, starting transfers between devices, group_sum(): x = x + lax.ppermute(x, axis, [(i, i ^ step) for i in range(count)])  11 us
    dot_general x1, matrix products, shards(): jnp.einsum('hts,htb->hsb', scores, delta_heads, preferred_element_type=jn...  8.39 us
    dot_general x1, matrix products, shards(): jnp.einsum('hts,hta->hsa', dscores, query_heads, preferred_element_type=j...  8.33 us
    dot_general x1, matrix products, shards(): jnp.einsum('hts,hsa->hta', dscores, key_heads, preferred_element_type=jnp...  7.96 us
    dot_general x1, matrix products, shards(): jnp.einsum('hts,hsb->htb', scores, value_heads, preferred_element_type=jn...  7.96 us
  transfers between devices with their start and end apart: 13, of which 7 were waited for; matrix products, arithmetic and copies ran while one was open for 26% of the time, Pallas kernels for 3%

profile of v6, /device:TPU:17, one launch (start us, length us, event | category | flops | bytes accessed | tf_op | source)
XLA Modules:
  0.0 183.4 jit_solution(9470186238119557806)
XLA Ops:
  2.6 2.0 %compare_convert_fusion = (bf16[768]{0:T(1024)(128)(2,1)S(1)}, bf16[768]{0:T(1024)(128)(2,1)S(1)}) fusion(s32[768]{0:T(1024)} %param.31, s32[]{:T(128)} %bitcast.5, s32[]{:T(128)} %bitcast.4), kind=kLoop, calls=%fused_computation.65 | loop fusion | flops 3072 | bytes 6152 | tf_op jit(solution)/shard_map/convert_element_type | solution.py:120
  4.6 2.8 %fusion.10 = bf16[8,128,128]{2,1,0:T(8,128)(2,1)S(1)} fusion(bf16[768]{0:T(1024)(128)(2,1)S(1)} %get-tuple-element.106, bf16[768,1024]{1,0:T(8,128)(2,1)} %refs_1_.4, bf16[768,1024]{1,0:T(8,128)(2,1)} %refs_1_.5), kind=kOutput, calls=%fused_computation.20 | convolution fusion | flops 204603392 | bytes 3409408 | tf_op jit(solution)/shard_map/hta,htb->hab/dot_general | solution.py:125
  7.5 3.8 %collective-permute-start = (bf16[1040,128]{1,0:T(8,128)(2,1)S(1)}, bf16[1040,128]{1,0:T(8,128)(2,1)S(1)}, u32[]{:S(2)}, u32[]{:S(2)}) collective-permute-start(bf16[1040,128]{1,0:T(8,128)(2,1)S(1)} %fusion.36), channel_id=1, source_target_pairs={{0,8},{8,16},{16,24},{24,32},{32,40},{40,48},{48,56},{56,64},{64,7... | collective-permute-start | bytes 798728 | tf_op jit(solution)/shard_map/ppermute | solution.py:19
  11.3 3.3 %collective-permute-done = bf16[1040,128]{1,0:T(8,128)(2,1)S(1)} collective-permute-done((bf16[1040,128]{1,0:T(8,128)(2,1)S(1)}, bf16[1040,128]{1,0:T(8,128)(2,1)S(1)}, u32[]{:S(2)}, u32[]{:S(2)}) %collective-permute-start) | collective-permute-done | bytes 266272 | tf_op jit(solution)/shard_map/ppermute | solution.py:19
  15.9 4.4 %collective-permute-start.1 = (bf16[1040,128]{1,0:T(8,128)(2,1)S(1)}, bf16[1040,128]{1,0:T(8,128)(2,1)S(1)}, u32[]{:S(2)}, u32[]{:S(2)}) collective-permute-start(bf16[1040,128]{1,0:T(8,128)(2,1)S(1)} %fusion.44), channel_id=1, source_target_pairs={{0,8},{8,16},{16,24},{24,32},{32,40},{40,48},{48,56},{56,64},{64,7... | collective-permute-start | bytes 798728 | tf_op jit(solution)/shard_map/ppermute | solution.py:19
  20.3 1.6 copy.37
  21.9 1.8 collective-permute-done.1
  26.2 3.1 %collective-permute-start.2 = (bf16[1040,128]{1,0:T(8,128)(2,1)S(1)}, bf16[1040,128]{1,0:T(8,128)(2,1)S(1)}, u32[]{:S(2)}, u32[]{:S(2)}) collective-permute-start(bf16[1040,128]{1,0:T(8,128)(2,1)S(1)} %fusion.43), channel_id=1, source_target_pairs={{0,16},{8,24},{16,32},{24,40},{32,48},{40,56},{48,64},{56,72},{64,... | collective-permute-start | bytes 798728 | tf_op jit(solution)/shard_map/ppermute | solution.py:19
  29.6 6.8 %collective-permute-done.2 = bf16[1040,128]{1,0:T(8,128)(2,1)S(1)} collective-permute-done((bf16[1040,128]{1,0:T(8,128)(2,1)S(1)}, bf16[1040,128]{1,0:T(8,128)(2,1)S(1)}, u32[]{:S(2)}, u32[]{:S(2)}) %collective-permute-start.2) | collective-permute-done | bytes 266272 | tf_op jit(solution)/shard_map/ppermute | solution.py:19
  39.1 5.3 %collective-permute-start.3 = (bf16[1040,128]{1,0:T(8,128)(2,1)S(1)}, bf16[1040,128]{1,0:T(8,128)(2,1)S(1)}, u32[]{:S(2)}, u32[]{:S(2)}) collective-permute-start(bf16[1040,128]{1,0:T(8,128)(2,1)S(1)} %fusion.42), channel_id=1, source_target_pairs={{0,32},{8,40},{16,48},{24,56},{32,64},{40,72},{48,80},{56,88},{64,... | collective-permute-start | bytes 798728 | tf_op jit(solution)/shard_map/ppermute | solution.py:19
  44.4 6.8 %multiply_convert_fusion.1 = bf16[8,768,768]{2,1,0:T(8,128)(2,1)} fusion(f32[768,768]{1,0:T(8,128)S(1)} %fusion.25, bf16[8,768,128]{1,2,0:T(8,128)(2,1)S(1)} %bitcast.113, bf16[768,1024]{1,0:T(8,128)(2,1)} %refs_1_.5), kind=kOutput, calls=%fused_computation.1 | convolution fusion | flops 1217396736 | bytes 14942208 | tf_op jit(solution)/shard_map/hta,hsa->hts/dot_general | solution.py:130
  53.9 1.9 %collective-permute-start.4 = (bf16[1040,128]{1,0:T(8,128)(2,1)S(1)}, bf16[1040,128]{1,0:T(8,128)(2,1)}, u32[]{:S(2)}, u32[]{:S(2)}) collective-permute-start(bf16[1040,128]{1,0:T(8,128)(2,1)S(1)} %fusion.45), channel_id=1, source_target_pairs={{0,64},{8,72},{16,80},{24,88},{32,96},{40,104},{48,112},{56,120},{... | collective-permute-start | bytes 798728 | tf_op jit(solution)/shard_map/ppermute | solution.py:19
  55.9 8.0 %fusion.5.refs_0_ = f32[8,768,128]{2,1,0:T(8,128)} fusion(bf16[8,768,768]{2,1,0:T(8,128)(2,1)} %multiply_convert_fusion.1, bf16[768,1024]{1,0:T(8,128)(2,1)S(1)} %copy-done.9), kind=kOutput, calls=%fused_computation.15 | convolution fusion | flops 1207959552 | bytes 14155776 | tf_op jit(solution)/shard_map/hts,hsb->htb/dot_general | solution.py:133
  68.5 1.9 %multiply_convert_fusion.4 = bf16[1024,128]{1,0:T(8,128)(2,1)} fusion(bf16[1040,128]{1,0:T(8,128)(2,1)} %collective-permute-done.4, f32[]{:T(128)S(6)} %convert_element_type.216, f32[]{:T(128)S(6)} %convert_element_type.227, f32[]{:T(128)S(6)} %convert_element_type.224, bf16[1040,128]{1,0:T(8,128)(2,1)S(1)} %collective-permute-done.3, ...), kind=kLoop, calls=%fused_computation.40 | loop fusion | flops 1966080 | bytes 1572884 | tf_op jit(solution)/shard_map/convert_element_type | solution.py:57
  70.4 5.3 %shard_map.93 = f32[768,1024]{1,0:T(8,128)} custom-call(f32[8,768,128]{2,1,0:T(8,128)} %fusion.5.refs_0_, bf16[768,1024]{1,0:T(8,128)(2,1)} %refs_1_.3, bf16[768,1]{1,0:T(8,128)(2,1)} %broadcast_in_dim.6.refs_2_, bf16[8,128,128]{2,1,0:T(8,128)(2,1)} %bitcast.116), custom_call_target="tpu_custom_call" | custom-call | tf_op jit(solution)/shard_map/pallas_call | solution.py:88
  75.7 3.2 %multiply_reduce_fusion.1 = (f32[768]{0:T(1024)S(1)}, f32[768]{0:T(1024)S(1)}) fusion(f32[768,1024]{1,0:T(8,128)} %shard_map.93, bf16[768,1024]{1,0:T(8,128)(2,1)} %param.29, f32[1024]{0:T(1024)S(1)} %copy-done.13), kind=kLoop, calls=%fused_computation.6 | loop fusion | flops 4717056 | bytes 4728832 | tf_op jit(solution)/shard_map/reduce_sum | solution.py:139
  79.0 1.7 collective-permute-start.5
  81.8 3.1 %collective-permute-start.6 = (f32[2,768]{1,0:T(2,128)S(1)}, f32[2,768]{1,0:T(2,128)S(1)}, u32[]{:S(2)}, u32[]{:S(2)}) collective-permute-start(f32[2,768]{1,0:T(2,128)S(1)} %fusion.51), channel_id=1, source_target_pairs={{0,2},{1,3},{2,0},{3,1},{4,6},{5,7},{6,4},{7,5},{8,10},{9,11},{10,... | collective-permute-start | bytes 18440 | tf_op jit(solution)/shard_map/ppermute | solution.py:64
  85.9 6.2 %collective-permute-start.7 = (f32[2,768]{1,0:T(2,128)S(1)}, f32[2,768]{1,0:T(2,128)S(1)}, u32[]{:S(2)}, u32[]{:S(2)}) collective-permute-start(f32[2,768]{1,0:T(2,128)S(1)} %fusion.62), channel_id=1, source_target_pairs={{0,4},{1,5},{2,6},{3,7},{4,0},{5,1},{6,2},{7,3},{8,12},{9,13},{10,... | collective-permute-start | bytes 18440 | tf_op jit(solution)/shard_map/ppermute | solution.py:64
  93.2 3.5 %subtract_convert_fusion = (bf16[768,1024]{1,0:T(8,128)(2,1)S(1)}, bf16[768,1024]{1,0:T(8,128)(2,1)}) fusion(f32[768,1024]{1,0:T(8,128)S(1)} %copy-done, bf16[768,1024]{1,0:T(8,128)(2,1)} %param.29, f32[768]{0:T(1024)S(1)} %fusion.47, f32[768]{0:T(1024)S(1)} %get-tuple-element.103, f32[1024]{0:T(1024)S(1)} %copy-done.13), kind=kLoop, calls=%fused_computation.2 | loop fusion | flops 7077888 | bytes 7874560 | tf_op jit(solution)/shard_map/convert_element_type | solution.py:146
  97.4 11.0 %collective-permute-start.8 = (bf16[1040,128]{1,0:T(8,128)(2,1)S(1)}, bf16[1040,128]{1,0:T(8,128)(2,1)S(1)}, u32[]{:S(2)}, u32[]{:S(2)}) collective-permute-start(bf16[1040,128]{1,0:T(8,128)(2,1)S(1)} %fusion.37), channel_id=1, source_target_pairs={{8,0},{16,8},{24,16},{32,24},{40,32},{48,40},{56,48},{64,56},{72,6... | collective-permute-start | bytes 798728 | tf_op jit(solution)/shard_map/ppermute | solution.py:19
  111.4 4.3 %collective-permute-start.9 = (bf16[1040,128]{1,0:T(8,128)(2,1)S(1)}, bf16[1040,128]{1,0:T(8,128)(2,1)S(1)}, u32[]{:S(2)}, u32[]{:S(2)}) collective-permute-start(bf16[1040,128]{1,0:T(8,128)(2,1)S(1)} %fusion.40), channel_id=1, source_target_pairs={{8,0},{16,8},{24,16},{32,24},{40,32},{48,40},{56,48},{64,56},{72,6... | collective-permute-start | bytes 798728 | tf_op jit(solution)/shard_map/ppermute | solution.py:19
  115.8 5.1 %multiply_convert_fusion = bf16[8,768,768]{2,1,0:T(8,128)(2,1)} fusion(f32[768,768]{1,0:T(8,128)S(1)} %copy-done.4, bf16[768,1024]{1,0:T(8,128)(2,1)S(1)} %get-tuple-element.104.refs_1_, bf16[768,1024]{1,0:T(8,128)(2,1)S(1)} %copy-done.10), kind=kOutput, calls=%fused_computation | convolution fusion | flops 1217396736 | bytes 14942208 | tf_op jit(solution)/shard_map/htb,hsb->hts/dot_general | solution.py:153
  123.4 8.1 %collective-permute-start.10 = (bf16[1040,128]{1,0:T(8,128)(2,1)S(1)}, bf16[1040,128]{1,0:T(8,128)(2,1)S(1)}, u32[]{:S(2)}, u32[]{:S(2)}) collective-permute-start(bf16[1040,128]{1,0:T(8,128)(2,1)S(1)} %fusion.39), channel_id=1, source_target_pairs={{16,0},{24,8},{32,16},{40,24},{48,32},{56,40},{64,48},{72,56},{80,... | collective-permute-start | bytes 798728 | tf_op jit(solution)/shard_map/ppermute | solution.py:19
  131.6 8.0 %fusion.6.refs_0_ = f32[8,768,128]{2,1,0:T(8,128)} fusion(bf16[8,768,768]{2,1,0:T(8,128)(2,1)} %multiply_convert_fusion, bf16[768,1024]{1,0:T(8,128)(2,1)S(1)} %copy-done.8), kind=kOutput, calls=%fused_computation.17 | convolution fusion | flops 1207959552 | bytes 14155776 | tf_op jit(solution)/shard_map/hts,hsa->hta/dot_general | solution.py:156
  142.1 1.9 %collective-permute-start.11 = (bf16[1040,128]{1,0:T(8,128)(2,1)S(1)}, bf16[1040,128]{1,0:T(8,128)(2,1)S(1)}, u32[]{:S(2)}, u32[]{:S(2)}) collective-permute-start(bf16[1040,128]{1,0:T(8,128)(2,1)S(1)} %fusion.38), channel_id=1, source_target_pairs={{32,0},{40,8},{48,16},{56,24},{64,32},{72,40},{80,48},{88,56},{96,... | collective-permute-start | bytes 798728 | tf_op jit(solution)/shard_map/ppermute | solution.py:19
  144.0 8.4 %fusion.2.refs_0_ = f32[8,768,128]{2,1,0:T(8,128)} fusion(bf16[8,768,768]{2,1,0:T(8,128)(2,1)} %multiply_convert_fusion.1, bf16[768,1024]{1,0:T(8,128)(2,1)S(1)} %copy-done.2), kind=kOutput, calls=%fused_computation.11 | convolution fusion | flops 1207959552 | bytes 14155776 | tf_op jit(solution)/shard_map/hts,htb->hsb/dot_general | solution.py:160
  155.1 2.4 %collective-permute-start.12 = (bf16[1040,128]{1,0:T(8,128)(2,1)S(1)}, bf16[1040,128]{1,0:T(8,128)(2,1)S(1)}, u32[]{:S(2)}, u32[]{:S(2)}) collective-permute-start(bf16[1040,128]{1,0:T(8,128)(2,1)S(1)} %fusion.41), channel_id=1, source_target_pairs={{64,0},{72,8},{80,16},{88,24},{96,32},{104,40},{112,48},{120,56},{... | collective-permute-start | bytes 798728 | tf_op jit(solution)/shard_map/ppermute | solution.py:19
  157.4 8.3 %fusion.55.refs_0_ = f32[8,768,128]{2,1,0:T(8,128)} fusion(bf16[8,768,768]{2,1,0:T(8,128)(2,1)} %multiply_convert_fusion, bf16[8,768,128]{1,2,0:T(8,128)(2,1)S(1)} %bitcast.115), kind=kOutput, calls=%fused_computation.76 | convolution fusion | flops 1207959552 | bytes 14155776 | tf_op jit(solution)/shard_map/hts,hta->hsa/dot_general | solution.py:159
  165.8 4.7 %shard_map.94 = bf16[768,1024]{1,0:T(8,128)(2,1)} custom-call(f32[8,768,128]{2,1,0:T(8,128)} %fusion.6.refs_0_, bf16[768,1024]{1,0:T(8,128)(2,1)} %copy-done.1, bf16[768,1]{1,0:T(8,128)(2,1)} %broadcast_in_dim.6.refs_2_, bf16[8,128,128]{2,1,0:T(8,128)(2,1)} %bitcast.117), custom_call_target="tpu_custom_call" | custom-call | tf_op jit(solution)/shard_map/pallas_call | solution.py:88
  173.9 4.7 %shard_map.96 = bf16[768,1024]{1,0:T(8,128)(2,1)} custom-call(f32[8,768,128]{2,1,0:T(8,128)} %fusion.2.refs_0_, bf16[768,1024]{1,0:T(8,128)(2,1)} %refs_1_.5, bf16[768,1]{1,0:T(8,128)(2,1)} %broadcast_in_dim.7.refs_2_, bf16[8,128,128]{2,1,0:T(8,128)(2,1)} %bitcast.118), custom_call_target="tpu_custom_call" | custom-call | tf_op jit(solution)/shard_map/pallas_call | solution.py:88
  178.6 4.7 %shard_map.95 = bf16[768,1024]{1,0:T(8,128)(2,1)} custom-call(f32[8,768,128]{2,1,0:T(8,128)} %fusion.55.refs_0_, bf16[768,1024]{1,0:T(8,128)(2,1)} %refs_1_.4, bf16[768,1]{1,0:T(8,128)(2,1)} %broadcast_in_dim.7.refs_2_, bf16[8,128,128]{2,1,0:T(8,128)(2,1)} %bitcast.119), custom_call_target="tpu_custom_call" | custom-call | tf_op jit(solution)/shard_map/pallas_call | solution.py:88
  (80 shorter events, 21.1 us)
Async XLA Ops:
  7.5 12.8 %copy-start.11 = (bf16[768,1024]{1,0:T(8,128)(2,1)S(1)}, bf16[768,1024]{1,0:T(8,128)(2,1)}, u32[]{:S(2)}) copy-start(bf16[768,1024]{1,0:T(8,128)(2,1)} %refs_1_.3) | copy-start | bytes 4718596
  7.5 7.2 %collective-permute-start = (bf16[1040,128]{1,0:T(8,128)(2,1)S(1)}, bf16[1040,128]{1,0:T(8,128)(2,1)S(1)}, u32[]{:S(2)}, u32[]{:S(2)}) collective-permute-start(bf16[1040,128]{1,0:T(8,128)(2,1)S(1)} %fusion.36), channel_id=1, source_target_pairs={{0,8},{8,16},{16,24},{24,32},{32,40},{40,48},{48,56},{56,64},{64,7... | collective-permute-start | bytes 798728 | tf_op jit(solution)/shard_map/ppermute | solution.py:19
  15.9 13.5 %copy-start.12 = (s32[768]{0:T(1024)S(1)}, s32[768]{0:T(1024)}, u32[]{:S(2)}) copy-start(s32[768]{0:T(1024)} %param.31) | copy-start | bytes 9220
  15.9 7.7 %collective-permute-start.1 = (bf16[1040,128]{1,0:T(8,128)(2,1)S(1)}, bf16[1040,128]{1,0:T(8,128)(2,1)S(1)}, u32[]{:S(2)}, u32[]{:S(2)}) collective-permute-start(bf16[1040,128]{1,0:T(8,128)(2,1)S(1)} %fusion.44), channel_id=1, source_target_pairs={{0,8},{8,16},{16,24},{24,32},{32,40},{40,48},{48,56},{56,64},{64,7... | collective-permute-start | bytes 798728 | tf_op jit(solution)/shard_map/ppermute | solution.py:19
  26.2 10.2 %collective-permute-start.2 = (bf16[1040,128]{1,0:T(8,128)(2,1)S(1)}, bf16[1040,128]{1,0:T(8,128)(2,1)S(1)}, u32[]{:S(2)}, u32[]{:S(2)}) collective-permute-start(bf16[1040,128]{1,0:T(8,128)(2,1)S(1)} %fusion.43), channel_id=1, source_target_pairs={{0,16},{8,24},{16,32},{24,40},{32,48},{40,56},{48,64},{56,72},{64,... | collective-permute-start | bytes 798728 | tf_op jit(solution)/shard_map/ppermute | solution.py:19
  29.6 21.6 %copy-start.3 = (f32[768,768]{1,0:T(8,128)}, f32[768,768]{1,0:T(8,128)S(1)}, u32[]{:S(2)}) copy-start(f32[768,768]{1,0:T(8,128)S(1)} %fusion.25) | copy-start | bytes 7077892
  38.2 6.2 %copy-start.5 = (bf16[768,1024]{0,1:T(8,128)(2,1)S(1)}, bf16[768,1024]{0,1:T(8,128)(2,1)}, u32[]{:S(2)}) copy-start(bf16[768,1024]{0,1:T(8,128)(2,1)} %copy.37) | copy-start | bytes 4718596
  39.1 12.1 %collective-permute-start.3 = (bf16[1040,128]{1,0:T(8,128)(2,1)S(1)}, bf16[1040,128]{1,0:T(8,128)(2,1)S(1)}, u32[]{:S(2)}, u32[]{:S(2)}) collective-permute-start(bf16[1040,128]{1,0:T(8,128)(2,1)S(1)} %fusion.42), channel_id=1, source_target_pairs={{0,32},{8,40},{16,48},{24,56},{32,64},{40,72},{48,80},{56,88},{64,... | collective-permute-start | bytes 798728 | tf_op jit(solution)/shard_map/ppermute | solution.py:19
  51.2 4.6 %copy-start.9 = (bf16[768,1024]{1,0:T(8,128)(2,1)S(1)}, bf16[768,1024]{1,0:T(8,128)(2,1)}, u32[]{:S(2)}) copy-start(bf16[768,1024]{1,0:T(8,128)(2,1)} %refs_1_.4) | copy-start | bytes 4718596
  53.9 12.1 %collective-permute-start.4 = (bf16[1040,128]{1,0:T(8,128)(2,1)S(1)}, bf16[1040,128]{1,0:T(8,128)(2,1)}, u32[]{:S(2)}, u32[]{:S(2)}) collective-permute-start(bf16[1040,128]{1,0:T(8,128)(2,1)S(1)} %fusion.45), channel_id=1, source_target_pairs={{0,64},{8,72},{16,80},{24,88},{32,96},{40,104},{48,112},{56,120},{... | collective-permute-start | bytes 798728 | tf_op jit(solution)/shard_map/ppermute | solution.py:19
  70.4 5.3 %copy-start.13 = (f32[1024]{0:T(1024)S(1)}, f32[1024]{0:T(1024)}, u32[]{:S(2)}) copy-start(f32[1024]{0:T(1024)} %param.30) | copy-start | bytes 12292
  75.7 17.4 %copy-start = (f32[768,1024]{1,0:T(8,128)S(1)}, f32[768,1024]{1,0:T(8,128)}, u32[]{:S(2)}) copy-start(f32[768,1024]{1,0:T(8,128)} %shard_map.93) | copy-start | bytes 9437188
  79.0 2.7 %collective-permute-start.5 = (f32[2,768]{1,0:T(2,128)S(1)}, f32[2,768]{1,0:T(2,128)S(1)}, u32[]{:S(2)}, u32[]{:S(2)}) collective-permute-start(f32[2,768]{1,0:T(2,128)S(1)} %pad_maximum_fusion), channel_id=1, source_target_pairs={{0,1},{1,0},{2,3},{3,2},{4,5},{5,4},{6,7},{7,6},{8,9},{9,8},{10,11... | collective-permute-start | bytes 18440 | tf_op jit(solution)/shard_map/ppermute | solution.py:64
  81.8 4.1 %collective-permute-start.6 = (f32[2,768]{1,0:T(2,128)S(1)}, f32[2,768]{1,0:T(2,128)S(1)}, u32[]{:S(2)}, u32[]{:S(2)}) collective-permute-start(f32[2,768]{1,0:T(2,128)S(1)} %fusion.51), channel_id=1, source_target_pairs={{0,2},{1,3},{2,0},{3,1},{4,6},{5,7},{6,4},{7,5},{8,10},{9,11},{10,... | collective-permute-start | bytes 18440 | tf_op jit(solution)/shard_map/ppermute | solution.py:64
  85.9 7.2 %collective-permute-start.7 = (f32[2,768]{1,0:T(2,128)S(1)}, f32[2,768]{1,0:T(2,128)S(1)}, u32[]{:S(2)}, u32[]{:S(2)}) collective-permute-start(f32[2,768]{1,0:T(2,128)S(1)} %fusion.62), channel_id=1, source_target_pairs={{0,4},{1,5},{2,6},{3,7},{4,0},{5,1},{6,2},{7,3},{8,12},{9,13},{10,... | collective-permute-start | bytes 18440 | tf_op jit(solution)/shard_map/ppermute | solution.py:64
  93.2 3.6 %copy-start.6 = (bf16[768,1024]{0,1:T(8,128)(2,1)S(1)}, bf16[768,1024]{0,1:T(8,128)(2,1)}, u32[]{:S(2)}) copy-start(bf16[768,1024]{0,1:T(8,128)(2,1)} %copy.37) | copy-start | bytes 4718596
  96.7 19.1 %copy-start.1 = (bf16[768,1024]{1,0:T(8,128)(2,1)}, bf16[768,1024]{1,0:T(8,128)(2,1)S(1)}, u32[]{:S(2)}) copy-start(bf16[768,1024]{1,0:T(8,128)(2,1)S(1)} %get-tuple-element.104.refs_1_) | copy-start | bytes 4718596
  96.7 19.1 %copy-start.4 = (f32[768,768]{1,0:T(8,128)S(1)}, f32[768,768]{1,0:T(8,128)}, u32[]{:S(2)}) copy-start(f32[768,768]{1,0:T(8,128)} %copy-done.3) | copy-start | bytes 7077892
  97.3 18.5 %copy-start.10 = (bf16[768,1024]{1,0:T(8,128)(2,1)S(1)}, bf16[768,1024]{1,0:T(8,128)(2,1)}, u32[]{:S(2)}) copy-start(bf16[768,1024]{1,0:T(8,128)(2,1)} %refs_1_.4) | copy-start | bytes 4718596
  97.4 12.8 %collective-permute-start.8 = (bf16[1040,128]{1,0:T(8,128)(2,1)S(1)}, bf16[1040,128]{1,0:T(8,128)(2,1)S(1)}, u32[]{:S(2)}, u32[]{:S(2)}) collective-permute-start(bf16[1040,128]{1,0:T(8,128)(2,1)S(1)} %fusion.37), channel_id=1, source_target_pairs={{8,0},{16,8},{24,16},{32,24},{40,32},{48,40},{56,48},{64,56},{72,6... | collective-permute-start | bytes 798728 | tf_op jit(solution)/shard_map/ppermute | solution.py:19
  111.4 20.2 %copy-start.8 = (bf16[768,1024]{1,0:T(8,128)(2,1)S(1)}, bf16[768,1024]{1,0:T(8,128)(2,1)}, u32[]{:S(2)}) copy-start(bf16[768,1024]{1,0:T(8,128)(2,1)} %refs_1_.5) | copy-start | bytes 4718596
  111.4 9.5 %collective-permute-start.9 = (bf16[1040,128]{1,0:T(8,128)(2,1)S(1)}, bf16[1040,128]{1,0:T(8,128)(2,1)S(1)}, u32[]{:S(2)}, u32[]{:S(2)}) collective-permute-start(bf16[1040,128]{1,0:T(8,128)(2,1)S(1)} %fusion.40), channel_id=1, source_target_pairs={{8,0},{16,8},{24,16},{32,24},{40,32},{48,40},{56,48},{64,56},{72,6... | collective-permute-start | bytes 798728 | tf_op jit(solution)/shard_map/ppermute | solution.py:19
  123.4 16.1 %collective-permute-start.10 = (bf16[1040,128]{1,0:T(8,128)(2,1)S(1)}, bf16[1040,128]{1,0:T(8,128)(2,1)S(1)}, u32[]{:S(2)}, u32[]{:S(2)}) collective-permute-start(bf16[1040,128]{1,0:T(8,128)(2,1)S(1)} %fusion.39), channel_id=1, source_target_pairs={{16,0},{24,8},{32,16},{40,24},{48,32},{56,40},{64,48},{72,56},{80,... | collective-permute-start | bytes 798728 | tf_op jit(solution)/shard_map/ppermute | solution.py:19
  139.5 4.5 %copy-start.2 = (bf16[768,1024]{1,0:T(8,128)(2,1)S(1)}, bf16[768,1024]{1,0:T(8,128)(2,1)}, u32[]{:S(2)}) copy-start(bf16[768,1024]{1,0:T(8,128)(2,1)} %copy-done.1) | copy-start | bytes 4718596
  142.1 10.3 %collective-permute-start.11 = (bf16[1040,128]{1,0:T(8,128)(2,1)S(1)}, bf16[1040,128]{1,0:T(8,128)(2,1)S(1)}, u32[]{:S(2)}, u32[]{:S(2)}) collective-permute-start(bf16[1040,128]{1,0:T(8,128)(2,1)S(1)} %fusion.38), channel_id=1, source_target_pairs={{32,0},{40,8},{48,16},{56,24},{64,32},{72,40},{80,48},{88,56},{96,... | collective-permute-start | bytes 798728 | tf_op jit(solution)/shard_map/ppermute | solution.py:19
  152.4 5.0 %copy-start.7 = (bf16[768,1024]{0,1:T(8,128)(2,1)S(1)}, bf16[768,1024]{0,1:T(8,128)(2,1)}, u32[]{:S(2)}) copy-start(bf16[768,1024]{0,1:T(8,128)(2,1)} %copy.37) | copy-start | bytes 4718596
  155.1 16.1 %collective-permute-start.12 = (bf16[1040,128]{1,0:T(8,128)(2,1)S(1)}, bf16[1040,128]{1,0:T(8,128)(2,1)S(1)}, u32[]{:S(2)}, u32[]{:S(2)}) collective-permute-start(bf16[1040,128]{1,0:T(8,128)(2,1)S(1)} %fusion.41), channel_id=1, source_target_pairs={{64,0},{72,8},{80,16},{88,24},{96,32},{104,40},{112,48},{120,56},{... | collective-permute-start | bytes 798728 | tf_op jit(solution)/shard_map/ppermute | solution.py:19

commit v7 on v6

--- a/solution.py
+++ b/solution.py
@@ -43,10 +43,15 @@
         link_tag, meet_tag = last_tag, first_tag
     window = min((DOC_MOST - 1) // tokens_here + 1, count)
     shape = state.shape
-    total, near_tags = unpacked(moved(packed(state, [link_tag]), axis, count, 1, backward), shape)
+    message = packed(state, [link_tag])
+    total, near_tags = unpacked(moved(message, axis, count, 1, backward), shape)
     total = total.astype(jnp.float32)
     before = near_tags[0]
     span = 1
+    if window > 1:
+        second, second_tags = unpacked(moved(message, axis, count, 2, backward), shape)
+        total = total + (second_tags[0] == before).astype(jnp.float32) * second.astype(jnp.float32)
+        span = 2
     while span < window:
         far, far_tags = unpacked(
             moved(packed(total.astype(partial_type), [before]), axis, count, span, backward), shape

time: 185 us -> 178 us (0.962)
  starting transfers between devices: 57.3 us -> 43.3 us
  waiting for transfers between devices: 15.9 us -> 22.7 us
    ppermute x10, starting transfers between devices: 46.3 us -> 32.3 us  [moved(): return lax.ppermute(x, axis, pairs)]
    ppermute x10, waiting for transfers between devices: 12.8 us -> 20.5 us  [moved(): return lax.ppermute(x, axis, pairs)]
    concatenate x10 -> x8, other arithmetic: 5.29 us -> 4 us  [packed(): return jnp.concatenate([rows, tail], axis=0)]
    slice x8 -> x6, local copies, waits for them, and re-layouts: 4.78 us -> 3.76 us  [carried(): reach = (far_tags[0] == before).astype(jnp.float32)]
  transfers between devices with their start and end apart: 13 -> 13, of which waited for: 7 -> 7; matrix products, arithmetic and copies ran while one was open for 26% -> 28% of each run, Pallas kernels for 3% -> 3%
where the time goes in v7:
time: 178 us; the launch traced here: 175 us
  matrix products  47.8 us (27%)
  starting transfers between devices  43.3 us (24%)
  waiting for transfers between devices  22.7 us (13%)
  Pallas kernels  19.5 us (11%)
  other arithmetic  16.8 us (9%)
  between operations  13.9 us (8%)
  local copies, waits for them, and re-layouts  10.5 us (6%)
    ppermute x10, starting transfers between devices, moved(): return lax.ppermute(x, axis, pairs)  32.3 us
    ppermute x10, waiting for transfers between devices, moved(): return lax.ppermute(x, axis, pairs)  20.5 us
    pallas_call x4, Pallas kernels, finished(): pl.pallas_call(lambda *refs: finish_body(*refs, flip=flip), grid=(tokens...  19.5 us
    ppermute x3, starting transfers between devices, group_sum(): x = x + lax.ppermute(x, axis, [(i, i ^ step) for i in range(count)])  11 us
    dot_general x1, matrix products, shards(): jnp.einsum('hts,htb->hsb', scores, delta_heads, preferred_element_type=jn...  8.33 us
    dot_general x1, matrix products, shards(): jnp.einsum('hts,hta->hsa', dscores, query_heads, preferred_element_type=j...  8.29 us
    dot_general x1, matrix products, shards(): jnp.einsum('hts,hsa->hta', dscores, key_heads, preferred_element_type=jnp...  7.95 us
    dot_general x1, matrix products, shards(): jnp.einsum('hts,hsb->htb', scores, value_heads, preferred_element_type=jn...  7.95 us
  transfers between devices with their start and end apart: 13, of which 7 were waited for; matrix products, arithmetic and copies ran while one was open for 28% of the time, Pallas kernels for 3%

profile of v7, /device:TPU:17, one launch (start us, length us, event | category | flops | bytes accessed | tf_op | source)
XLA Modules:
  0.0 174.5 jit_solution(10459791107899254132)
XLA Ops:
  2.6 2.0 %compare_convert_fusion = (bf16[768]{0:T(1024)(128)(2,1)S(1)}, bf16[768]{0:T(1024)(128)(2,1)S(1)}) fusion(s32[768]{0:T(1024)} %param.27, s32[]{:T(128)} %bitcast.5, s32[]{:T(128)} %bitcast.4), kind=kLoop, calls=%fused_computation.63 | loop fusion | flops 3072 | bytes 6152 | tf_op jit(solution)/shard_map/convert_element_type | solution.py:125
  4.6 3.0 %fusion.10 = bf16[8,128,128]{2,1,0:T(8,128)(2,1)S(1)} fusion(bf16[768]{0:T(1024)(128)(2,1)S(1)} %get-tuple-element.90, bf16[768,1024]{1,0:T(8,128)(2,1)} %refs_1_.4, bf16[768,1024]{1,0:T(8,128)(2,1)} %refs_1_.5), kind=kOutput, calls=%fused_computation.20 | convolution fusion | flops 204603392 | bytes 3409408 | tf_op jit(solution)/shard_map/hta,htb->hab/dot_general | solution.py:130
  7.6 3.7 %collective-permute-start = (bf16[1040,128]{1,0:T(8,128)(2,1)S(1)}, bf16[1040,128]{1,0:T(8,128)(2,1)S(1)}, u32[]{:S(2)}, u32[]{:S(2)}) collective-permute-start(bf16[1040,128]{1,0:T(8,128)(2,1)S(1)} %fusion.36), channel_id=1, source_target_pairs={{0,8},{8,16},{16,24},{24,32},{32,40},{40,48},{48,56},{56,64},{64,7... | collective-permute-start | bytes 798728 | tf_op jit(solution)/shard_map/ppermute | solution.py:19
  11.3 3.1 %collective-permute-start.1 = (bf16[1040,128]{1,0:T(8,128)(2,1)S(1)}, bf16[1040,128]{1,0:T(8,128)(2,1)S(1)}, u32[]{:S(2)}, u32[]{:S(2)}) collective-permute-start(bf16[1040,128]{1,0:T(8,128)(2,1)S(1)} %fusion.36), channel_id=1, source_target_pairs={{0,16},{8,24},{16,32},{24,40},{32,48},{40,56},{48,64},{56,72},{64,... | collective-permute-start | bytes 798728 | tf_op jit(solution)/shard_map/ppermute | solution.py:19
  16.5 6.6 %collective-permute-done.1 = bf16[1040,128]{1,0:T(8,128)(2,1)S(1)} collective-permute-done((bf16[1040,128]{1,0:T(8,128)(2,1)S(1)}, bf16[1040,128]{1,0:T(8,128)(2,1)S(1)}, u32[]{:S(2)}, u32[]{:S(2)}) %collective-permute-start.1) | collective-permute-done | bytes 266272 | tf_op jit(solution)/shard_map/ppermute | solution.py:19
  25.7 1.9 %collective-permute-start.2 = (bf16[1040,128]{1,0:T(8,128)(2,1)S(1)}, bf16[1040,128]{1,0:T(8,128)(2,1)S(1)}, u32[]{:S(2)}, u32[]{:S(2)}) collective-permute-start(bf16[1040,128]{1,0:T(8,128)(2,1)S(1)} %fusion.42), channel_id=1, source_target_pairs={{0,16},{8,24},{16,32},{24,40},{32,48},{40,56},{48,64},{56,72},{64,... | collective-permute-start | bytes 798728 | tf_op jit(solution)/shard_map/ppermute | solution.py:19
  28.0 9.4 %collective-permute-done.2 = bf16[1040,128]{1,0:T(8,128)(2,1)S(1)} collective-permute-done((bf16[1040,128]{1,0:T(8,128)(2,1)S(1)}, bf16[1040,128]{1,0:T(8,128)(2,1)S(1)}, u32[]{:S(2)}, u32[]{:S(2)}) %collective-permute-start.2) | collective-permute-done | bytes 266272 | tf_op jit(solution)/shard_map/ppermute | solution.py:19
  40.1 1.9 %collective-permute-start.3 = (bf16[1040,128]{1,0:T(8,128)(2,1)S(1)}, bf16[1040,128]{1,0:T(8,128)(2,1)S(1)}, u32[]{:S(2)}, u32[]{:S(2)}) collective-permute-start(bf16[1040,128]{1,0:T(8,128)(2,1)S(1)} %fusion.41), channel_id=1, source_target_pairs={{0,32},{8,40},{16,48},{24,56},{32,64},{40,72},{48,80},{56,88},{64,... | collective-permute-start | bytes 798728 | tf_op jit(solution)/shard_map/ppermute | solution.py:19
  42.0 6.6 %multiply_convert_fusion.1 = bf16[8,768,768]{2,1,0:T(8,128)(2,1)} fusion(f32[768,768]{1,0:T(8,128)S(1)} %fusion.25, bf16[8,768,128]{1,2,0:T(8,128)(2,1)S(1)} %bitcast.113, bf16[768,1024]{1,0:T(8,128)(2,1)} %refs_1_.5), kind=kOutput, calls=%fused_computation.1 | convolution fusion | flops 1217396736 | bytes 14942208 | tf_op jit(solution)/shard_map/hta,hsa->hts/dot_general | solution.py:135
  48.6 2.5 %collective-permute-done.3 = bf16[1040,128]{1,0:T(8,128)(2,1)S(1)} collective-permute-done((bf16[1040,128]{1,0:T(8,128)(2,1)S(1)}, bf16[1040,128]{1,0:T(8,128)(2,1)S(1)}, u32[]{:S(2)}, u32[]{:S(2)}) %collective-permute-start.3) | collective-permute-done | bytes 266272 | tf_op jit(solution)/shard_map/ppermute | solution.py:19
  53.9 2.9 %collective-permute-start.4 = (bf16[1040,128]{1,0:T(8,128)(2,1)S(1)}, bf16[1040,128]{1,0:T(8,128)(2,1)}, u32[]{:S(2)}, u32[]{:S(2)}) collective-permute-start(bf16[1040,128]{1,0:T(8,128)(2,1)S(1)} %fusion.43), channel_id=1, source_target_pairs={{0,64},{8,72},{16,80},{24,88},{32,96},{40,104},{48,112},{56,120},{... | collective-permute-start | bytes 798728 | tf_op jit(solution)/shard_map/ppermute | solution.py:19
  56.8 7.9 %fusion.5.refs_0_ = f32[8,768,128]{2,1,0:T(8,128)} fusion(bf16[8,768,768]{2,1,0:T(8,128)(2,1)} %multiply_convert_fusion.1, bf16[768,1024]{1,0:T(8,128)(2,1)S(1)} %copy-done.9), kind=kOutput, calls=%fused_computation.15 | convolution fusion | flops 1207959552 | bytes 14155776 | tf_op jit(solution)/shard_map/hts,hsb->htb/dot_general | solution.py:138
  69.4 1.9 %multiply_convert_fusion.4 = bf16[1024,128]{1,0:T(8,128)(2,1)} fusion(bf16[1040,128]{1,0:T(8,128)(2,1)} %collective-permute-done.4, f32[]{:T(128)S(6)} %convert_element_type.212, f32[]{:T(128)S(6)} %convert_element_type.223, f32[]{:T(128)S(6)} %convert_element_type.220, bf16[1040,128]{1,0:T(8,128)(2,1)S(1)} %collective-permute-done.3, ...), kind=kLoop, calls=%fused_computation.40 | loop fusion | flops 1966080 | bytes 1572884 | tf_op jit(solution)/shard_map/convert_element_type | solution.py:62
  71.3 5.3 %shard_map.93 = f32[768,1024]{1,0:T(8,128)} custom-call(f32[8,768,128]{2,1,0:T(8,128)} %fusion.5.refs_0_, bf16[768,1024]{1,0:T(8,128)(2,1)} %refs_1_.3, bf16[768,1]{1,0:T(8,128)(2,1)} %broadcast_in_dim.6.refs_2_, bf16[8,128,128]{2,1,0:T(8,128)(2,1)} %bitcast.116), custom_call_target="tpu_custom_call" | custom-call | tf_op jit(solution)/shard_map/pallas_call | solution.py:93
  76.7 3.2 %multiply_reduce_fusion.1 = (f32[768]{0:T(1024)S(1)}, f32[768]{0:T(1024)S(1)}) fusion(f32[768,1024]{1,0:T(8,128)} %shard_map.93, bf16[768,1024]{1,0:T(8,128)(2,1)} %param.25, f32[1024]{0:T(1024)S(1)} %copy-done.13), kind=kLoop, calls=%fused_computation.6 | loop fusion | flops 4717056 | bytes 4728832 | tf_op jit(solution)/shard_map/reduce_sum | solution.py:144
  79.9 1.7 collective-permute-start.5
  82.7 3.1 %collective-permute-start.6 = (f32[2,768]{1,0:T(2,128)S(1)}, f32[2,768]{1,0:T(2,128)S(1)}, u32[]{:S(2)}, u32[]{:S(2)}) collective-permute-start(f32[2,768]{1,0:T(2,128)S(1)} %fusion.49), channel_id=1, source_target_pairs={{0,2},{1,3},{2,0},{3,1},{4,6},{5,7},{6,4},{7,5},{8,10},{9,11},{10,... | collective-permute-start | bytes 18440 | tf_op jit(solution)/shard_map/ppermute | solution.py:69
  86.8 6.2 %collective-permute-start.7 = (f32[2,768]{1,0:T(2,128)S(1)}, f32[2,768]{1,0:T(2,128)S(1)}, u32[]{:S(2)}, u32[]{:S(2)}) collective-permute-start(f32[2,768]{1,0:T(2,128)S(1)} %fusion.60), channel_id=1, source_target_pairs={{0,4},{1,5},{2,6},{3,7},{4,0},{5,1},{6,2},{7,3},{8,12},{9,13},{10,... | collective-permute-start | bytes 18440 | tf_op jit(solution)/shard_map/ppermute | solution.py:69
  94.1 3.5 %subtract_convert_fusion = (bf16[768,1024]{1,0:T(8,128)(2,1)S(1)}, bf16[768,1024]{1,0:T(8,128)(2,1)}) fusion(f32[768,1024]{1,0:T(8,128)S(1)} %copy-done, bf16[768,1024]{1,0:T(8,128)(2,1)} %param.25, f32[768]{0:T(1024)S(1)} %fusion.45, f32[768]{0:T(1024)S(1)} %get-tuple-element.87, f32[1024]{0:T(1024)S(1)} %copy-done.13), kind=kLoop, calls=%fused_computation.2 | loop fusion | flops 7077888 | bytes 7874560 | tf_op jit(solution)/shard_map/convert_element_type | solution.py:151
  98.3 7.7 %collective-permute-start.8 = (bf16[1040,128]{1,0:T(8,128)(2,1)S(1)}, bf16[1040,128]{1,0:T(8,128)(2,1)S(1)}, u32[]{:S(2)}, u32[]{:S(2)}) collective-permute-start(bf16[1040,128]{1,0:T(8,128)(2,1)S(1)} %fusion.37), channel_id=1, source_target_pairs={{8,0},{16,8},{24,16},{32,24},{40,32},{48,40},{56,48},{64,56},{72,6... | collective-permute-start | bytes 798728 | tf_op jit(solution)/shard_map/ppermute | solution.py:19
  106.0 2.1 %collective-permute-start.9 = (bf16[1040,128]{1,0:T(8,128)(2,1)S(1)}, bf16[1040,128]{1,0:T(8,128)(2,1)S(1)}, u32[]{:S(2)}, u32[]{:S(2)}) collective-permute-start(bf16[1040,128]{1,0:T(8,128)(2,1)S(1)} %fusion.37), channel_id=1, source_target_pairs={{16,0},{24,8},{32,16},{40,24},{48,32},{56,40},{64,48},{72,56},{80,... | collective-permute-start | bytes 798728 | tf_op jit(solution)/shard_map/ppermute | solution.py:19
  108.2 5.1 %multiply_convert_fusion = bf16[8,768,768]{2,1,0:T(8,128)(2,1)} fusion(f32[768,768]{1,0:T(8,128)S(1)} %copy-done.4, bf16[768,1024]{1,0:T(8,128)(2,1)S(1)} %get-tuple-element.88.refs_1_, bf16[768,1024]{1,0:T(8,128)(2,1)S(1)} %copy-done.10), kind=kOutput, calls=%fused_computation | convolution fusion | flops 1217396736 | bytes 14942208 | tf_op jit(solution)/shard_map/htb,hsb->hts/dot_general | solution.py:158
  113.8 1.9 %collective-permute-done.9 = bf16[1040,128]{1,0:T(8,128)(2,1)S(1)} collective-permute-done((bf16[1040,128]{1,0:T(8,128)(2,1)S(1)}, bf16[1040,128]{1,0:T(8,128)(2,1)S(1)}, u32[]{:S(2)}, u32[]{:S(2)}) %collective-permute-start.9) | collective-permute-done | bytes 266272 | tf_op jit(solution)/shard_map/ppermute | solution.py:19
  118.2 4.6 %collective-permute-start.10 = (bf16[1040,128]{1,0:T(8,128)(2,1)S(1)}, bf16[1040,128]{1,0:T(8,128)(2,1)S(1)}, u32[]{:S(2)}, u32[]{:S(2)}) collective-permute-start(bf16[1040,128]{1,0:T(8,128)(2,1)S(1)} %fusion.39), channel_id=1, source_target_pairs={{16,0},{24,8},{32,16},{40,24},{48,32},{56,40},{64,48},{72,56},{80,... | collective-permute-start | bytes 798728 | tf_op jit(solution)/shard_map/ppermute | solution.py:19
  122.9 7.9 %fusion.6.refs_0_ = f32[8,768,128]{2,1,0:T(8,128)} fusion(bf16[8,768,768]{2,1,0:T(8,128)(2,1)} %multiply_convert_fusion, bf16[768,1024]{1,0:T(8,128)(2,1)S(1)} %copy-done.8), kind=kOutput, calls=%fused_computation.17 | convolution fusion | flops 1207959552 | bytes 14155776 | tf_op jit(solution)/shard_map/hts,hsa->hta/dot_general | solution.py:161
  133.4 1.9 %collective-permute-start.11 = (bf16[1040,128]{1,0:T(8,128)(2,1)S(1)}, bf16[1040,128]{1,0:T(8,128)(2,1)S(1)}, u32[]{:S(2)}, u32[]{:S(2)}) collective-permute-start(bf16[1040,128]{1,0:T(8,128)(2,1)S(1)} %fusion.38), channel_id=1, source_target_pairs={{32,0},{40,8},{48,16},{56,24},{64,32},{72,40},{80,48},{88,56},{96,... | collective-permute-start | bytes 798728 | tf_op jit(solution)/shard_map/ppermute | solution.py:19
  135.3 8.3 %fusion.2.refs_0_ = f32[8,768,128]{2,1,0:T(8,128)} fusion(bf16[8,768,768]{2,1,0:T(8,128)(2,1)} %multiply_convert_fusion.1, bf16[768,1024]{1,0:T(8,128)(2,1)S(1)} %copy-done.2), kind=kOutput, calls=%fused_computation.11 | convolution fusion | flops 1207959552 | bytes 14155776 | tf_op jit(solution)/shard_map/hts,htb->hsb/dot_general | solution.py:165
  146.3 2.4 %collective-permute-start.12 = (bf16[1040,128]{1,0:T(8,128)(2,1)S(1)}, bf16[1040,128]{1,0:T(8,128)(2,1)S(1)}, u32[]{:S(2)}, u32[]{:S(2)}) collective-permute-start(bf16[1040,128]{1,0:T(8,128)(2,1)S(1)} %fusion.40), channel_id=1, source_target_pairs={{64,0},{72,8},{80,16},{88,24},{96,32},{104,40},{112,48},{120,56},{... | collective-permute-start | bytes 798728 | tf_op jit(solution)/shard_map/ppermute | solution.py:19
  148.7 8.3 %fusion.53.refs_0_ = f32[8,768,128]{2,1,0:T(8,128)} fusion(bf16[8,768,768]{2,1,0:T(8,128)(2,1)} %multiply_convert_fusion, bf16[8,768,128]{1,2,0:T(8,128)(2,1)S(1)} %bitcast.115), kind=kOutput, calls=%fused_computation.74 | convolution fusion | flops 1207959552 | bytes 14155776 | tf_op jit(solution)/shard_map/hts,hta->hsa/dot_general | solution.py:164
  157.0 4.7 %shard_map.94 = bf16[768,1024]{1,0:T(8,128)(2,1)} custom-call(f32[8,768,128]{2,1,0:T(8,128)} %fusion.6.refs_0_, bf16[768,1024]{1,0:T(8,128)(2,1)} %copy-done.1, bf16[768,1]{1,0:T(8,128)(2,1)} %broadcast_in_dim.6.refs_2_, bf16[8,128,128]{2,1,0:T(8,128)(2,1)} %bitcast.117), custom_call_target="tpu_custom_call" | custom-call | tf_op jit(solution)/shard_map/pallas_call | solution.py:93
  165.1 4.7 %shard_map.96 = bf16[768,1024]{1,0:T(8,128)(2,1)} custom-call(f32[8,768,128]{2,1,0:T(8,128)} %fusion.2.refs_0_, bf16[768,1024]{1,0:T(8,128)(2,1)} %refs_1_.5, bf16[768,1]{1,0:T(8,128)(2,1)} %broadcast_in_dim.7.refs_2_, bf16[8,128,128]{2,1,0:T(8,128)(2,1)} %bitcast.118), custom_call_target="tpu_custom_call" | custom-call | tf_op jit(solution)/shard_map/pallas_call | solution.py:93
  169.8 4.7 %shard_map.95 = bf16[768,1024]{1,0:T(8,128)(2,1)} custom-call(f32[8,768,128]{2,1,0:T(8,128)} %fusion.53.refs_0_, bf16[768,1024]{1,0:T(8,128)(2,1)} %refs_1_.4, bf16[768,1]{1,0:T(8,128)(2,1)} %broadcast_in_dim.7.refs_2_, bf16[8,128,128]{2,1,0:T(8,128)(2,1)} %bitcast.119), custom_call_target="tpu_custom_call" | custom-call | tf_op jit(solution)/shard_map/pallas_call | solution.py:93
  (76 shorter events, 19.5 us)
Async XLA Ops:
  4.6 9.8 %copy-start.11 = (bf16[768,1024]{1,0:T(8,128)(2,1)S(1)}, bf16[768,1024]{1,0:T(8,128)(2,1)}, u32[]{:S(2)}) copy-start(bf16[768,1024]{1,0:T(8,128)(2,1)} %refs_1_.3) | copy-start | bytes 4718596
  7.6 20.1 %copy-start.12 = (s32[768]{0:T(1024)S(1)}, s32[768]{0:T(1024)}, u32[]{:S(2)}) copy-start(s32[768]{0:T(1024)} %param.27) | copy-start | bytes 9220
  7.6 8.4 %collective-permute-start = (bf16[1040,128]{1,0:T(8,128)(2,1)S(1)}, bf16[1040,128]{1,0:T(8,128)(2,1)S(1)}, u32[]{:S(2)}, u32[]{:S(2)}) collective-permute-start(bf16[1040,128]{1,0:T(8,128)(2,1)S(1)} %fusion.36), channel_id=1, source_target_pairs={{0,8},{8,16},{16,24},{24,32},{32,40},{40,48},{48,56},{56,64},{64,7... | collective-permute-start | bytes 798728 | tf_op jit(solution)/shard_map/ppermute | solution.py:19
  11.3 11.8 %collective-permute-start.1 = (bf16[1040,128]{1,0:T(8,128)(2,1)S(1)}, bf16[1040,128]{1,0:T(8,128)(2,1)S(1)}, u32[]{:S(2)}, u32[]{:S(2)}) collective-permute-start(bf16[1040,128]{1,0:T(8,128)(2,1)S(1)} %fusion.36), channel_id=1, source_target_pairs={{0,16},{8,24},{16,32},{24,40},{32,48},{40,56},{48,64},{56,72},{64,... | collective-permute-start | bytes 798728 | tf_op jit(solution)/shard_map/ppermute | solution.py:19
  25.7 11.6 %collective-permute-start.2 = (bf16[1040,128]{1,0:T(8,128)(2,1)S(1)}, bf16[1040,128]{1,0:T(8,128)(2,1)S(1)}, u32[]{:S(2)}, u32[]{:S(2)}) collective-permute-start(bf16[1040,128]{1,0:T(8,128)(2,1)S(1)} %fusion.42), channel_id=1, source_target_pairs={{0,16},{8,24},{16,32},{24,40},{32,48},{40,56},{48,64},{56,72},{64,... | collective-permute-start | bytes 798728 | tf_op jit(solution)/shard_map/ppermute | solution.py:19
  27.9 20.7 %copy-start.3 = (f32[768,768]{1,0:T(8,128)}, f32[768,768]{1,0:T(8,128)S(1)}, u32[]{:S(2)}) copy-start(f32[768,768]{1,0:T(8,128)S(1)} %fusion.25) | copy-start | bytes 7077892
  39.2 2.9 %copy-start.5 = (bf16[768,1024]{0,1:T(8,128)(2,1)S(1)}, bf16[768,1024]{0,1:T(8,128)(2,1)}, u32[]{:S(2)}) copy-start(bf16[768,1024]{0,1:T(8,128)(2,1)} %copy.37) | copy-start | bytes 4718596
  40.1 11.1 %collective-permute-start.3 = (bf16[1040,128]{1,0:T(8,128)(2,1)S(1)}, bf16[1040,128]{1,0:T(8,128)(2,1)S(1)}, u32[]{:S(2)}, u32[]{:S(2)}) collective-permute-start(bf16[1040,128]{1,0:T(8,128)(2,1)S(1)} %fusion.41), channel_id=1, source_target_pairs={{0,32},{8,40},{16,48},{24,56},{32,64},{40,72},{48,80},{56,88},{64,... | collective-permute-start | bytes 798728 | tf_op jit(solution)/shard_map/ppermute | solution.py:19
  51.2 5.6 %copy-start.9 = (bf16[768,1024]{1,0:T(8,128)(2,1)S(1)}, bf16[768,1024]{1,0:T(8,128)(2,1)}, u32[]{:S(2)}) copy-start(bf16[768,1024]{1,0:T(8,128)(2,1)} %refs_1_.4) | copy-start | bytes 4718596
  53.9 13.1 %collective-permute-start.4 = (bf16[1040,128]{1,0:T(8,128)(2,1)S(1)}, bf16[1040,128]{1,0:T(8,128)(2,1)}, u32[]{:S(2)}, u32[]{:S(2)}) collective-permute-start(bf16[1040,128]{1,0:T(8,128)(2,1)S(1)} %fusion.43), channel_id=1, source_target_pairs={{0,64},{8,72},{16,80},{24,88},{32,96},{40,104},{48,112},{56,120},{... | collective-permute-start | bytes 798728 | tf_op jit(solution)/shard_map/ppermute | solution.py:19
  71.3 5.3 %copy-start.13 = (f32[1024]{0:T(1024)S(1)}, f32[1024]{0:T(1024)}, u32[]{:S(2)}) copy-start(f32[1024]{0:T(1024)} %param.26) | copy-start | bytes 12292
  76.7 17.4 %copy-start = (f32[768,1024]{1,0:T(8,128)S(1)}, f32[768,1024]{1,0:T(8,128)}, u32[]{:S(2)}) copy-start(f32[768,1024]{1,0:T(8,128)} %shard_map.93) | copy-start | bytes 9437188
  79.9 2.7 %collective-permute-start.5 = (f32[2,768]{1,0:T(2,128)S(1)}, f32[2,768]{1,0:T(2,128)S(1)}, u32[]{:S(2)}, u32[]{:S(2)}) collective-permute-start(f32[2,768]{1,0:T(2,128)S(1)} %pad_maximum_fusion), channel_id=1, source_target_pairs={{0,1},{1,0},{2,3},{3,2},{4,5},{5,4},{6,7},{7,6},{8,9},{9,8},{10,11... | collective-permute-start | bytes 18440 | tf_op jit(solution)/shard_map/ppermute | solution.py:69
  82.7 4.1 %collective-permute-start.6 = (f32[2,768]{1,0:T(2,128)S(1)}, f32[2,768]{1,0:T(2,128)S(1)}, u32[]{:S(2)}, u32[]{:S(2)}) collective-permute-start(f32[2,768]{1,0:T(2,128)S(1)} %fusion.49), channel_id=1, source_target_pairs={{0,2},{1,3},{2,0},{3,1},{4,6},{5,7},{6,4},{7,5},{8,10},{9,11},{10,... | collective-permute-start | bytes 18440 | tf_op jit(solution)/shard_map/ppermute | solution.py:69
  86.8 7.2 %collective-permute-start.7 = (f32[2,768]{1,0:T(2,128)S(1)}, f32[2,768]{1,0:T(2,128)S(1)}, u32[]{:S(2)}, u32[]{:S(2)}) collective-permute-start(f32[2,768]{1,0:T(2,128)S(1)} %fusion.60), channel_id=1, source_target_pairs={{0,4},{1,5},{2,6},{3,7},{4,0},{5,1},{6,2},{7,3},{8,12},{9,13},{10,... | collective-permute-start | bytes 18440 | tf_op jit(solution)/shard_map/ppermute | solution.py:69
  94.1 3.6 %copy-start.6 = (bf16[768,1024]{0,1:T(8,128)(2,1)S(1)}, bf16[768,1024]{0,1:T(8,128)(2,1)}, u32[]{:S(2)}) copy-start(bf16[768,1024]{0,1:T(8,128)(2,1)} %copy.37) | copy-start | bytes 4718596
  97.6 10.5 %copy-start.1 = (bf16[768,1024]{1,0:T(8,128)(2,1)}, bf16[768,1024]{1,0:T(8,128)(2,1)S(1)}, u32[]{:S(2)}) copy-start(bf16[768,1024]{1,0:T(8,128)(2,1)S(1)} %get-tuple-element.88.refs_1_) | copy-start | bytes 4718596
  97.6 10.5 %copy-start.4 = (f32[768,768]{1,0:T(8,128)S(1)}, f32[768,768]{1,0:T(8,128)}, u32[]{:S(2)}) copy-start(f32[768,768]{1,0:T(8,128)} %copy-done.3) | copy-start | bytes 7077892
  97.6 10.5 %copy-start.10 = (bf16[768,1024]{1,0:T(8,128)(2,1)S(1)}, bf16[768,1024]{1,0:T(8,128)(2,1)}, u32[]{:S(2)}) copy-start(bf16[768,1024]{1,0:T(8,128)(2,1)} %refs_1_.4) | copy-start | bytes 4718596
  98.3 24.6 %copy-start.8 = (bf16[768,1024]{1,0:T(8,128)(2,1)S(1)}, bf16[768,1024]{1,0:T(8,128)(2,1)}, u32[]{:S(2)}) copy-start(bf16[768,1024]{1,0:T(8,128)(2,1)} %refs_1_.5) | copy-start | bytes 4718596
  98.3 15.0 %collective-permute-start.8 = (bf16[1040,128]{1,0:T(8,128)(2,1)S(1)}, bf16[1040,128]{1,0:T(8,128)(2,1)S(1)}, u32[]{:S(2)}, u32[]{:S(2)}) collective-permute-start(bf16[1040,128]{1,0:T(8,128)(2,1)S(1)} %fusion.37), channel_id=1, source_target_pairs={{8,0},{16,8},{24,16},{32,24},{40,32},{48,40},{56,48},{64,56},{72,6... | collective-permute-start | bytes 798728 | tf_op jit(solution)/shard_map/ppermute | solution.py:19
  106.0 9.7 %collective-permute-start.9 = (bf16[1040,128]{1,0:T(8,128)(2,1)S(1)}, bf16[1040,128]{1,0:T(8,128)(2,1)S(1)}, u32[]{:S(2)}, u32[]{:S(2)}) collective-permute-start(bf16[1040,128]{1,0:T(8,128)(2,1)S(1)} %fusion.37), channel_id=1, source_target_pairs={{16,0},{24,8},{32,16},{40,24},{48,32},{56,40},{64,48},{72,56},{80,... | collective-permute-start | bytes 798728 | tf_op jit(solution)/shard_map/ppermute | solution.py:19
  118.2 12.6 %collective-permute-start.10 = (bf16[1040,128]{1,0:T(8,128)(2,1)S(1)}, bf16[1040,128]{1,0:T(8,128)(2,1)S(1)}, u32[]{:S(2)}, u32[]{:S(2)}) collective-permute-start(bf16[1040,128]{1,0:T(8,128)(2,1)S(1)} %fusion.39), channel_id=1, source_target_pairs={{16,0},{24,8},{32,16},{40,24},{48,32},{56,40},{64,48},{72,56},{80,... | collective-permute-start | bytes 798728 | tf_op jit(solution)/shard_map/ppermute | solution.py:19
  130.8 4.5 %copy-start.2 = (bf16[768,1024]{1,0:T(8,128)(2,1)S(1)}, bf16[768,1024]{1,0:T(8,128)(2,1)}, u32[]{:S(2)}) copy-start(bf16[768,1024]{1,0:T(8,128)(2,1)} %copy-done.1) | copy-start | bytes 4718596
  133.4 10.3 %collective-permute-start.11 = (bf16[1040,128]{1,0:T(8,128)(2,1)S(1)}, bf16[1040,128]{1,0:T(8,128)(2,1)S(1)}, u32[]{:S(2)}, u32[]{:S(2)}) collective-permute-start(bf16[1040,128]{1,0:T(8,128)(2,1)S(1)} %fusion.38), channel_id=1, source_target_pairs={{32,0},{40,8},{48,16},{56,24},{64,32},{72,40},{80,48},{88,56},{96,... | collective-permute-start | bytes 798728 | tf_op jit(solution)/shard_map/ppermute | solution.py:19
  143.7 5.0 %copy-start.7 = (bf16[768,1024]{0,1:T(8,128)(2,1)S(1)}, bf16[768,1024]{0,1:T(8,128)(2,1)}, u32[]{:S(2)}) copy-start(bf16[768,1024]{0,1:T(8,128)(2,1)} %copy.37) | copy-start | bytes 4718596
  146.3 16.0 %collective-permute-start.12 = (bf16[1040,128]{1,0:T(8,128)(2,1)S(1)}, bf16[1040,128]{1,0:T(8,128)(2,1)S(1)}, u32[]{:S(2)}, u32[]{:S(2)}) collective-permute-start(bf16[1040,128]{1,0:T(8,128)(2,1)S(1)} %fusion.40), channel_id=1, source_target_pairs={{64,0},{72,8},{80,16},{88,24},{96,32},{104,40},{112,48},{120,56},{... | collective-permute-start | bytes 798728 | tf_op jit(solution)/shard_map/ppermute | solution.py:19

commit v8 on v7

--- a/solution.py
+++ b/solution.py
@@ -71,38 +71,48 @@
     return x
 
 
-def finish_body(local_ref, rows_ref, mask_ref, state_ref, out_ref, *, flip):
-    width = local_ref.shape[2]
+def finish_body(*refs, flips):
+    parts = len(flips)
+    locals_, rows_, mask_ref, state_ref = refs[:parts], refs[parts : 2 * parts], refs[2 * parts], refs[2 * parts + 1]
+    outs = refs[2 * parts + 2 :]
+    width = locals_[0].shape[2]
     mask = mask_ref[...]
-    for head in range(local_ref.shape[0]):
+    for head in range(locals_[0].shape[0]):
         cols = slice(head * width, (head + 1) * width)
-        rows = rows_ref[:, cols] * mask
         state = state_ref[head]
-        if flip:
-            extra = lax.dot_general(
-                rows, state, (((1,), (1,)), ((), ())), preferred_element_type=jnp.float32
-            )
-        else:
-            extra = jnp.dot(rows, state, preferred_element_type=jnp.float32)
-        out_ref[:, cols] = (local_ref[head] + extra).astype(out_ref.dtype)
+        for local_ref, rows_ref, out_ref, flip in zip(locals_, rows_, outs, flips):
+            rows = rows_ref[:, cols] * mask
+            if flip:
+                extra = lax.dot_general(
+                    rows, state, (((1,), (1,)), ((), ())), preferred_element_type=jnp.float32
+                )
+            else:
+                extra = jnp.dot(rows, state, preferred_element_type=jnp.float32)
+            out_ref[:, cols] = (local_ref[head] + extra).astype(out_ref.dtype)
+
+
+def finished_all(locals_, rows_, mask, state, flips, kinds, interpret=False):
+    heads, tokens, width = locals_[0].shape
+    block = 128 if tokens % 128 == 0 else tokens
+    local_spec = pl.BlockSpec((heads, block, width), lambda t: (0, t, 0))
+    row_spec = pl.BlockSpec((block, heads * width), lambda t: (t, 0))
+    return pl.pallas_call(
+        lambda *refs: finish_body(*refs, flips=flips),
+        grid=(tokens // block,),
+        in_specs=[local_spec] * len(flips)
+        + [row_spec] * len(flips)
+        + [
+            pl.BlockSpec((block, 1), lambda t: (t, 0)),
+            pl.BlockSpec((heads, width, width), lambda t: (0, 0, 0)),
+        ],
+        out_specs=[row_spec] * len(flips),
+        out_shape=[jax.ShapeDtypeStruct((tokens, heads * width), kind) for kind in kinds],
+        interpret=interpret,
+    )(*locals_, *rows_, mask, state)
 
 
 def finished(local, rows, mask, state, flip, kind, interpret=False):
-    heads, tokens, width = local.shape
-    block = 256 if tokens % 256 == 0 else tokens
-    return pl.pallas_call(
-        lambda *refs: finish_body(*refs, flip=flip),
-        grid=(tokens // block,),
-        in_specs=[
-            pl.BlockSpec((heads, block, width), lambda t: (0, t, 0)),
-            pl.BlockSpec((block, heads * width), lambda t: (t, 0)),
-            pl.BlockSpec((block, 1), lambda t: (t, 0)),
-            pl.BlockSpec((heads, width, width), lambda t: (0, 0, 0)),
-        ],
-        out_specs=pl.BlockSpec((block, heads * width), lambda t: (t, 0)),
-        out_shape=jax.ShapeDtypeStruct((tokens, heads * width), kind),
-        interpret=interpret,
-    )(local, rows, mask, state)
+    return finished_all([local], [rows], mask, state, (flip,), (kind,), interpret)[0]
 
 
 def shards(queries, keys, values, out_grad, gain, doc_ids):
@@ -166,8 +176,14 @@
     return (
         normed,
         finished(grad_query, delta, first_mask, incoming, True, jnp.bfloat16),
-        finished(grad_key, values, last_mask, outgoing, True, jnp.bfloat16),
-        finished(grad_value, keys, last_mask, outgoing, False, jnp.bfloat16),
+        *finished_all(
+            [grad_key, grad_value],
+            [values, keys],
+            last_mask,
+            outgoing,
+            (True, False),
+            (jnp.bfloat16, jnp.bfloat16),
+        ),
     )
 
 

time: 178 us -> 174 us (0.978)
  waiting for transfers between devices: 22.7 us -> 11.9 us
  starting transfers between devices: 43.3 us -> 50 us
    ppermute x10, waiting for transfers between devices: 20.5 us -> 9.65 us  [moved(): return lax.ppermute(x, axis, pairs)]
    ppermute x10, starting transfers between devices: 32.3 us -> 39 us  [moved(): return lax.ppermute(x, axis, pairs)]
    pallas_call x4 -> x3, Pallas kernels: 19.5 us -> 20 us  [finished_all(): pl.pallas_call(lambda *refs: finish_body(*refs, flips=flips), grid=(token...]
  transfers between devices with their start and end apart: 13 -> 13, of which waited for: 7 -> 8; matrix products, arithmetic and copies ran while one was open for 28% -> 29% of each run, Pallas kernels for 3% -> 4%
where the time goes in v8:
time: 174 us; the launch traced here: 171 us
  starting transfers between devices  50 us (29%)
  matrix products  47.8 us (27%)
  Pallas kernels  20 us (11%)
  other arithmetic  16.9 us (10%)
  between operations  14 us (8%)
  waiting for transfers between devices  11.9 us (7%)
  local copies, waits for them, and re-layouts  10.5 us (6%)
    ppermute x10, starting transfers between devices, moved(): return lax.ppermute(x, axis, pairs)  39 us
    pallas_call x3, Pallas kernels, finished_all(): pl.pallas_call(lambda *refs: finish_body(*refs, flips=flips), grid=(token...  20 us
    ppermute x3, starting transfers between devices, group_sum(): x = x + lax.ppermute(x, axis, [(i, i ^ step) for i in range(count)])  11 us
    ppermute x10, waiting for transfers between devices, moved(): return lax.ppermute(x, axis, pairs)  9.65 us
    dot_general x1, matrix products, shards(): jnp.einsum('hts,htb->hsb', scores, delta_heads, preferred_element_type=jn...  8.33 us
    dot_general x1, matrix products, shards(): jnp.einsum('hts,hta->hsa', dscores, query_heads, preferred_element_type=j...  8.29 us
    dot_general x1, matrix products, shards(): jnp.einsum('hts,hsa->hta', dscores, key_heads, preferred_element_type=jnp...  7.97 us
    dot_general x1, matrix products, shards(): jnp.einsum('hts,hsb->htb', scores, value_heads, preferred_element_type=jn...  7.94 us
  transfers between devices with their start and end apart: 13, of which 8 were waited for; matrix products, arithmetic and copies ran while one was open for 29% of the time, Pallas kernels for 4%

profile of v8, /device:TPU:17, one launch (start us, length us, event | category | flops | bytes accessed | tf_op | source)
XLA Modules:
  0.0 171.1 jit_solution(17965243527822268533)
XLA Ops:
  0.6 1.3 fusion.52
  2.6 2.0 %compare_convert_fusion = (bf16[768]{0:T(1024)(128)(2,1)S(1)}, bf16[768]{0:T(1024)(128)(2,1)S(1)}) fusion(s32[768]{0:T(1024)} %param.27, s32[]{:T(128)} %bitcast.5, s32[]{:T(128)} %bitcast.4), kind=kLoop, calls=%fused_computation.63 | loop fusion | flops 3072 | bytes 6152 | tf_op jit(solution)/shard_map/convert_element_type | solution.py:135
  4.6 3.0 %fusion.10 = bf16[8,128,128]{2,1,0:T(8,128)(2,1)S(1)} fusion(bf16[768]{0:T(1024)(128)(2,1)S(1)} %get-tuple-element.94, bf16[768,1024]{1,0:T(8,128)(2,1)} %refs_2_.1, bf16[768,1024]{1,0:T(8,128)(2,1)} %refs_3_.1), kind=kOutput, calls=%fused_computation.20 | convolution fusion | flops 204603392 | bytes 3409408 | tf_op jit(solution)/shard_map/hta,htb->hab/dot_general | solution.py:140
  7.6 3.1 %collective-permute-start.1 = (bf16[1040,128]{1,0:T(8,128)(2,1)S(1)}, bf16[1040,128]{1,0:T(8,128)(2,1)S(1)}, u32[]{:S(2)}, u32[]{:S(2)}) collective-permute-start(bf16[1040,128]{1,0:T(8,128)(2,1)S(1)} %fusion.36), channel_id=1, source_target_pairs={{0,16},{8,24},{16,32},{24,40},{32,48},{40,56},{48,64},{56,72},{64,... | collective-permute-start | bytes 798728 | tf_op jit(solution)/shard_map/ppermute | solution.py:19
  10.8 4.0 %collective-permute-start = (bf16[1040,128]{1,0:T(8,128)(2,1)S(1)}, bf16[1040,128]{1,0:T(8,128)(2,1)S(1)}, u32[]{:S(2)}, u32[]{:S(2)}) collective-permute-start(bf16[1040,128]{1,0:T(8,128)(2,1)S(1)} %fusion.36), channel_id=1, source_target_pairs={{0,8},{8,16},{16,24},{24,32},{32,40},{40,48},{48,56},{56,64},{64,7... | collective-permute-start | bytes 798728 | tf_op jit(solution)/shard_map/ppermute | solution.py:19
  14.7 1.6 copy.36
  16.3 2.6 %collective-permute-done.1 = bf16[1040,128]{1,0:T(8,128)(2,1)S(1)} collective-permute-done((bf16[1040,128]{1,0:T(8,128)(2,1)S(1)}, bf16[1040,128]{1,0:T(8,128)(2,1)S(1)}, u32[]{:S(2)}, u32[]{:S(2)}) %collective-permute-start.1) | collective-permute-done | bytes 266272 | tf_op jit(solution)/shard_map/ppermute | solution.py:19
  22.4 3.1 %collective-permute-start.2 = (bf16[1040,128]{1,0:T(8,128)(2,1)S(1)}, bf16[1040,128]{1,0:T(8,128)(2,1)S(1)}, u32[]{:S(2)}, u32[]{:S(2)}) collective-permute-start(bf16[1040,128]{1,0:T(8,128)(2,1)S(1)} %fusion.42), channel_id=1, source_target_pairs={{0,16},{8,24},{16,32},{24,40},{32,48},{40,56},{48,64},{56,72},{64,... | collective-permute-start | bytes 798728 | tf_op jit(solution)/shard_map/ppermute | solution.py:19
  25.8 5.9 %collective-permute-done.2 = bf16[1040,128]{1,0:T(8,128)(2,1)S(1)} collective-permute-done((bf16[1040,128]{1,0:T(8,128)(2,1)S(1)}, bf16[1040,128]{1,0:T(8,128)(2,1)S(1)}, u32[]{:S(2)}, u32[]{:S(2)}) %collective-permute-start.2) | collective-permute-done | bytes 266272 | tf_op jit(solution)/shard_map/ppermute | solution.py:19
  34.4 3.3 %collective-permute-start.3 = (bf16[1040,128]{1,0:T(8,128)(2,1)S(1)}, bf16[1040,128]{1,0:T(8,128)(2,1)S(1)}, u32[]{:S(2)}, u32[]{:S(2)}) collective-permute-start(bf16[1040,128]{1,0:T(8,128)(2,1)S(1)} %fusion.41), channel_id=1, source_target_pairs={{0,32},{8,40},{16,48},{24,56},{32,64},{40,72},{48,80},{56,88},{64,... | collective-permute-start | bytes 798728 | tf_op jit(solution)/shard_map/ppermute | solution.py:19
  37.7 6.6 %multiply_convert_fusion.1 = bf16[8,768,768]{2,1,0:T(8,128)(2,1)} fusion(f32[768,768]{1,0:T(8,128)S(1)} %fusion.25, bf16[8,768,128]{1,2,0:T(8,128)(2,1)S(1)} %bitcast.113, bf16[768,1024]{1,0:T(8,128)(2,1)} %refs_3_.1), kind=kOutput, calls=%fused_computation.1 | convolution fusion | flops 1217396736 | bytes 14942208 | tf_op jit(solution)/shard_map/hta,hsa->hts/dot_general | solution.py:145
  47.0 2.9 %collective-permute-start.4 = (bf16[1040,128]{1,0:T(8,128)(2,1)S(1)}, bf16[1040,128]{1,0:T(8,128)(2,1)}, u32[]{:S(2)}, u32[]{:S(2)}) collective-permute-start(bf16[1040,128]{1,0:T(8,128)(2,1)S(1)} %fusion.43), channel_id=1, source_target_pairs={{0,64},{8,72},{16,80},{24,88},{32,96},{40,104},{48,112},{56,120},{... | collective-permute-start | bytes 798728 | tf_op jit(solution)/shard_map/ppermute | solution.py:19
  49.9 7.9 %fusion.5.refs_0_ = f32[8,768,128]{2,1,0:T(8,128)} fusion(bf16[8,768,768]{2,1,0:T(8,128)(2,1)} %multiply_convert_fusion.1, bf16[768,1024]{1,0:T(8,128)(2,1)S(1)} %copy-done.9), kind=kOutput, calls=%fused_computation.15 | convolution fusion | flops 1207959552 | bytes 14155776 | tf_op jit(solution)/shard_map/hts,hsb->htb/dot_general | solution.py:148
  60.0 1.2 slice.248
  62.5 1.9 %multiply_convert_fusion.4 = bf16[1024,128]{1,0:T(8,128)(2,1)} fusion(bf16[1040,128]{1,0:T(8,128)(2,1)} %collective-permute-done.4, f32[]{:T(128)S(6)} %convert_element_type.212, f32[]{:T(128)S(6)} %convert_element_type.223, f32[]{:T(128)S(6)} %convert_element_type.220, bf16[1040,128]{1,0:T(8,128)(2,1)S(1)} %collective-permute-done.3, ...), kind=kLoop, calls=%fused_computation.40 | loop fusion | flops 1966080 | bytes 1572884 | tf_op jit(solution)/shard_map/convert_element_type | solution.py:62
  64.5 6.3 %shard_map.93 = f32[768,1024]{1,0:T(8,128)} custom-call(f32[8,768,128]{2,1,0:T(8,128)} %fusion.5.refs_0_, bf16[768,1024]{1,0:T(8,128)(2,1)} %refs_1_.1, bf16[768,1]{1,0:T(8,128)(2,1)} %broadcast_in_dim.7.refs_2_, bf16[8,128,128]{2,1,0:T(8,128)(2,1)} %bitcast.116), custom_call_target="tpu_custom_call" | custom-call | tf_op jit(solution)/shard_map/pallas_call | solution.py:99
  70.8 3.2 %multiply_reduce_fusion.1 = (f32[768]{0:T(1024)S(1)}, f32[768]{0:T(1024)S(1)}) fusion(f32[768,1024]{1,0:T(8,128)} %shard_map.93, bf16[768,1024]{1,0:T(8,128)(2,1)} %param.25, f32[1024]{0:T(1024)S(1)} %copy-done.13), kind=kLoop, calls=%fused_computation.6 | loop fusion | flops 4717056 | bytes 4728832 | tf_op jit(solution)/shard_map/reduce_sum | solution.py:154
  74.1 1.7 %collective-permute-start.5 = (f32[2,768]{1,0:T(2,128)S(1)}, f32[2,768]{1,0:T(2,128)S(1)}, u32[]{:S(2)}, u32[]{:S(2)}) collective-permute-start(f32[2,768]{1,0:T(2,128)S(1)} %pad_maximum_fusion), channel_id=1, source_target_pairs={{0,1},{1,0},{2,3},{3,2},{4,5},{5,4},{6,7},{7,6},{8,9},{9,8},{10,11... | collective-permute-start | bytes 18440 | tf_op jit(solution)/shard_map/ppermute | solution.py:69
  76.8 3.1 %collective-permute-start.6 = (f32[2,768]{1,0:T(2,128)S(1)}, f32[2,768]{1,0:T(2,128)S(1)}, u32[]{:S(2)}, u32[]{:S(2)}) collective-permute-start(f32[2,768]{1,0:T(2,128)S(1)} %fusion.49), channel_id=1, source_target_pairs={{0,2},{1,3},{2,0},{3,1},{4,6},{5,7},{6,4},{7,5},{8,10},{9,11},{10,... | collective-permute-start | bytes 18440 | tf_op jit(solution)/shard_map/ppermute | solution.py:69
  80.9 6.2 %collective-permute-start.7 = (f32[2,768]{1,0:T(2,128)S(1)}, f32[2,768]{1,0:T(2,128)S(1)}, u32[]{:S(2)}, u32[]{:S(2)}) collective-permute-start(f32[2,768]{1,0:T(2,128)S(1)} %fusion.60), channel_id=1, source_target_pairs={{0,4},{1,5},{2,6},{3,7},{4,0},{5,1},{6,2},{7,3},{8,12},{9,13},{10,... | collective-permute-start | bytes 18440 | tf_op jit(solution)/shard_map/ppermute | solution.py:69
  88.2 3.5 %subtract_convert_fusion = (bf16[768,1024]{1,0:T(8,128)(2,1)S(1)}, bf16[768,1024]{1,0:T(8,128)(2,1)}) fusion(f32[768,1024]{1,0:T(8,128)S(1)} %copy-done, bf16[768,1024]{1,0:T(8,128)(2,1)} %param.25, f32[768]{0:T(1024)S(1)} %fusion.45, f32[768]{0:T(1024)S(1)} %get-tuple-element.91, f32[1024]{0:T(1024)S(1)} %copy-done.13), kind=kLoop, calls=%fused_computation.2 | loop fusion | flops 7077888 | bytes 7874560 | tf_op jit(solution)/shard_map/convert_element_type | solution.py:161
  92.4 3.9 %collective-permute-start.9 = (bf16[1040,128]{1,0:T(8,128)(2,1)S(1)}, bf16[1040,128]{1,0:T(8,128)(2,1)S(1)}, u32[]{:S(2)}, u32[]{:S(2)}) collective-permute-start(bf16[1040,128]{1,0:T(8,128)(2,1)S(1)} %fusion.37), channel_id=1, source_target_pairs={{16,0},{24,8},{32,16},{40,24},{48,32},{56,40},{64,48},{72,56},{80,... | collective-permute-start | bytes 798728 | tf_op jit(solution)/shard_map/ppermute | solution.py:19
  96.3 9.4 %collective-permute-start.8 = (bf16[1040,128]{1,0:T(8,128)(2,1)S(1)}, bf16[1040,128]{1,0:T(8,128)(2,1)S(1)}, u32[]{:S(2)}, u32[]{:S(2)}) collective-permute-start(bf16[1040,128]{1,0:T(8,128)(2,1)S(1)} %fusion.37), channel_id=1, source_target_pairs={{8,0},{16,8},{24,16},{32,24},{40,32},{48,40},{56,48},{64,56},{72,6... | collective-permute-start | bytes 798728 | tf_op jit(solution)/shard_map/ppermute | solution.py:19
  105.7 5.1 %multiply_convert_fusion = bf16[8,768,768]{2,1,0:T(8,128)(2,1)} fusion(f32[768,768]{1,0:T(8,128)S(1)} %copy-done.4, bf16[768,1024]{1,0:T(8,128)(2,1)S(1)} %get-tuple-element.92.refs_1_, bf16[768,1024]{1,0:T(8,128)(2,1)S(1)} %copy-done.10), kind=kOutput, calls=%fused_computation | convolution fusion | flops 1217396736 | bytes 14942208 | tf_op jit(solution)/shard_map/htb,hsb->hts/dot_general | solution.py:168
  114.6 3.9 %collective-permute-start.10 = (bf16[1040,128]{1,0:T(8,128)(2,1)S(1)}, bf16[1040,128]{1,0:T(8,128)(2,1)S(1)}, u32[]{:S(2)}, u32[]{:S(2)}) collective-permute-start(bf16[1040,128]{1,0:T(8,128)(2,1)S(1)} %fusion.39), channel_id=1, source_target_pairs={{16,0},{24,8},{32,16},{40,24},{48,32},{56,40},{64,48},{72,56},{80,... | collective-permute-start | bytes 798728 | tf_op jit(solution)/shard_map/ppermute | solution.py:19
  118.5 8.0 %fusion.6.refs_0_ = f32[8,768,128]{2,1,0:T(8,128)} fusion(bf16[8,768,768]{2,1,0:T(8,128)(2,1)} %multiply_convert_fusion, bf16[768,1024]{1,0:T(8,128)(2,1)S(1)} %copy-done.8), kind=kOutput, calls=%fused_computation.17 | convolution fusion | flops 1207959552 | bytes 14155776 | tf_op jit(solution)/shard_map/hts,hsa->hta/dot_general | solution.py:171
  129.1 2.8 %collective-permute-start.11 = (bf16[1040,128]{1,0:T(8,128)(2,1)S(1)}, bf16[1040,128]{1,0:T(8,128)(2,1)S(1)}, u32[]{:S(2)}, u32[]{:S(2)}) collective-permute-start(bf16[1040,128]{1,0:T(8,128)(2,1)S(1)} %fusion.38), channel_id=1, source_target_pairs={{32,0},{40,8},{48,16},{56,24},{64,32},{72,40},{80,48},{88,56},{96,... | collective-permute-start | bytes 798728 | tf_op jit(solution)/shard_map/ppermute | solution.py:19
  131.9 8.3 %fusion.3.refs_1_ = f32[8,768,128]{2,1,0:T(8,128)} fusion(bf16[8,768,768]{2,1,0:T(8,128)(2,1)} %multiply_convert_fusion.1, bf16[768,1024]{1,0:T(8,128)(2,1)S(1)} %copy-done.2), kind=kOutput, calls=%fused_computation.12 | convolution fusion | flops 1207959552 | bytes 14155776 | tf_op jit(solution)/shard_map/hts,htb->hsb/dot_general | solution.py:175
  143.0 2.7 %collective-permute-start.12 = (bf16[1040,128]{1,0:T(8,128)(2,1)S(1)}, bf16[1040,128]{1,0:T(8,128)(2,1)S(1)}, u32[]{:S(2)}, u32[]{:S(2)}) collective-permute-start(bf16[1040,128]{1,0:T(8,128)(2,1)S(1)} %fusion.40), channel_id=1, source_target_pairs={{64,0},{72,8},{80,16},{88,24},{96,32},{104,40},{112,48},{120,56},{... | collective-permute-start | bytes 798728 | tf_op jit(solution)/shard_map/ppermute | solution.py:19
  145.8 8.3 %fusion.53.refs_0_ = f32[8,768,128]{2,1,0:T(8,128)} fusion(bf16[8,768,768]{2,1,0:T(8,128)(2,1)} %multiply_convert_fusion, bf16[8,768,128]{1,2,0:T(8,128)(2,1)S(1)} %bitcast.115), kind=kOutput, calls=%fused_computation.74 | convolution fusion | flops 1207959552 | bytes 14155776 | tf_op jit(solution)/shard_map/hts,hta->hsa/dot_general | solution.py:174
  154.0 6.1 %shard_map.94 = bf16[768,1024]{1,0:T(8,128)(2,1)} custom-call(f32[8,768,128]{2,1,0:T(8,128)} %fusion.6.refs_0_, bf16[768,1024]{1,0:T(8,128)(2,1)} %copy-done.1, bf16[768,1]{1,0:T(8,128)(2,1)} %broadcast_in_dim.7.refs_2_, bf16[8,128,128]{2,1,0:T(8,128)(2,1)} %bitcast.117), custom_call_target="tpu_custom_call" | custom-call | tf_op jit(solution)/shard_map/pallas_call | solution.py:99
  163.6 7.5 %shard_map.95 = (bf16[768,1024]{1,0:T(8,128)(2,1)}, bf16[768,1024]{1,0:T(8,128)(2,1)}) custom-call(f32[8,768,128]{2,1,0:T(8,128)} %fusion.53.refs_0_, f32[8,768,128]{2,1,0:T(8,128)} %fusion.3.refs_1_, bf16[768,1024]{1,0:T(8,128)(2,1)} %refs_2_.1, bf16[768,1024]{1,0:T(8,128)(2,1)} %refs_3_.1, bf16[768,1]{1,0:T(8,128)(2,1)} %broadcast_in_dim.6.refs_4_, ...), custom_call_target="tpu_custom_call" | custom-call | tf_op jit(solution)/shard_map/pallas_call | solution.py:99
  (75 shorter events, 16.7 us)
Async XLA Ops:
  4.6 10.1 %copy-start.11 = (bf16[768,1024]{1,0:T(8,128)(2,1)S(1)}, bf16[768,1024]{1,0:T(8,128)(2,1)}, u32[]{:S(2)}) copy-start(bf16[768,1024]{1,0:T(8,128)(2,1)} %refs_1_.1) | copy-start | bytes 4718596
  7.6 17.9 %copy-start.12 = (s32[768]{0:T(1024)S(1)}, s32[768]{0:T(1024)}, u32[]{:S(2)}) copy-start(s32[768]{0:T(1024)} %param.27) | copy-start | bytes 9220
  7.6 11.3 %collective-permute-start.1 = (bf16[1040,128]{1,0:T(8,128)(2,1)S(1)}, bf16[1040,128]{1,0:T(8,128)(2,1)S(1)}, u32[]{:S(2)}, u32[]{:S(2)}) collective-permute-start(bf16[1040,128]{1,0:T(8,128)(2,1)S(1)} %fusion.36), channel_id=1, source_target_pairs={{0,16},{8,24},{16,32},{24,40},{32,48},{40,56},{48,64},{56,72},{64,... | collective-permute-start | bytes 798728 | tf_op jit(solution)/shard_map/ppermute | solution.py:19
  10.8 9.0 %collective-permute-start = (bf16[1040,128]{1,0:T(8,128)(2,1)S(1)}, bf16[1040,128]{1,0:T(8,128)(2,1)S(1)}, u32[]{:S(2)}, u32[]{:S(2)}) collective-permute-start(bf16[1040,128]{1,0:T(8,128)(2,1)S(1)} %fusion.36), channel_id=1, source_target_pairs={{0,8},{8,16},{16,24},{24,32},{32,40},{40,48},{48,56},{56,64},{64,7... | collective-permute-start | bytes 798728 | tf_op jit(solution)/shard_map/ppermute | solution.py:19
  22.4 9.3 %collective-permute-start.2 = (bf16[1040,128]{1,0:T(8,128)(2,1)S(1)}, bf16[1040,128]{1,0:T(8,128)(2,1)S(1)}, u32[]{:S(2)}, u32[]{:S(2)}) collective-permute-start(bf16[1040,128]{1,0:T(8,128)(2,1)S(1)} %fusion.42), channel_id=1, source_target_pairs={{0,16},{8,24},{16,32},{24,40},{32,48},{40,56},{48,64},{56,72},{64,... | collective-permute-start | bytes 798728 | tf_op jit(solution)/shard_map/ppermute | solution.py:19
  25.8 18.5 %copy-start.3 = (f32[768,768]{1,0:T(8,128)}, f32[768,768]{1,0:T(8,128)S(1)}, u32[]{:S(2)}) copy-start(f32[768,768]{1,0:T(8,128)S(1)} %fusion.25) | copy-start | bytes 7077892
  33.5 4.2 %copy-start.5 = (bf16[768,1024]{0,1:T(8,128)(2,1)S(1)}, bf16[768,1024]{0,1:T(8,128)(2,1)}, u32[]{:S(2)}) copy-start(bf16[768,1024]{0,1:T(8,128)(2,1)} %copy.36) | copy-start | bytes 4718596
  34.4 9.9 %collective-permute-start.3 = (bf16[1040,128]{1,0:T(8,128)(2,1)S(1)}, bf16[1040,128]{1,0:T(8,128)(2,1)S(1)}, u32[]{:S(2)}, u32[]{:S(2)}) collective-permute-start(bf16[1040,128]{1,0:T(8,128)(2,1)S(1)} %fusion.41), channel_id=1, source_target_pairs={{0,32},{8,40},{16,48},{24,56},{32,64},{40,72},{48,80},{56,88},{64,... | collective-permute-start | bytes 798728 | tf_op jit(solution)/shard_map/ppermute | solution.py:19
  44.3 5.6 %copy-start.9 = (bf16[768,1024]{1,0:T(8,128)(2,1)S(1)}, bf16[768,1024]{1,0:T(8,128)(2,1)}, u32[]{:S(2)}) copy-start(bf16[768,1024]{1,0:T(8,128)(2,1)} %refs_2_.1) | copy-start | bytes 4718596
  47.0 13.0 %collective-permute-start.4 = (bf16[1040,128]{1,0:T(8,128)(2,1)S(1)}, bf16[1040,128]{1,0:T(8,128)(2,1)}, u32[]{:S(2)}, u32[]{:S(2)}) collective-permute-start(bf16[1040,128]{1,0:T(8,128)(2,1)S(1)} %fusion.43), channel_id=1, source_target_pairs={{0,64},{8,72},{16,80},{24,88},{32,96},{40,104},{48,112},{56,120},{... | collective-permute-start | bytes 798728 | tf_op jit(solution)/shard_map/ppermute | solution.py:19
  64.5 6.3 %copy-start.13 = (f32[1024]{0:T(1024)S(1)}, f32[1024]{0:T(1024)}, u32[]{:S(2)}) copy-start(f32[1024]{0:T(1024)} %param.26) | copy-start | bytes 12292
  70.8 17.4 %copy-start = (f32[768,1024]{1,0:T(8,128)S(1)}, f32[768,1024]{1,0:T(8,128)}, u32[]{:S(2)}) copy-start(f32[768,1024]{1,0:T(8,128)} %shard_map.93) | copy-start | bytes 9437188
  74.1 2.7 %collective-permute-start.5 = (f32[2,768]{1,0:T(2,128)S(1)}, f32[2,768]{1,0:T(2,128)S(1)}, u32[]{:S(2)}, u32[]{:S(2)}) collective-permute-start(f32[2,768]{1,0:T(2,128)S(1)} %pad_maximum_fusion), channel_id=1, source_target_pairs={{0,1},{1,0},{2,3},{3,2},{4,5},{5,4},{6,7},{7,6},{8,9},{9,8},{10,11... | collective-permute-start | bytes 18440 | tf_op jit(solution)/shard_map/ppermute | solution.py:69
  76.8 4.1 %collective-permute-start.6 = (f32[2,768]{1,0:T(2,128)S(1)}, f32[2,768]{1,0:T(2,128)S(1)}, u32[]{:S(2)}, u32[]{:S(2)}) collective-permute-start(f32[2,768]{1,0:T(2,128)S(1)} %fusion.49), channel_id=1, source_target_pairs={{0,2},{1,3},{2,0},{3,1},{4,6},{5,7},{6,4},{7,5},{8,10},{9,11},{10,... | collective-permute-start | bytes 18440 | tf_op jit(solution)/shard_map/ppermute | solution.py:69
  80.9 7.3 %collective-permute-start.7 = (f32[2,768]{1,0:T(2,128)S(1)}, f32[2,768]{1,0:T(2,128)S(1)}, u32[]{:S(2)}, u32[]{:S(2)}) collective-permute-start(f32[2,768]{1,0:T(2,128)S(1)} %fusion.60), channel_id=1, source_target_pairs={{0,4},{1,5},{2,6},{3,7},{4,0},{5,1},{6,2},{7,3},{8,12},{9,13},{10,... | collective-permute-start | bytes 18440 | tf_op jit(solution)/shard_map/ppermute | solution.py:69
  88.2 3.6 %copy-start.6 = (bf16[768,1024]{0,1:T(8,128)(2,1)S(1)}, bf16[768,1024]{0,1:T(8,128)(2,1)}, u32[]{:S(2)}) copy-start(bf16[768,1024]{0,1:T(8,128)(2,1)} %copy.36) | copy-start | bytes 4718596
  91.8 13.9 %copy-start.1 = (bf16[768,1024]{1,0:T(8,128)(2,1)}, bf16[768,1024]{1,0:T(8,128)(2,1)S(1)}, u32[]{:S(2)}) copy-start(bf16[768,1024]{1,0:T(8,128)(2,1)S(1)} %get-tuple-element.92.refs_1_) | copy-start | bytes 4718596
  91.8 14.0 %copy-start.4 = (f32[768,768]{1,0:T(8,128)S(1)}, f32[768,768]{1,0:T(8,128)}, u32[]{:S(2)}) copy-start(f32[768,768]{1,0:T(8,128)} %copy-done.3) | copy-start | bytes 7077892
  91.8 14.0 %copy-start.10 = (bf16[768,1024]{1,0:T(8,128)(2,1)S(1)}, bf16[768,1024]{1,0:T(8,128)(2,1)}, u32[]{:S(2)}) copy-start(bf16[768,1024]{1,0:T(8,128)(2,1)} %refs_2_.1) | copy-start | bytes 4718596
  92.4 26.1 %copy-start.8 = (bf16[768,1024]{1,0:T(8,128)(2,1)S(1)}, bf16[768,1024]{1,0:T(8,128)(2,1)}, u32[]{:S(2)}) copy-start(bf16[768,1024]{1,0:T(8,128)(2,1)} %refs_3_.1) | copy-start | bytes 4718596
  92.4 18.4 %collective-permute-start.9 = (bf16[1040,128]{1,0:T(8,128)(2,1)S(1)}, bf16[1040,128]{1,0:T(8,128)(2,1)S(1)}, u32[]{:S(2)}, u32[]{:S(2)}) collective-permute-start(bf16[1040,128]{1,0:T(8,128)(2,1)S(1)} %fusion.37), channel_id=1, source_target_pairs={{16,0},{24,8},{32,16},{40,24},{48,32},{56,40},{64,48},{72,56},{80,... | collective-permute-start | bytes 798728 | tf_op jit(solution)/shard_map/ppermute | solution.py:19
  96.3 15.7 %collective-permute-start.8 = (bf16[1040,128]{1,0:T(8,128)(2,1)S(1)}, bf16[1040,128]{1,0:T(8,128)(2,1)S(1)}, u32[]{:S(2)}, u32[]{:S(2)}) collective-permute-start(bf16[1040,128]{1,0:T(8,128)(2,1)S(1)} %fusion.37), channel_id=1, source_target_pairs={{8,0},{16,8},{24,16},{32,24},{40,32},{48,40},{56,48},{64,56},{72,6... | collective-permute-start | bytes 798728 | tf_op jit(solution)/shard_map/ppermute | solution.py:19
  114.6 11.9 %collective-permute-start.10 = (bf16[1040,128]{1,0:T(8,128)(2,1)S(1)}, bf16[1040,128]{1,0:T(8,128)(2,1)S(1)}, u32[]{:S(2)}, u32[]{:S(2)}) collective-permute-start(bf16[1040,128]{1,0:T(8,128)(2,1)S(1)} %fusion.39), channel_id=1, source_target_pairs={{16,0},{24,8},{32,16},{40,24},{48,32},{56,40},{64,48},{72,56},{80,... | collective-permute-start | bytes 798728 | tf_op jit(solution)/shard_map/ppermute | solution.py:19
  126.5 5.4 %copy-start.2 = (bf16[768,1024]{1,0:T(8,128)(2,1)S(1)}, bf16[768,1024]{1,0:T(8,128)(2,1)}, u32[]{:S(2)}) copy-start(bf16[768,1024]{1,0:T(8,128)(2,1)} %copy-done.1) | copy-start | bytes 4718596
  129.1 11.3 %collective-permute-start.11 = (bf16[1040,128]{1,0:T(8,128)(2,1)S(1)}, bf16[1040,128]{1,0:T(8,128)(2,1)S(1)}, u32[]{:S(2)}, u32[]{:S(2)}) collective-permute-start(bf16[1040,128]{1,0:T(8,128)(2,1)S(1)} %fusion.38), channel_id=1, source_target_pairs={{32,0},{40,8},{48,16},{56,24},{64,32},{72,40},{80,48},{88,56},{96,... | collective-permute-start | bytes 798728 | tf_op jit(solution)/shard_map/ppermute | solution.py:19
  140.3 5.5 %copy-start.7 = (bf16[768,1024]{0,1:T(8,128)(2,1)S(1)}, bf16[768,1024]{0,1:T(8,128)(2,1)}, u32[]{:S(2)}) copy-start(bf16[768,1024]{0,1:T(8,128)(2,1)} %copy.36) | copy-start | bytes 4718596
  143.0 17.8 %collective-permute-start.12 = (bf16[1040,128]{1,0:T(8,128)(2,1)S(1)}, bf16[1040,128]{1,0:T(8,128)(2,1)S(1)}, u32[]{:S(2)}, u32[]{:S(2)}) collective-permute-start(bf16[1040,128]{1,0:T(8,128)(2,1)S(1)} %fusion.40), channel_id=1, source_target_pairs={{64,0},{72,8},{80,16},{88,24},{96,32},{104,40},{112,48},{120,56},{... | collective-permute-start | bytes 798728 | tf_op jit(solution)/shard_map/ppermute | solution.py:19

commit v9 on v8

--- a/solution.py
+++ b/solution.py
@@ -93,7 +93,8 @@
 
 def finished_all(locals_, rows_, mask, state, flips, kinds, interpret=False):
     heads, tokens, width = locals_[0].shape
-    block = 128 if tokens % 128 == 0 else tokens
+    size = 128 if len(flips) > 1 else 256
+    block = size if tokens % size == 0 else tokens
     local_spec = pl.BlockSpec((heads, block, width), lambda t: (0, t, 0))
     row_spec = pl.BlockSpec((block, heads * width), lambda t: (t, 0))
     return pl.pallas_call(
@@ -115,6 +116,46 @@
     return finished_all([local], [rows], mask, state, (flip,), (kind,), interpret)[0]
 
 
+def attend_body(local_ref, rows_ref, mask_ref, state_ref, grad_ref, gain_ref, out_ref, sums_ref):
+    width = local_ref.shape[2]
+    mask = mask_ref[...]
+    square = jnp.zeros((local_ref.shape[1], 1), jnp.float32)
+    cross = jnp.zeros((local_ref.shape[1], 1), jnp.float32)
+    for head in range(local_ref.shape[0]):
+        cols = slice(head * width, (head + 1) * width)
+        rows = rows_ref[:, cols] * mask
+        flat = local_ref[head] + jnp.dot(rows, state_ref[head], preferred_element_type=jnp.float32)
+        out_ref[:, cols] = flat
+        scaled = gain_ref[:, cols] * grad_ref[:, cols].astype(jnp.float32)
+        square = square + jnp.sum(flat * flat, axis=1, keepdims=True)
+        cross = cross + jnp.sum(scaled * flat, axis=1, keepdims=True)
+    sums_ref[...] = jnp.concatenate([square, cross], axis=1)
+
+
+def attended_with_sums(local, rows, mask, state, out_grad, gain, interpret=False):
+    heads, tokens, width = local.shape
+    block = 256 if tokens % 256 == 0 else tokens
+    row_spec = pl.BlockSpec((block, heads * width), lambda t: (t, 0))
+    return pl.pallas_call(
+        attend_body,
+        grid=(tokens // block,),
+        in_specs=[
+            pl.BlockSpec((heads, block, width), lambda t: (0, t, 0)),
+            row_spec,
+            pl.BlockSpec((block, 1), lambda t: (t, 0)),
+            pl.BlockSpec((heads, width, width), lambda t: (0, 0, 0)),
+            row_spec,
+            pl.BlockSpec((1, heads * width), lambda t: (0, 0)),
+        ],
+        out_specs=[row_spec, pl.BlockSpec((block, 2), lambda t: (t, 0))],
+        out_shape=[
+            jax.ShapeDtypeStruct((tokens, heads * width), jnp.float32),
+            jax.ShapeDtypeStruct((tokens, 2), jnp.float32),
+        ],
+        interpret=interpret,
+    )(local, rows, mask, state, out_grad, gain[None, :])
+
+
 def shards(queries, keys, values, out_grad, gain, doc_ids):
     tokens_here = queries.shape[0]
     heads_here = queries.shape[1] // HD
@@ -148,12 +189,12 @@
     attended_local = jnp.einsum(
         "hts,hsb->htb", scores, value_heads, preferred_element_type=jnp.float32
     )
-    flat = finished(attended_local, queries, first_mask, incoming, False, jnp.float32)
+    flat, row_sums = attended_with_sums(
+        attended_local, queries, first_mask, incoming, out_grad, gain
+    )
     scaled_grad = gain[None, :] * out_grad.astype(jnp.float32)
-    sums = group_sum(
-        jnp.stack([jnp.sum(flat * flat, axis=1), jnp.sum(scaled_grad * flat, axis=1)]), "tp"
-    )
-    square_sum, cross_sum = sums[0], sums[1]
+    sums = group_sum(row_sums, "tp")
+    square_sum, cross_sum = sums[:, 0], sums[:, 1]
     inverse = lax.rsqrt(square_sum / width_all + NORM_EPS)
     normed = (flat * inverse[:, None] * gain[None, :]).astype(jnp.bfloat16)
     delta = (

time: 174 us -> 211 us (1.21)
  waiting for transfers between devices: 11.9 us -> 35.8 us
  starting transfers between devices: 50 us -> 58.6 us
  other arithmetic: 16.9 us -> 19.1 us
    ppermute x3, waiting for transfers between devices: 2.24 us -> 26.6 us  [group_sum(): x = x + lax.ppermute(x, axis, [(i, i ^ step) for i in range(count)])]
    ppermute x10, starting transfers between devices: 39 us -> 47.7 us  [moved(): return lax.ppermute(x, axis, pairs)]
    pallas_call x3 -> x2, Pallas kernels: 20 us -> 12.3 us  [finished_all(): pl.pallas_call(lambda *refs: finish_body(*refs, flips=flips), grid=(token...]
    pallas_call x0 -> x1, Pallas kernels: none -> 5.98 us  [attended_with_sums(): pl.pallas_call(attend_body, grid=(tokens // block,), in_specs=[pl.BlockSp...]
    reduce_sum x1 -> x0, other arithmetic: 3.21 us -> none  [shards(): jnp.sum(flat * flat, axis=1)]
    convert_element_type x6, other arithmetic: 0.85 us -> 3.94 us  [carried(): total.astype(partial_type)]
    unnamed x28 -> x32, local copies, waits for them, and re-layouts: 0.06 us -> 2.19 us
  transfers between devices with their start and end apart: 13 -> 13, of which waited for: 8 -> 7; matrix products, arithmetic and copies ran while one was open for 29% -> 24% of each run, Pallas kernels for 4% -> 2%
where the time goes in v9:
time: 211 us; the launch traced here: 206 us
  starting transfers between devices  58.6 us (28%)
  matrix products  48.1 us (23%)
  waiting for transfers between devices  35.8 us (17%)
  other arithmetic  19.1 us (9%)
  Pallas kernels  18.3 us (9%)
  between operations  13.9 us (7%)
  local copies, waits for them, and re-layouts  12.6 us (6%)
    ppermute x10, starting transfers between devices, moved(): return lax.ppermute(x, axis, pairs)  47.7 us
    ppermute x3, waiting for transfers between devices, group_sum(): x = x + lax.ppermute(x, axis, [(i, i ^ step) for i in range(count)])  26.6 us
    pallas_call x2, Pallas kernels, finished_all(): pl.pallas_call(lambda *refs: finish_body(*refs, flips=flips), grid=(token...  12.3 us
    ppermute x3, starting transfers between devices, group_sum(): x = x + lax.ppermute(x, axis, [(i, i ^ step) for i in range(count)])  10.9 us
    ppermute x10, waiting for transfers between devices, moved(): return lax.ppermute(x, axis, pairs)  9.19 us
    dot_general x1, matrix products, shards(): jnp.einsum('hts,hsa->hta', dscores, key_heads, preferred_element_type=jnp...  8.41 us
    dot_general x1, matrix products, shards(): jnp.einsum('hts,htb->hsb', scores, delta_heads, preferred_element_type=jn...  8.34 us
    dot_general x1, matrix products, shards(): jnp.einsum('hts,hta->hsa', dscores, query_heads, preferred_element_type=j...  8.27 us
  transfers between devices with their start and end apart: 13, of which 7 were waited for; matrix products, arithmetic and copies ran while one was open for 24% of the time, Pallas kernels for 2%

profile of v9, /device:TPU:17, one launch (start us, length us, event | category | flops | bytes accessed | tf_op | source)
XLA Modules:
  0.0 206.5 jit_solution(7571277251744740101)
XLA Ops:
  2.6 2.0 compare_convert_fusion
  4.6 3.0 %fusion.10 = bf16[8,128,128]{2,1,0:T(8,128)(2,1)S(1)} fusion(bf16[768]{0:T(1024)(128)(2,1)S(1)} %get-tuple-element.96, bf16[768,1024]{1,0:T(8,128)(2,1)} %refs_2_.1, bf16[768,1024]{1,0:T(8,128)(2,1)} %refs_3_.1), kind=kOutput, calls=%fused_computation.17 | convolution fusion | flops 204603392 | bytes 3409408 | tf_op jit(solution)/shard_map/hta,htb->hab/dot_general | solution.py:181
  7.6 3.1 %collective-permute-start.1 = (bf16[1040,128]{1,0:T(8,128)(2,1)S(1)}, bf16[1040,128]{1,0:T(8,128)(2,1)S(1)}, u32[]{:S(2)}, u32[]{:S(2)}) collective-permute-start(bf16[1040,128]{1,0:T(8,128)(2,1)S(1)} %fusion.42), channel_id=1, source_target_pairs={{0,16},{8,24},{16,32},{24,40},{32,48},{40,56},{48,64},{56,72},{64,... | collective-permute-start | bytes 798728 | tf_op jit(solution)/shard_map/ppermute | solution.py:19
  10.8 4.0 %collective-permute-start = (bf16[1040,128]{1,0:T(8,128)(2,1)S(1)}, bf16[1040,128]{1,0:T(8,128)(2,1)S(1)}, u32[]{:S(2)}, u32[]{:S(2)}) collective-permute-start(bf16[1040,128]{1,0:T(8,128)(2,1)S(1)} %fusion.42), channel_id=1, source_target_pairs={{0,8},{8,16},{16,24},{24,32},{32,40},{40,48},{48,56},{56,64},{64,7... | collective-permute-start | bytes 798728 | tf_op jit(solution)/shard_map/ppermute | solution.py:19
  14.7 1.6 copy.50
  16.3 2.6 %collective-permute-done.1 = bf16[1040,128]{1,0:T(8,128)(2,1)S(1)} collective-permute-done((bf16[1040,128]{1,0:T(8,128)(2,1)S(1)}, bf16[1040,128]{1,0:T(8,128)(2,1)S(1)}, u32[]{:S(2)}, u32[]{:S(2)}) %collective-permute-start.1) | collective-permute-done | bytes 266272 | tf_op jit(solution)/shard_map/ppermute | solution.py:19
  22.4 3.1 %collective-permute-start.2 = (bf16[1040,128]{1,0:T(8,128)(2,1)S(1)}, bf16[1040,128]{1,0:T(8,128)(2,1)S(1)}, u32[]{:S(2)}, u32[]{:S(2)}) collective-permute-start(bf16[1040,128]{1,0:T(8,128)(2,1)S(1)} %fusion.48), channel_id=1, source_target_pairs={{0,16},{8,24},{16,32},{24,40},{32,48},{40,56},{48,64},{56,72},{64,... | collective-permute-start | bytes 798728 | tf_op jit(solution)/shard_map/ppermute | solution.py:19
  25.8 5.9 %collective-permute-done.2 = bf16[1040,128]{1,0:T(8,128)(2,1)S(1)} collective-permute-done((bf16[1040,128]{1,0:T(8,128)(2,1)S(1)}, bf16[1040,128]{1,0:T(8,128)(2,1)S(1)}, u32[]{:S(2)}, u32[]{:S(2)}) %collective-permute-start.2) | collective-permute-done | bytes 266272 | tf_op jit(solution)/shard_map/ppermute | solution.py:19
  34.4 3.3 %collective-permute-start.3 = (bf16[1040,128]{1,0:T(8,128)(2,1)S(1)}, bf16[1040,128]{1,0:T(8,128)(2,1)S(1)}, u32[]{:S(2)}, u32[]{:S(2)}) collective-permute-start(bf16[1040,128]{1,0:T(8,128)(2,1)S(1)} %fusion.47), channel_id=1, source_target_pairs={{0,32},{8,40},{16,48},{24,56},{32,64},{40,72},{48,80},{56,88},{64,... | collective-permute-start | bytes 798728 | tf_op jit(solution)/shard_map/ppermute | solution.py:19
  37.7 6.6 %multiply_convert_fusion.1 = bf16[8,768,768]{2,1,0:T(8,128)(2,1)} fusion(f32[768,768]{1,0:T(8,128)S(1)} %fusion.25, bf16[8,768,128]{1,2,0:T(8,128)(2,1)S(1)} %bitcast.114, bf16[768,1024]{1,0:T(8,128)(2,1)} %refs_3_.1), kind=kOutput, calls=%fused_computation.1 | convolution fusion | flops 1217396736 | bytes 14942208 | tf_op jit(solution)/shard_map/hta,hsa->hts/dot_general | solution.py:186
  46.9 2.9 %collective-permute-start.4 = (bf16[1040,128]{1,0:T(8,128)(2,1)S(1)}, bf16[1040,128]{1,0:T(8,128)(2,1)}, u32[]{:S(2)}, u32[]{:S(2)}) collective-permute-start(bf16[1040,128]{1,0:T(8,128)(2,1)S(1)} %fusion.49), channel_id=1, source_target_pairs={{0,64},{8,72},{16,80},{24,88},{32,96},{40,104},{48,112},{56,120},{... | collective-permute-start | bytes 798728 | tf_op jit(solution)/shard_map/ppermute | solution.py:19
  49.9 8.0 %fusion.5.local_ref = f32[8,768,128]{2,1,0:T(8,128)} fusion(bf16[8,768,768]{2,1,0:T(8,128)(2,1)} %multiply_convert_fusion.1, bf16[768,1024]{1,0:T(8,128)(2,1)S(1)} %copy-done.5), kind=kOutput, calls=%fused_computation.12 | convolution fusion | flops 1207959552 | bytes 14155776 | tf_op jit(solution)/shard_map/hts,hsb->htb/dot_general | solution.py:189
  62.5 2.0 multiply_convert_fusion.4
  64.4 6.0 %shard_map.93 = (f32[768,1024]{1,0:T(8,128)}, f32[768,2]{1,0:T(8,128)}) custom-call(f32[8,768,128]{2,1,0:T(8,128)} %fusion.5.local_ref, bf16[768,1024]{1,0:T(8,128)(2,1)} %rows_ref.1, bf16[768,1]{1,0:T(8,128)(2,1)} %broadcast_in_dim.10.mask_ref.refs_2_, bf16[8,128,128]{2,1,0:T(8,128)(2,1)} %bitcast.117, bf16[768,1024]{1,0:T(8,128)(2,1)} %grad_ref.1, ...), custom_call_target="tpu_custom_call" | custom-call | tf_op jit(solution)/shard_map/pallas_call | solution.py:139
  70.4 1.6 collective-permute-start.5
  72.0 5.4 %collective-permute-done.5 = f32[768,2]{1,0:T(8,128)S(1)} collective-permute-done((f32[768,2]{1,0:T(8,128)}, f32[768,2]{1,0:T(8,128)S(1)}, u32[]{:S(2)}, u32[]{:S(2)}) %collective-permute-start.5) | collective-permute-done | bytes 6176 | tf_op jit(solution)/shard_map/ppermute | solution.py:69
  78.5 3.1 %collective-permute-start.6 = (f32[768,2]{1,0:T(8,128)S(1)}, f32[768,2]{1,0:T(8,128)S(1)}, u32[]{:S(2)}, u32[]{:S(2)}) collective-permute-start(f32[768,2]{1,0:T(8,128)S(1)} %add.99), channel_id=1, source_target_pairs={{0,2},{1,3},{2,0},{3,1},{4,6},{5,7},{6,4},{7,5},{8,10},{9,11},{10,... | collective-permute-start | bytes 18440 | tf_op jit(solution)/shard_map/ppermute | solution.py:69
  81.5 9.4 %collective-permute-done.6 = f32[768,2]{1,0:T(8,128)S(1)} collective-permute-done((f32[768,2]{1,0:T(8,128)S(1)}, f32[768,2]{1,0:T(8,128)S(1)}, u32[]{:S(2)}, u32[]{:S(2)}) %collective-permute-start.6) | collective-permute-done | bytes 6176 | tf_op jit(solution)/shard_map/ppermute | solution.py:69
  91.0 6.2 %collective-permute-start.7 = (f32[768,2]{1,0:T(8,128)S(1)}, f32[768,2]{1,0:T(8,128)S(1)}, u32[]{:S(2)}, u32[]{:S(2)}) collective-permute-start(f32[768,2]{1,0:T(8,128)S(1)} %add.100), channel_id=1, source_target_pairs={{0,4},{1,5},{2,6},{3,7},{4,0},{5,1},{6,2},{7,3},{8,12},{9,13},{10,... | collective-permute-start | bytes 18440 | tf_op jit(solution)/shard_map/ppermute | solution.py:69
  98.0 11.8 %collective-permute-done.7 = f32[768,2]{1,0:T(8,128)S(1)} collective-permute-done((f32[768,2]{1,0:T(8,128)S(1)}, f32[768,2]{1,0:T(8,128)S(1)}, u32[]{:S(2)}, u32[]{:S(2)}) %collective-permute-start.7) | collective-permute-done | bytes 6176 | tf_op jit(solution)/shard_map/ppermute | solution.py:69
  110.3 4.5 %subtract_convert_fusion = (bf16[768,1024]{1,0:T(8,128)(2,1)S(1)}, bf16[768,1024]{1,0:T(8,128)(2,1)}) fusion(f32[768,1024]{1,0:T(8,128)} %get-tuple-element.88, bf16[768,1024]{1,0:T(8,128)(2,1)} %grad_ref.1, f32[768]{0:T(1024)S(1)} %get-tuple-element.92, f32[1024]{0:T(1024)S(1)} %copy-done.15, f32[768]{0:T(1024)S(1)} %get-tuple-element.93), kind=kLoop, calls=%fused_computation.2 | loop fusion | flops 7077888 | bytes 7874560 | tf_op jit(solution)/shard_map/convert_element_type | solution.py:202
  115.4 16.9 %collective-permute-start.9 = (bf16[1040,128]{1,0:T(8,128)(2,1)S(1)}, bf16[1040,128]{1,0:T(8,128)(2,1)S(1)}, u32[]{:S(2)}, u32[]{:S(2)}) collective-permute-start(bf16[1040,128]{1,0:T(8,128)(2,1)S(1)} %fusion.43), channel_id=1, source_target_pairs={{16,0},{24,8},{32,16},{40,24},{48,32},{56,40},{64,48},{72,56},{80,... | collective-permute-start | bytes 798728 | tf_op jit(solution)/shard_map/ppermute | solution.py:19
  132.4 4.0 %collective-permute-start.8 = (bf16[1040,128]{1,0:T(8,128)(2,1)S(1)}, bf16[1040,128]{1,0:T(8,128)(2,1)S(1)}, u32[]{:S(2)}, u32[]{:S(2)}) collective-permute-start(bf16[1040,128]{1,0:T(8,128)(2,1)S(1)} %fusion.43), channel_id=1, source_target_pairs={{8,0},{16,8},{24,16},{32,24},{40,32},{48,40},{56,48},{64,56},{72,6... | collective-permute-start | bytes 798728 | tf_op jit(solution)/shard_map/ppermute | solution.py:19
  136.4 5.0 %multiply_convert_fusion = bf16[8,768,768]{2,1,0:T(8,128)(2,1)} fusion(f32[768,768]{1,0:T(8,128)S(1)} %copy-done.2, bf16[768,1024]{1,0:T(8,128)(2,1)S(1)} %get-tuple-element.94.refs_1_, bf16[768,1024]{1,0:T(8,128)(2,1)S(1)} %copy-done.6), kind=kOutput, calls=%fused_computation | convolution fusion | flops 1217396736 | bytes 14942208 | tf_op jit(solution)/shard_map/htb,hsb->hts/dot_general | solution.py:209
  146.2 5.4 %collective-permute-start.10 = (bf16[1040,128]{1,0:T(8,128)(2,1)S(1)}, bf16[1040,128]{1,0:T(8,128)(2,1)S(1)}, u32[]{:S(2)}, u32[]{:S(2)}) collective-permute-start(bf16[1040,128]{1,0:T(8,128)(2,1)S(1)} %fusion.45), channel_id=1, source_target_pairs={{16,0},{24,8},{32,16},{40,24},{48,32},{56,40},{64,48},{72,56},{80,... | collective-permute-start | bytes 798728 | tf_op jit(solution)/shard_map/ppermute | solution.py:19
  151.6 8.4 %fusion.6.refs_0_ = f32[8,768,128]{2,1,0:T(8,128)} fusion(bf16[8,768,768]{2,1,0:T(8,128)(2,1)} %multiply_convert_fusion, bf16[768,1024]{1,0:T(8,128)(2,1)} %refs_3_.1), kind=kOutput, calls=%fused_computation.14 | convolution fusion | flops 1207959552 | bytes 14155776 | tf_op jit(solution)/shard_map/hts,hsa->hta/dot_general | solution.py:212
  164.3 1.9 collective-permute-start.11
  166.2 8.3 %fusion.3.refs_1_ = f32[8,768,128]{2,1,0:T(8,128)} fusion(bf16[8,768,768]{2,1,0:T(8,128)(2,1)} %multiply_convert_fusion.1, bf16[768,1024]{1,0:T(8,128)(2,1)S(1)} %get-tuple-element.94.refs_1_), kind=kOutput, calls=%fused_computation.9 | convolution fusion | flops 1207959552 | bytes 14155776 | tf_op jit(solution)/shard_map/hts,htb->hsb/dot_general | solution.py:216
  179.3 3.1 %collective-permute-start.12 = (bf16[1040,128]{1,0:T(8,128)(2,1)S(1)}, bf16[1040,128]{1,0:T(8,128)(2,1)S(1)}, u32[]{:S(2)}, u32[]{:S(2)}) collective-permute-start(bf16[1040,128]{1,0:T(8,128)(2,1)S(1)} %fusion.46), channel_id=1, source_target_pairs={{64,0},{72,8},{80,16},{88,24},{96,32},{104,40},{112,48},{120,56},{... | collective-permute-start | bytes 798728 | tf_op jit(solution)/shard_map/ppermute | solution.py:19
  182.4 8.3 %fusion.53.refs_0_ = f32[8,768,128]{2,1,0:T(8,128)} fusion(bf16[8,768,768]{2,1,0:T(8,128)(2,1)} %multiply_convert_fusion, bf16[8,768,128]{1,2,0:T(8,128)(2,1)S(1)} %bitcast.116), kind=kOutput, calls=%fused_computation.69 | convolution fusion | flops 1207959552 | bytes 14155776 | tf_op jit(solution)/shard_map/hts,hta->hsa/dot_general | solution.py:215
  190.7 4.8 %shard_map.94 = bf16[768,1024]{1,0:T(8,128)(2,1)} custom-call(f32[8,768,128]{2,1,0:T(8,128)} %fusion.6.refs_0_, bf16[768,1024]{1,0:T(8,128)(2,1)} %copy-done, bf16[768,1]{1,0:T(8,128)(2,1)} %broadcast_in_dim.10.mask_ref.refs_2_, bf16[8,128,128]{2,1,0:T(8,128)(2,1)} %bitcast.118), custom_call_target="tpu_custom_call" | custom-call | tf_op jit(solution)/shard_map/pallas_call | solution.py:100
  198.9 7.5 %shard_map.95 = (bf16[768,1024]{1,0:T(8,128)(2,1)}, bf16[768,1024]{1,0:T(8,128)(2,1)}) custom-call(f32[8,768,128]{2,1,0:T(8,128)} %fusion.53.refs_0_, f32[8,768,128]{2,1,0:T(8,128)} %fusion.3.refs_1_, bf16[768,1024]{1,0:T(8,128)(2,1)} %refs_2_.1, bf16[768,1024]{1,0:T(8,128)(2,1)} %refs_3_.1, bf16[768,1]{1,0:T(8,128)(2,1)} %broadcast_in_dim.9.refs_4_, ...), custom_call_target="tpu_custom_call" | custom-call | tf_op jit(solution)/shard_map/pallas_call | solution.py:100
  (74 shorter events, 23.1 us)
Async XLA Ops:
  4.6 10.1 %copy-start.7 = (bf16[768,1024]{1,0:T(8,128)(2,1)S(1)}, bf16[768,1024]{1,0:T(8,128)(2,1)}, u32[]{:S(2)}) copy-start(bf16[768,1024]{1,0:T(8,128)(2,1)} %rows_ref.1) | copy-start | bytes 4718596
  7.6 17.9 %copy-start.14 = (s32[768]{0:T(1024)S(1)}, s32[768]{0:T(1024)}, u32[]{:S(2)}) copy-start(s32[768]{0:T(1024)} %param.27) | copy-start | bytes 9220
  7.6 11.3 %collective-permute-start.1 = (bf16[1040,128]{1,0:T(8,128)(2,1)S(1)}, bf16[1040,128]{1,0:T(8,128)(2,1)S(1)}, u32[]{:S(2)}, u32[]{:S(2)}) collective-permute-start(bf16[1040,128]{1,0:T(8,128)(2,1)S(1)} %fusion.42), channel_id=1, source_target_pairs={{0,16},{8,24},{16,32},{24,40},{32,48},{40,56},{48,64},{56,72},{64,... | collective-permute-start | bytes 798728 | tf_op jit(solution)/shard_map/ppermute | solution.py:19
  10.8 9.0 %collective-permute-start = (bf16[1040,128]{1,0:T(8,128)(2,1)S(1)}, bf16[1040,128]{1,0:T(8,128)(2,1)S(1)}, u32[]{:S(2)}, u32[]{:S(2)}) collective-permute-start(bf16[1040,128]{1,0:T(8,128)(2,1)S(1)} %fusion.42), channel_id=1, source_target_pairs={{0,8},{8,16},{16,24},{24,32},{32,40},{40,48},{48,56},{56,64},{64,7... | collective-permute-start | bytes 798728 | tf_op jit(solution)/shard_map/ppermute | solution.py:19
  22.4 9.3 %collective-permute-start.2 = (bf16[1040,128]{1,0:T(8,128)(2,1)S(1)}, bf16[1040,128]{1,0:T(8,128)(2,1)S(1)}, u32[]{:S(2)}, u32[]{:S(2)}) collective-permute-start(bf16[1040,128]{1,0:T(8,128)(2,1)S(1)} %fusion.48), channel_id=1, source_target_pairs={{0,16},{8,24},{16,32},{24,40},{32,48},{40,56},{48,64},{56,72},{64,... | collective-permute-start | bytes 798728 | tf_op jit(solution)/shard_map/ppermute | solution.py:19
  25.8 18.4 %copy-start.1 = (f32[768,768]{1,0:T(8,128)}, f32[768,768]{1,0:T(8,128)S(1)}, u32[]{:S(2)}) copy-start(f32[768,768]{1,0:T(8,128)S(1)} %fusion.25) | copy-start | bytes 7077892
  33.5 4.2 %copy-start.3 = (bf16[768,1024]{0,1:T(8,128)(2,1)S(1)}, bf16[768,1024]{0,1:T(8,128)(2,1)}, u32[]{:S(2)}) copy-start(bf16[768,1024]{0,1:T(8,128)(2,1)} %copy.50) | copy-start | bytes 4718596
  34.4 9.8 %collective-permute-start.3 = (bf16[1040,128]{1,0:T(8,128)(2,1)S(1)}, bf16[1040,128]{1,0:T(8,128)(2,1)S(1)}, u32[]{:S(2)}, u32[]{:S(2)}) collective-permute-start(bf16[1040,128]{1,0:T(8,128)(2,1)S(1)} %fusion.47), channel_id=1, source_target_pairs={{0,32},{8,40},{16,48},{24,56},{32,64},{40,72},{48,80},{56,88},{64,... | collective-permute-start | bytes 798728 | tf_op jit(solution)/shard_map/ppermute | solution.py:19
  44.2 5.6 %copy-start.5 = (bf16[768,1024]{1,0:T(8,128)(2,1)S(1)}, bf16[768,1024]{1,0:T(8,128)(2,1)}, u32[]{:S(2)}) copy-start(bf16[768,1024]{1,0:T(8,128)(2,1)} %refs_2_.1) | copy-start | bytes 4718596
  46.9 13.0 %collective-permute-start.4 = (bf16[1040,128]{1,0:T(8,128)(2,1)S(1)}, bf16[1040,128]{1,0:T(8,128)(2,1)}, u32[]{:S(2)}, u32[]{:S(2)}) collective-permute-start(bf16[1040,128]{1,0:T(8,128)(2,1)S(1)} %fusion.49), channel_id=1, source_target_pairs={{0,64},{8,72},{16,80},{24,88},{32,96},{40,104},{48,112},{56,120},{... | collective-permute-start | bytes 798728 | tf_op jit(solution)/shard_map/ppermute | solution.py:19
  70.4 7.0 %collective-permute-start.5 = (f32[768,2]{1,0:T(8,128)}, f32[768,2]{1,0:T(8,128)S(1)}, u32[]{:S(2)}, u32[]{:S(2)}) collective-permute-start(f32[768,2]{1,0:T(8,128)} %get-tuple-element.89), channel_id=1, source_target_pairs={{0,1},{1,0},{2,3},{3,2},{4,5},{5,4},{6,7},{7,6},{8,9},{9,8},{10,11... | collective-permute-start | bytes 18440 | tf_op jit(solution)/shard_map/ppermute | solution.py:69
  78.5 31.8 %copy-start.15 = (f32[1024]{0:T(1024)S(1)}, f32[1024]{0:T(1024)}, u32[]{:S(2)}) copy-start(f32[1024]{0:T(1024)} %param.26) | copy-start | bytes 12292
  78.5 12.5 %collective-permute-start.6 = (f32[768,2]{1,0:T(8,128)S(1)}, f32[768,2]{1,0:T(8,128)S(1)}, u32[]{:S(2)}, u32[]{:S(2)}) collective-permute-start(f32[768,2]{1,0:T(8,128)S(1)} %add.99), channel_id=1, source_target_pairs={{0,2},{1,3},{2,0},{3,1},{4,6},{5,7},{6,4},{7,5},{8,10},{9,11},{10,... | collective-permute-start | bytes 18440 | tf_op jit(solution)/shard_map/ppermute | solution.py:69
  91.0 18.8 %collective-permute-start.7 = (f32[768,2]{1,0:T(8,128)S(1)}, f32[768,2]{1,0:T(8,128)S(1)}, u32[]{:S(2)}, u32[]{:S(2)}) collective-permute-start(f32[768,2]{1,0:T(8,128)S(1)} %add.100), channel_id=1, source_target_pairs={{0,4},{1,5},{2,6},{3,7},{4,0},{5,1},{6,2},{7,3},{8,12},{9,13},{10,... | collective-permute-start | bytes 18440 | tf_op jit(solution)/shard_map/ppermute | solution.py:69
  110.3 4.5 %copy-start.4 = (bf16[768,1024]{0,1:T(8,128)(2,1)S(1)}, bf16[768,1024]{0,1:T(8,128)(2,1)}, u32[]{:S(2)}) copy-start(bf16[768,1024]{0,1:T(8,128)(2,1)} %copy.50) | copy-start | bytes 4718596
  114.8 51.4 %copy-start = (bf16[768,1024]{1,0:T(8,128)(2,1)}, bf16[768,1024]{1,0:T(8,128)(2,1)S(1)}, u32[]{:S(2)}) copy-start(bf16[768,1024]{1,0:T(8,128)(2,1)S(1)} %get-tuple-element.94.refs_1_) | copy-start | bytes 4718596
  114.8 21.6 %copy-start.2 = (f32[768,768]{1,0:T(8,128)S(1)}, f32[768,768]{1,0:T(8,128)}, u32[]{:S(2)}) copy-start(f32[768,768]{1,0:T(8,128)} %copy-done.1) | copy-start | bytes 7077892
  114.8 21.6 %copy-start.6 = (bf16[768,1024]{1,0:T(8,128)(2,1)S(1)}, bf16[768,1024]{1,0:T(8,128)(2,1)}, u32[]{:S(2)}) copy-start(bf16[768,1024]{1,0:T(8,128)(2,1)} %refs_2_.1) | copy-start | bytes 4718596
  115.4 26.0 %collective-permute-start.9 = (bf16[1040,128]{1,0:T(8,128)(2,1)S(1)}, bf16[1040,128]{1,0:T(8,128)(2,1)S(1)}, u32[]{:S(2)}, u32[]{:S(2)}) collective-permute-start(bf16[1040,128]{1,0:T(8,128)(2,1)S(1)} %fusion.43), channel_id=1, source_target_pairs={{16,0},{24,8},{32,16},{40,24},{48,32},{56,40},{64,48},{72,56},{80,... | collective-permute-start | bytes 798728 | tf_op jit(solution)/shard_map/ppermute | solution.py:19
  132.4 9.6 %collective-permute-start.8 = (bf16[1040,128]{1,0:T(8,128)(2,1)S(1)}, bf16[1040,128]{1,0:T(8,128)(2,1)S(1)}, u32[]{:S(2)}, u32[]{:S(2)}) collective-permute-start(bf16[1040,128]{1,0:T(8,128)(2,1)S(1)} %fusion.43), channel_id=1, source_target_pairs={{8,0},{16,8},{24,16},{32,24},{40,32},{48,40},{56,48},{64,56},{72,6... | collective-permute-start | bytes 798728 | tf_op jit(solution)/shard_map/ppermute | solution.py:19
  142.0 0.7 copy-start.8
  146.2 13.8 %collective-permute-start.10 = (bf16[1040,128]{1,0:T(8,128)(2,1)S(1)}, bf16[1040,128]{1,0:T(8,128)(2,1)S(1)}, u32[]{:S(2)}, u32[]{:S(2)}) collective-permute-start(bf16[1040,128]{1,0:T(8,128)(2,1)S(1)} %fusion.45), channel_id=1, source_target_pairs={{16,0},{24,8},{32,16},{40,24},{48,32},{56,40},{64,48},{72,56},{80,... | collective-permute-start | bytes 798728 | tf_op jit(solution)/shard_map/ppermute | solution.py:19
  160.0 0.7 copy-start.10
  164.3 10.6 %collective-permute-start.11 = (bf16[1040,128]{1,0:T(8,128)(2,1)S(1)}, bf16[1040,128]{1,0:T(8,128)(2,1)S(1)}, u32[]{:S(2)}, u32[]{:S(2)}) collective-permute-start(bf16[1040,128]{1,0:T(8,128)(2,1)S(1)} %fusion.44), channel_id=1, source_target_pairs={{32,0},{40,8},{48,16},{56,24},{64,32},{72,40},{80,48},{88,56},{96,... | collective-permute-start | bytes 798728 | tf_op jit(solution)/shard_map/ppermute | solution.py:19
  174.9 0.7 copy-start.12
  179.3 16.9 %collective-permute-start.12 = (bf16[1040,128]{1,0:T(8,128)(2,1)S(1)}, bf16[1040,128]{1,0:T(8,128)(2,1)S(1)}, u32[]{:S(2)}, u32[]{:S(2)}) collective-permute-start(bf16[1040,128]{1,0:T(8,128)(2,1)S(1)} %fusion.46), channel_id=1, source_target_pairs={{64,0},{72,8},{80,16},{88,24},{96,32},{104,40},{112,48},{120,56},{... | collective-permute-start | bytes 798728 | tf_op jit(solution)/shard_map/ppermute | solution.py:19
  190.7 7.2 %copy-start.9 = (bf16[1040,128]{1,0:T(8,128)(2,1)S(1)}, bf16[1040,128]{1,0:T(8,128)(2,1)}, u32[]{:S(2)}) copy-start(bf16[1040,128]{1,0:T(8,128)(2,1)} %copy-done.8) | copy-start | bytes 798724
  190.7 7.2 %copy-start.11 = (bf16[1040,128]{1,0:T(8,128)(2,1)S(1)}, bf16[1040,128]{1,0:T(8,128)(2,1)}, u32[]{:S(2)}) copy-start(bf16[1040,128]{1,0:T(8,128)(2,1)} %copy-done.10) | copy-start | bytes 798724
  190.7 7.2 %copy-start.13 = (bf16[1040,128]{1,0:T(8,128)(2,1)S(1)}, bf16[1040,128]{1,0:T(8,128)(2,1)}, u32[]{:S(2)}) copy-start(bf16[1040,128]{1,0:T(8,128)(2,1)} %copy-done.12) | copy-start | bytes 798724

commit v10 on v9

--- a/solution.py
+++ b/solution.py
@@ -193,8 +193,8 @@
         attended_local, queries, first_mask, incoming, out_grad, gain
     )
     scaled_grad = gain[None, :] * out_grad.astype(jnp.float32)
-    sums = group_sum(row_sums, "tp")
-    square_sum, cross_sum = sums[:, 0], sums[:, 1]
+    sums = group_sum(row_sums.T, "tp")
+    square_sum, cross_sum = sums[0], sums[1]
     inverse = lax.rsqrt(square_sum / width_all + NORM_EPS)
     normed = (flat * inverse[:, None] * gain[None, :]).astype(jnp.bfloat16)
     delta = (

time: 211 us -> 211 us (level)
  no operation moved by 1% of the time
where the time goes in v10:
time: 211 us; the launch traced here: 206 us
  starting transfers between devices  58.6 us (28%)
  matrix products  48.1 us (23%)
  waiting for transfers between devices  35.8 us (17%)
  other arithmetic  19.1 us (9%)
  Pallas kernels  18.3 us (9%)
  between operations  13.9 us (7%)
  local copies, waits for them, and re-layouts  12.6 us (6%)
    ppermute x10, starting transfers between devices, moved(): return lax.ppermute(x, axis, pairs)  47.7 us
    ppermute x3, waiting for transfers between devices, group_sum(): x = x + lax.ppermute(x, axis, [(i, i ^ step) for i in range(count)])  26.6 us
    pallas_call x2, Pallas kernels, finished_all(): pl.pallas_call(lambda *refs: finish_body(*refs, flips=flips), grid=(token...  12.3 us
    ppermute x3, starting transfers between devices, group_sum(): x = x + lax.ppermute(x, axis, [(i, i ^ step) for i in range(count)])  10.9 us
    ppermute x10, waiting for transfers between devices, moved(): return lax.ppermute(x, axis, pairs)  9.19 us
    dot_general x1, matrix products, shards(): jnp.einsum('hts,hsa->hta', dscores, key_heads, preferred_element_type=jnp...  8.41 us
    dot_general x1, matrix products, shards(): jnp.einsum('hts,htb->hsb', scores, delta_heads, preferred_element_type=jn...  8.34 us
    dot_general x1, matrix products, shards(): jnp.einsum('hts,hta->hsa', dscores, query_heads, preferred_element_type=j...  8.27 us
  transfers between devices with their start and end apart: 13, of which 7 were waited for; matrix products, arithmetic and copies ran while one was open for 24% of the time, Pallas kernels for 2%

profile of v10, /device:TPU:17, one launch (start us, length us, event | category | flops | bytes accessed | tf_op | source)
XLA Modules:
  0.0 206.5 jit_solution(7860320348946147591)
XLA Ops:
  2.6 2.0 compare_convert_fusion
  4.6 3.0 %fusion.10 = bf16[8,128,128]{2,1,0:T(8,128)(2,1)S(1)} fusion(bf16[768]{0:T(1024)(128)(2,1)S(1)} %get-tuple-element.96, bf16[768,1024]{1,0:T(8,128)(2,1)} %refs_2_.1, bf16[768,1024]{1,0:T(8,128)(2,1)} %refs_3_.1), kind=kOutput, calls=%fused_computation.17 | convolution fusion | flops 204603392 | bytes 3409408 | tf_op jit(solution)/shard_map/hta,htb->hab/dot_general | solution.py:181
  7.6 3.1 %collective-permute-start.1 = (bf16[1040,128]{1,0:T(8,128)(2,1)S(1)}, bf16[1040,128]{1,0:T(8,128)(2,1)S(1)}, u32[]{:S(2)}, u32[]{:S(2)}) collective-permute-start(bf16[1040,128]{1,0:T(8,128)(2,1)S(1)} %fusion.39), channel_id=1, source_target_pairs={{0,16},{8,24},{16,32},{24,40},{32,48},{40,56},{48,64},{56,72},{64,... | collective-permute-start | bytes 798728 | tf_op jit(solution)/shard_map/ppermute | solution.py:19
  10.8 4.0 %collective-permute-start = (bf16[1040,128]{1,0:T(8,128)(2,1)S(1)}, bf16[1040,128]{1,0:T(8,128)(2,1)S(1)}, u32[]{:S(2)}, u32[]{:S(2)}) collective-permute-start(bf16[1040,128]{1,0:T(8,128)(2,1)S(1)} %fusion.39), channel_id=1, source_target_pairs={{0,8},{8,16},{16,24},{24,32},{32,40},{40,48},{48,56},{56,64},{64,7... | collective-permute-start | bytes 798728 | tf_op jit(solution)/shard_map/ppermute | solution.py:19
  14.7 1.6 copy.36
  16.3 2.6 %collective-permute-done.1 = bf16[1040,128]{1,0:T(8,128)(2,1)S(1)} collective-permute-done((bf16[1040,128]{1,0:T(8,128)(2,1)S(1)}, bf16[1040,128]{1,0:T(8,128)(2,1)S(1)}, u32[]{:S(2)}, u32[]{:S(2)}) %collective-permute-start.1) | collective-permute-done | bytes 266272 | tf_op jit(solution)/shard_map/ppermute | solution.py:19
  22.4 3.1 %collective-permute-start.2 = (bf16[1040,128]{1,0:T(8,128)(2,1)S(1)}, bf16[1040,128]{1,0:T(8,128)(2,1)S(1)}, u32[]{:S(2)}, u32[]{:S(2)}) collective-permute-start(bf16[1040,128]{1,0:T(8,128)(2,1)S(1)} %fusion.45), channel_id=1, source_target_pairs={{0,16},{8,24},{16,32},{24,40},{32,48},{40,56},{48,64},{56,72},{64,... | collective-permute-start | bytes 798728 | tf_op jit(solution)/shard_map/ppermute | solution.py:19
  25.8 5.9 %collective-permute-done.2 = bf16[1040,128]{1,0:T(8,128)(2,1)S(1)} collective-permute-done((bf16[1040,128]{1,0:T(8,128)(2,1)S(1)}, bf16[1040,128]{1,0:T(8,128)(2,1)S(1)}, u32[]{:S(2)}, u32[]{:S(2)}) %collective-permute-start.2) | collective-permute-done | bytes 266272 | tf_op jit(solution)/shard_map/ppermute | solution.py:19
  34.4 3.3 %collective-permute-start.3 = (bf16[1040,128]{1,0:T(8,128)(2,1)S(1)}, bf16[1040,128]{1,0:T(8,128)(2,1)S(1)}, u32[]{:S(2)}, u32[]{:S(2)}) collective-permute-start(bf16[1040,128]{1,0:T(8,128)(2,1)S(1)} %fusion.44), channel_id=1, source_target_pairs={{0,32},{8,40},{16,48},{24,56},{32,64},{40,72},{48,80},{56,88},{64,... | collective-permute-start | bytes 798728 | tf_op jit(solution)/shard_map/ppermute | solution.py:19
  37.7 6.6 %multiply_convert_fusion.1 = bf16[8,768,768]{2,1,0:T(8,128)(2,1)} fusion(f32[768,768]{1,0:T(8,128)S(1)} %fusion.25, bf16[8,768,128]{1,2,0:T(8,128)(2,1)S(1)} %bitcast.116, bf16[768,1024]{1,0:T(8,128)(2,1)} %refs_3_.1), kind=kOutput, calls=%fused_computation.1 | convolution fusion | flops 1217396736 | bytes 14942208 | tf_op jit(solution)/shard_map/hta,hsa->hts/dot_general | solution.py:186
  46.9 2.9 %collective-permute-start.4 = (bf16[1040,128]{1,0:T(8,128)(2,1)S(1)}, bf16[1040,128]{1,0:T(8,128)(2,1)}, u32[]{:S(2)}, u32[]{:S(2)}) collective-permute-start(bf16[1040,128]{1,0:T(8,128)(2,1)S(1)} %fusion.46), channel_id=1, source_target_pairs={{0,64},{8,72},{16,80},{24,88},{32,96},{40,104},{48,112},{56,120},{... | collective-permute-start | bytes 798728 | tf_op jit(solution)/shard_map/ppermute | solution.py:19
  49.9 8.0 %fusion.5.local_ref = f32[8,768,128]{2,1,0:T(8,128)} fusion(bf16[8,768,768]{2,1,0:T(8,128)(2,1)} %multiply_convert_fusion.1, bf16[768,1024]{1,0:T(8,128)(2,1)S(1)} %copy-done.5), kind=kOutput, calls=%fused_computation.12 | convolution fusion | flops 1207959552 | bytes 14155776 | tf_op jit(solution)/shard_map/hts,hsb->htb/dot_general | solution.py:189
  62.5 2.0 multiply_convert_fusion.4
  64.4 6.0 %shard_map.93 = (f32[768,1024]{1,0:T(8,128)}, f32[768,2]{1,0:T(8,128)}) custom-call(f32[8,768,128]{2,1,0:T(8,128)} %fusion.5.local_ref, bf16[768,1024]{1,0:T(8,128)(2,1)} %rows_ref.1, bf16[768,1]{1,0:T(8,128)(2,1)} %broadcast_in_dim.10.mask_ref.refs_2_, bf16[8,128,128]{2,1,0:T(8,128)(2,1)} %bitcast.119, bf16[768,1024]{1,0:T(8,128)(2,1)} %grad_ref.1, ...), custom_call_target="tpu_custom_call" | custom-call | tf_op jit(solution)/shard_map/pallas_call | solution.py:139
  70.4 1.6 collective-permute-start.5
  72.0 5.4 %collective-permute-done.5 = f32[2,768]{0,1:T(8,128)S(1)} collective-permute-done((f32[2,768]{0,1:T(8,128)}, f32[2,768]{0,1:T(8,128)S(1)}, u32[]{:S(2)}, u32[]{:S(2)}) %collective-permute-start.5) | collective-permute-done | bytes 6176 | tf_op jit(solution)/shard_map/ppermute | solution.py:69
  78.5 3.1 %collective-permute-start.6 = (f32[2,768]{0,1:T(8,128)S(1)}, f32[2,768]{0,1:T(8,128)S(1)}, u32[]{:S(2)}, u32[]{:S(2)}) collective-permute-start(f32[2,768]{0,1:T(8,128)S(1)} %bitcast_add_fusion), channel_id=1, source_target_pairs={{0,2},{1,3},{2,0},{3,1},{4,6},{5,7},{6,4},{7,5},{8,10},{9,11},{10,... | collective-permute-start | bytes 18440 | tf_op jit(solution)/shard_map/ppermute | solution.py:69
  81.5 9.4 %collective-permute-done.6 = f32[2,768]{0,1:T(8,128)S(1)} collective-permute-done((f32[2,768]{0,1:T(8,128)S(1)}, f32[2,768]{0,1:T(8,128)S(1)}, u32[]{:S(2)}, u32[]{:S(2)}) %collective-permute-start.6) | collective-permute-done | bytes 6176 | tf_op jit(solution)/shard_map/ppermute | solution.py:69
  91.0 6.2 %collective-permute-start.7 = (f32[2,768]{0,1:T(8,128)S(1)}, f32[2,768]{0,1:T(8,128)S(1)}, u32[]{:S(2)}, u32[]{:S(2)}) collective-permute-start(f32[2,768]{0,1:T(8,128)S(1)} %add.106), channel_id=1, source_target_pairs={{0,4},{1,5},{2,6},{3,7},{4,0},{5,1},{6,2},{7,3},{8,12},{9,13},{10,... | collective-permute-start | bytes 18440 | tf_op jit(solution)/shard_map/ppermute | solution.py:69
  98.0 11.8 %collective-permute-done.7 = f32[2,768]{0,1:T(8,128)S(1)} collective-permute-done((f32[2,768]{0,1:T(8,128)S(1)}, f32[2,768]{0,1:T(8,128)S(1)}, u32[]{:S(2)}, u32[]{:S(2)}) %collective-permute-start.7) | collective-permute-done | bytes 6176 | tf_op jit(solution)/shard_map/ppermute | solution.py:69
  110.3 4.5 %subtract_convert_fusion = (bf16[768,1024]{1,0:T(8,128)(2,1)S(1)}, bf16[768,1024]{1,0:T(8,128)(2,1)}) fusion(f32[768,1024]{1,0:T(8,128)} %get-tuple-element.88, bf16[768,1024]{1,0:T(8,128)(2,1)} %grad_ref.1, f32[768]{0:T(1024)S(1)} %fusion.48, f32[1024]{0:T(1024)S(1)} %copy-done.15, f32[768]{0:T(1024)S(1)} %get-tuple-element.93), kind=kLoop, calls=%fused_computation.2 | loop fusion | flops 7077888 | bytes 7874560 | tf_op jit(solution)/shard_map/convert_element_type | solution.py:202
  115.5 16.9 %collective-permute-start.9 = (bf16[1040,128]{1,0:T(8,128)(2,1)S(1)}, bf16[1040,128]{1,0:T(8,128)(2,1)S(1)}, u32[]{:S(2)}, u32[]{:S(2)}) collective-permute-start(bf16[1040,128]{1,0:T(8,128)(2,1)S(1)} %fusion.40), channel_id=1, source_target_pairs={{16,0},{24,8},{32,16},{40,24},{48,32},{56,40},{64,48},{72,56},{80,... | collective-permute-start | bytes 798728 | tf_op jit(solution)/shard_map/ppermute | solution.py:19
  132.4 4.0 %collective-permute-start.8 = (bf16[1040,128]{1,0:T(8,128)(2,1)S(1)}, bf16[1040,128]{1,0:T(8,128)(2,1)S(1)}, u32[]{:S(2)}, u32[]{:S(2)}) collective-permute-start(bf16[1040,128]{1,0:T(8,128)(2,1)S(1)} %fusion.40), channel_id=1, source_target_pairs={{8,0},{16,8},{24,16},{32,24},{40,32},{48,40},{56,48},{64,56},{72,6... | collective-permute-start | bytes 798728 | tf_op jit(solution)/shard_map/ppermute | solution.py:19
  136.4 5.0 %multiply_convert_fusion = bf16[8,768,768]{2,1,0:T(8,128)(2,1)} fusion(f32[768,768]{1,0:T(8,128)S(1)} %copy-done.2, bf16[768,1024]{1,0:T(8,128)(2,1)S(1)} %get-tuple-element.94.refs_1_, bf16[768,1024]{1,0:T(8,128)(2,1)S(1)} %copy-done.6), kind=kOutput, calls=%fused_computation | convolution fusion | flops 1217396736 | bytes 14942208 | tf_op jit(solution)/shard_map/htb,hsb->hts/dot_general | solution.py:209
  146.2 5.4 %collective-permute-start.10 = (bf16[1040,128]{1,0:T(8,128)(2,1)S(1)}, bf16[1040,128]{1,0:T(8,128)(2,1)S(1)}, u32[]{:S(2)}, u32[]{:S(2)}) collective-permute-start(bf16[1040,128]{1,0:T(8,128)(2,1)S(1)} %fusion.42), channel_id=1, source_target_pairs={{16,0},{24,8},{32,16},{40,24},{48,32},{56,40},{64,48},{72,56},{80,... | collective-permute-start | bytes 798728 | tf_op jit(solution)/shard_map/ppermute | solution.py:19
  151.6 8.4 %fusion.6.refs_0_ = f32[8,768,128]{2,1,0:T(8,128)} fusion(bf16[8,768,768]{2,1,0:T(8,128)(2,1)} %multiply_convert_fusion, bf16[768,1024]{1,0:T(8,128)(2,1)} %refs_3_.1), kind=kOutput, calls=%fused_computation.14 | convolution fusion | flops 1207959552 | bytes 14155776 | tf_op jit(solution)/shard_map/hts,hsa->hta/dot_general | solution.py:212
  164.3 1.9 collective-permute-start.11
  166.2 8.3 %fusion.3.refs_1_ = f32[8,768,128]{2,1,0:T(8,128)} fusion(bf16[8,768,768]{2,1,0:T(8,128)(2,1)} %multiply_convert_fusion.1, bf16[768,1024]{1,0:T(8,128)(2,1)S(1)} %get-tuple-element.94.refs_1_), kind=kOutput, calls=%fused_computation.9 | convolution fusion | flops 1207959552 | bytes 14155776 | tf_op jit(solution)/shard_map/hts,htb->hsb/dot_general | solution.py:216
  179.3 3.1 %collective-permute-start.12 = (bf16[1040,128]{1,0:T(8,128)(2,1)S(1)}, bf16[1040,128]{1,0:T(8,128)(2,1)S(1)}, u32[]{:S(2)}, u32[]{:S(2)}) collective-permute-start(bf16[1040,128]{1,0:T(8,128)(2,1)S(1)} %fusion.43), channel_id=1, source_target_pairs={{64,0},{72,8},{80,16},{88,24},{96,32},{104,40},{112,48},{120,56},{... | collective-permute-start | bytes 798728 | tf_op jit(solution)/shard_map/ppermute | solution.py:19
  182.5 8.3 %fusion.52.refs_0_ = f32[8,768,128]{2,1,0:T(8,128)} fusion(bf16[8,768,768]{2,1,0:T(8,128)(2,1)} %multiply_convert_fusion, bf16[8,768,128]{1,2,0:T(8,128)(2,1)S(1)} %bitcast.118), kind=kOutput, calls=%fused_computation.70 | convolution fusion | flops 1207959552 | bytes 14155776 | tf_op jit(solution)/shard_map/hts,hta->hsa/dot_general | solution.py:215
  190.7 4.8 %shard_map.94 = bf16[768,1024]{1,0:T(8,128)(2,1)} custom-call(f32[8,768,128]{2,1,0:T(8,128)} %fusion.6.refs_0_, bf16[768,1024]{1,0:T(8,128)(2,1)} %copy-done, bf16[768,1]{1,0:T(8,128)(2,1)} %broadcast_in_dim.10.mask_ref.refs_2_, bf16[8,128,128]{2,1,0:T(8,128)(2,1)} %bitcast.120), custom_call_target="tpu_custom_call" | custom-call | tf_op jit(solution)/shard_map/pallas_call | solution.py:100
  199.0 7.5 %shard_map.95 = (bf16[768,1024]{1,0:T(8,128)(2,1)}, bf16[768,1024]{1,0:T(8,128)(2,1)}) custom-call(f32[8,768,128]{2,1,0:T(8,128)} %fusion.52.refs_0_, f32[8,768,128]{2,1,0:T(8,128)} %fusion.3.refs_1_, bf16[768,1024]{1,0:T(8,128)(2,1)} %refs_2_.1, bf16[768,1024]{1,0:T(8,128)(2,1)} %refs_3_.1, bf16[768,1]{1,0:T(8,128)(2,1)} %broadcast_in_dim.9.refs_4_, ...), custom_call_target="tpu_custom_call" | custom-call | tf_op jit(solution)/shard_map/pallas_call | solution.py:100
  (75 shorter events, 23.1 us)
Async XLA Ops:
  4.6 10.1 %copy-start.7 = (bf16[768,1024]{1,0:T(8,128)(2,1)S(1)}, bf16[768,1024]{1,0:T(8,128)(2,1)}, u32[]{:S(2)}) copy-start(bf16[768,1024]{1,0:T(8,128)(2,1)} %rows_ref.1) | copy-start | bytes 4718596
  7.6 17.9 %copy-start.14 = (s32[768]{0:T(1024)S(1)}, s32[768]{0:T(1024)}, u32[]{:S(2)}) copy-start(s32[768]{0:T(1024)} %param.27) | copy-start | bytes 9220
  7.6 11.3 %collective-permute-start.1 = (bf16[1040,128]{1,0:T(8,128)(2,1)S(1)}, bf16[1040,128]{1,0:T(8,128)(2,1)S(1)}, u32[]{:S(2)}, u32[]{:S(2)}) collective-permute-start(bf16[1040,128]{1,0:T(8,128)(2,1)S(1)} %fusion.39), channel_id=1, source_target_pairs={{0,16},{8,24},{16,32},{24,40},{32,48},{40,56},{48,64},{56,72},{64,... | collective-permute-start | bytes 798728 | tf_op jit(solution)/shard_map/ppermute | solution.py:19
  10.8 9.0 %collective-permute-start = (bf16[1040,128]{1,0:T(8,128)(2,1)S(1)}, bf16[1040,128]{1,0:T(8,128)(2,1)S(1)}, u32[]{:S(2)}, u32[]{:S(2)}) collective-permute-start(bf16[1040,128]{1,0:T(8,128)(2,1)S(1)} %fusion.39), channel_id=1, source_target_pairs={{0,8},{8,16},{16,24},{24,32},{32,40},{40,48},{48,56},{56,64},{64,7... | collective-permute-start | bytes 798728 | tf_op jit(solution)/shard_map/ppermute | solution.py:19
  22.4 9.3 %collective-permute-start.2 = (bf16[1040,128]{1,0:T(8,128)(2,1)S(1)}, bf16[1040,128]{1,0:T(8,128)(2,1)S(1)}, u32[]{:S(2)}, u32[]{:S(2)}) collective-permute-start(bf16[1040,128]{1,0:T(8,128)(2,1)S(1)} %fusion.45), channel_id=1, source_target_pairs={{0,16},{8,24},{16,32},{24,40},{32,48},{40,56},{48,64},{56,72},{64,... | collective-permute-start | bytes 798728 | tf_op jit(solution)/shard_map/ppermute | solution.py:19
  25.8 18.4 %copy-start.1 = (f32[768,768]{1,0:T(8,128)}, f32[768,768]{1,0:T(8,128)S(1)}, u32[]{:S(2)}) copy-start(f32[768,768]{1,0:T(8,128)S(1)} %fusion.25) | copy-start | bytes 7077892
  33.5 4.2 %copy-start.3 = (bf16[768,1024]{0,1:T(8,128)(2,1)S(1)}, bf16[768,1024]{0,1:T(8,128)(2,1)}, u32[]{:S(2)}) copy-start(bf16[768,1024]{0,1:T(8,128)(2,1)} %copy.36) | copy-start | bytes 4718596
  34.4 9.8 %collective-permute-start.3 = (bf16[1040,128]{1,0:T(8,128)(2,1)S(1)}, bf16[1040,128]{1,0:T(8,128)(2,1)S(1)}, u32[]{:S(2)}, u32[]{:S(2)}) collective-permute-start(bf16[1040,128]{1,0:T(8,128)(2,1)S(1)} %fusion.44), channel_id=1, source_target_pairs={{0,32},{8,40},{16,48},{24,56},{32,64},{40,72},{48,80},{56,88},{64,... | collective-permute-start | bytes 798728 | tf_op jit(solution)/shard_map/ppermute | solution.py:19
  44.2 5.6 %copy-start.5 = (bf16[768,1024]{1,0:T(8,128)(2,1)S(1)}, bf16[768,1024]{1,0:T(8,128)(2,1)}, u32[]{:S(2)}) copy-start(bf16[768,1024]{1,0:T(8,128)(2,1)} %refs_2_.1) | copy-start | bytes 4718596
  46.9 13.0 %collective-permute-start.4 = (bf16[1040,128]{1,0:T(8,128)(2,1)S(1)}, bf16[1040,128]{1,0:T(8,128)(2,1)}, u32[]{:S(2)}, u32[]{:S(2)}) collective-permute-start(bf16[1040,128]{1,0:T(8,128)(2,1)S(1)} %fusion.46), channel_id=1, source_target_pairs={{0,64},{8,72},{16,80},{24,88},{32,96},{40,104},{48,112},{56,120},{... | collective-permute-start | bytes 798728 | tf_op jit(solution)/shard_map/ppermute | solution.py:19
  70.4 7.0 %collective-permute-start.5 = (f32[2,768]{0,1:T(8,128)}, f32[2,768]{0,1:T(8,128)S(1)}, u32[]{:S(2)}, u32[]{:S(2)}) collective-permute-start(f32[2,768]{0,1:T(8,128)} %bitcast.122), channel_id=1, source_target_pairs={{0,1},{1,0},{2,3},{3,2},{4,5},{5,4},{6,7},{7,6},{8,9},{9,8},{10,11... | collective-permute-start | bytes 18440 | tf_op jit(solution)/shard_map/ppermute | solution.py:69
  78.5 31.8 %copy-start.15 = (f32[1024]{0:T(1024)S(1)}, f32[1024]{0:T(1024)}, u32[]{:S(2)}) copy-start(f32[1024]{0:T(1024)} %param.26) | copy-start | bytes 12292
  78.5 12.5 %collective-permute-start.6 = (f32[2,768]{0,1:T(8,128)S(1)}, f32[2,768]{0,1:T(8,128)S(1)}, u32[]{:S(2)}, u32[]{:S(2)}) collective-permute-start(f32[2,768]{0,1:T(8,128)S(1)} %bitcast_add_fusion), channel_id=1, source_target_pairs={{0,2},{1,3},{2,0},{3,1},{4,6},{5,7},{6,4},{7,5},{8,10},{9,11},{10,... | collective-permute-start | bytes 18440 | tf_op jit(solution)/shard_map/ppermute | solution.py:69
  91.0 18.8 %collective-permute-start.7 = (f32[2,768]{0,1:T(8,128)S(1)}, f32[2,768]{0,1:T(8,128)S(1)}, u32[]{:S(2)}, u32[]{:S(2)}) collective-permute-start(f32[2,768]{0,1:T(8,128)S(1)} %add.106), channel_id=1, source_target_pairs={{0,4},{1,5},{2,6},{3,7},{4,0},{5,1},{6,2},{7,3},{8,12},{9,13},{10,... | collective-permute-start | bytes 18440 | tf_op jit(solution)/shard_map/ppermute | solution.py:69
  110.3 4.5 %copy-start.4 = (bf16[768,1024]{0,1:T(8,128)(2,1)S(1)}, bf16[768,1024]{0,1:T(8,128)(2,1)}, u32[]{:S(2)}) copy-start(bf16[768,1024]{0,1:T(8,128)(2,1)} %copy.36) | copy-start | bytes 4718596
  114.8 51.4 %copy-start = (bf16[768,1024]{1,0:T(8,128)(2,1)}, bf16[768,1024]{1,0:T(8,128)(2,1)S(1)}, u32[]{:S(2)}) copy-start(bf16[768,1024]{1,0:T(8,128)(2,1)S(1)} %get-tuple-element.94.refs_1_) | copy-start | bytes 4718596
  114.8 21.6 %copy-start.2 = (f32[768,768]{1,0:T(8,128)S(1)}, f32[768,768]{1,0:T(8,128)}, u32[]{:S(2)}) copy-start(f32[768,768]{1,0:T(8,128)} %copy-done.1) | copy-start | bytes 7077892
  114.8 21.6 %copy-start.6 = (bf16[768,1024]{1,0:T(8,128)(2,1)S(1)}, bf16[768,1024]{1,0:T(8,128)(2,1)}, u32[]{:S(2)}) copy-start(bf16[768,1024]{1,0:T(8,128)(2,1)} %refs_2_.1) | copy-start | bytes 4718596
  115.5 26.0 %collective-permute-start.9 = (bf16[1040,128]{1,0:T(8,128)(2,1)S(1)}, bf16[1040,128]{1,0:T(8,128)(2,1)S(1)}, u32[]{:S(2)}, u32[]{:S(2)}) collective-permute-start(bf16[1040,128]{1,0:T(8,128)(2,1)S(1)} %fusion.40), channel_id=1, source_target_pairs={{16,0},{24,8},{32,16},{40,24},{48,32},{56,40},{64,48},{72,56},{80,... | collective-permute-start | bytes 798728 | tf_op jit(solution)/shard_map/ppermute | solution.py:19
  132.4 9.6 %collective-permute-start.8 = (bf16[1040,128]{1,0:T(8,128)(2,1)S(1)}, bf16[1040,128]{1,0:T(8,128)(2,1)S(1)}, u32[]{:S(2)}, u32[]{:S(2)}) collective-permute-start(bf16[1040,128]{1,0:T(8,128)(2,1)S(1)} %fusion.40), channel_id=1, source_target_pairs={{8,0},{16,8},{24,16},{32,24},{40,32},{48,40},{56,48},{64,56},{72,6... | collective-permute-start | bytes 798728 | tf_op jit(solution)/shard_map/ppermute | solution.py:19
  142.0 0.7 copy-start.8
  146.2 13.8 %collective-permute-start.10 = (bf16[1040,128]{1,0:T(8,128)(2,1)S(1)}, bf16[1040,128]{1,0:T(8,128)(2,1)S(1)}, u32[]{:S(2)}, u32[]{:S(2)}) collective-permute-start(bf16[1040,128]{1,0:T(8,128)(2,1)S(1)} %fusion.42), channel_id=1, source_target_pairs={{16,0},{24,8},{32,16},{40,24},{48,32},{56,40},{64,48},{72,56},{80,... | collective-permute-start | bytes 798728 | tf_op jit(solution)/shard_map/ppermute | solution.py:19
  160.0 0.7 copy-start.10
  164.3 10.6 %collective-permute-start.11 = (bf16[1040,128]{1,0:T(8,128)(2,1)S(1)}, bf16[1040,128]{1,0:T(8,128)(2,1)S(1)}, u32[]{:S(2)}, u32[]{:S(2)}) collective-permute-start(bf16[1040,128]{1,0:T(8,128)(2,1)S(1)} %fusion.41), channel_id=1, source_target_pairs={{32,0},{40,8},{48,16},{56,24},{64,32},{72,40},{80,48},{88,56},{96,... | collective-permute-start | bytes 798728 | tf_op jit(solution)/shard_map/ppermute | solution.py:19
  174.9 0.7 copy-start.12
  179.3 16.8 %collective-permute-start.12 = (bf16[1040,128]{1,0:T(8,128)(2,1)S(1)}, bf16[1040,128]{1,0:T(8,128)(2,1)S(1)}, u32[]{:S(2)}, u32[]{:S(2)}) collective-permute-start(bf16[1040,128]{1,0:T(8,128)(2,1)S(1)} %fusion.43), channel_id=1, source_target_pairs={{64,0},{72,8},{80,16},{88,24},{96,32},{104,40},{112,48},{120,56},{... | collective-permute-start | bytes 798728 | tf_op jit(solution)/shard_map/ppermute | solution.py:19
  190.7 7.2 %copy-start.9 = (bf16[1040,128]{1,0:T(8,128)(2,1)S(1)}, bf16[1040,128]{1,0:T(8,128)(2,1)}, u32[]{:S(2)}) copy-start(bf16[1040,128]{1,0:T(8,128)(2,1)} %copy-done.8) | copy-start | bytes 798724
  190.7 7.2 %copy-start.11 = (bf16[1040,128]{1,0:T(8,128)(2,1)S(1)}, bf16[1040,128]{1,0:T(8,128)(2,1)}, u32[]{:S(2)}) copy-start(bf16[1040,128]{1,0:T(8,128)(2,1)} %copy-done.10) | copy-start | bytes 798724
  190.7 7.2 %copy-start.13 = (bf16[1040,128]{1,0:T(8,128)(2,1)S(1)}, bf16[1040,128]{1,0:T(8,128)(2,1)}, u32[]{:S(2)}) copy-start(bf16[1040,128]{1,0:T(8,128)(2,1)} %copy-done.12) | copy-start | bytes 798724

commit v11 on v8

--- a/solution.py
+++ b/solution.py
@@ -93,7 +93,8 @@
 
 def finished_all(locals_, rows_, mask, state, flips, kinds, interpret=False):
     heads, tokens, width = locals_[0].shape
-    block = 128 if tokens % 128 == 0 else tokens
+    size = 128 if len(flips) > 1 else 256
+    block = size if tokens % size == 0 else tokens
     local_spec = pl.BlockSpec((heads, block, width), lambda t: (0, t, 0))
     row_spec = pl.BlockSpec((block, heads * width), lambda t: (t, 0))
     return pl.pallas_call(

time: 174 us -> 171 us (0.983)
  Pallas kernels: 20 us -> 17.6 us
    pallas_call x3, Pallas kernels: 20 us -> 17.6 us  [finished_all(): pl.pallas_call(lambda *refs: finish_body(*refs, flips=flips), grid=(token...]
  transfers between devices with their start and end apart: 13 -> 13, of which waited for: 8 -> 8; matrix products, arithmetic and copies ran while one was open for 29% -> 29% of each run, Pallas kernels for 4% -> 3%
where the time goes in v11:
time: 171 us; the launch traced here: 169 us
  starting transfers between devices  50 us (29%)
  matrix products  47.8 us (28%)
  Pallas kernels  17.6 us (10%)
  other arithmetic  16.9 us (10%)
  between operations  14 us (8%)
  waiting for transfers between devices  11.9 us (7%)
  local copies, waits for them, and re-layouts  10.5 us (6%)
    ppermute x10, starting transfers between devices, moved(): return lax.ppermute(x, axis, pairs)  39 us
    pallas_call x3, Pallas kernels, finished_all(): pl.pallas_call(lambda *refs: finish_body(*refs, flips=flips), grid=(token...  17.6 us
    ppermute x3, starting transfers between devices, group_sum(): x = x + lax.ppermute(x, axis, [(i, i ^ step) for i in range(count)])  11 us
    ppermute x10, waiting for transfers between devices, moved(): return lax.ppermute(x, axis, pairs)  9.65 us
    dot_general x1, matrix products, shards(): jnp.einsum('hts,htb->hsb', scores, delta_heads, preferred_element_type=jn...  8.33 us
    dot_general x1, matrix products, shards(): jnp.einsum('hts,hta->hsa', dscores, query_heads, preferred_element_type=j...  8.29 us
    dot_general x1, matrix products, shards(): jnp.einsum('hts,hsa->hta', dscores, key_heads, preferred_element_type=jnp...  7.96 us
    dot_general x1, matrix products, shards(): jnp.einsum('hts,hsb->htb', scores, value_heads, preferred_element_type=jn...  7.94 us
  transfers between devices with their start and end apart: 13, of which 8 were waited for; matrix products, arithmetic and copies ran while one was open for 29% of the time, Pallas kernels for 3%

profile of v11, /device:TPU:17, one launch (start us, length us, event | category | flops | bytes accessed | tf_op | source)
XLA Modules:
  0.0 168.7 jit_solution(1200299025656256605)
XLA Ops:
  0.6 1.3 fusion.52
  2.6 2.0 %compare_convert_fusion = (bf16[768]{0:T(1024)(128)(2,1)S(1)}, bf16[768]{0:T(1024)(128)(2,1)S(1)}) fusion(s32[768]{0:T(1024)} %param.27, s32[]{:T(128)} %bitcast.5, s32[]{:T(128)} %bitcast.4), kind=kLoop, calls=%fused_computation.63 | loop fusion | flops 3072 | bytes 6152 | tf_op jit(solution)/shard_map/convert_element_type | solution.py:136
  4.6 3.0 %fusion.10 = bf16[8,128,128]{2,1,0:T(8,128)(2,1)S(1)} fusion(bf16[768]{0:T(1024)(128)(2,1)S(1)} %get-tuple-element.94, bf16[768,1024]{1,0:T(8,128)(2,1)} %refs_2_.1, bf16[768,1024]{1,0:T(8,128)(2,1)} %refs_3_.1), kind=kOutput, calls=%fused_computation.20 | convolution fusion | flops 204603392 | bytes 3409408 | tf_op jit(solution)/shard_map/hta,htb->hab/dot_general | solution.py:141
  7.6 3.1 %collective-permute-start.1 = (bf16[1040,128]{1,0:T(8,128)(2,1)S(1)}, bf16[1040,128]{1,0:T(8,128)(2,1)S(1)}, u32[]{:S(2)}, u32[]{:S(2)}) collective-permute-start(bf16[1040,128]{1,0:T(8,128)(2,1)S(1)} %fusion.36), channel_id=1, source_target_pairs={{0,16},{8,24},{16,32},{24,40},{32,48},{40,56},{48,64},{56,72},{64,... | collective-permute-start | bytes 798728 | tf_op jit(solution)/shard_map/ppermute | solution.py:19
  10.8 4.0 %collective-permute-start = (bf16[1040,128]{1,0:T(8,128)(2,1)S(1)}, bf16[1040,128]{1,0:T(8,128)(2,1)S(1)}, u32[]{:S(2)}, u32[]{:S(2)}) collective-permute-start(bf16[1040,128]{1,0:T(8,128)(2,1)S(1)} %fusion.36), channel_id=1, source_target_pairs={{0,8},{8,16},{16,24},{24,32},{32,40},{40,48},{48,56},{56,64},{64,7... | collective-permute-start | bytes 798728 | tf_op jit(solution)/shard_map/ppermute | solution.py:19
  14.7 1.6 copy.36
  16.3 2.6 %collective-permute-done.1 = bf16[1040,128]{1,0:T(8,128)(2,1)S(1)} collective-permute-done((bf16[1040,128]{1,0:T(8,128)(2,1)S(1)}, bf16[1040,128]{1,0:T(8,128)(2,1)S(1)}, u32[]{:S(2)}, u32[]{:S(2)}) %collective-permute-start.1) | collective-permute-done | bytes 266272 | tf_op jit(solution)/shard_map/ppermute | solution.py:19
  22.4 3.1 %collective-permute-start.2 = (bf16[1040,128]{1,0:T(8,128)(2,1)S(1)}, bf16[1040,128]{1,0:T(8,128)(2,1)S(1)}, u32[]{:S(2)}, u32[]{:S(2)}) collective-permute-start(bf16[1040,128]{1,0:T(8,128)(2,1)S(1)} %fusion.42), channel_id=1, source_target_pairs={{0,16},{8,24},{16,32},{24,40},{32,48},{40,56},{48,64},{56,72},{64,... | collective-permute-start | bytes 798728 | tf_op jit(solution)/shard_map/ppermute | solution.py:19
  25.8 5.9 %collective-permute-done.2 = bf16[1040,128]{1,0:T(8,128)(2,1)S(1)} collective-permute-done((bf16[1040,128]{1,0:T(8,128)(2,1)S(1)}, bf16[1040,128]{1,0:T(8,128)(2,1)S(1)}, u32[]{:S(2)}, u32[]{:S(2)}) %collective-permute-start.2) | collective-permute-done | bytes 266272 | tf_op jit(solution)/shard_map/ppermute | solution.py:19
  34.4 3.3 %collective-permute-start.3 = (bf16[1040,128]{1,0:T(8,128)(2,1)S(1)}, bf16[1040,128]{1,0:T(8,128)(2,1)S(1)}, u32[]{:S(2)}, u32[]{:S(2)}) collective-permute-start(bf16[1040,128]{1,0:T(8,128)(2,1)S(1)} %fusion.41), channel_id=1, source_target_pairs={{0,32},{8,40},{16,48},{24,56},{32,64},{40,72},{48,80},{56,88},{64,... | collective-permute-start | bytes 798728 | tf_op jit(solution)/shard_map/ppermute | solution.py:19
  37.7 6.6 %multiply_convert_fusion.1 = bf16[8,768,768]{2,1,0:T(8,128)(2,1)} fusion(f32[768,768]{1,0:T(8,128)S(1)} %fusion.25, bf16[8,768,128]{1,2,0:T(8,128)(2,1)S(1)} %bitcast.113, bf16[768,1024]{1,0:T(8,128)(2,1)} %refs_3_.1), kind=kOutput, calls=%fused_computation.1 | convolution fusion | flops 1217396736 | bytes 14942208 | tf_op jit(solution)/shard_map/hta,hsa->hts/dot_general | solution.py:146
  47.0 2.9 %collective-permute-start.4 = (bf16[1040,128]{1,0:T(8,128)(2,1)S(1)}, bf16[1040,128]{1,0:T(8,128)(2,1)}, u32[]{:S(2)}, u32[]{:S(2)}) collective-permute-start(bf16[1040,128]{1,0:T(8,128)(2,1)S(1)} %fusion.43), channel_id=1, source_target_pairs={{0,64},{8,72},{16,80},{24,88},{32,96},{40,104},{48,112},{56,120},{... | collective-permute-start | bytes 798728 | tf_op jit(solution)/shard_map/ppermute | solution.py:19
  49.9 7.9 %fusion.5.refs_0_ = f32[8,768,128]{2,1,0:T(8,128)} fusion(bf16[8,768,768]{2,1,0:T(8,128)(2,1)} %multiply_convert_fusion.1, bf16[768,1024]{1,0:T(8,128)(2,1)S(1)} %copy-done.9), kind=kOutput, calls=%fused_computation.15 | convolution fusion | flops 1207959552 | bytes 14155776 | tf_op jit(solution)/shard_map/hts,hsb->htb/dot_general | solution.py:149
  60.0 1.2 slice.248
  62.5 1.9 %multiply_convert_fusion.4 = bf16[1024,128]{1,0:T(8,128)(2,1)} fusion(bf16[1040,128]{1,0:T(8,128)(2,1)} %collective-permute-done.4, f32[]{:T(128)S(6)} %convert_element_type.212, f32[]{:T(128)S(6)} %convert_element_type.223, f32[]{:T(128)S(6)} %convert_element_type.220, bf16[1040,128]{1,0:T(8,128)(2,1)S(1)} %collective-permute-done.3, ...), kind=kLoop, calls=%fused_computation.40 | loop fusion | flops 1966080 | bytes 1572884 | tf_op jit(solution)/shard_map/convert_element_type | solution.py:62
  64.5 5.3 %shard_map.93 = f32[768,1024]{1,0:T(8,128)} custom-call(f32[8,768,128]{2,1,0:T(8,128)} %fusion.5.refs_0_, bf16[768,1024]{1,0:T(8,128)(2,1)} %refs_1_.1, bf16[768,1]{1,0:T(8,128)(2,1)} %broadcast_in_dim.7.refs_2_, bf16[8,128,128]{2,1,0:T(8,128)(2,1)} %bitcast.116), custom_call_target="tpu_custom_call" | custom-call | tf_op jit(solution)/shard_map/pallas_call | solution.py:100
  69.8 3.2 %multiply_reduce_fusion.1 = (f32[768]{0:T(1024)S(1)}, f32[768]{0:T(1024)S(1)}) fusion(f32[768,1024]{1,0:T(8,128)} %shard_map.93, bf16[768,1024]{1,0:T(8,128)(2,1)} %param.25, f32[1024]{0:T(1024)S(1)} %copy-done.13), kind=kLoop, calls=%fused_computation.6 | loop fusion | flops 4717056 | bytes 4728832 | tf_op jit(solution)/shard_map/reduce_sum | solution.py:155
  73.0 1.7 %collective-permute-start.5 = (f32[2,768]{1,0:T(2,128)S(1)}, f32[2,768]{1,0:T(2,128)S(1)}, u32[]{:S(2)}, u32[]{:S(2)}) collective-permute-start(f32[2,768]{1,0:T(2,128)S(1)} %pad_maximum_fusion), channel_id=1, source_target_pairs={{0,1},{1,0},{2,3},{3,2},{4,5},{5,4},{6,7},{7,6},{8,9},{9,8},{10,11... | collective-permute-start | bytes 18440 | tf_op jit(solution)/shard_map/ppermute | solution.py:69
  75.8 3.1 %collective-permute-start.6 = (f32[2,768]{1,0:T(2,128)S(1)}, f32[2,768]{1,0:T(2,128)S(1)}, u32[]{:S(2)}, u32[]{:S(2)}) collective-permute-start(f32[2,768]{1,0:T(2,128)S(1)} %fusion.49), channel_id=1, source_target_pairs={{0,2},{1,3},{2,0},{3,1},{4,6},{5,7},{6,4},{7,5},{8,10},{9,11},{10,... | collective-permute-start | bytes 18440 | tf_op jit(solution)/shard_map/ppermute | solution.py:69
  79.9 6.2 %collective-permute-start.7 = (f32[2,768]{1,0:T(2,128)S(1)}, f32[2,768]{1,0:T(2,128)S(1)}, u32[]{:S(2)}, u32[]{:S(2)}) collective-permute-start(f32[2,768]{1,0:T(2,128)S(1)} %fusion.60), channel_id=1, source_target_pairs={{0,4},{1,5},{2,6},{3,7},{4,0},{5,1},{6,2},{7,3},{8,12},{9,13},{10,... | collective-permute-start | bytes 18440 | tf_op jit(solution)/shard_map/ppermute | solution.py:69
  87.2 3.5 %subtract_convert_fusion = (bf16[768,1024]{1,0:T(8,128)(2,1)S(1)}, bf16[768,1024]{1,0:T(8,128)(2,1)}) fusion(f32[768,1024]{1,0:T(8,128)S(1)} %copy-done, bf16[768,1024]{1,0:T(8,128)(2,1)} %param.25, f32[768]{0:T(1024)S(1)} %fusion.45, f32[768]{0:T(1024)S(1)} %get-tuple-element.91, f32[1024]{0:T(1024)S(1)} %copy-done.13), kind=kLoop, calls=%fused_computation.2 | loop fusion | flops 7077888 | bytes 7874560 | tf_op jit(solution)/shard_map/convert_element_type | solution.py:162
  91.4 3.9 %collective-permute-start.9 = (bf16[1040,128]{1,0:T(8,128)(2,1)S(1)}, bf16[1040,128]{1,0:T(8,128)(2,1)S(1)}, u32[]{:S(2)}, u32[]{:S(2)}) collective-permute-start(bf16[1040,128]{1,0:T(8,128)(2,1)S(1)} %fusion.37), channel_id=1, source_target_pairs={{16,0},{24,8},{32,16},{40,24},{48,32},{56,40},{64,48},{72,56},{80,... | collective-permute-start | bytes 798728 | tf_op jit(solution)/shard_map/ppermute | solution.py:19
  95.3 9.4 %collective-permute-start.8 = (bf16[1040,128]{1,0:T(8,128)(2,1)S(1)}, bf16[1040,128]{1,0:T(8,128)(2,1)S(1)}, u32[]{:S(2)}, u32[]{:S(2)}) collective-permute-start(bf16[1040,128]{1,0:T(8,128)(2,1)S(1)} %fusion.37), channel_id=1, source_target_pairs={{8,0},{16,8},{24,16},{32,24},{40,32},{48,40},{56,48},{64,56},{72,6... | collective-permute-start | bytes 798728 | tf_op jit(solution)/shard_map/ppermute | solution.py:19
  104.7 5.1 %multiply_convert_fusion = bf16[8,768,768]{2,1,0:T(8,128)(2,1)} fusion(f32[768,768]{1,0:T(8,128)S(1)} %copy-done.4, bf16[768,1024]{1,0:T(8,128)(2,1)S(1)} %get-tuple-element.92.refs_1_, bf16[768,1024]{1,0:T(8,128)(2,1)S(1)} %copy-done.10), kind=kOutput, calls=%fused_computation | convolution fusion | flops 1217396736 | bytes 14942208 | tf_op jit(solution)/shard_map/htb,hsb->hts/dot_general | solution.py:169
  113.6 3.9 %collective-permute-start.10 = (bf16[1040,128]{1,0:T(8,128)(2,1)S(1)}, bf16[1040,128]{1,0:T(8,128)(2,1)S(1)}, u32[]{:S(2)}, u32[]{:S(2)}) collective-permute-start(bf16[1040,128]{1,0:T(8,128)(2,1)S(1)} %fusion.39), channel_id=1, source_target_pairs={{16,0},{24,8},{32,16},{40,24},{48,32},{56,40},{64,48},{72,56},{80,... | collective-permute-start | bytes 798728 | tf_op jit(solution)/shard_map/ppermute | solution.py:19
  117.5 8.0 %fusion.6.refs_0_ = f32[8,768,128]{2,1,0:T(8,128)} fusion(bf16[8,768,768]{2,1,0:T(8,128)(2,1)} %multiply_convert_fusion, bf16[768,1024]{1,0:T(8,128)(2,1)S(1)} %copy-done.8), kind=kOutput, calls=%fused_computation.17 | convolution fusion | flops 1207959552 | bytes 14155776 | tf_op jit(solution)/shard_map/hts,hsa->hta/dot_general | solution.py:172
  128.1 2.8 %collective-permute-start.11 = (bf16[1040,128]{1,0:T(8,128)(2,1)S(1)}, bf16[1040,128]{1,0:T(8,128)(2,1)S(1)}, u32[]{:S(2)}, u32[]{:S(2)}) collective-permute-start(bf16[1040,128]{1,0:T(8,128)(2,1)S(1)} %fusion.38), channel_id=1, source_target_pairs={{32,0},{40,8},{48,16},{56,24},{64,32},{72,40},{80,48},{88,56},{96,... | collective-permute-start | bytes 798728 | tf_op jit(solution)/shard_map/ppermute | solution.py:19
  130.9 8.3 %fusion.3.refs_1_ = f32[8,768,128]{2,1,0:T(8,128)} fusion(bf16[8,768,768]{2,1,0:T(8,128)(2,1)} %multiply_convert_fusion.1, bf16[768,1024]{1,0:T(8,128)(2,1)S(1)} %copy-done.2), kind=kOutput, calls=%fused_computation.12 | convolution fusion | flops 1207959552 | bytes 14155776 | tf_op jit(solution)/shard_map/hts,htb->hsb/dot_general | solution.py:176
  142.0 2.7 %collective-permute-start.12 = (bf16[1040,128]{1,0:T(8,128)(2,1)S(1)}, bf16[1040,128]{1,0:T(8,128)(2,1)S(1)}, u32[]{:S(2)}, u32[]{:S(2)}) collective-permute-start(bf16[1040,128]{1,0:T(8,128)(2,1)S(1)} %fusion.40), channel_id=1, source_target_pairs={{64,0},{72,8},{80,16},{88,24},{96,32},{104,40},{112,48},{120,56},{... | collective-permute-start | bytes 798728 | tf_op jit(solution)/shard_map/ppermute | solution.py:19
  144.7 8.3 %fusion.53.refs_0_ = f32[8,768,128]{2,1,0:T(8,128)} fusion(bf16[8,768,768]{2,1,0:T(8,128)(2,1)} %multiply_convert_fusion, bf16[8,768,128]{1,2,0:T(8,128)(2,1)S(1)} %bitcast.115), kind=kOutput, calls=%fused_computation.74 | convolution fusion | flops 1207959552 | bytes 14155776 | tf_op jit(solution)/shard_map/hts,hta->hsa/dot_general | solution.py:175
  153.0 4.7 %shard_map.94 = bf16[768,1024]{1,0:T(8,128)(2,1)} custom-call(f32[8,768,128]{2,1,0:T(8,128)} %fusion.6.refs_0_, bf16[768,1024]{1,0:T(8,128)(2,1)} %copy-done.1, bf16[768,1]{1,0:T(8,128)(2,1)} %broadcast_in_dim.7.refs_2_, bf16[8,128,128]{2,1,0:T(8,128)(2,1)} %bitcast.117), custom_call_target="tpu_custom_call" | custom-call | tf_op jit(solution)/shard_map/pallas_call | solution.py:100
  161.2 7.5 %shard_map.95 = (bf16[768,1024]{1,0:T(8,128)(2,1)}, bf16[768,1024]{1,0:T(8,128)(2,1)}) custom-call(f32[8,768,128]{2,1,0:T(8,128)} %fusion.53.refs_0_, f32[8,768,128]{2,1,0:T(8,128)} %fusion.3.refs_1_, bf16[768,1024]{1,0:T(8,128)(2,1)} %refs_2_.1, bf16[768,1024]{1,0:T(8,128)(2,1)} %refs_3_.1, bf16[768,1]{1,0:T(8,128)(2,1)} %broadcast_in_dim.6.refs_4_, ...), custom_call_target="tpu_custom_call" | custom-call | tf_op jit(solution)/shard_map/pallas_call | solution.py:100
  (75 shorter events, 16.7 us)
Async XLA Ops:
  4.6 10.1 %copy-start.11 = (bf16[768,1024]{1,0:T(8,128)(2,1)S(1)}, bf16[768,1024]{1,0:T(8,128)(2,1)}, u32[]{:S(2)}) copy-start(bf16[768,1024]{1,0:T(8,128)(2,1)} %refs_1_.1) | copy-start | bytes 4718596
  7.6 17.9 %copy-start.12 = (s32[768]{0:T(1024)S(1)}, s32[768]{0:T(1024)}, u32[]{:S(2)}) copy-start(s32[768]{0:T(1024)} %param.27) | copy-start | bytes 9220
  7.6 11.3 %collective-permute-start.1 = (bf16[1040,128]{1,0:T(8,128)(2,1)S(1)}, bf16[1040,128]{1,0:T(8,128)(2,1)S(1)}, u32[]{:S(2)}, u32[]{:S(2)}) collective-permute-start(bf16[1040,128]{1,0:T(8,128)(2,1)S(1)} %fusion.36), channel_id=1, source_target_pairs={{0,16},{8,24},{16,32},{24,40},{32,48},{40,56},{48,64},{56,72},{64,... | collective-permute-start | bytes 798728 | tf_op jit(solution)/shard_map/ppermute | solution.py:19
  10.8 9.0 %collective-permute-start = (bf16[1040,128]{1,0:T(8,128)(2,1)S(1)}, bf16[1040,128]{1,0:T(8,128)(2,1)S(1)}, u32[]{:S(2)}, u32[]{:S(2)}) collective-permute-start(bf16[1040,128]{1,0:T(8,128)(2,1)S(1)} %fusion.36), channel_id=1, source_target_pairs={{0,8},{8,16},{16,24},{24,32},{32,40},{40,48},{48,56},{56,64},{64,7... | collective-permute-start | bytes 798728 | tf_op jit(solution)/shard_map/ppermute | solution.py:19
  22.4 9.3 %collective-permute-start.2 = (bf16[1040,128]{1,0:T(8,128)(2,1)S(1)}, bf16[1040,128]{1,0:T(8,128)(2,1)S(1)}, u32[]{:S(2)}, u32[]{:S(2)}) collective-permute-start(bf16[1040,128]{1,0:T(8,128)(2,1)S(1)} %fusion.42), channel_id=1, source_target_pairs={{0,16},{8,24},{16,32},{24,40},{32,48},{40,56},{48,64},{56,72},{64,... | collective-permute-start | bytes 798728 | tf_op jit(solution)/shard_map/ppermute | solution.py:19
  25.8 18.5 %copy-start.3 = (f32[768,768]{1,0:T(8,128)}, f32[768,768]{1,0:T(8,128)S(1)}, u32[]{:S(2)}) copy-start(f32[768,768]{1,0:T(8,128)S(1)} %fusion.25) | copy-start | bytes 7077892
  33.5 4.2 %copy-start.5 = (bf16[768,1024]{0,1:T(8,128)(2,1)S(1)}, bf16[768,1024]{0,1:T(8,128)(2,1)}, u32[]{:S(2)}) copy-start(bf16[768,1024]{0,1:T(8,128)(2,1)} %copy.36) | copy-start | bytes 4718596
  34.4 9.9 %collective-permute-start.3 = (bf16[1040,128]{1,0:T(8,128)(2,1)S(1)}, bf16[1040,128]{1,0:T(8,128)(2,1)S(1)}, u32[]{:S(2)}, u32[]{:S(2)}) collective-permute-start(bf16[1040,128]{1,0:T(8,128)(2,1)S(1)} %fusion.41), channel_id=1, source_target_pairs={{0,32},{8,40},{16,48},{24,56},{32,64},{40,72},{48,80},{56,88},{64,... | collective-permute-start | bytes 798728 | tf_op jit(solution)/shard_map/ppermute | solution.py:19
  44.3 5.6 %copy-start.9 = (bf16[768,1024]{1,0:T(8,128)(2,1)S(1)}, bf16[768,1024]{1,0:T(8,128)(2,1)}, u32[]{:S(2)}) copy-start(bf16[768,1024]{1,0:T(8,128)(2,1)} %refs_2_.1) | copy-start | bytes 4718596
  47.0 13.0 %collective-permute-start.4 = (bf16[1040,128]{1,0:T(8,128)(2,1)S(1)}, bf16[1040,128]{1,0:T(8,128)(2,1)}, u32[]{:S(2)}, u32[]{:S(2)}) collective-permute-start(bf16[1040,128]{1,0:T(8,128)(2,1)S(1)} %fusion.43), channel_id=1, source_target_pairs={{0,64},{8,72},{16,80},{24,88},{32,96},{40,104},{48,112},{56,120},{... | collective-permute-start | bytes 798728 | tf_op jit(solution)/shard_map/ppermute | solution.py:19
  64.5 5.3 %copy-start.13 = (f32[1024]{0:T(1024)S(1)}, f32[1024]{0:T(1024)}, u32[]{:S(2)}) copy-start(f32[1024]{0:T(1024)} %param.26) | copy-start | bytes 12292
  69.8 17.4 %copy-start = (f32[768,1024]{1,0:T(8,128)S(1)}, f32[768,1024]{1,0:T(8,128)}, u32[]{:S(2)}) copy-start(f32[768,1024]{1,0:T(8,128)} %shard_map.93) | copy-start | bytes 9437188
  73.0 2.7 %collective-permute-start.5 = (f32[2,768]{1,0:T(2,128)S(1)}, f32[2,768]{1,0:T(2,128)S(1)}, u32[]{:S(2)}, u32[]{:S(2)}) collective-permute-start(f32[2,768]{1,0:T(2,128)S(1)} %pad_maximum_fusion), channel_id=1, source_target_pairs={{0,1},{1,0},{2,3},{3,2},{4,5},{5,4},{6,7},{7,6},{8,9},{9,8},{10,11... | collective-permute-start | bytes 18440 | tf_op jit(solution)/shard_map/ppermute | solution.py:69
  75.8 4.1 %collective-permute-start.6 = (f32[2,768]{1,0:T(2,128)S(1)}, f32[2,768]{1,0:T(2,128)S(1)}, u32[]{:S(2)}, u32[]{:S(2)}) collective-permute-start(f32[2,768]{1,0:T(2,128)S(1)} %fusion.49), channel_id=1, source_target_pairs={{0,2},{1,3},{2,0},{3,1},{4,6},{5,7},{6,4},{7,5},{8,10},{9,11},{10,... | collective-permute-start | bytes 18440 | tf_op jit(solution)/shard_map/ppermute | solution.py:69
  79.9 7.2 %collective-permute-start.7 = (f32[2,768]{1,0:T(2,128)S(1)}, f32[2,768]{1,0:T(2,128)S(1)}, u32[]{:S(2)}, u32[]{:S(2)}) collective-permute-start(f32[2,768]{1,0:T(2,128)S(1)} %fusion.60), channel_id=1, source_target_pairs={{0,4},{1,5},{2,6},{3,7},{4,0},{5,1},{6,2},{7,3},{8,12},{9,13},{10,... | collective-permute-start | bytes 18440 | tf_op jit(solution)/shard_map/ppermute | solution.py:69
  87.2 3.6 %copy-start.6 = (bf16[768,1024]{0,1:T(8,128)(2,1)S(1)}, bf16[768,1024]{0,1:T(8,128)(2,1)}, u32[]{:S(2)}) copy-start(bf16[768,1024]{0,1:T(8,128)(2,1)} %copy.36) | copy-start | bytes 4718596
  90.8 14.0 %copy-start.1 = (bf16[768,1024]{1,0:T(8,128)(2,1)}, bf16[768,1024]{1,0:T(8,128)(2,1)S(1)}, u32[]{:S(2)}) copy-start(bf16[768,1024]{1,0:T(8,128)(2,1)S(1)} %get-tuple-element.92.refs_1_) | copy-start | bytes 4718596
  90.8 14.0 %copy-start.4 = (f32[768,768]{1,0:T(8,128)S(1)}, f32[768,768]{1,0:T(8,128)}, u32[]{:S(2)}) copy-start(f32[768,768]{1,0:T(8,128)} %copy-done.3) | copy-start | bytes 7077892
  90.8 14.0 %copy-start.10 = (bf16[768,1024]{1,0:T(8,128)(2,1)S(1)}, bf16[768,1024]{1,0:T(8,128)(2,1)}, u32[]{:S(2)}) copy-start(bf16[768,1024]{1,0:T(8,128)(2,1)} %refs_2_.1) | copy-start | bytes 4718596
  91.4 26.1 %copy-start.8 = (bf16[768,1024]{1,0:T(8,128)(2,1)S(1)}, bf16[768,1024]{1,0:T(8,128)(2,1)}, u32[]{:S(2)}) copy-start(bf16[768,1024]{1,0:T(8,128)(2,1)} %refs_3_.1) | copy-start | bytes 4718596
  91.4 18.4 %collective-permute-start.9 = (bf16[1040,128]{1,0:T(8,128)(2,1)S(1)}, bf16[1040,128]{1,0:T(8,128)(2,1)S(1)}, u32[]{:S(2)}, u32[]{:S(2)}) collective-permute-start(bf16[1040,128]{1,0:T(8,128)(2,1)S(1)} %fusion.37), channel_id=1, source_target_pairs={{16,0},{24,8},{32,16},{40,24},{48,32},{56,40},{64,48},{72,56},{80,... | collective-permute-start | bytes 798728 | tf_op jit(solution)/shard_map/ppermute | solution.py:19
  95.3 15.7 %collective-permute-start.8 = (bf16[1040,128]{1,0:T(8,128)(2,1)S(1)}, bf16[1040,128]{1,0:T(8,128)(2,1)S(1)}, u32[]{:S(2)}, u32[]{:S(2)}) collective-permute-start(bf16[1040,128]{1,0:T(8,128)(2,1)S(1)} %fusion.37), channel_id=1, source_target_pairs={{8,0},{16,8},{24,16},{32,24},{40,32},{48,40},{56,48},{64,56},{72,6... | collective-permute-start | bytes 798728 | tf_op jit(solution)/shard_map/ppermute | solution.py:19
  113.6 11.9 %collective-permute-start.10 = (bf16[1040,128]{1,0:T(8,128)(2,1)S(1)}, bf16[1040,128]{1,0:T(8,128)(2,1)S(1)}, u32[]{:S(2)}, u32[]{:S(2)}) collective-permute-start(bf16[1040,128]{1,0:T(8,128)(2,1)S(1)} %fusion.39), channel_id=1, source_target_pairs={{16,0},{24,8},{32,16},{40,24},{48,32},{56,40},{64,48},{72,56},{80,... | collective-permute-start | bytes 798728 | tf_op jit(solution)/shard_map/ppermute | solution.py:19
  125.5 5.4 %copy-start.2 = (bf16[768,1024]{1,0:T(8,128)(2,1)S(1)}, bf16[768,1024]{1,0:T(8,128)(2,1)}, u32[]{:S(2)}) copy-start(bf16[768,1024]{1,0:T(8,128)(2,1)} %copy-done.1) | copy-start | bytes 4718596
  128.1 11.3 %collective-permute-start.11 = (bf16[1040,128]{1,0:T(8,128)(2,1)S(1)}, bf16[1040,128]{1,0:T(8,128)(2,1)S(1)}, u32[]{:S(2)}, u32[]{:S(2)}) collective-permute-start(bf16[1040,128]{1,0:T(8,128)(2,1)S(1)} %fusion.38), channel_id=1, source_target_pairs={{32,0},{40,8},{48,16},{56,24},{64,32},{72,40},{80,48},{88,56},{96,... | collective-permute-start | bytes 798728 | tf_op jit(solution)/shard_map/ppermute | solution.py:19
  139.3 5.5 %copy-start.7 = (bf16[768,1024]{0,1:T(8,128)(2,1)S(1)}, bf16[768,1024]{0,1:T(8,128)(2,1)}, u32[]{:S(2)}) copy-start(bf16[768,1024]{0,1:T(8,128)(2,1)} %copy.36) | copy-start | bytes 4718596
  142.0 16.4 %collective-permute-start.12 = (bf16[1040,128]{1,0:T(8,128)(2,1)S(1)}, bf16[1040,128]{1,0:T(8,128)(2,1)S(1)}, u32[]{:S(2)}, u32[]{:S(2)}) collective-permute-start(bf16[1040,128]{1,0:T(8,128)(2,1)S(1)} %fusion.40), channel_id=1, source_target_pairs={{64,0},{72,8},{80,16},{88,24},{96,32},{104,40},{112,48},{120,56},{... | collective-permute-start | bytes 798728 | tf_op jit(solution)/shard_map/ppermute | solution.py:19
